TPU v7x, 32 devices: a whole 2x2x4 slice. The times are simulated.
32 devices in a mesh: depth: 4 (over y, x), row: 4 (over z), col: 2 (over core).
Axes of the slice: x: 2, y: 2, z: 4, core: 2. Of those that a mesh axis runs over, the one named last changes fastest.
Arguments:
- phase: float32 [4, 1024, 512], P('depth', 'row', 'col'), may hold values from -4 to 4
- absorption: float32 [4, 1024, 512], P('depth', 'row', 'col'), may hold values from 0 to 0.5
- probe: float32 [2, 256, 256], replicated, may hold values from -4 to 4
- measured: float32 [4, 2, 4, 256, 256], P('row', 'col'), may hold values from 0 to 3
- offsets: int32 [4, 2, 4, 2], P('row', 'col'), may hold values from -128 to 896, as said below
Outputs:
- grad_phase: float32 [4, 1024, 512], P('depth', 'row', 'col')
- grad_absorption: float32 [4, 1024, 512], P('depth', 'row', 'col')
Inputs may be any that keep to these rules, and one draw needn't show every extreme that they name: `offsets`: probe k of tile (i, j) has row i * 256 + s, with s in -128 .. -1 when k mod 4 is 0 or 1 and in 1 .. 128 otherwise; its column is j * 256 + t, with t in -128 .. -1 for even k and in 1 .. 128 for odd k.
All inputs are finite; a program needn't handle non-finite values.
Results may differ from a plain program's by a relative error of at most 0.0003.
Values sent between devices are 32-bit elements; how exact they have to be, the bound alone decides.
No kernel may reach another device: no remote copies, remote signals or barrier semaphores. Data moves between devices by JAX's collectives and lax.ppermute only.
A program may use at most 128 MiB of HBM per device.

v0:
```python
import math

import jax
import jax.numpy as jnp
from jax import lax
from jax.sharding import PartitionSpec as P

exact_mode = lax.Precision.HIGHEST
wave_mode = lax.Precision.HIGH


def from_behind(value, axis, steps):
    count = lax.axis_size(axis)
    leading, last = (max(0, -steps), min(count, count - steps))
    return lax.ppermute(value, axis, [(source, source + steps) for source in range(leading, last)])


def with_halo(block, sides, width):
    for axis, dim in sides:
        count = lax.axis_size(axis)
        forward = [(i, i + 1) for i in range(count - 1)]
        backward = [(target, source) for source, target in forward]
        low = lax.ppermute(
            lax.slice_in_dim(block, block.shape[dim] - width, None, axis=dim), axis, forward
        )
        high = lax.ppermute(lax.slice_in_dim(block, 0, width, axis=dim), axis, backward)
        block = jnp.concatenate([low, block, high], axis=dim)
    return block


def matmul_exact(first, second):
    return jnp.dot(first, second, precision=exact_mode, preferred_element_type=jnp.float32)


def build_tables(width):
    index = jnp.arange(width, dtype=jnp.int32)
    product = index[:, None] * index[None, :] % width
    angle = product.astype(jnp.float32) * (2.0 * math.pi / width)
    cosine = jnp.cos(angle)
    sine = jnp.sin(angle)
    signed = jnp.where(index < width // 2, index, index - width)
    chirp = -(signed * signed % (4 * width)).astype(jnp.float32) * (2.0 * math.pi / (4 * width))
    chirp_re = jnp.cos(chirp)[None, :]
    chirp_im = jnp.sin(chirp)[None, :]
    scaled_re = cosine * chirp_re - sine * chirp_im
    scaled_im = cosine * chirp_im + sine * chirp_re
    fresnel_re = matmul_exact(scaled_re, cosine) + matmul_exact(scaled_im, sine)
    fresnel_im = matmul_exact(scaled_im, cosine) - matmul_exact(scaled_re, sine)
    fresnel = jnp.stack((fresnel_re, fresnel_im)) / width
    far_field = jnp.stack((cosine, -sine)) / math.sqrt(width)
    return (fresnel, far_field)


def adjoint_of(matrix):
    return jnp.stack((matrix[0].T, -matrix[1].T))


def left_product(matrix, waves, mode):
    return jnp.einsum(
        "ij,bjk->bik", matrix, waves, precision=mode, preferred_element_type=jnp.float32
    )


def right_product(waves, matrix, mode):
    return jnp.einsum(
        "bij,kj->bik", waves, matrix, precision=mode, preferred_element_type=jnp.float32
    )


def propagate(matrix, waves, mode):
    width = matrix.shape[1]
    tall = matrix.reshape(2 * width, width)
    batch = waves.shape[1]
    both = left_product(tall, waves.reshape((2 * batch,) + waves.shape[2:]), mode)
    from_real = both[:batch]
    from_imag = both[batch:]
    inner_re = from_real[:, :width] - from_imag[:, width:]
    inner_im = from_real[:, width:] + from_imag[:, :width]
    right = right_product(jnp.concatenate((inner_re, inner_im)), tall, mode)
    right_re = right[:batch]
    right_im = right[batch:]
    outer_re = right_re[:, :, :width] - right_im[:, :, width:]
    outer_im = right_re[:, :, width:] + right_im[:, :, :width]
    return jnp.stack((outer_re, outer_im))


def forward_layers(wave, slab, matrices):
    moved_list = []
    for layer in range(slab.shape[1]):
        trans_re = slab[0, layer]
        trans_im = slab[1, layer]
        moved = jnp.stack(
            (trans_re * wave[0] - trans_im * wave[1], trans_re * wave[1] + trans_im * wave[0])
        )
        moved_list.append(moved)
        wave = propagate(matrices[layer], moved, exact_mode)
    return (wave, jnp.stack(moved_list, axis=1))


def backward_layers(grad, slab, moved, adjoints):
    layers = slab.shape[1]
    phase_parts = [None] * layers
    absorb_parts = [None] * layers
    for layer in reversed(range(layers)):
        grad_moved = propagate(adjoints[layer], grad, wave_mode)
        moved_re = moved[0, layer]
        moved_im = moved[1, layer]
        phase_parts[layer] = grad_moved[1] * moved_re - grad_moved[0] * moved_im
        absorb_parts[layer] = -(grad_moved[0] * moved_re + grad_moved[1] * moved_im)
        trans_re = slab[0, layer]
        trans_im = slab[1, layer]
        grad = jnp.stack(
            (
                trans_re * grad_moved[0] + trans_im * grad_moved[1],
                trans_re * grad_moved[1] - trans_im * grad_moved[0],
            )
        )
    return (grad, jnp.stack(phase_parts), jnp.stack(absorb_parts))


def pass_rows_all(strip, steps):
    return from_behind(strip, "row", steps)


def pass_cols_all(strip, steps):
    return from_behind(strip, "col", steps)


def fold_rows(grid, rim, mover):
    inner = grid.shape[2] - 2 * rim
    from_above = mover(grid[:, :, inner + rim :], 1)
    from_below = mover(grid[:, :, :rim], -1)
    core = grid[:, :, rim : rim + inner]
    core = core.at[:, :, :rim].add(from_above)
    return core.at[:, :, inner - rim :].add(from_below)


def fold_cols(grid, rim, mover):
    inner = grid.shape[3] - 2 * rim
    from_left = mover(grid[:, :, :, inner + rim :], 1)
    from_right = mover(grid[:, :, :, :rim], -1)
    core = grid[:, :, :, rim : rim + inner]
    core = core.at[:, :, :, :rim].add(from_left)
    return core.at[:, :, :, inner - rim :].add(from_right)


def fold_both(grid, rim, row_mover, col_mover):
    return fold_rows(fold_cols(grid, rim, col_mover), rim, row_mover)


def to_transmit(extended):
    damping = jnp.exp(-extended[1])
    return jnp.stack((damping * jnp.cos(extended[0]), damping * jnp.sin(extended[0])))


def place(patch, row, col, frame):
    height, span = frame
    extra_rows = height - patch.shape[-2]
    extra_cols = span - patch.shape[-1]
    padded = jnp.pad(patch, ((0, 0), (0, 0), (extra_rows, extra_rows), (extra_cols, extra_cols)))
    anchor = jnp.zeros((), jnp.int32)
    start = (anchor, anchor, extra_rows - row, extra_cols - col)
    return lax.dynamic_slice(padded, start, patch.shape[:2] + (height, span))


def per_device(phase, absorption, probe, measured, offsets):
    layers, tile_rows, tile_cols = phase.shape
    width = probe.shape[1]
    rim = width // 2
    probes = offsets.shape[2]
    depth_count = lax.axis_size("depth")
    depth_index = lax.axis_index("depth")
    row_index = lax.axis_index("row")
    col_index = lax.axis_index("col")
    corners = offsets[0, 0]
    row_starts = corners[:, 0] - row_index * tile_rows + rim
    col_starts = corners[:, 1] - col_index * tile_cols + rim
    row_starts = [jnp.clip(row_starts[k], 0, 2 * rim + tile_rows - width) for k in range(probes)]
    col_starts = [jnp.clip(col_starts[k], 0, 2 * rim + tile_cols - width) for k in range(probes)]
    stacked = jnp.stack((phase, absorption))
    row_starts, col_starts, stacked = lax.optimization_barrier((row_starts, col_starts, stacked))
    extended = with_halo(stacked, (("row", 2), ("col", 3)), rim)
    anchor = jnp.zeros((), jnp.int32)
    fresnel, far_field = build_tables(width)
    share = probes // depth_count
    first = depth_index * share
    cut = jnp.stack(
        [
            lax.dynamic_slice(
                extended, (anchor, anchor, row_starts[k], col_starts[k]), (2, layers, width, width)
            )
            for k in range(probes)
        ],
        axis=2,
    )
    gathered = lax.all_to_all(cut, "depth", 2, 1, tiled=True)
    windows = to_transmit(gathered)
    total_layers = windows.shape[1]
    matrices = [fresnel] * (total_layers - 1) + [far_field]
    adjoints = [adjoint_of(matrix) for matrix in matrices]
    start_wave = probe[:, None]
    far_wave, moved = forward_layers(start_wave, windows, matrices)
    target = lax.dynamic_slice_in_dim(measured[0, 0], first, share)
    power = far_wave[0] ** 2 + far_wave[1] ** 2
    detector = far_wave * (0.25 * (power - target))[None]
    unused, phase_grad, absorb_grad = backward_layers(detector, windows, moved, adjoints)
    parts = jnp.stack((phase_grad, absorb_grad))
    returned = lax.all_to_all(parts, "depth", 1, 2, tiled=True)
    grid = jnp.zeros((2, layers) + extended.shape[2:], jnp.float32)
    for k in range(probes):
        grid = grid + place(returned[:, :, k], row_starts[k], col_starts[k], extended.shape[2:])
    owned = fold_both(grid, rim, pass_rows_all, pass_cols_all)
    return (owned[0], owned[1])


def solution(mesh):
    return jax.shard_map(
        per_device,
        mesh=mesh,
        in_specs=(
            P("depth", "row", "col"),
            P("depth", "row", "col"),
            P(),
            P("row", "col", None, None, None),
            P("row", "col", None, None),
        ),
        out_specs=(P("depth", "row", "col"), P("depth", "row", "col")),
        check_vma=False,
    )
```

profile of v0, /device:TPU:0, one launch (start us, length us, event | category | flops | bytes accessed | tf_op | source)
XLA Modules:
  0.0 139.7 jit_solution(9959872649002636950)
XLA Ops:
  7.1 1.1 pad_maximum_fusion.3
  8.3 4.9 %collective-permute-start = (f32[2,1,128,256]{3,2,1,0:T(8,128)S(1)}, f32[2,1,128,256]{3,2,1,0:T(8,128)S(1)}, u32[]{:S(2)}, u32[]{:S(2)}) collective-permute-start(f32[2,1,128,256]{3,2,1,0:T(8,128)S(1)} %get-tuple-element.146), channel_id=1, source_target_pairs={{0,2},{2,4},{4,6},{1,3},{3,5},{5,7},{8,10},{10,12},{12,14},{9,11},... | collective-permute-start | bytes 786440 | tf_op jit(solution)/shard_map/ppermute | solution.py:23
  13.2 1.3 collective-permute-start.1
  14.5 4.2 %collective-permute-done = f32[2,1,128,256]{3,2,1,0:T(8,128)S(1)} collective-permute-done((f32[2,1,128,256]{3,2,1,0:T(8,128)S(1)}, f32[2,1,128,256]{3,2,1,0:T(8,128)S(1)}, u32[]{:S(2)}, u32[]{:S(2)}) %collective-permute-start) | collective-permute-done | bytes 262176 | tf_op jit(solution)/shard_map/ppermute | solution.py:23
  18.8 4.1 %collective-permute-done.1 = f32[2,1,128,256]{3,2,1,0:T(8,128)S(1)} collective-permute-done((f32[2,1,128,256]{3,2,1,0:T(8,128)S(1)}, f32[2,1,128,256]{3,2,1,0:T(8,128)S(1)}, u32[]{:S(2)}, u32[]{:S(2)}) %collective-permute-start.1) | collective-permute-done | bytes 262176 | tf_op jit(solution)/shard_map/ppermute | solution.py:26
  23.0 2.1 %collective-permute-start.2 = (f32[2,1,512,128]{3,2,1,0:T(8,128)S(1)}, f32[2,1,512,128]{3,2,1,0:T(8,128)}, u32[]{:S(2)}, u32[]{:S(2)}) collective-permute-start(f32[2,1,512,128]{3,2,1,0:T(8,128)S(1)} %get-tuple-element.132), channel_id=1, source_target_pairs={{0,1},{2,3},{4,5},{6,7},{8,9},{10,11},{12,13},{14,15},{16,17},{18,... | collective-permute-start | bytes 1572872 | tf_op jit(solution)/shard_map/ppermute | solution.py:23
  25.1 1.3 collective-permute-start.3
  29.0 1.4 %pad_maximum_fusion = f32[2,1,512,512]{3,2,1,0:T(8,128)S(1)} fusion(f32[2,1,512,128]{3,2,1,0:T(8,128)} %collective-permute-done.3, f32[2,1,512,256]{3,2,1,0:T(8,128)S(1)} %constant_dynamic-update-slice_fusion, f32[2,1,512,128]{3,2,1,0:T(8,128)} %collective-permute-done.2), kind=kLoop, calls=%fused_computation.7 | loop fusion | flops 1048576 | bytes 4194304 | tf_op jit(solution)/shard_map/concatenate | solution.py:27
  31.9 1.6 %pad_maximum_fusion.1 = f32[2,1,4,256,256]{3,4,1,0,2:T(8,128)} fusion(f32[2,1,1,256,256]{3,4,1,0,2:T(8,128)S(1)} %bitcast.297, f32[2,1,1,256,256]{3,4,1,0,2:T(8,128)S(1)} %bitcast.296, f32[2,1,1,256,256]{3,4,1,0,2:T(8,128)S(1)} %bitcast.295, f32[2,1,1,256,256]{3,4,1,0,2:T(8,128)S(1)} %bitcast.294), kind=kLoop, calls=%fused_computation.8 | loop fusion | flops 1572864 | bytes 4194304 | tf_op jit(solution)/shard_map/stack | solution.py:187
  33.5 3.8 %all-to-all-start = ((f32[2,1,4,256,256]{3,4,1,0,2:T(8,128)}), f32[2,1,4,256,256]{3,4,1,0,2:T(8,128)S(1)}, u32[]{:S(2)}, u32[]{:S(2)}) async-start(f32[2,1,4,256,256]{3,4,1,0,2:T(8,128)} %pad_maximum_fusion.1), calls=%async_computation | async-start | bytes 4194304 | tf_op jit(solution)/shard_map/all_to_all | solution.py:196
  39.1 1.1 pad_maximum_fusion.4
  41.2 1.4 %fusion.72 = f32[256,256]{1,0:T(8,128)S(1)} fusion(f32[256]{0:T(256)S(1)} %get-tuple-element.161, f32[256]{0:T(256)S(1)} %get-tuple-element.162), kind=kOutput, calls=%fused_computation.191 | convolution fusion | flops 203358208 | bytes 264192 | tf_op jit(solution)/shard_map/dot_general | solution.py:32
  42.7 1.5 %fusion.3 = f32[1,256,256]{2,1,0:T(8,128)S(1)} fusion(f32[256,256]{1,0:T(8,128)S(1)} %fusion.72, f32[256]{0:T(256)S(1)} %get-tuple-element.161, f32[256]{0:T(256)S(1)} %get-tuple-element.162), kind=kOutput, calls=%fused_computation.19 | convolution fusion | flops 203423744 | bytes 526336 | tf_op jit(solution)/shard_map/dot_general | solution.py:32
  44.2 1.4 %fusion.73 = f32[256,256]{1,0:T(8,128)S(1)} fusion(f32[256]{0:T(256)S(1)} %get-tuple-element.161, f32[256]{0:T(256)S(1)} %get-tuple-element.162), kind=kOutput, calls=%fused_computation.193 | convolution fusion | flops 203358208 | bytes 264192 | tf_op jit(solution)/shard_map/dot_general | solution.py:32
  45.6 1.5 %fusion.4 = f32[1,256,256]{2,1,0:T(8,128)S(1)} fusion(f32[256,256]{1,0:T(8,128)S(1)} %fusion.73, f32[256]{0:T(256)S(1)} %get-tuple-element.161, f32[256]{0:T(256)S(1)} %get-tuple-element.162), kind=kOutput, calls=%fused_computation.21 | convolution fusion | flops 203423744 | bytes 526336 | tf_op jit(solution)/shard_map/dot_general | solution.py:32
  48.0 1.2 copy.146
  49.2 14.2 %all-to-all-done = f32[2,1,4,256,256]{3,4,1,0,2:T(8,128)S(1)} async-done(((f32[2,1,4,256,256]{3,4,1,0,2:T(8,128)}), f32[2,1,4,256,256]{3,4,1,0,2:T(8,128)S(1)}, u32[]{:S(2)}, u32[]{:S(2)}) %all-to-all-start) | async-done | bytes 2097184 | tf_op jit(solution)/shard_map/all_to_all | solution.py:196
  63.4 4.0 %multiply_bitcast_fusion = (f32[1,4,1,256,256]{3,4,2,1,0:T(8,128)S(1)}, f32[1,4,1,256,256]{3,4,2,1,0:T(8,128)S(1)}) fusion(f32[2,1,4,256,256]{3,4,1,0,2:T(8,128)S(1)} %all-to-all-done), kind=kLoop, calls=%fused_computation.28 | loop fusion | flops 786432 | bytes 4194304 | tf_op jit(solution)/shard_map/mul | solution.py:153
  68.6 1.1 fusion.11
  75.5 1.9 %fusion.29 = f32[2,256,512]{2,1,0:T(8,128)S(1)} fusion(f32[512,256,1]{1,0,2:T(8,128)S(1)} %bitcast.283, f32[1,256,256]{1,2,0:T(8,128)S(1)} %get-tuple-element.125, f32[1,256,256]{1,2,0:T(8,128)S(1)} %get-tuple-element.124), kind=kOutput, calls=%fused_computation.65 | convolution fusion | flops 805437440 | bytes 2097152 | tf_op jit(solution)/shard_map/bij,kj->bik/dot_general | solution.py:65
  78.5 1.1 convolution_bitcast_fusion.3
  85.5 1.5 %copy.165 = f32[2,4,1,256,256]{3,4,2,0,1:T(8,128)} copy(f32[2,4,1,256,256]{3,4,1,2,0:T(8,128)S(1)} %pad_maximum_fusion.2) | data formatting | bytes 4194304 | tf_op jit(solution)/shard_map/stack | solution.py:207
  87.0 3.6 %all-to-all-start.1 = ((f32[2,4,1,256,256]{3,4,2,0,1:T(8,128)}), f32[2,4,1,256,256]{3,4,2,0,1:T(8,128)S(1)}, u32[]{:S(2)}, u32[]{:S(2)}) async-start(f32[2,4,1,256,256]{3,4,2,0,1:T(8,128)} %copy.165), calls=%async_computation.1 | async-start | bytes 4194304 | tf_op jit(solution)/shard_map/all_to_all | solution.py:208
  90.7 25.3 %all-to-all-done.1 = f32[2,4,1,256,256]{3,4,2,0,1:T(8,128)S(1)} async-done(((f32[2,4,1,256,256]{3,4,2,0,1:T(8,128)}), f32[2,4,1,256,256]{3,4,2,0,1:T(8,128)S(1)}, u32[]{:S(2)}, u32[]{:S(2)}) %all-to-all-start.1) | async-done | bytes 2097184 | tf_op jit(solution)/shard_map/all_to_all | solution.py:208
  116.1 2.9 %fusion.2 = f32[2,1,512,512]{2,3,0,1:T(8,128)S(1)} fusion(s32[]{:T(128)S(6)} %select_n.136, s32[]{:T(128)S(6)} %select_n.137, f32[2,1,256,256]{2,3,0,1:T(8,128)S(1)} %get-tuple-element.105, s32[]{:T(128)S(6)} %select_n.138, s32[]{:T(128)S(6)} %select_n.139, f32[2,1,256,256]{2,3,0,1:T(8,128)S(1)} %get-tuple-element.104, s32[]{:T(128)S(6)} %select_n.140, ...), kind=kLoop, calls=%fused_computation.6 | loop fusion | flops 1572864 | bytes 4194336 | tf_op jit(solution)/shard_map/add | solution.py:211
  119.2 1.3 collective-permute-start.4
  120.5 1.3 collective-permute-start.5
  122.1 2.2 %collective-permute-done.5 = f32[2,1,512,128]{2,3,0,1:T(8,128)S(1)} collective-permute-done((f32[2,1,512,128]{2,3,0,1:T(8,128)S(1)}, f32[2,1,512,128]{2,3,0,1:T(8,128)S(1)}, u32[]{:S(2)}, u32[]{:S(2)}) %collective-permute-start.5) | collective-permute-done | bytes 524320 | tf_op jit(solution)/shard_map/ppermute | solution.py:15
  124.5 3.5 %collective-permute-start.6 = (f32[2,1,128,256]{2,3,0,1:T(8,128)S(1)}, f32[2,1,128,256]{2,3,0,1:T(8,128)S(1)}, u32[]{:S(2)}, u32[]{:S(2)}) collective-permute-start(f32[2,1,128,256]{2,3,0,1:T(8,128)S(1)} %get-tuple-element.115), channel_id=1, source_target_pairs={{0,2},{2,4},{4,6},{1,3},{3,5},{5,7},{8,10},{10,12},{12,14},{9,11},... | collective-permute-start | bytes 786440 | tf_op jit(solution)/shard_map/ppermute | solution.py:15
  128.0 1.3 collective-permute-start.7
  129.3 4.5 %collective-permute-done.6 = f32[2,1,128,256]{2,3,0,1:T(8,128)S(1)} collective-permute-done((f32[2,1,128,256]{2,3,0,1:T(8,128)S(1)}, f32[2,1,128,256]{2,3,0,1:T(8,128)S(1)}, u32[]{:S(2)}, u32[]{:S(2)}) %collective-permute-start.6) | collective-permute-done | bytes 262176 | tf_op jit(solution)/shard_map/ppermute | solution.py:15
  133.9 4.1 %collective-permute-done.7 = f32[2,1,128,256]{2,3,0,1:T(8,128)S(1)} collective-permute-done((f32[2,1,128,256]{2,3,0,1:T(8,128)S(1)}, f32[2,1,128,256]{2,3,0,1:T(8,128)S(1)}, u32[]{:S(2)}, u32[]{:S(2)}) %collective-permute-start.7) | collective-permute-done | bytes 262176 | tf_op jit(solution)/shard_map/ppermute | solution.py:15
  (88 shorter events, 25.7 us)
Async XLA Ops:
  8.3 10.5 %collective-permute-start = (f32[2,1,128,256]{3,2,1,0:T(8,128)S(1)}, f32[2,1,128,256]{3,2,1,0:T(8,128)S(1)}, u32[]{:S(2)}, u32[]{:S(2)}) collective-permute-start(f32[2,1,128,256]{3,2,1,0:T(8,128)S(1)} %get-tuple-element.146), channel_id=1, source_target_pairs={{0,2},{2,4},{4,6},{1,3},{3,5},{5,7},{8,10},{10,12},{12,14},{9,11},... | collective-permute-start | bytes 786440 | tf_op jit(solution)/shard_map/ppermute | solution.py:23
  13.2 9.7 %collective-permute-start.1 = (f32[2,1,128,256]{3,2,1,0:T(8,128)S(1)}, f32[2,1,128,256]{3,2,1,0:T(8,128)S(1)}, u32[]{:S(2)}, u32[]{:S(2)}) collective-permute-start(f32[2,1,128,256]{3,2,1,0:T(8,128)S(1)} %get-tuple-element.145), channel_id=1, source_target_pairs={{2,0},{4,2},{6,4},{3,1},{5,3},{7,5},{10,8},{12,10},{14,12},{11,9},... | collective-permute-start | bytes 786440 | tf_op jit(solution)/shard_map/ppermute | solution.py:26
  18.8 8.6 %copy-start.6 = (f32[2,256,256]{2,1,0:T(8,128)S(1)}, f32[2,256,256]{2,1,0:T(8,128)}, u32[]{:S(2)}) copy-start(f32[2,256,256]{2,1,0:T(8,128)} %param.15) | copy-start | bytes 1572868
  23.0 5.4 %collective-permute-start.2 = (f32[2,1,512,128]{3,2,1,0:T(8,128)S(1)}, f32[2,1,512,128]{3,2,1,0:T(8,128)}, u32[]{:S(2)}, u32[]{:S(2)}) collective-permute-start(f32[2,1,512,128]{3,2,1,0:T(8,128)S(1)} %get-tuple-element.132), channel_id=1, source_target_pairs={{0,1},{2,3},{4,5},{6,7},{8,9},{10,11},{12,13},{14,15},{16,17},{18,... | collective-permute-start | bytes 1572872 | tf_op jit(solution)/shard_map/ppermute | solution.py:23
  25.1 3.9 %collective-permute-start.3 = (f32[2,1,512,128]{3,2,1,0:T(8,128)S(1)}, f32[2,1,512,128]{3,2,1,0:T(8,128)}, u32[]{:S(2)}, u32[]{:S(2)}) collective-permute-start(f32[2,1,512,128]{3,2,1,0:T(8,128)S(1)} %get-tuple-element.133), channel_id=1, source_target_pairs={{1,0},{3,2},{5,4},{7,6},{9,8},{11,10},{13,12},{15,14},{17,16},{19,... | collective-permute-start | bytes 1572872 | tf_op jit(solution)/shard_map/ppermute | solution.py:26
  27.5 9.9 %copy-start = (f32[2,256,256]{2,1,0:T(8,128)}, f32[2,256,256]{2,1,0:T(8,128)S(1)}, u32[]{:S(2)}) copy-start(f32[2,256,256]{2,1,0:T(8,128)S(1)} %maximum_multiply_fusion.1) | copy-start | bytes 1572868
  33.5 4.7 %copy-start.5 = (f32[1,256,256]{2,1,0:T(8,128)S(1)}, f32[1,256,256]{2,1,0:T(8,128)}, u32[]{:S(2)}) copy-start(f32[1,256,256]{2,1,0:T(8,128)} %get-tuple-element.144) | copy-start | bytes 786436
  33.5 4.8 %copy-start.4 = (f32[1,256,256]{2,1,0:T(8,128)S(1)}, f32[1,256,256]{2,1,0:T(8,128)}, u32[]{:S(2)}) copy-start(f32[1,256,256]{2,1,0:T(8,128)} %get-tuple-element.143) | copy-start | bytes 786436
  33.5 29.9 %all-to-all-start = ((f32[2,1,4,256,256]{3,4,1,0,2:T(8,128)}), f32[2,1,4,256,256]{3,4,1,0,2:T(8,128)S(1)}, u32[]{:S(2)}, u32[]{:S(2)}) async-start(f32[2,1,4,256,256]{3,4,1,0,2:T(8,128)} %pad_maximum_fusion.1), calls=%async_computation | async-start | bytes 4194304 | tf_op jit(solution)/shard_map/all_to_all | solution.py:196
  63.4 4.0 %copy-start.3 = (f32[1,256,256]{1,2,0:T(8,128)S(1)}, f32[1,256,256]{1,2,0:T(8,128)}, u32[]{:S(2)}) copy-start(f32[1,256,256]{1,2,0:T(8,128)} %copy.187) | copy-start | bytes 786436
  73.2 1.2 copy-start.1
  75.5 3.0 %copy-start.2 = (f32[2,256,256]{2,1,0:T(8,128)S(1)}, f32[2,256,256]{2,1,0:T(8,128)}, u32[]{:S(2)}) copy-start(f32[2,256,256]{2,1,0:T(8,128)} %copy.139) | copy-start | bytes 1572868
  87.0 29.0 %all-to-all-start.1 = ((f32[2,4,1,256,256]{3,4,2,0,1:T(8,128)}), f32[2,4,1,256,256]{3,4,2,0,1:T(8,128)S(1)}, u32[]{:S(2)}, u32[]{:S(2)}) async-start(f32[2,4,1,256,256]{3,4,2,0,1:T(8,128)} %copy.165), calls=%async_computation.1 | async-start | bytes 4194304 | tf_op jit(solution)/shard_map/all_to_all | solution.py:208
  119.2 2.8 %collective-permute-start.4 = (f32[2,1,512,128]{2,3,0,1:T(8,128)S(1)}, f32[2,1,512,128]{2,3,0,1:T(8,128)S(1)}, u32[]{:S(2)}, u32[]{:S(2)}) collective-permute-start(f32[2,1,512,128]{2,3,0,1:T(8,128)S(1)} %get-tuple-element.101), channel_id=1, source_target_pairs={{0,1},{2,3},{4,5},{6,7},{8,9},{10,11},{12,13},{14,15},{16,17},{18,... | collective-permute-start | bytes 1572872 | tf_op jit(solution)/shard_map/ppermute | solution.py:15
  120.5 3.8 %collective-permute-start.5 = (f32[2,1,512,128]{2,3,0,1:T(8,128)S(1)}, f32[2,1,512,128]{2,3,0,1:T(8,128)S(1)}, u32[]{:S(2)}, u32[]{:S(2)}) collective-permute-start(f32[2,1,512,128]{2,3,0,1:T(8,128)S(1)} %get-tuple-element.100), channel_id=1, source_target_pairs={{1,0},{3,2},{5,4},{7,6},{9,8},{11,10},{13,12},{15,14},{17,16},{19,... | collective-permute-start | bytes 1572872 | tf_op jit(solution)/shard_map/ppermute | solution.py:15
  124.5 9.3 %collective-permute-start.6 = (f32[2,1,128,256]{2,3,0,1:T(8,128)S(1)}, f32[2,1,128,256]{2,3,0,1:T(8,128)S(1)}, u32[]{:S(2)}, u32[]{:S(2)}) collective-permute-start(f32[2,1,128,256]{2,3,0,1:T(8,128)S(1)} %get-tuple-element.115), channel_id=1, source_target_pairs={{0,2},{2,4},{4,6},{1,3},{3,5},{5,7},{8,10},{10,12},{12,14},{9,11},... | collective-permute-start | bytes 786440 | tf_op jit(solution)/shard_map/ppermute | solution.py:15
  128.0 10.0 %collective-permute-start.7 = (f32[2,1,128,256]{2,3,0,1:T(8,128)S(1)}, f32[2,1,128,256]{2,3,0,1:T(8,128)S(1)}, u32[]{:S(2)}, u32[]{:S(2)}) collective-permute-start(f32[2,1,128,256]{2,3,0,1:T(8,128)S(1)} %get-tuple-element.114), channel_id=1, source_target_pairs={{2,0},{4,2},{6,4},{3,1},{5,3},{7,5},{10,8},{12,10},{14,12},{11,9},... | collective-permute-start | bytes 786440 | tf_op jit(solution)/shard_map/ppermute | solution.py:15
where the time goes:
time: 140 us
  waiting for transfers between devices  59.3 us (42%)
  starting transfers between devices  24.5 us (18%)
  matrix products  20.5 us (15%)
  other arithmetic  19 us (14%)
  local copies, waits for them, and re-layouts  9.96 us (7%)
  between operations  6.44 us (5%)
    all_to_all x1, waiting for transfers between devices, per_device(): returned = lax.all_to_all(parts, 'depth', 1, 2, tiled=True)  25.3 us
    all_to_all x1, waiting for transfers between devices, per_device(): gathered = lax.all_to_all(cut, 'depth', 2, 1, tiled=True)  14.2 us
    ppermute x4, waiting for transfers between devices, from_behind(): lax.ppermute(value, axis, [(source, source + steps) for source in range(l...  10.9 us
    dot_general x8, matrix products, right_product(): jnp.einsum('bij,kj->bik', waves, matrix, precision=mode, preferred_elemen...  7.44 us
    ppermute x4, starting transfers between devices, from_behind(): lax.ppermute(value, axis, [(source, source + steps) for source in range(l...  7.39 us
    dot_general x8, matrix products, left_product(): jnp.einsum('ij,bjk->bik', matrix, waves, precision=mode, preferred_elemen...  7.3 us
    ppermute x2, starting transfers between devices, with_halo(): lax.ppermute(lax.slice_in_dim(block, block.shape[dim] - width, None, axis...  7.04 us
    dot_general x4, matrix products, matmul_exact(): jnp.dot(first, second, precision=exact_mode, preferred_element_type=jnp.f...  5.8 us
  transfers between devices with their start and end apart: 10, of which 9 were waited for; matrix products, arithmetic and copies ran while one was open for 10% of the time, Pallas kernels for 0%

commit v1 on v0

--- a/solution.py
+++ b/solution.py
@@ -161,6 +161,16 @@
     anchor = jnp.zeros((), jnp.int32)
     start = (anchor, anchor, extra_rows - row, extra_cols - col)
     return lax.dynamic_slice(padded, start, patch.shape[:2] + (height, span))
+
+
+def exchange(chunks, axis, count, index):
+    pieces = [chunks[0]]
+    for shift in range(1, count):
+        pieces.append(
+            lax.ppermute(chunks[shift], axis, [(i, (i + shift) % count) for i in range(count)])
+        )
+    stacked = jnp.stack(pieces)
+    return [lax.dynamic_index_in_dim(stacked, (index - j) % count, keepdims=False) for j in range(count)]
 
 
 def per_device(phase, absorption, probe, measured, offsets):
@@ -193,7 +203,11 @@
         ],
         axis=2,
     )
-    gathered = lax.all_to_all(cut, "depth", 2, 1, tiled=True)
+    outgoing = [
+        lax.dynamic_slice_in_dim(cut, ((depth_index + shift) % depth_count) * share, share, axis=2)
+        for shift in range(depth_count)
+    ]
+    gathered = jnp.concatenate(exchange(outgoing, "depth", depth_count, depth_index), axis=1)
     windows = to_transmit(gathered)
     total_layers = windows.shape[1]
     matrices = [fresnel] * (total_layers - 1) + [far_field]
@@ -205,7 +219,11 @@
     detector = far_wave * (0.25 * (power - target))[None]
     unused, phase_grad, absorb_grad = backward_layers(detector, windows, moved, adjoints)
     parts = jnp.stack((phase_grad, absorb_grad))
-    returned = lax.all_to_all(parts, "depth", 1, 2, tiled=True)
+    outgoing = [
+        lax.dynamic_slice_in_dim(parts, ((depth_index + shift) % depth_count) * layers, layers, axis=1)
+        for shift in range(depth_count)
+    ]
+    returned = jnp.concatenate(exchange(outgoing, "depth", depth_count, depth_index), axis=2)
     grid = jnp.zeros((2, layers) + extended.shape[2:], jnp.float32)
     for k in range(probes):
         grid = grid + place(returned[:, :, k], row_starts[k], col_starts[k], extended.shape[2:])

time: 140 us -> 145 us (1.036)
  local copies, waits for them, and re-layouts: 9.96 us -> 14.4 us
  waiting for transfers between devices: 59.3 us -> 55.5 us
  starting transfers between devices: 24.5 us -> 26.1 us
    ppermute x0 -> x6, waiting for transfers between devices: none -> 42.2 us  [exchange(): lax.ppermute(chunks[shift], axis, [(i, (i + shift) % count) for i in rang...]
    all_to_all x2 -> x0, waiting for transfers between devices: 39.5 us -> none  [the longest x1 25.3 us: per_device(): returned = lax.all_to_all(parts, 'depth', 1, 2, tiled=True)]
    ppermute x0 -> x6, starting transfers between devices: none -> 7.98 us  [exchange(): lax.ppermute(chunks[shift], axis, [(i, (i + shift) % count) for i in rang...]
    all_to_all x2 -> x0, starting transfers between devices: 7.45 us -> none  [the longest x1 3.85 us: per_device(): gathered = lax.all_to_all(cut, 'depth', 2, 1, tiled=True)]
    dynamic_slice x5 -> x10, local copies, waits for them, and re-layouts: 1.46 us -> 8.48 us  [exchange(): lax.dynamic_index_in_dim(stacked, (index - j) % count, keepdims=False)]
    ppermute x2, waiting for transfers between devices: 4.23 us -> 0.01 us  [with_halo(): lax.ppermute(lax.slice_in_dim(block, block.shape[dim] - width, None, axis...]
    another operation x0 -> x3, other arithmetic: none -> 2.82 us  [exchange(): stacked = jnp.stack(pieces)]
    another operation x4, other arithmetic: 2.74 us -> 0.15 us  [adjoint_of(): return jnp.stack((matrix[0].T, -matrix[1].T))]
  transfers between devices with their start and end apart: 10 -> 14, of which waited for: 9 -> 11; matrix products, arithmetic and copies ran while one was open for 10% -> 8% of each run, Pallas kernels for 0% -> 0%
where the time goes in v1:
time: 145 us; the launch traced here: 144 us
  waiting for transfers between devices  55.5 us (38%)
  starting transfers between devices  26.1 us (18%)
  matrix products  21.9 us (15%)
  other arithmetic  20 us (14%)
  local copies, waits for them, and re-layouts  14.4 us (10%)
  between operations  6.44 us (4%)
    ppermute x6, waiting for transfers between devices, exchange(): lax.ppermute(chunks[shift], axis, [(i, (i + shift) % count) for i in rang...  42.2 us
    ppermute x4, waiting for transfers between devices, from_behind(): lax.ppermute(value, axis, [(source, source + steps) for source in range(l...  10.9 us
    dynamic_slice x10, local copies, waits for them, and re-layouts, exchange(): lax.dynamic_index_in_dim(stacked, (index - j) % count, keepdims=False)  8.48 us
    ppermute x4, starting transfers between devices, from_behind(): lax.ppermute(value, axis, [(source, source + steps) for source in range(l...  8.31 us
    ppermute x6, starting transfers between devices, exchange(): lax.ppermute(chunks[shift], axis, [(i, (i + shift) % count) for i in rang...  7.98 us
    dot_general x8, matrix products, right_product(): jnp.einsum('bij,kj->bik', waves, matrix, precision=mode, preferred_elemen...  7.45 us
    dot_general x8, matrix products, left_product(): jnp.einsum('ij,bjk->bik', matrix, waves, precision=mode, preferred_elemen...  7.27 us
    dot_general x4, matrix products, matmul_exact(): jnp.dot(first, second, precision=exact_mode, preferred_element_type=jnp.f...  7.22 us
  transfers between devices with their start and end apart: 14, of which 11 were waited for; matrix products, arithmetic and copies ran while one was open for 8% of the time, Pallas kernels for 0%

profile of v1, /device:TPU:0, one launch (start us, length us, event | category | flops | bytes accessed | tf_op | source)
XLA Modules:
  0.0 144.4 jit_solution(7777790071385790828)
XLA Ops:
  8.1 4.9 %collective-permute-start = (f32[2,1,128,256]{3,2,0,1:T(8,128)S(1)}, f32[2,1,128,256]{3,2,0,1:T(8,128)S(1)}, u32[]{:S(2)}, u32[]{:S(2)}) collective-permute-start(f32[2,1,128,256]{3,2,0,1:T(8,128)S(1)} %get-tuple-element.152), channel_id=1, source_target_pairs={{0,2},{2,4},{4,6},{1,3},{3,5},{5,7},{8,10},{10,12},{12,14},{9,11},... | collective-permute-start | bytes 786440 | tf_op jit(solution)/shard_map/ppermute | solution.py:23
  13.1 1.3 collective-permute-start.1
  14.4 1.5 %fusion.78 = f32[256,256]{1,0:T(8,128)S(1)} fusion(f32[256]{0:T(256)S(1)} %get-tuple-element.167, f32[256]{0:T(256)S(1)} %get-tuple-element.168), kind=kOutput, calls=%fused_computation.207 | convolution fusion | flops 203358208 | bytes 264192 | tf_op jit(solution)/shard_map/dot_general | solution.py:32
  15.9 1.4 %fusion.79 = f32[256,256]{1,0:T(8,128)S(1)} fusion(f32[256]{0:T(256)S(1)} %get-tuple-element.167, f32[256]{0:T(256)S(1)} %get-tuple-element.168), kind=kOutput, calls=%fused_computation.209 | convolution fusion | flops 203358208 | bytes 264192 | tf_op jit(solution)/shard_map/dot_general | solution.py:32
  17.4 2.2 %fusion.3 = f32[1,256,256]{2,1,0:T(8,128)} fusion(f32[256,256]{1,0:T(8,128)S(1)} %fusion.78, f32[256]{0:T(256)S(1)} %get-tuple-element.167, f32[256]{0:T(256)S(1)} %get-tuple-element.168), kind=kOutput, calls=%fused_computation.29 | convolution fusion | flops 203423744 | bytes 526336 | tf_op jit(solution)/shard_map/dot_general | solution.py:32
  19.5 2.2 %fusion.4 = f32[1,256,256]{2,1,0:T(8,128)} fusion(f32[256,256]{1,0:T(8,128)S(1)} %fusion.79, f32[256]{0:T(256)S(1)} %get-tuple-element.167, f32[256]{0:T(256)S(1)} %get-tuple-element.168), kind=kOutput, calls=%fused_computation.31 | convolution fusion | flops 203423744 | bytes 526336 | tf_op jit(solution)/shard_map/dot_general | solution.py:32
  23.7 2.3 %collective-permute-start.2 = (f32[2,1,512,128]{3,2,0,1:T(8,128)}, f32[2,1,512,128]{3,2,0,1:T(8,128)}, u32[]{:S(2)}, u32[]{:S(2)}) collective-permute-start(f32[2,1,512,128]{3,2,0,1:T(8,128)} %get-tuple-element.138), channel_id=1, source_target_pairs={{0,1},{2,3},{4,5},{6,7},{8,9},{10,11},{12,13},{14,15},{16,17},{18,... | collective-permute-start | bytes 1572872 | tf_op jit(solution)/shard_map/ppermute | solution.py:23
  27.5 2.4 %collective-permute-done.3 = f32[2,1,512,128]{3,2,0,1:T(8,128)} collective-permute-done((f32[2,1,512,128]{3,2,0,1:T(8,128)S(1)}, f32[2,1,512,128]{3,2,0,1:T(8,128)}, u32[]{:S(2)}, u32[]{:S(2)}) %collective-permute-start.3) | collective-permute-done | bytes 524320 | tf_op jit(solution)/shard_map/ppermute | solution.py:26
  29.9 1.4 pad_maximum_fusion
  33.3 1.5 %collective-permute-start.4 = (f32[2,1,1,256,256]{4,3,0,2,1:T(8,128)}, f32[2,1,1,256,256]{4,3,0,2,1:T(8,128)}, u32[]{:S(2)}, u32[]{:S(2)}) collective-permute-start(f32[2,1,1,256,256]{4,3,0,2,1:T(8,128)} %get-tuple-element.113), channel_id=1, source_target_pairs={{0,8},{8,16},{16,24},{24,0},{1,9},{9,17},{17,25},{25,1},{2,10},{10... | collective-permute-start | bytes 1572872 | tf_op jit(solution)/shard_map/ppermute | solution.py:170
  34.8 1.5 %collective-permute-start.5 = (f32[2,1,1,256,256]{4,3,0,2,1:T(8,128)}, f32[2,1,1,256,256]{4,3,0,2,1:T(8,128)}, u32[]{:S(2)}, u32[]{:S(2)}) collective-permute-start(f32[2,1,1,256,256]{4,3,0,2,1:T(8,128)} %get-tuple-element.112), channel_id=1, source_target_pairs={{0,16},{8,24},{16,0},{24,8},{1,17},{9,25},{17,1},{25,9},{2,18},{10... | collective-permute-start | bytes 1572872 | tf_op jit(solution)/shard_map/ppermute | solution.py:170
  36.4 1.4 collective-permute-start.6
  40.5 8.9 %collective-permute-done.4 = f32[2,1,1,256,256]{4,3,0,2,1:T(8,128)} collective-permute-done((f32[2,1,1,256,256]{4,3,0,2,1:T(8,128)}, f32[2,1,1,256,256]{4,3,0,2,1:T(8,128)}, u32[]{:S(2)}, u32[]{:S(2)}) %collective-permute-start.4) | collective-permute-done | bytes 524320 | tf_op jit(solution)/shard_map/ppermute | solution.py:170
  49.4 10.4 %collective-permute-done.5 = f32[2,1,1,256,256]{4,3,0,2,1:T(8,128)} collective-permute-done((f32[2,1,1,256,256]{4,3,0,2,1:T(8,128)}, f32[2,1,1,256,256]{4,3,0,2,1:T(8,128)}, u32[]{:S(2)}, u32[]{:S(2)}) %collective-permute-start.5) | collective-permute-done | bytes 524320 | tf_op jit(solution)/shard_map/ppermute | solution.py:170
  59.9 1.5 %pad_maximum_fusion.2 = f32[4,2,1,1,256,256]{5,4,1,3,2,0:T(8,128)S(1)} fusion(f32[1,2,1,1,256,256]{5,4,1,3,2,0:T(8,128)} %bitcast.18, f32[1,2,1,1,256,256]{5,4,1,3,2,0:T(8,128)} %bitcast.17, f32[1,2,1,1,256,256]{5,4,1,3,2,0:T(8,128)} %bitcast.16, f32[1,2,1,1,256,256]{5,4,1,3,2,0:T(8,128)S(1)} %get-tuple-element.110), kind=kLoop, calls=%fused_computation.17 | loop fusion | flops 1572864 | bytes 4194304 | tf_op jit(solution)/shard_map/stack | solution.py:172
  63.8 2.0 %copy.54 = f32[1,2,1,1,256,256]{4,5,1,3,2,0:T(8,128)} copy(f32[1,2,1,1,256,256]{5,4,1,3,2,0:T(8,128)} %get-tuple-element.109) | data formatting | bytes 1048576 | tf_op jit(solution)/shard_map/jit(dynamic_index_in_dim)/dynamic_slice | solution.py:173
  65.9 2.1 %copy.55 = f32[1,2,1,1,256,256]{4,5,1,3,2,0:T(8,128)} copy(f32[1,2,1,1,256,256]{5,4,1,3,2,0:T(8,128)} %get-tuple-element.108) | data formatting | bytes 1048576 | tf_op jit(solution)/shard_map/jit(dynamic_index_in_dim)/dynamic_slice | solution.py:173
  68.9 1.5 %pad_maximum_fusion.3 = f32[2,4,1,256,256]{3,4,2,1,0:T(8,128)S(1)} fusion(f32[2,1,1,256,256]{3,4,2,1,0:T(8,128)} %bitcast.297, f32[2,1,1,256,256]{3,4,2,1,0:T(8,128)} %bitcast.296, f32[2,1,1,256,256]{3,4,2,1,0:T(8,128)} %bitcast.295, f32[2,1,1,256,256]{3,4,2,1,0:T(8,128)S(1)} %bitcast.294), kind=kLoop, calls=%fused_computation.18 | loop fusion | flops 1572864 | bytes 4194304 | tf_op jit(solution)/shard_map/concatenate | solution.py:210
  70.4 3.8 %sine_multiply_fusion = (f32[1,4,1,256,256]{3,4,2,1,0:T(8,128)S(1)}, f32[1,4,1,256,256]{3,4,2,1,0:T(8,128)S(1)}) fusion(f32[2,4,1,256,256]{3,4,2,1,0:T(8,128)S(1)} %pad_maximum_fusion.3), kind=kLoop, calls=%fused_computation.36 | loop fusion | flops 786432 | bytes 4194304 | tf_op jit(solution)/shard_map/mul | solution.py:153
  82.3 1.9 %fusion.35 = f32[2,256,512]{2,1,0:T(8,128)S(1)} fusion(f32[512,256,1]{1,0,2:T(8,128)S(1)} %bitcast.279, f32[1,256,256]{1,2,0:T(8,128)S(1)} %get-tuple-element.131, f32[1,256,256]{1,2,0:T(8,128)S(1)} %get-tuple-element.130), kind=kOutput, calls=%fused_computation.76 | convolution fusion | flops 805437440 | bytes 2097152 | tf_op jit(solution)/shard_map/bij,kj->bik/dot_general | solution.py:65
  92.3 1.5 %collective-permute-start.8 = (f32[2,1,1,256,256]{3,4,0,2,1:T(8,128)S(1)}, f32[2,1,1,256,256]{3,4,0,2,1:T(8,128)S(1)}, u32[]{:S(2)}, u32[]{:S(2)}) collective-permute-start(f32[2,1,1,256,256]{3,4,0,2,1:T(8,128)S(1)} %get-tuple-element.102), channel_id=1, source_target_pairs={{0,16},{8,24},{16,0},{24,8},{1,17},{9,25},{17,1},{25,9},{2,18},{10... | collective-permute-start | bytes 1572872 | tf_op jit(solution)/shard_map/ppermute | solution.py:170
  93.8 1.7 %collective-permute-start.9 = (f32[2,1,1,256,256]{3,4,1,2,0:T(8,128)S(1)}, f32[2,1,1,256,256]{3,4,1,2,0:T(8,128)S(1)}, u32[]{:S(2)}, u32[]{:S(2)}) collective-permute-start(f32[2,1,1,256,256]{3,4,1,2,0:T(8,128)S(1)} %get-tuple-element.103), channel_id=1, source_target_pairs={{0,24},{8,0},{16,8},{24,16},{1,25},{9,1},{17,9},{25,17},{2,26},{10... | collective-permute-start | bytes 1572872 | tf_op jit(solution)/shard_map/ppermute | solution.py:170
  95.9 10.5 %collective-permute-done.8 = f32[2,1,1,256,256]{3,4,0,2,1:T(8,128)S(1)} collective-permute-done((f32[2,1,1,256,256]{3,4,0,2,1:T(8,128)S(1)}, f32[2,1,1,256,256]{3,4,0,2,1:T(8,128)S(1)}, u32[]{:S(2)}, u32[]{:S(2)}) %collective-permute-start.8) | collective-permute-done | bytes 524320 | tf_op jit(solution)/shard_map/ppermute | solution.py:170
  106.3 2.3 %collective-permute-done.9 = f32[2,1,1,256,256]{3,4,1,2,0:T(8,128)S(1)} collective-permute-done((f32[2,1,1,256,256]{3,4,1,2,0:T(8,128)S(1)}, f32[2,1,1,256,256]{3,4,1,2,0:T(8,128)S(1)}, u32[]{:S(2)}, u32[]{:S(2)}) %collective-permute-start.9) | collective-permute-done | bytes 524320 | tf_op jit(solution)/shard_map/ppermute | solution.py:170
  108.7 10.0 %collective-permute-done.7 = f32[2,1,1,256,256]{3,4,0,2,1:T(8,128)} collective-permute-done((f32[2,1,1,256,256]{3,4,0,2,1:T(8,128)S(1)}, f32[2,1,1,256,256]{3,4,0,2,1:T(8,128)}, u32[]{:S(2)}, u32[]{:S(2)}) %collective-permute-start.7) | collective-permute-done | bytes 524320 | tf_op jit(solution)/shard_map/ppermute | solution.py:170
  120.8 2.9 %fusion.2 = f32[2,1,512,512]{3,2,0,1:T(8,128)S(1)} fusion(s32[]{:T(128)S(6)} %select_n.229, s32[]{:T(128)S(6)} %select_n.230, f32[2,1,256,256]{3,2,0,1:T(8,128)S(1)} %bitcast.290, s32[]{:T(128)S(6)} %select_n.231, s32[]{:T(128)S(6)} %select_n.232, f32[2,1,256,256]{3,2,0,1:T(8,128)S(1)} %bitcast.291, s32[]{:T(128)S(6)} %select_n.233, s32[]{:T(128)S(6)} %select_n.234, ...), kind=kLoop, calls=%fused_computation.14 | loop fusion | flops 1572864 | bytes 4194336 | tf_op jit(solution)/shard_map/add | solution.py:229
  123.8 1.3 collective-permute-start.10
  125.1 1.3 collective-permute-start.11
  126.7 2.2 %collective-permute-done.11 = f32[2,1,512,128]{3,2,0,1:T(8,128)S(1)} collective-permute-done((f32[2,1,512,128]{3,2,0,1:T(8,128)S(1)}, f32[2,1,512,128]{3,2,0,1:T(8,128)S(1)}, u32[]{:S(2)}, u32[]{:S(2)}) %collective-permute-start.11) | collective-permute-done | bytes 524320 | tf_op jit(solution)/shard_map/ppermute | solution.py:15
  129.1 4.4 %collective-permute-start.12 = (f32[2,1,128,256]{3,2,0,1:T(8,128)S(1)}, f32[2,1,128,256]{3,2,0,1:T(8,128)S(1)}, u32[]{:S(2)}, u32[]{:S(2)}) collective-permute-start(f32[2,1,128,256]{3,2,0,1:T(8,128)S(1)} %get-tuple-element.121), channel_id=1, source_target_pairs={{0,2},{2,4},{4,6},{1,3},{3,5},{5,7},{8,10},{10,12},{12,14},{9,11},... | collective-permute-start | bytes 786440 | tf_op jit(solution)/shard_map/ppermute | solution.py:15
  134.9 4.5 %collective-permute-done.12 = f32[2,1,128,256]{3,2,0,1:T(8,128)S(1)} collective-permute-done((f32[2,1,128,256]{3,2,0,1:T(8,128)S(1)}, f32[2,1,128,256]{3,2,0,1:T(8,128)S(1)}, u32[]{:S(2)}, u32[]{:S(2)}) %collective-permute-start.12) | collective-permute-done | bytes 262176 | tf_op jit(solution)/shard_map/ppermute | solution.py:15
  139.4 4.1 %collective-permute-done.13 = f32[2,1,128,256]{3,2,0,1:T(8,128)S(1)} collective-permute-done((f32[2,1,128,256]{3,2,0,1:T(8,128)S(1)}, f32[2,1,128,256]{3,2,0,1:T(8,128)S(1)}, u32[]{:S(2)}, u32[]{:S(2)}) %collective-permute-start.13) | collective-permute-done | bytes 262176 | tf_op jit(solution)/shard_map/ppermute | solution.py:15
  (92 shorter events, 35.0 us)
Async XLA Ops:
  8.1 14.6 %collective-permute-start = (f32[2,1,128,256]{3,2,0,1:T(8,128)S(1)}, f32[2,1,128,256]{3,2,0,1:T(8,128)S(1)}, u32[]{:S(2)}, u32[]{:S(2)}) collective-permute-start(f32[2,1,128,256]{3,2,0,1:T(8,128)S(1)} %get-tuple-element.152), channel_id=1, source_target_pairs={{0,2},{2,4},{4,6},{1,3},{3,5},{5,7},{8,10},{10,12},{12,14},{9,11},... | collective-permute-start | bytes 786440 | tf_op jit(solution)/shard_map/ppermute | solution.py:23
  13.1 9.7 %collective-permute-start.1 = (f32[2,1,128,256]{3,2,0,1:T(8,128)S(1)}, f32[2,1,128,256]{3,2,0,1:T(8,128)S(1)}, u32[]{:S(2)}, u32[]{:S(2)}) collective-permute-start(f32[2,1,128,256]{3,2,0,1:T(8,128)S(1)} %get-tuple-element.151), channel_id=1, source_target_pairs={{2,0},{4,2},{6,4},{3,1},{5,3},{7,5},{10,8},{12,10},{14,12},{11,9},... | collective-permute-start | bytes 786440 | tf_op jit(solution)/shard_map/ppermute | solution.py:26
  22.8 4.6 %copy-start.1 = (f32[2,256,256]{2,1,0:T(8,128)S(1)}, f32[2,256,256]{2,1,0:T(8,128)}, u32[]{:S(2)}) copy-start(f32[2,256,256]{2,1,0:T(8,128)} %param.15) | copy-start | bytes 1572868
  23.7 3.8 %collective-permute-start.2 = (f32[2,1,512,128]{3,2,0,1:T(8,128)}, f32[2,1,512,128]{3,2,0,1:T(8,128)}, u32[]{:S(2)}, u32[]{:S(2)}) collective-permute-start(f32[2,1,512,128]{3,2,0,1:T(8,128)} %get-tuple-element.138), channel_id=1, source_target_pairs={{0,1},{2,3},{4,5},{6,7},{8,9},{10,11},{12,13},{14,15},{16,17},{18,... | collective-permute-start | bytes 1572872 | tf_op jit(solution)/shard_map/ppermute | solution.py:23
  26.0 3.9 %collective-permute-start.3 = (f32[2,1,512,128]{3,2,0,1:T(8,128)S(1)}, f32[2,1,512,128]{3,2,0,1:T(8,128)}, u32[]{:S(2)}, u32[]{:S(2)}) collective-permute-start(f32[2,1,512,128]{3,2,0,1:T(8,128)S(1)} %get-tuple-element.139), channel_id=1, source_target_pairs={{1,0},{3,2},{5,4},{7,6},{9,8},{11,10},{13,12},{15,14},{17,16},{19,... | collective-permute-start | bytes 1572872 | tf_op jit(solution)/shard_map/ppermute | solution.py:26
  33.3 16.0 %collective-permute-start.4 = (f32[2,1,1,256,256]{4,3,0,2,1:T(8,128)}, f32[2,1,1,256,256]{4,3,0,2,1:T(8,128)}, u32[]{:S(2)}, u32[]{:S(2)}) collective-permute-start(f32[2,1,1,256,256]{4,3,0,2,1:T(8,128)} %get-tuple-element.113), channel_id=1, source_target_pairs={{0,8},{8,16},{16,24},{24,0},{1,9},{9,17},{17,25},{25,1},{2,10},{10... | collective-permute-start | bytes 1572872 | tf_op jit(solution)/shard_map/ppermute | solution.py:170
  34.8 24.9 %collective-permute-start.5 = (f32[2,1,1,256,256]{4,3,0,2,1:T(8,128)}, f32[2,1,1,256,256]{4,3,0,2,1:T(8,128)}, u32[]{:S(2)}, u32[]{:S(2)}) collective-permute-start(f32[2,1,1,256,256]{4,3,0,2,1:T(8,128)} %get-tuple-element.112), channel_id=1, source_target_pairs={{0,16},{8,24},{16,0},{24,8},{1,17},{9,25},{17,1},{25,9},{2,18},{10... | collective-permute-start | bytes 1572872 | tf_op jit(solution)/shard_map/ppermute | solution.py:170
  36.4 23.5 %collective-permute-start.6 = (f32[2,1,1,256,256]{4,3,0,2,1:T(8,128)}, f32[2,1,1,256,256]{4,3,0,2,1:T(8,128)}, u32[]{:S(2)}, u32[]{:S(2)}) collective-permute-start(f32[2,1,1,256,256]{4,3,0,2,1:T(8,128)} %get-tuple-element.111), channel_id=1, source_target_pairs={{0,24},{8,0},{16,8},{24,16},{1,25},{9,1},{17,9},{25,17},{2,26},{10... | collective-permute-start | bytes 1572872 | tf_op jit(solution)/shard_map/ppermute | solution.py:170
  70.4 3.9 %copy-start = (f32[1,256,256]{1,2,0:T(8,128)S(1)}, f32[1,256,256]{1,2,0:T(8,128)}, u32[]{:S(2)}) copy-start(f32[1,256,256]{1,2,0:T(8,128)} %copy.125) | copy-start | bytes 786436
  92.3 14.0 %collective-permute-start.8 = (f32[2,1,1,256,256]{3,4,0,2,1:T(8,128)S(1)}, f32[2,1,1,256,256]{3,4,0,2,1:T(8,128)S(1)}, u32[]{:S(2)}, u32[]{:S(2)}) collective-permute-start(f32[2,1,1,256,256]{3,4,0,2,1:T(8,128)S(1)} %get-tuple-element.102), channel_id=1, source_target_pairs={{0,16},{8,24},{16,0},{24,8},{1,17},{9,25},{17,1},{25,9},{2,18},{10... | collective-permute-start | bytes 1572872 | tf_op jit(solution)/shard_map/ppermute | solution.py:170
  93.8 14.8 %collective-permute-start.9 = (f32[2,1,1,256,256]{3,4,1,2,0:T(8,128)S(1)}, f32[2,1,1,256,256]{3,4,1,2,0:T(8,128)S(1)}, u32[]{:S(2)}, u32[]{:S(2)}) collective-permute-start(f32[2,1,1,256,256]{3,4,1,2,0:T(8,128)S(1)} %get-tuple-element.103), channel_id=1, source_target_pairs={{0,24},{8,0},{16,8},{24,16},{1,25},{9,1},{17,9},{25,17},{2,26},{10... | collective-permute-start | bytes 1572872 | tf_op jit(solution)/shard_map/ppermute | solution.py:170
  95.6 23.1 %collective-permute-start.7 = (f32[2,1,1,256,256]{3,4,0,2,1:T(8,128)S(1)}, f32[2,1,1,256,256]{3,4,0,2,1:T(8,128)}, u32[]{:S(2)}, u32[]{:S(2)}) collective-permute-start(f32[2,1,1,256,256]{3,4,0,2,1:T(8,128)S(1)} %get-tuple-element.101), channel_id=1, source_target_pairs={{0,8},{8,16},{16,24},{24,0},{1,9},{9,17},{17,25},{25,1},{2,10},{10... | collective-permute-start | bytes 1572872 | tf_op jit(solution)/shard_map/ppermute | solution.py:170
  123.8 2.8 %collective-permute-start.10 = (f32[2,1,512,128]{3,2,0,1:T(8,128)S(1)}, f32[2,1,512,128]{3,2,0,1:T(8,128)S(1)}, u32[]{:S(2)}, u32[]{:S(2)}) collective-permute-start(f32[2,1,512,128]{3,2,0,1:T(8,128)S(1)} %get-tuple-element.95), channel_id=1, source_target_pairs={{0,1},{2,3},{4,5},{6,7},{8,9},{10,11},{12,13},{14,15},{16,17},{18,... | collective-permute-start | bytes 1572872 | tf_op jit(solution)/shard_map/ppermute | solution.py:15
  125.1 3.8 %collective-permute-start.11 = (f32[2,1,512,128]{3,2,0,1:T(8,128)S(1)}, f32[2,1,512,128]{3,2,0,1:T(8,128)S(1)}, u32[]{:S(2)}, u32[]{:S(2)}) collective-permute-start(f32[2,1,512,128]{3,2,0,1:T(8,128)S(1)} %get-tuple-element.94), channel_id=1, source_target_pairs={{1,0},{3,2},{5,4},{7,6},{9,8},{11,10},{13,12},{15,14},{17,16},{19,... | collective-permute-start | bytes 1572872 | tf_op jit(solution)/shard_map/ppermute | solution.py:15
  129.1 10.2 %collective-permute-start.12 = (f32[2,1,128,256]{3,2,0,1:T(8,128)S(1)}, f32[2,1,128,256]{3,2,0,1:T(8,128)S(1)}, u32[]{:S(2)}, u32[]{:S(2)}) collective-permute-start(f32[2,1,128,256]{3,2,0,1:T(8,128)S(1)} %get-tuple-element.121), channel_id=1, source_target_pairs={{0,2},{2,4},{4,6},{1,3},{3,5},{5,7},{8,10},{10,12},{12,14},{9,11},... | collective-permute-start | bytes 786440 | tf_op jit(solution)/shard_map/ppermute | solution.py:15
  133.5 10.0 %collective-permute-start.13 = (f32[2,1,128,256]{3,2,0,1:T(8,128)S(1)}, f32[2,1,128,256]{3,2,0,1:T(8,128)S(1)}, u32[]{:S(2)}, u32[]{:S(2)}) collective-permute-start(f32[2,1,128,256]{3,2,0,1:T(8,128)S(1)} %get-tuple-element.120), channel_id=1, source_target_pairs={{2,0},{4,2},{6,4},{3,1},{5,3},{7,5},{10,8},{12,10},{14,12},{11,9},... | collective-permute-start | bytes 786440 | tf_op jit(solution)/shard_map/ppermute | solution.py:15

commit v2 on v0

--- a/solution.py
+++ b/solution.py
@@ -15,15 +15,22 @@
     return lax.ppermute(value, axis, [(source, source + steps) for source in range(leading, last)])
 
 
+def outside_filled(strip, edge):
+    return jnp.stack((jnp.where(edge, 1.0, strip[0]), jnp.where(edge, 0.0, strip[1])))
+
+
 def with_halo(block, sides, width):
     for axis, dim in sides:
         count = lax.axis_size(axis)
+        index = lax.axis_index(axis)
         forward = [(i, i + 1) for i in range(count - 1)]
         backward = [(target, source) for source, target in forward]
         low = lax.ppermute(
             lax.slice_in_dim(block, block.shape[dim] - width, None, axis=dim), axis, forward
         )
         high = lax.ppermute(lax.slice_in_dim(block, 0, width, axis=dim), axis, backward)
+        low = outside_filled(low, index == 0)
+        high = outside_filled(high, index == count - 1)
         block = jnp.concatenate([low, block, high], axis=dim)
     return block
 
@@ -177,7 +184,7 @@
     col_starts = corners[:, 1] - col_index * tile_cols + rim
     row_starts = [jnp.clip(row_starts[k], 0, 2 * rim + tile_rows - width) for k in range(probes)]
     col_starts = [jnp.clip(col_starts[k], 0, 2 * rim + tile_cols - width) for k in range(probes)]
-    stacked = jnp.stack((phase, absorption))
+    stacked = to_transmit(jnp.stack((phase, absorption)))
     row_starts, col_starts, stacked = lax.optimization_barrier((row_starts, col_starts, stacked))
     extended = with_halo(stacked, (("row", 2), ("col", 3)), rim)
     anchor = jnp.zeros((), jnp.int32)
@@ -194,7 +201,7 @@
         axis=2,
     )
     gathered = lax.all_to_all(cut, "depth", 2, 1, tiled=True)
-    windows = to_transmit(gathered)
+    windows = gathered
     total_layers = windows.shape[1]
     matrices = [fresnel] * (total_layers - 1) + [far_field]
     adjoints = [adjoint_of(matrix) for matrix in matrices]

time: 140 us -> 137 us (0.979)
  other arithmetic: 19 us -> 14.9 us
  local copies, waits for them, and re-layouts: 9.96 us -> 12.5 us
  waiting for transfers between devices: 59.3 us -> 57.8 us
    mul x1 -> x0, other arithmetic: 3.99 us -> none  [to_transmit(): damping * jnp.sin(extended[0])]
    all_to_all x1, waiting for transfers between devices: 14.2 us -> 12.6 us  [per_device(): gathered = lax.all_to_all(cut, 'depth', 2, 1, tiled=True)]
    unnamed x20 -> x18, local copies, waits for them, and re-layouts: 2.72 us -> 4.17 us
  transfers between devices with their start and end apart: 10 -> 10, of which waited for: 9 -> 9; matrix products, arithmetic and copies ran while one was open for 10% -> 11% of each run, Pallas kernels for 0% -> 0%
where the time goes in v2:
time: 137 us; the launch traced here: 136 us
  waiting for transfers between devices  57.8 us (42%)
  starting transfers between devices  24 us (18%)
  matrix products  20.6 us (15%)
  other arithmetic  14.9 us (11%)
  local copies, waits for them, and re-layouts  12.5 us (9%)
  between operations  6.53 us (5%)
    all_to_all x1, waiting for transfers between devices, per_device(): returned = lax.all_to_all(parts, 'depth', 1, 2, tiled=True)  24.1 us
    all_to_all x1, waiting for transfers between devices, per_device(): gathered = lax.all_to_all(cut, 'depth', 2, 1, tiled=True)  12.6 us
    ppermute x4, waiting for transfers between devices, from_behind(): lax.ppermute(value, axis, [(source, source + steps) for source in range(l...  10.9 us
    dot_general x8, matrix products, right_product(): jnp.einsum('bij,kj->bik', waves, matrix, precision=mode, preferred_elemen...  7.44 us
    ppermute x4, starting transfers between devices, from_behind(): lax.ppermute(value, axis, [(source, source + steps) for source in range(l...  7.39 us
    dot_general x8, matrix products, left_product(): jnp.einsum('ij,bjk->bik', matrix, waves, precision=mode, preferred_elemen...  7.31 us
    ppermute x2, starting transfers between devices, with_halo(): lax.ppermute(lax.slice_in_dim(block, block.shape[dim] - width, None, axis...  6.25 us
    ppermute x2, waiting for transfers between devices, with_halo(): lax.ppermute(lax.slice_in_dim(block, 0, width, axis=dim), axis, backward)  5.88 us
  transfers between devices with their start and end apart: 10, of which 9 were waited for; matrix products, arithmetic and copies ran while one was open for 11% of the time, Pallas kernels for 0%

profile of v2, /device:TPU:0, one launch (start us, length us, event | category | flops | bytes accessed | tf_op | source)
XLA Modules:
  0.0 136.3 jit_solution(5652936316117911918)
XLA Ops:
  7.2 2.0 %multiply_bitcast_fusion.1 = (f32[1,1,256,256]{3,2,1,0:T(8,128)S(1)}, f32[1,1,256,256]{3,2,1,0:T(8,128)S(1)}) fusion(f32[1,256,256]{2,1,0:T(8,128)} %param.13, f32[1,256,256]{2,1,0:T(8,128)} %param.14), kind=kLoop, calls=%fused_computation.199 | loop fusion | flops 196608 | bytes 1048576 | tf_op jit(solution)/shard_map/stack | solution.py:160
  9.3 4.9 %collective-permute-start = (f32[2,1,128,256]{3,2,1,0:T(8,128)S(1)}, f32[2,1,128,256]{3,2,1,0:T(8,128)S(1)}, u32[]{:S(2)}, u32[]{:S(2)}) collective-permute-start(f32[2,1,128,256]{3,2,1,0:T(8,128)S(1)} %get-tuple-element.147), channel_id=1, source_target_pairs={{0,2},{2,4},{4,6},{1,3},{3,5},{5,7},{8,10},{10,12},{12,14},{9,11},... | collective-permute-start | bytes 786440 | tf_op jit(solution)/shard_map/ppermute | solution.py:28
  14.2 1.3 collective-permute-start.1
  15.5 4.2 %collective-permute-done = f32[2,1,128,256]{3,2,1,0:T(8,128)S(1)} collective-permute-done((f32[2,1,128,256]{3,2,1,0:T(8,128)S(1)}, f32[2,1,128,256]{3,2,1,0:T(8,128)S(1)}, u32[]{:S(2)}, u32[]{:S(2)}) %collective-permute-start) | collective-permute-done | bytes 262176 | tf_op jit(solution)/shard_map/ppermute | solution.py:28
  19.8 4.1 %collective-permute-done.1 = f32[2,1,128,256]{3,2,1,0:T(8,128)S(1)} collective-permute-done((f32[2,1,128,256]{3,2,1,0:T(8,128)S(1)}, f32[2,1,128,256]{3,2,1,0:T(8,128)S(1)}, u32[]{:S(2)}, u32[]{:S(2)}) %collective-permute-start.1) | collective-permute-done | bytes 262176 | tf_op jit(solution)/shard_map/ppermute | solution.py:31
  24.0 1.1 fusion.136
  25.1 1.3 collective-permute-start.2
  27.5 1.3 collective-permute-start.3
  29.7 1.8 %collective-permute-done.3 = f32[2,1,512,128]{3,2,1,0:T(8,128)S(1)} collective-permute-done((f32[2,1,512,128]{3,2,1,0:T(8,128)}, f32[2,1,512,128]{3,2,1,0:T(8,128)S(1)}, u32[]{:S(2)}, u32[]{:S(2)}) %collective-permute-start.3) | collective-permute-done | bytes 524320 | tf_op jit(solution)/shard_map/ppermute | solution.py:31
  33.2 1.6 %pad_maximum_fusion = f32[2,1,4,256,256]{3,4,0,1,2:T(8,128)} fusion(f32[2,1,1,256,256]{3,4,0,1,2:T(8,128)S(1)} %bitcast.289, f32[2,1,1,256,256]{3,4,0,1,2:T(8,128)S(1)} %bitcast.288, f32[2,1,1,256,256]{3,4,0,1,2:T(8,128)S(1)} %bitcast.287, f32[2,1,1,256,256]{3,4,0,1,2:T(8,128)S(1)} %bitcast.286), kind=kLoop, calls=%fused_computation.8 | loop fusion | flops 1572864 | bytes 4194304 | tf_op jit(solution)/shard_map/stack | solution.py:194
  34.8 3.9 %all-to-all-start = ((f32[2,1,4,256,256]{3,4,0,1,2:T(8,128)}), f32[2,1,4,256,256]{3,4,0,1,2:T(8,128)S(1)}, u32[]{:S(2)}, u32[]{:S(2)}) async-start(f32[2,1,4,256,256]{3,4,0,1,2:T(8,128)} %pad_maximum_fusion), calls=%async_computation | async-start | bytes 4194304 | tf_op jit(solution)/shard_map/all_to_all | solution.py:203
  41.2 1.1 pad_maximum_fusion.3
  43.3 1.5 %fusion.70 = f32[256,256]{1,0:T(8,128)S(1)} fusion(f32[256]{0:T(256)S(1)} %get-tuple-element.169, f32[256]{0:T(256)S(1)} %get-tuple-element.170), kind=kOutput, calls=%fused_computation.191 | convolution fusion | flops 203358208 | bytes 264192 | tf_op jit(solution)/shard_map/dot_general | solution.py:39
  44.8 1.5 %fusion.3 = f32[1,256,256]{2,1,0:T(8,128)S(1)} fusion(f32[256,256]{1,0:T(8,128)S(1)} %fusion.70, f32[256]{0:T(256)S(1)} %get-tuple-element.169, f32[256]{0:T(256)S(1)} %get-tuple-element.170), kind=kOutput, calls=%fused_computation.20 | convolution fusion | flops 203423744 | bytes 526336 | tf_op jit(solution)/shard_map/dot_general | solution.py:39
  46.3 1.4 %fusion.71 = f32[256,256]{1,0:T(8,128)S(1)} fusion(f32[256]{0:T(256)S(1)} %get-tuple-element.169, f32[256]{0:T(256)S(1)} %get-tuple-element.170), kind=kOutput, calls=%fused_computation.193 | convolution fusion | flops 203358208 | bytes 264192 | tf_op jit(solution)/shard_map/dot_general | solution.py:39
  47.7 1.5 %fusion.4 = f32[1,256,256]{2,1,0:T(8,128)S(1)} fusion(f32[256,256]{1,0:T(8,128)S(1)} %fusion.71, f32[256]{0:T(256)S(1)} %get-tuple-element.169, f32[256]{0:T(256)S(1)} %get-tuple-element.170), kind=kOutput, calls=%fused_computation.22 | convolution fusion | flops 203423744 | bytes 526336 | tf_op jit(solution)/shard_map/dot_general | solution.py:39
  50.1 1.2 copy.145
  51.3 12.6 %all-to-all-done = f32[2,1,4,256,256]{3,4,0,1,2:T(8,128)S(1)} async-done(((f32[2,1,4,256,256]{3,4,0,1,2:T(8,128)}), f32[2,1,4,256,256]{3,4,0,1,2:T(8,128)S(1)}, u32[]{:S(2)}, u32[]{:S(2)}) %all-to-all-start) | async-done | bytes 2097184 | tf_op jit(solution)/shard_map/all_to_all | solution.py:203
  69.5 1.3 convolution_bitcast_fusion.5
  73.2 1.9 %fusion.27 = f32[2,256,512]{2,1,0:T(8,128)S(1)} fusion(f32[512,256,1]{1,0,2:T(8,128)S(1)} %bitcast.275, f32[1,256,256]{1,2,0:T(8,128)S(1)} %get-tuple-element.123, f32[1,256,256]{1,2,0:T(8,128)S(1)} %get-tuple-element.122), kind=kOutput, calls=%fused_computation.61 | convolution fusion | flops 805437440 | bytes 2097152 | tf_op jit(solution)/shard_map/bij,kj->bik/dot_general | solution.py:72
  76.2 1.1 convolution_bitcast_fusion.3
  83.0 1.5 %copy.164 = f32[2,4,1,256,256]{3,4,2,0,1:T(8,128)} copy(f32[2,4,1,256,256]{3,4,1,2,0:T(8,128)S(1)} %pad_maximum_fusion.1) | data formatting | bytes 4194304 | tf_op jit(solution)/shard_map/stack | solution.py:214
  84.5 3.9 %all-to-all-start.1 = ((f32[2,4,1,256,256]{3,4,2,0,1:T(8,128)}), f32[2,4,1,256,256]{3,4,2,0,1:T(8,128)S(1)}, u32[]{:S(2)}, u32[]{:S(2)}) async-start(f32[2,4,1,256,256]{3,4,2,0,1:T(8,128)} %copy.164), calls=%async_computation.1 | async-start | bytes 4194304 | tf_op jit(solution)/shard_map/all_to_all | solution.py:215
  88.4 24.1 %all-to-all-done.1 = f32[2,4,1,256,256]{3,4,2,0,1:T(8,128)S(1)} async-done(((f32[2,4,1,256,256]{3,4,2,0,1:T(8,128)}), f32[2,4,1,256,256]{3,4,2,0,1:T(8,128)S(1)}, u32[]{:S(2)}, u32[]{:S(2)}) %all-to-all-start.1) | async-done | bytes 2097184 | tf_op jit(solution)/shard_map/all_to_all | solution.py:215
  112.7 2.9 %fusion.2 = f32[2,1,512,512]{2,3,0,1:T(8,128)S(1)} fusion(s32[]{:T(128)S(6)} %select_n.216, s32[]{:T(128)S(6)} %select_n.217, f32[2,1,256,256]{2,3,0,1:T(8,128)S(1)} %get-tuple-element.105, s32[]{:T(128)S(6)} %select_n.218, s32[]{:T(128)S(6)} %select_n.219, f32[2,1,256,256]{2,3,0,1:T(8,128)S(1)} %get-tuple-element.104, s32[]{:T(128)S(6)} %select_n.220, ...), kind=kLoop, calls=%fused_computation.6 | loop fusion | flops 1572864 | bytes 4194336 | tf_op jit(solution)/shard_map/add | solution.py:218
  115.7 1.3 collective-permute-start.4
  117.1 1.3 collective-permute-start.5
  118.6 2.2 %collective-permute-done.5 = f32[2,1,512,128]{2,3,0,1:T(8,128)S(1)} collective-permute-done((f32[2,1,512,128]{2,3,0,1:T(8,128)S(1)}, f32[2,1,512,128]{2,3,0,1:T(8,128)S(1)}, u32[]{:S(2)}, u32[]{:S(2)}) %collective-permute-start.5) | collective-permute-done | bytes 524320 | tf_op jit(solution)/shard_map/ppermute | solution.py:15
  121.1 3.5 %collective-permute-start.6 = (f32[2,1,128,256]{2,3,0,1:T(8,128)S(1)}, f32[2,1,128,256]{2,3,0,1:T(8,128)S(1)}, u32[]{:S(2)}, u32[]{:S(2)}) collective-permute-start(f32[2,1,128,256]{2,3,0,1:T(8,128)S(1)} %get-tuple-element.113), channel_id=1, source_target_pairs={{0,2},{2,4},{4,6},{1,3},{3,5},{5,7},{8,10},{10,12},{12,14},{9,11},... | collective-permute-start | bytes 786440 | tf_op jit(solution)/shard_map/ppermute | solution.py:15
  124.5 1.3 collective-permute-start.7
  125.9 4.5 %collective-permute-done.6 = f32[2,1,128,256]{2,3,0,1:T(8,128)S(1)} collective-permute-done((f32[2,1,128,256]{2,3,0,1:T(8,128)S(1)}, f32[2,1,128,256]{2,3,0,1:T(8,128)S(1)}, u32[]{:S(2)}, u32[]{:S(2)}) %collective-permute-start.6) | collective-permute-done | bytes 262176 | tf_op jit(solution)/shard_map/ppermute | solution.py:15
  130.4 4.1 %collective-permute-done.7 = f32[2,1,128,256]{2,3,0,1:T(8,128)S(1)} collective-permute-done((f32[2,1,128,256]{2,3,0,1:T(8,128)S(1)}, f32[2,1,128,256]{2,3,0,1:T(8,128)S(1)}, u32[]{:S(2)}, u32[]{:S(2)}) %collective-permute-start.7) | collective-permute-done | bytes 262176 | tf_op jit(solution)/shard_map/ppermute | solution.py:15
  (91 shorter events, 26.7 us)
Async XLA Ops:
  9.3 10.5 %collective-permute-start = (f32[2,1,128,256]{3,2,1,0:T(8,128)S(1)}, f32[2,1,128,256]{3,2,1,0:T(8,128)S(1)}, u32[]{:S(2)}, u32[]{:S(2)}) collective-permute-start(f32[2,1,128,256]{3,2,1,0:T(8,128)S(1)} %get-tuple-element.147), channel_id=1, source_target_pairs={{0,2},{2,4},{4,6},{1,3},{3,5},{5,7},{8,10},{10,12},{12,14},{9,11},... | collective-permute-start | bytes 786440 | tf_op jit(solution)/shard_map/ppermute | solution.py:28
  14.2 9.7 %collective-permute-start.1 = (f32[2,1,128,256]{3,2,1,0:T(8,128)S(1)}, f32[2,1,128,256]{3,2,1,0:T(8,128)S(1)}, u32[]{:S(2)}, u32[]{:S(2)}) collective-permute-start(f32[2,1,128,256]{3,2,1,0:T(8,128)S(1)} %get-tuple-element.148), channel_id=1, source_target_pairs={{2,0},{4,2},{6,4},{3,1},{5,3},{7,5},{10,8},{12,10},{14,12},{11,9},... | collective-permute-start | bytes 786440 | tf_op jit(solution)/shard_map/ppermute | solution.py:31
  24.0 4.8 %copy-start.6 = (f32[2,256,256]{2,1,0:T(8,128)S(1)}, f32[2,256,256]{2,1,0:T(8,128)}, u32[]{:S(2)}) copy-start(f32[2,256,256]{2,1,0:T(8,128)} %param.15) | copy-start | bytes 1572868
  25.1 4.6 %collective-permute-start.2 = (f32[2,1,512,128]{3,2,1,0:T(8,128)}, f32[2,1,512,128]{3,2,1,0:T(8,128)S(1)}, u32[]{:S(2)}, u32[]{:S(2)}) collective-permute-start(f32[2,1,512,128]{3,2,1,0:T(8,128)} %get-tuple-element.130), channel_id=1, source_target_pairs={{0,1},{2,3},{4,5},{6,7},{8,9},{10,11},{12,13},{14,15},{16,17},{18,... | collective-permute-start | bytes 1572872 | tf_op jit(solution)/shard_map/ppermute | solution.py:28
  27.5 4.0 %collective-permute-start.3 = (f32[2,1,512,128]{3,2,1,0:T(8,128)}, f32[2,1,512,128]{3,2,1,0:T(8,128)S(1)}, u32[]{:S(2)}, u32[]{:S(2)}) collective-permute-start(f32[2,1,512,128]{3,2,1,0:T(8,128)} %get-tuple-element.131), channel_id=1, source_target_pairs={{1,0},{3,2},{5,4},{7,6},{9,8},{11,10},{13,12},{15,14},{17,16},{19,... | collective-permute-start | bytes 1572872 | tf_op jit(solution)/shard_map/ppermute | solution.py:31
  28.8 9.9 %copy-start = (f32[2,256,256]{2,1,0:T(8,128)}, f32[2,256,256]{2,1,0:T(8,128)S(1)}, u32[]{:S(2)}) copy-start(f32[2,256,256]{2,1,0:T(8,128)S(1)} %maximum_multiply_fusion.1) | copy-start | bytes 1572868
  34.8 4.8 %copy-start.3 = (f32[1,256,256]{2,1,0:T(8,128)S(1)}, f32[1,256,256]{2,1,0:T(8,128)}, u32[]{:S(2)}) copy-start(f32[1,256,256]{2,1,0:T(8,128)} %get-tuple-element.142) | copy-start | bytes 786436
  34.8 29.2 %all-to-all-start = ((f32[2,1,4,256,256]{3,4,0,1,2:T(8,128)}), f32[2,1,4,256,256]{3,4,0,1,2:T(8,128)S(1)}, u32[]{:S(2)}, u32[]{:S(2)}) async-start(f32[2,1,4,256,256]{3,4,0,1,2:T(8,128)} %pad_maximum_fusion), calls=%async_computation | async-start | bytes 4194304 | tf_op jit(solution)/shard_map/all_to_all | solution.py:203
  51.3 12.8 %copy-start.4 = (f32[1,256,256]{1,2,0:T(8,128)S(1)}, f32[1,256,256]{1,2,0:T(8,128)}, u32[]{:S(2)}) copy-start(f32[1,256,256]{1,2,0:T(8,128)} %copy.183) | copy-start | bytes 786436
  64.0 1.0 copy-start.5
  70.9 1.2 copy-start.1
  73.2 3.0 %copy-start.2 = (f32[2,256,256]{2,1,0:T(8,128)S(1)}, f32[2,256,256]{2,1,0:T(8,128)}, u32[]{:S(2)}) copy-start(f32[2,256,256]{2,1,0:T(8,128)} %copy.138) | copy-start | bytes 1572868
  84.5 28.1 %all-to-all-start.1 = ((f32[2,4,1,256,256]{3,4,2,0,1:T(8,128)}), f32[2,4,1,256,256]{3,4,2,0,1:T(8,128)S(1)}, u32[]{:S(2)}, u32[]{:S(2)}) async-start(f32[2,4,1,256,256]{3,4,2,0,1:T(8,128)} %copy.164), calls=%async_computation.1 | async-start | bytes 4194304 | tf_op jit(solution)/shard_map/all_to_all | solution.py:215
  115.7 2.8 %collective-permute-start.4 = (f32[2,1,512,128]{2,3,0,1:T(8,128)S(1)}, f32[2,1,512,128]{2,3,0,1:T(8,128)S(1)}, u32[]{:S(2)}, u32[]{:S(2)}) collective-permute-start(f32[2,1,512,128]{2,3,0,1:T(8,128)S(1)} %get-tuple-element.101), channel_id=1, source_target_pairs={{0,1},{2,3},{4,5},{6,7},{8,9},{10,11},{12,13},{14,15},{16,17},{18,... | collective-permute-start | bytes 1572872 | tf_op jit(solution)/shard_map/ppermute | solution.py:15
  117.1 3.8 %collective-permute-start.5 = (f32[2,1,512,128]{2,3,0,1:T(8,128)S(1)}, f32[2,1,512,128]{2,3,0,1:T(8,128)S(1)}, u32[]{:S(2)}, u32[]{:S(2)}) collective-permute-start(f32[2,1,512,128]{2,3,0,1:T(8,128)S(1)} %get-tuple-element.100), channel_id=1, source_target_pairs={{1,0},{3,2},{5,4},{7,6},{9,8},{11,10},{13,12},{15,14},{17,16},{19,... | collective-permute-start | bytes 1572872 | tf_op jit(solution)/shard_map/ppermute | solution.py:15
  121.1 9.3 %collective-permute-start.6 = (f32[2,1,128,256]{2,3,0,1:T(8,128)S(1)}, f32[2,1,128,256]{2,3,0,1:T(8,128)S(1)}, u32[]{:S(2)}, u32[]{:S(2)}) collective-permute-start(f32[2,1,128,256]{2,3,0,1:T(8,128)S(1)} %get-tuple-element.113), channel_id=1, source_target_pairs={{0,2},{2,4},{4,6},{1,3},{3,5},{5,7},{8,10},{10,12},{12,14},{9,11},... | collective-permute-start | bytes 786440 | tf_op jit(solution)/shard_map/ppermute | solution.py:15
  124.5 10.0 %collective-permute-start.7 = (f32[2,1,128,256]{2,3,0,1:T(8,128)S(1)}, f32[2,1,128,256]{2,3,0,1:T(8,128)S(1)}, u32[]{:S(2)}, u32[]{:S(2)}) collective-permute-start(f32[2,1,128,256]{2,3,0,1:T(8,128)S(1)} %get-tuple-element.112), channel_id=1, source_target_pairs={{2,0},{4,2},{6,4},{3,1},{5,3},{7,5},{10,8},{12,10},{14,12},{11,9},... | collective-permute-start | bytes 786440 | tf_op jit(solution)/shard_map/ppermute | solution.py:15

commit v3 on v2

--- a/solution.py
+++ b/solution.py
@@ -184,8 +184,17 @@
     col_starts = corners[:, 1] - col_index * tile_cols + rim
     row_starts = [jnp.clip(row_starts[k], 0, 2 * rim + tile_rows - width) for k in range(probes)]
     col_starts = [jnp.clip(col_starts[k], 0, 2 * rim + tile_cols - width) for k in range(probes)]
+    share = probes // depth_count
+    source_rows = []
+    source_cols = []
+    for shift in range(depth_count):
+        source = (depth_index - shift) % depth_count
+        source_rows.append([lax.select_n(source * share + slot, *row_starts) for slot in range(share)])
+        source_cols.append([lax.select_n(source * share + slot, *col_starts) for slot in range(share)])
     stacked = to_transmit(jnp.stack((phase, absorption)))
-    row_starts, col_starts, stacked = lax.optimization_barrier((row_starts, col_starts, stacked))
+    row_starts, col_starts, source_rows, source_cols, stacked = lax.optimization_barrier(
+        (row_starts, col_starts, source_rows, source_cols, stacked)
+    )
     extended = with_halo(stacked, (("row", 2), ("col", 3)), rim)
     anchor = jnp.zeros((), jnp.int32)
     fresnel, far_field = build_tables(width)
@@ -212,10 +221,18 @@
     detector = far_wave * (0.25 * (power - target))[None]
     unused, phase_grad, absorb_grad = backward_layers(detector, windows, moved, adjoints)
     parts = jnp.stack((phase_grad, absorb_grad))
-    returned = lax.all_to_all(parts, "depth", 1, 2, tiled=True)
     grid = jnp.zeros((2, layers) + extended.shape[2:], jnp.float32)
-    for k in range(probes):
-        grid = grid + place(returned[:, :, k], row_starts[k], col_starts[k], extended.shape[2:])
+    for shift in range(depth_count):
+        chunk = lax.dynamic_slice_in_dim(
+            parts, ((depth_index + shift) % depth_count) * layers, layers, axis=1
+        )
+        if shift > 0:
+            pairs = [(i, (i + shift) % depth_count) for i in range(depth_count)]
+            chunk = lax.ppermute(chunk, "depth", pairs)
+        for slot in range(share):
+            grid = grid + place(
+                chunk[:, :, slot], source_rows[shift][slot], source_cols[shift][slot], extended.shape[2:]
+            )
     owned = fold_both(grid, rim, pass_rows_all, pass_cols_all)
     return (owned[0], owned[1])
 

time: 137 us -> 135 us (0.985)
  waiting for transfers between devices: 57.8 us -> 54.2 us
  other arithmetic: 14.9 us -> 16.8 us
  starting transfers between devices: 24 us -> 25.9 us
  local copies, waits for them, and re-layouts: 12.5 us -> 10.9 us
    all_to_all x1 -> x0, waiting for transfers between devices: 24.1 us -> none  [per_device(): returned = lax.all_to_all(parts, 'depth', 1, 2, tiled=True)]
    ppermute x0 -> x3, waiting for transfers between devices: none -> 21.3 us  [per_device(): chunk = lax.ppermute(chunk, 'depth', pairs)]
    ppermute x0 -> x3, starting transfers between devices: none -> 4.38 us  [per_device(): chunk = lax.ppermute(chunk, 'depth', pairs)]
    all_to_all x1 -> x0, starting transfers between devices: 3.87 us -> none  [per_device(): returned = lax.all_to_all(parts, 'depth', 1, 2, tiled=True)]
    another operation x1 -> x0, local copies, waits for them, and re-layouts: 1.5 us -> none  [per_device(): parts = jnp.stack((phase_grad, absorb_grad))]
  transfers between devices with their start and end apart: 10 -> 12, of which waited for: 9 -> 11; matrix products, arithmetic and copies ran while one was open for 11% -> 12% of each run, Pallas kernels for 0% -> 0%
where the time goes in v3:
time: 135 us
  waiting for transfers between devices  54.2 us (40%)
  starting transfers between devices  25.9 us (19%)
  matrix products  20.6 us (15%)
  other arithmetic  16.8 us (12%)
  local copies, waits for them, and re-layouts  10.9 us (8%)
  between operations  6.6 us (5%)
    ppermute x3, waiting for transfers between devices, per_device(): chunk = lax.ppermute(chunk, 'depth', pairs)  21.3 us
    all_to_all x1, waiting for transfers between devices, per_device(): gathered = lax.all_to_all(cut, 'depth', 2, 1, tiled=True)  12.9 us
    ppermute x4, waiting for transfers between devices, from_behind(): lax.ppermute(value, axis, [(source, source + steps) for source in range(l...  10.9 us
    ppermute x4, starting transfers between devices, from_behind(): lax.ppermute(value, axis, [(source, source + steps) for source in range(l...  8 us
    dot_general x8, matrix products, right_product(): jnp.einsum('bij,kj->bik', waves, matrix, precision=mode, preferred_elemen...  7.44 us
    dot_general x8, matrix products, left_product(): jnp.einsum('ij,bjk->bik', matrix, waves, precision=mode, preferred_elemen...  7.31 us
    ppermute x2, starting transfers between devices, with_halo(): lax.ppermute(lax.slice_in_dim(block, block.shape[dim] - width, None, axis...  7.02 us
    dot_general x4, matrix products, matmul_exact(): jnp.dot(first, second, precision=exact_mode, preferred_element_type=jnp.f...  5.8 us
  transfers between devices with their start and end apart: 12, of which 11 were waited for; matrix products, arithmetic and copies ran while one was open for 12% of the time, Pallas kernels for 0%

profile of v3, /device:TPU:0, one launch (start us, length us, event | category | flops | bytes accessed | tf_op | source)
XLA Modules:
  0.0 134.9 jit_solution(8054885039142625454)
XLA Ops:
  7.4 2.0 %multiply_bitcast_fusion.1 = (f32[1,1,256,256]{3,2,1,0:T(8,128)S(1)}, f32[1,1,256,256]{3,2,1,0:T(8,128)S(1)}) fusion(f32[1,256,256]{2,1,0:T(8,128)} %param.13, f32[1,256,256]{2,1,0:T(8,128)} %param.14), kind=kLoop, calls=%fused_computation.209 | loop fusion | flops 196608 | bytes 1048576 | tf_op jit(solution)/shard_map/stack | solution.py:160
  9.4 4.9 %collective-permute-start = (f32[2,1,128,256]{3,2,1,0:T(8,128)S(1)}, f32[2,1,128,256]{3,2,1,0:T(8,128)S(1)}, u32[]{:S(2)}, u32[]{:S(2)}) collective-permute-start(f32[2,1,128,256]{3,2,1,0:T(8,128)S(1)} %get-tuple-element.163), channel_id=1, source_target_pairs={{0,2},{2,4},{4,6},{1,3},{3,5},{5,7},{8,10},{10,12},{12,14},{9,11},... | collective-permute-start | bytes 786440 | tf_op jit(solution)/shard_map/ppermute | solution.py:28
  14.4 1.3 collective-permute-start.1
  15.7 4.2 %collective-permute-done = f32[2,1,128,256]{3,2,1,0:T(8,128)S(1)} collective-permute-done((f32[2,1,128,256]{3,2,1,0:T(8,128)S(1)}, f32[2,1,128,256]{3,2,1,0:T(8,128)S(1)}, u32[]{:S(2)}, u32[]{:S(2)}) %collective-permute-start) | collective-permute-done | bytes 262176 | tf_op jit(solution)/shard_map/ppermute | solution.py:28
  19.9 4.1 %collective-permute-done.1 = f32[2,1,128,256]{3,2,1,0:T(8,128)S(1)} collective-permute-done((f32[2,1,128,256]{3,2,1,0:T(8,128)S(1)}, f32[2,1,128,256]{3,2,1,0:T(8,128)S(1)}, u32[]{:S(2)}, u32[]{:S(2)}) %collective-permute-start.1) | collective-permute-done | bytes 262176 | tf_op jit(solution)/shard_map/ppermute | solution.py:31
  24.2 1.1 fusion.143
  25.2 2.1 %collective-permute-start.2 = (f32[2,1,512,128]{3,2,1,0:T(8,128)}, f32[2,1,512,128]{3,2,1,0:T(8,128)}, u32[]{:S(2)}, u32[]{:S(2)}) collective-permute-start(f32[2,1,512,128]{3,2,1,0:T(8,128)} %get-tuple-element.146), channel_id=1, source_target_pairs={{0,1},{2,3},{4,5},{6,7},{8,9},{10,11},{12,13},{14,15},{16,17},{18,... | collective-permute-start | bytes 1572872 | tf_op jit(solution)/shard_map/ppermute | solution.py:28
  28.4 1.3 collective-permute-start.3
  30.6 1.1 slice_select_fusion.3
  34.1 1.6 %pad_maximum_fusion = f32[2,1,4,256,256]{3,4,0,1,2:T(8,128)} fusion(f32[2,1,1,256,256]{3,4,0,1,2:T(8,128)S(1)} %bitcast.288, f32[2,1,1,256,256]{3,4,0,1,2:T(8,128)S(1)} %bitcast.287, f32[2,1,1,256,256]{3,4,0,1,2:T(8,128)S(1)} %bitcast.286, f32[2,1,1,256,256]{3,4,0,1,2:T(8,128)S(1)} %bitcast.285), kind=kLoop, calls=%fused_computation.16 | loop fusion | flops 1572864 | bytes 4194304 | tf_op jit(solution)/shard_map/stack | solution.py:203
  35.7 3.9 %all-to-all-start = ((f32[2,1,4,256,256]{3,4,0,1,2:T(8,128)}), f32[2,1,4,256,256]{3,4,0,1,2:T(8,128)S(1)}, u32[]{:S(2)}, u32[]{:S(2)}) async-start(f32[2,1,4,256,256]{3,4,0,1,2:T(8,128)} %pad_maximum_fusion), calls=%async_computation | async-start | bytes 4194304 | tf_op jit(solution)/shard_map/all_to_all | solution.py:212
  42.2 1.1 pad_maximum_fusion.2
  44.3 1.4 %fusion.77 = f32[256,256]{1,0:T(8,128)S(1)} fusion(f32[256]{0:T(256)S(1)} %get-tuple-element.185, f32[256]{0:T(256)S(1)} %get-tuple-element.186), kind=kOutput, calls=%fused_computation.201 | convolution fusion | flops 203358208 | bytes 264192 | tf_op jit(solution)/shard_map/dot_general | solution.py:39
  45.7 1.4 %fusion.3 = f32[1,256,256]{2,1,0:T(8,128)S(1)} fusion(f32[256,256]{1,0:T(8,128)S(1)} %fusion.77, f32[256]{0:T(256)S(1)} %get-tuple-element.185, f32[256]{0:T(256)S(1)} %get-tuple-element.186), kind=kOutput, calls=%fused_computation.27 | convolution fusion | flops 203423744 | bytes 526336 | tf_op jit(solution)/shard_map/dot_general | solution.py:39
  47.2 1.5 %fusion.78 = f32[256,256]{1,0:T(8,128)S(1)} fusion(f32[256]{0:T(256)S(1)} %get-tuple-element.185, f32[256]{0:T(256)S(1)} %get-tuple-element.186), kind=kOutput, calls=%fused_computation.203 | convolution fusion | flops 203358208 | bytes 264192 | tf_op jit(solution)/shard_map/dot_general | solution.py:39
  48.6 1.5 %fusion.4 = f32[1,256,256]{2,1,0:T(8,128)S(1)} fusion(f32[256,256]{1,0:T(8,128)S(1)} %fusion.78, f32[256]{0:T(256)S(1)} %get-tuple-element.185, f32[256]{0:T(256)S(1)} %get-tuple-element.186), kind=kOutput, calls=%fused_computation.29 | convolution fusion | flops 203423744 | bytes 526336 | tf_op jit(solution)/shard_map/dot_general | solution.py:39
  51.0 1.2 copy.143
  52.3 12.9 %all-to-all-done = f32[2,1,4,256,256]{3,4,0,1,2:T(8,128)S(1)} async-done(((f32[2,1,4,256,256]{3,4,0,1,2:T(8,128)}), f32[2,1,4,256,256]{3,4,0,1,2:T(8,128)S(1)}, u32[]{:S(2)}, u32[]{:S(2)}) %all-to-all-start) | async-done | bytes 2097184 | tf_op jit(solution)/shard_map/all_to_all | solution.py:212
  70.8 1.3 convolution_bitcast_fusion.5
  74.4 1.9 %fusion.34 = f32[2,256,512]{2,1,0:T(8,128)S(1)} fusion(f32[512,256,1]{1,0,2:T(8,128)S(1)} %bitcast.274, f32[1,256,256]{1,2,0:T(8,128)S(1)} %get-tuple-element.139, f32[1,256,256]{1,2,0:T(8,128)S(1)} %get-tuple-element.138), kind=kOutput, calls=%fused_computation.71 | convolution fusion | flops 805437440 | bytes 2097152 | tf_op jit(solution)/shard_map/bij,kj->bik/dot_general | solution.py:72
  85.0 1.4 %collective-permute-start.4 = (f32[2,1,1,256,256]{3,4,0,2,1:T(8,128)}, f32[2,1,1,256,256]{3,4,0,2,1:T(8,128)S(1)}, u32[]{:S(2)}, u32[]{:S(2)}) collective-permute-start(f32[2,1,1,256,256]{3,4,0,2,1:T(8,128)} %get-tuple-element.120), channel_id=1, source_target_pairs={{0,8},{8,16},{16,24},{24,0},{1,9},{9,17},{17,25},{25,1},{2,10},{10... | collective-permute-start | bytes 1572872 | tf_op jit(solution)/shard_map/ppermute | solution.py:231
  87.0 2.4 %collective-permute-start.6 = (f32[2,1,1,256,256]{3,4,1,2,0:T(8,128)S(1)}, f32[2,1,1,256,256]{3,4,1,2,0:T(8,128)S(1)}, u32[]{:S(2)}, u32[]{:S(2)}) collective-permute-start(f32[2,1,1,256,256]{3,4,1,2,0:T(8,128)S(1)} %get-tuple-element.118), channel_id=1, source_target_pairs={{0,24},{8,0},{16,8},{24,16},{1,25},{9,1},{17,9},{25,17},{2,26},{10... | collective-permute-start | bytes 1572872 | tf_op jit(solution)/shard_map/ppermute | solution.py:231
  89.4 11.6 %collective-permute-done.4 = f32[2,1,1,256,256]{3,4,0,2,1:T(8,128)S(1)} collective-permute-done((f32[2,1,1,256,256]{3,4,0,2,1:T(8,128)}, f32[2,1,1,256,256]{3,4,0,2,1:T(8,128)S(1)}, u32[]{:S(2)}, u32[]{:S(2)}) %collective-permute-start.4) | collective-permute-done | bytes 524320 | tf_op jit(solution)/shard_map/ppermute | solution.py:231
  101.0 9.6 %collective-permute-done.5 = f32[2,1,1,256,256]{3,4,0,2,1:T(8,128)S(1)} collective-permute-done((f32[2,1,1,256,256]{3,4,0,2,1:T(8,128)S(1)}, f32[2,1,1,256,256]{3,4,0,2,1:T(8,128)S(1)}, u32[]{:S(2)}, u32[]{:S(2)}) %collective-permute-start.5) | collective-permute-done | bytes 524320 | tf_op jit(solution)/shard_map/ppermute | solution.py:231
  110.7 2.9 %fusion.2 = f32[2,1,512,512]{2,3,0,1:T(8,128)S(1)} fusion(s32[]{:T(128)S(6)} %select_n.421, s32[]{:T(128)S(6)} %select_n.422, f32[2,1,256,256]{2,3,0,1:T(8,128)S(1)} %get-tuple-element.119, s32[]{:T(128)S(6)} %select_n.425, s32[]{:T(128)S(6)} %select_n.426, f32[2,1,256,256]{2,3,0,1:T(8,128)S(1)} %bitcast.289, s32[]{:T(128)S(6)} %select_n.429, ...), kind=kLoop, calls=%fused_computation.14 | loop fusion | flops 1572864 | bytes 4194336 | tf_op jit(solution)/shard_map/add | solution.py:233
  113.7 1.9 %collective-permute-start.7 = (f32[2,1,512,128]{2,3,0,1:T(8,128)S(1)}, f32[2,1,512,128]{2,3,0,1:T(8,128)S(1)}, u32[]{:S(2)}, u32[]{:S(2)}) collective-permute-start(f32[2,1,512,128]{2,3,0,1:T(8,128)S(1)} %get-tuple-element.117), channel_id=1, source_target_pairs={{0,1},{2,3},{4,5},{6,7},{8,9},{10,11},{12,13},{14,15},{16,17},{18,... | collective-permute-start | bytes 1572872 | tf_op jit(solution)/shard_map/ppermute | solution.py:15
  115.6 1.3 collective-permute-start.8
  117.2 2.2 %collective-permute-done.8 = f32[2,1,512,128]{2,3,0,1:T(8,128)S(1)} collective-permute-done((f32[2,1,512,128]{2,3,0,1:T(8,128)S(1)}, f32[2,1,512,128]{2,3,0,1:T(8,128)S(1)}, u32[]{:S(2)}, u32[]{:S(2)}) %collective-permute-start.8) | collective-permute-done | bytes 524320 | tf_op jit(solution)/shard_map/ppermute | solution.py:15
  119.6 3.5 %collective-permute-start.9 = (f32[2,1,128,256]{2,3,0,1:T(8,128)S(1)}, f32[2,1,128,256]{2,3,0,1:T(8,128)S(1)}, u32[]{:S(2)}, u32[]{:S(2)}) collective-permute-start(f32[2,1,128,256]{2,3,0,1:T(8,128)S(1)} %get-tuple-element.129), channel_id=1, source_target_pairs={{0,2},{2,4},{4,6},{1,3},{3,5},{5,7},{8,10},{10,12},{12,14},{9,11},... | collective-permute-start | bytes 786440 | tf_op jit(solution)/shard_map/ppermute | solution.py:15
  123.2 1.3 collective-permute-start.10
  124.5 4.5 %collective-permute-done.9 = f32[2,1,128,256]{2,3,0,1:T(8,128)S(1)} collective-permute-done((f32[2,1,128,256]{2,3,0,1:T(8,128)S(1)}, f32[2,1,128,256]{2,3,0,1:T(8,128)S(1)}, u32[]{:S(2)}, u32[]{:S(2)}) %collective-permute-start.9) | collective-permute-done | bytes 262176 | tf_op jit(solution)/shard_map/ppermute | solution.py:15
  129.0 4.1 %collective-permute-done.10 = f32[2,1,128,256]{2,3,0,1:T(8,128)S(1)} collective-permute-done((f32[2,1,128,256]{2,3,0,1:T(8,128)S(1)}, f32[2,1,128,256]{2,3,0,1:T(8,128)S(1)}, u32[]{:S(2)}, u32[]{:S(2)}) %collective-permute-start.10) | collective-permute-done | bytes 262176 | tf_op jit(solution)/shard_map/ppermute | solution.py:15
  (93 shorter events, 29.8 us)
Async XLA Ops:
  9.4 10.5 %collective-permute-start = (f32[2,1,128,256]{3,2,1,0:T(8,128)S(1)}, f32[2,1,128,256]{3,2,1,0:T(8,128)S(1)}, u32[]{:S(2)}, u32[]{:S(2)}) collective-permute-start(f32[2,1,128,256]{3,2,1,0:T(8,128)S(1)} %get-tuple-element.163), channel_id=1, source_target_pairs={{0,2},{2,4},{4,6},{1,3},{3,5},{5,7},{8,10},{10,12},{12,14},{9,11},... | collective-permute-start | bytes 786440 | tf_op jit(solution)/shard_map/ppermute | solution.py:28
  14.4 9.7 %collective-permute-start.1 = (f32[2,1,128,256]{3,2,1,0:T(8,128)S(1)}, f32[2,1,128,256]{3,2,1,0:T(8,128)S(1)}, u32[]{:S(2)}, u32[]{:S(2)}) collective-permute-start(f32[2,1,128,256]{3,2,1,0:T(8,128)S(1)} %get-tuple-element.164), channel_id=1, source_target_pairs={{2,0},{4,2},{6,4},{3,1},{5,3},{7,5},{10,8},{12,10},{14,12},{11,9},... | collective-permute-start | bytes 786440 | tf_op jit(solution)/shard_map/ppermute | solution.py:31
  24.1 5.6 %copy-start.6 = (f32[2,256,256]{2,1,0:T(8,128)S(1)}, f32[2,256,256]{2,1,0:T(8,128)}, u32[]{:S(2)}) copy-start(f32[2,256,256]{2,1,0:T(8,128)} %param.15) | copy-start | bytes 1572868
  25.2 5.3 %collective-permute-start.2 = (f32[2,1,512,128]{3,2,1,0:T(8,128)}, f32[2,1,512,128]{3,2,1,0:T(8,128)}, u32[]{:S(2)}, u32[]{:S(2)}) collective-permute-start(f32[2,1,512,128]{3,2,1,0:T(8,128)} %get-tuple-element.146), channel_id=1, source_target_pairs={{0,1},{2,3},{4,5},{6,7},{8,9},{10,11},{12,13},{14,15},{16,17},{18,... | collective-permute-start | bytes 1572872 | tf_op jit(solution)/shard_map/ppermute | solution.py:28
  28.4 4.0 %collective-permute-start.3 = (f32[2,1,512,128]{3,2,1,0:T(8,128)}, f32[2,1,512,128]{3,2,1,0:T(8,128)S(1)}, u32[]{:S(2)}, u32[]{:S(2)}) collective-permute-start(f32[2,1,512,128]{3,2,1,0:T(8,128)} %get-tuple-element.147), channel_id=1, source_target_pairs={{1,0},{3,2},{5,4},{7,6},{9,8},{11,10},{13,12},{15,14},{17,16},{19,... | collective-permute-start | bytes 1572872 | tf_op jit(solution)/shard_map/ppermute | solution.py:31
  29.7 9.9 %copy-start = (f32[2,256,256]{2,1,0:T(8,128)}, f32[2,256,256]{2,1,0:T(8,128)S(1)}, u32[]{:S(2)}) copy-start(f32[2,256,256]{2,1,0:T(8,128)S(1)} %maximum_multiply_fusion.1) | copy-start | bytes 1572868
  35.7 4.8 %copy-start.3 = (f32[1,256,256]{2,1,0:T(8,128)S(1)}, f32[1,256,256]{2,1,0:T(8,128)}, u32[]{:S(2)}) copy-start(f32[1,256,256]{2,1,0:T(8,128)} %get-tuple-element.158) | copy-start | bytes 786436
  35.7 29.5 %all-to-all-start = ((f32[2,1,4,256,256]{3,4,0,1,2:T(8,128)}), f32[2,1,4,256,256]{3,4,0,1,2:T(8,128)S(1)}, u32[]{:S(2)}, u32[]{:S(2)}) async-start(f32[2,1,4,256,256]{3,4,0,1,2:T(8,128)} %pad_maximum_fusion), calls=%async_computation | async-start | bytes 4194304 | tf_op jit(solution)/shard_map/all_to_all | solution.py:212
  52.3 13.0 %copy-start.4 = (f32[1,256,256]{1,2,0:T(8,128)S(1)}, f32[1,256,256]{1,2,0:T(8,128)}, u32[]{:S(2)}) copy-start(f32[1,256,256]{1,2,0:T(8,128)} %copy.182) | copy-start | bytes 786436
  65.2 1.0 copy-start.5
  72.1 1.2 copy-start.1
  74.4 3.0 %copy-start.2 = (f32[2,256,256]{2,1,0:T(8,128)S(1)}, f32[2,256,256]{2,1,0:T(8,128)}, u32[]{:S(2)}) copy-start(f32[2,256,256]{2,1,0:T(8,128)} %copy.136) | copy-start | bytes 1572868
  85.0 16.0 %collective-permute-start.4 = (f32[2,1,1,256,256]{3,4,0,2,1:T(8,128)}, f32[2,1,1,256,256]{3,4,0,2,1:T(8,128)S(1)}, u32[]{:S(2)}, u32[]{:S(2)}) collective-permute-start(f32[2,1,1,256,256]{3,4,0,2,1:T(8,128)} %get-tuple-element.120), channel_id=1, source_target_pairs={{0,8},{8,16},{16,24},{24,0},{1,9},{9,17},{17,25},{25,1},{2,10},{10... | collective-permute-start | bytes 1572872 | tf_op jit(solution)/shard_map/ppermute | solution.py:231
  86.4 24.2 %collective-permute-start.5 = (f32[2,1,1,256,256]{3,4,0,2,1:T(8,128)S(1)}, f32[2,1,1,256,256]{3,4,0,2,1:T(8,128)S(1)}, u32[]{:S(2)}, u32[]{:S(2)}) collective-permute-start(f32[2,1,1,256,256]{3,4,0,2,1:T(8,128)S(1)} %get-tuple-element.121), channel_id=1, source_target_pairs={{0,16},{8,24},{16,0},{24,8},{1,17},{9,25},{17,1},{25,9},{2,18},{10... | collective-permute-start | bytes 1572872 | tf_op jit(solution)/shard_map/ppermute | solution.py:231
  87.0 23.7 %collective-permute-start.6 = (f32[2,1,1,256,256]{3,4,1,2,0:T(8,128)S(1)}, f32[2,1,1,256,256]{3,4,1,2,0:T(8,128)S(1)}, u32[]{:S(2)}, u32[]{:S(2)}) collective-permute-start(f32[2,1,1,256,256]{3,4,1,2,0:T(8,128)S(1)} %get-tuple-element.118), channel_id=1, source_target_pairs={{0,24},{8,0},{16,8},{24,16},{1,25},{9,1},{17,9},{25,17},{2,26},{10... | collective-permute-start | bytes 1572872 | tf_op jit(solution)/shard_map/ppermute | solution.py:231
  113.7 3.4 %collective-permute-start.7 = (f32[2,1,512,128]{2,3,0,1:T(8,128)S(1)}, f32[2,1,512,128]{2,3,0,1:T(8,128)S(1)}, u32[]{:S(2)}, u32[]{:S(2)}) collective-permute-start(f32[2,1,512,128]{2,3,0,1:T(8,128)S(1)} %get-tuple-element.117), channel_id=1, source_target_pairs={{0,1},{2,3},{4,5},{6,7},{8,9},{10,11},{12,13},{14,15},{16,17},{18,... | collective-permute-start | bytes 1572872 | tf_op jit(solution)/shard_map/ppermute | solution.py:15
  115.6 3.8 %collective-permute-start.8 = (f32[2,1,512,128]{2,3,0,1:T(8,128)S(1)}, f32[2,1,512,128]{2,3,0,1:T(8,128)S(1)}, u32[]{:S(2)}, u32[]{:S(2)}) collective-permute-start(f32[2,1,512,128]{2,3,0,1:T(8,128)S(1)} %get-tuple-element.116), channel_id=1, source_target_pairs={{1,0},{3,2},{5,4},{7,6},{9,8},{11,10},{13,12},{15,14},{17,16},{19,... | collective-permute-start | bytes 1572872 | tf_op jit(solution)/shard_map/ppermute | solution.py:15
  119.6 9.3 %collective-permute-start.9 = (f32[2,1,128,256]{2,3,0,1:T(8,128)S(1)}, f32[2,1,128,256]{2,3,0,1:T(8,128)S(1)}, u32[]{:S(2)}, u32[]{:S(2)}) collective-permute-start(f32[2,1,128,256]{2,3,0,1:T(8,128)S(1)} %get-tuple-element.129), channel_id=1, source_target_pairs={{0,2},{2,4},{4,6},{1,3},{3,5},{5,7},{8,10},{10,12},{12,14},{9,11},... | collective-permute-start | bytes 786440 | tf_op jit(solution)/shard_map/ppermute | solution.py:15
  123.2 10.0 %collective-permute-start.10 = (f32[2,1,128,256]{2,3,0,1:T(8,128)S(1)}, f32[2,1,128,256]{2,3,0,1:T(8,128)S(1)}, u32[]{:S(2)}, u32[]{:S(2)}) collective-permute-start(f32[2,1,128,256]{2,3,0,1:T(8,128)S(1)} %get-tuple-element.128), channel_id=1, source_target_pairs={{2,0},{4,2},{6,4},{3,1},{5,3},{7,5},{10,8},{12,10},{14,12},{11,9},... | collective-permute-start | bytes 786440 | tf_op jit(solution)/shard_map/ppermute | solution.py:15

commit v4 on v3

--- a/solution.py
+++ b/solution.py
@@ -179,7 +179,10 @@
     depth_index = lax.axis_index("depth")
     row_index = lax.axis_index("row")
     col_index = lax.axis_index("col")
-    corners = offsets[0, 0]
+    stacked = to_transmit(jnp.stack((phase, absorption)))
+    tall_slab = with_halo(stacked, (("row", 2),), rim)
+    after = (stacked[0, 0, 0, 0] * 0.0).astype(jnp.int32)
+    corners = offsets[0, 0] + after
     row_starts = corners[:, 0] - row_index * tile_rows + rim
     col_starts = corners[:, 1] - col_index * tile_cols + rim
     row_starts = [jnp.clip(row_starts[k], 0, 2 * rim + tile_rows - width) for k in range(probes)]
@@ -191,11 +194,10 @@
         source = (depth_index - shift) % depth_count
         source_rows.append([lax.select_n(source * share + slot, *row_starts) for slot in range(share)])
         source_cols.append([lax.select_n(source * share + slot, *col_starts) for slot in range(share)])
-    stacked = to_transmit(jnp.stack((phase, absorption)))
-    row_starts, col_starts, source_rows, source_cols, stacked = lax.optimization_barrier(
-        (row_starts, col_starts, source_rows, source_cols, stacked)
-    )
-    extended = with_halo(stacked, (("row", 2), ("col", 3)), rim)
+    row_starts, col_starts, source_rows, source_cols, tall_slab = lax.optimization_barrier(
+        (row_starts, col_starts, source_rows, source_cols, tall_slab)
+    )
+    extended = with_halo(tall_slab, (("col", 3),), rim)
     anchor = jnp.zeros((), jnp.int32)
     fresnel, far_field = build_tables(width)
     share = probes // depth_count

time: 135 us -> 127 us (0.941)
  waiting for transfers between devices: 54.2 us -> 47.7 us
  other arithmetic: 16.8 us -> 14.9 us
    ppermute x2, waiting for transfers between devices: 4.23 us -> 0.01 us  [with_halo(): lax.ppermute(lax.slice_in_dim(block, block.shape[dim] - width, None, axis...]
    ppermute x2, waiting for transfers between devices: 4.84 us -> 3.08 us  [with_halo(): lax.ppermute(lax.slice_in_dim(block, 0, width, axis=dim), axis, backward)]
    unnamed x18 -> x20, local copies, waits for them, and re-layouts: 4.17 us -> 4.18 us
  transfers between devices with their start and end apart: 12 -> 12, of which waited for: 11 -> 9; matrix products, arithmetic and copies ran while one was open for 12% -> 13% of each run, Pallas kernels for 0% -> 0%
where the time goes in v4:
time: 127 us
  waiting for transfers between devices  47.7 us (38%)
  starting transfers between devices  25.1 us (20%)
  matrix products  20.6 us (16%)
  other arithmetic  14.9 us (12%)
  local copies, waits for them, and re-layouts  11.4 us (9%)
  between operations  7.1 us (6%)
    ppermute x3, waiting for transfers between devices, per_device(): chunk = lax.ppermute(chunk, 'depth', pairs)  21 us
    all_to_all x1, waiting for transfers between devices, per_device(): gathered = lax.all_to_all(cut, 'depth', 2, 1, tiled=True)  12.7 us
    ppermute x4, waiting for transfers between devices, from_behind(): lax.ppermute(value, axis, [(source, source + steps) for source in range(l...  10.9 us
    ppermute x4, starting transfers between devices, from_behind(): lax.ppermute(value, axis, [(source, source + steps) for source in range(l...  7.97 us
    dot_general x8, matrix products, right_product(): jnp.einsum('bij,kj->bik', waves, matrix, precision=mode, preferred_elemen...  7.44 us
    dot_general x8, matrix products, left_product(): jnp.einsum('ij,bjk->bik', matrix, waves, precision=mode, preferred_elemen...  7.31 us
    ppermute x2, starting transfers between devices, with_halo(): lax.ppermute(lax.slice_in_dim(block, block.shape[dim] - width, None, axis...  6.25 us
    dot_general x4, matrix products, matmul_exact(): jnp.dot(first, second, precision=exact_mode, preferred_element_type=jnp.f...  5.8 us
  transfers between devices with their start and end apart: 12, of which 9 were waited for; matrix products, arithmetic and copies ran while one was open for 13% of the time, Pallas kernels for 0%

profile of v4, /device:TPU:0, one launch (start us, length us, event | category | flops | bytes accessed | tf_op | source)
XLA Modules:
  0.0 126.7 jit_solution(4213345411305253255)
XLA Ops:
  0.6 2.0 %multiply_bitcast_fusion = (f32[1,1,256,256]{3,2,1,0:T(8,128)S(1)}, f32[1,1,256,256]{3,2,1,0:T(8,128)S(1)}) fusion(f32[1,256,256]{2,1,0:T(8,128)} %param.13, f32[1,256,256]{2,1,0:T(8,128)} %param.14), kind=kLoop, calls=%fused_computation.211 | loop fusion | flops 196608 | bytes 1048576 | tf_op jit(solution)/shard_map/stack | solution.py:160
  2.7 4.9 %collective-permute-start = (f32[2,1,128,256]{3,2,1,0:T(8,128)S(1)}, f32[2,1,128,256]{3,2,1,0:T(8,128)S(1)}, u32[]{:S(2)}, u32[]{:S(2)}) collective-permute-start(f32[2,1,128,256]{3,2,1,0:T(8,128)S(1)} %get-tuple-element.163), channel_id=1, source_target_pairs={{0,2},{2,4},{4,6},{1,3},{3,5},{5,7},{8,10},{10,12},{12,14},{9,11},... | collective-permute-start | bytes 786440 | tf_op jit(solution)/shard_map/ppermute | solution.py:28
  7.6 1.3 %collective-permute-start.1 = (f32[2,1,128,256]{3,2,1,0:T(8,128)S(1)}, f32[2,1,128,256]{3,2,1,0:T(8,128)S(1)}, u32[]{:S(2)}, u32[]{:S(2)}) collective-permute-start(f32[2,1,128,256]{3,2,1,0:T(8,128)S(1)} %get-tuple-element.164), channel_id=1, source_target_pairs={{2,0},{4,2},{6,4},{3,1},{5,3},{7,5},{10,8},{12,10},{14,12},{11,9},... | collective-permute-start | bytes 786440 | tf_op jit(solution)/shard_map/ppermute | solution.py:31
  15.9 1.3 %collective-permute-done.1 = f32[2,1,128,256]{3,2,1,0:T(8,128)S(1)} collective-permute-done((f32[2,1,128,256]{3,2,1,0:T(8,128)S(1)}, f32[2,1,128,256]{3,2,1,0:T(8,128)S(1)}, u32[]{:S(2)}, u32[]{:S(2)}) %collective-permute-start.1) | collective-permute-done | bytes 262176 | tf_op jit(solution)/shard_map/ppermute | solution.py:31
  17.4 1.1 fusion.144
  18.5 1.3 %collective-permute-start.2 = (f32[2,1,512,128]{3,2,1,0:T(8,128)}, f32[2,1,512,128]{3,2,1,0:T(8,128)S(1)}, u32[]{:S(2)}, u32[]{:S(2)}) collective-permute-start(f32[2,1,512,128]{3,2,1,0:T(8,128)} %get-tuple-element.146), channel_id=1, source_target_pairs={{0,1},{2,3},{4,5},{6,7},{8,9},{10,11},{12,13},{14,15},{16,17},{18,... | collective-permute-start | bytes 1572872 | tf_op jit(solution)/shard_map/ppermute | solution.py:28
  19.8 1.0 sine_negate_fusion
  20.8 1.3 %collective-permute-start.3 = (f32[2,1,512,128]{3,2,1,0:T(8,128)}, f32[2,1,512,128]{3,2,1,0:T(8,128)S(1)}, u32[]{:S(2)}, u32[]{:S(2)}) collective-permute-start(f32[2,1,512,128]{3,2,1,0:T(8,128)} %get-tuple-element.147), channel_id=1, source_target_pairs={{1,0},{3,2},{5,4},{7,6},{9,8},{11,10},{13,12},{15,14},{17,16},{19,... | collective-permute-start | bytes 1572872 | tf_op jit(solution)/shard_map/ppermute | solution.py:31
  23.1 1.8 %collective-permute-done.3 = f32[2,1,512,128]{3,2,1,0:T(8,128)S(1)} collective-permute-done((f32[2,1,512,128]{3,2,1,0:T(8,128)}, f32[2,1,512,128]{3,2,1,0:T(8,128)S(1)}, u32[]{:S(2)}, u32[]{:S(2)}) %collective-permute-start.3) | collective-permute-done | bytes 524320 | tf_op jit(solution)/shard_map/ppermute | solution.py:31
  26.6 1.6 %pad_maximum_fusion = f32[2,1,4,256,256]{3,4,0,1,2:T(8,128)} fusion(f32[2,1,1,256,256]{3,4,0,1,2:T(8,128)S(1)} %bitcast.290, f32[2,1,1,256,256]{3,4,0,1,2:T(8,128)S(1)} %bitcast.289, f32[2,1,1,256,256]{3,4,0,1,2:T(8,128)S(1)} %bitcast.288, f32[2,1,1,256,256]{3,4,0,1,2:T(8,128)S(1)} %bitcast.287), kind=kLoop, calls=%fused_computation.16 | loop fusion | flops 1572864 | bytes 4194304 | tf_op jit(solution)/shard_map/stack | solution.py:205
  28.2 3.9 %all-to-all-start = ((f32[2,1,4,256,256]{3,4,0,1,2:T(8,128)}), f32[2,1,4,256,256]{3,4,0,1,2:T(8,128)S(1)}, u32[]{:S(2)}, u32[]{:S(2)}) async-start(f32[2,1,4,256,256]{3,4,0,1,2:T(8,128)} %pad_maximum_fusion), calls=%async_computation | async-start | bytes 4194304 | tf_op jit(solution)/shard_map/all_to_all | solution.py:214
  36.6 1.4 %fusion.78 = f32[256,256]{1,0:T(8,128)S(1)} fusion(f32[256]{0:T(256)S(1)} %get-tuple-element.185, f32[256]{0:T(256)S(1)} %get-tuple-element.186), kind=kOutput, calls=%fused_computation.204 | convolution fusion | flops 203358208 | bytes 264192 | tf_op jit(solution)/shard_map/dot_general | solution.py:39
  38.1 1.5 %fusion.3 = f32[1,256,256]{2,1,0:T(8,128)S(1)} fusion(f32[256,256]{1,0:T(8,128)S(1)} %fusion.78, f32[256]{0:T(256)S(1)} %get-tuple-element.185, f32[256]{0:T(256)S(1)} %get-tuple-element.186), kind=kOutput, calls=%fused_computation.27 | convolution fusion | flops 203423744 | bytes 526336 | tf_op jit(solution)/shard_map/dot_general | solution.py:39
  39.5 1.4 %fusion.79 = f32[256,256]{1,0:T(8,128)S(1)} fusion(f32[256]{0:T(256)S(1)} %get-tuple-element.185, f32[256]{0:T(256)S(1)} %get-tuple-element.186), kind=kOutput, calls=%fused_computation.206 | convolution fusion | flops 203358208 | bytes 264192 | tf_op jit(solution)/shard_map/dot_general | solution.py:39
  41.0 1.5 %fusion.4 = f32[1,256,256]{2,1,0:T(8,128)S(1)} fusion(f32[256,256]{1,0:T(8,128)S(1)} %fusion.79, f32[256]{0:T(256)S(1)} %get-tuple-element.185, f32[256]{0:T(256)S(1)} %get-tuple-element.186), kind=kOutput, calls=%fused_computation.29 | convolution fusion | flops 203423744 | bytes 526336 | tf_op jit(solution)/shard_map/dot_general | solution.py:39
  43.4 1.2 copy.143
  44.6 12.7 %all-to-all-done = f32[2,1,4,256,256]{3,4,0,1,2:T(8,128)S(1)} async-done(((f32[2,1,4,256,256]{3,4,0,1,2:T(8,128)}), f32[2,1,4,256,256]{3,4,0,1,2:T(8,128)S(1)}, u32[]{:S(2)}, u32[]{:S(2)}) %all-to-all-start) | async-done | bytes 2097184 | tf_op jit(solution)/shard_map/all_to_all | solution.py:214
  63.0 1.3 %convolution_bitcast_fusion.5 = f32[2,512,256]{1,2,0:T(8,128)S(1)} fusion(f32[512,256,1]{1,0,2:T(8,128)S(1)} %bitcast.260, f32[1,1,256,256]{2,3,1,0:T(8,128)S(1)} %bitcast.282, f32[1,1,256,256]{2,3,1,0:T(8,128)S(1)} %bitcast.281), kind=kOutput, calls=%fused_computation.23 | convolution fusion | flops 805437440 | bytes 2097152 | tf_op jit(solution)/shard_map/ij,bjk->bik/dot_general | solution.py:66
  66.6 1.9 %fusion.34 = f32[2,256,512]{2,1,0:T(8,128)S(1)} fusion(f32[512,256,1]{1,0,2:T(8,128)S(1)} %bitcast.276, f32[1,256,256]{1,2,0:T(8,128)S(1)} %get-tuple-element.139, f32[1,256,256]{1,2,0:T(8,128)S(1)} %get-tuple-element.138), kind=kOutput, calls=%fused_computation.72 | convolution fusion | flops 805437440 | bytes 2097152 | tf_op jit(solution)/shard_map/bij,kj->bik/dot_general | solution.py:72
  69.6 1.1 convolution_bitcast_fusion.3
  77.2 1.4 %collective-permute-start.4 = (f32[2,1,1,256,256]{3,4,0,2,1:T(8,128)}, f32[2,1,1,256,256]{3,4,0,2,1:T(8,128)S(1)}, u32[]{:S(2)}, u32[]{:S(2)}) collective-permute-start(f32[2,1,1,256,256]{3,4,0,2,1:T(8,128)} %get-tuple-element.120), channel_id=1, source_target_pairs={{0,8},{8,16},{16,24},{24,0},{1,9},{9,17},{17,25},{25,1},{2,10},{10... | collective-permute-start | bytes 1572872 | tf_op jit(solution)/shard_map/ppermute | solution.py:233
  79.2 2.4 %collective-permute-start.6 = (f32[2,1,1,256,256]{3,4,1,2,0:T(8,128)S(1)}, f32[2,1,1,256,256]{3,4,1,2,0:T(8,128)S(1)}, u32[]{:S(2)}, u32[]{:S(2)}) collective-permute-start(f32[2,1,1,256,256]{3,4,1,2,0:T(8,128)S(1)} %get-tuple-element.118), channel_id=1, source_target_pairs={{0,24},{8,0},{16,8},{24,16},{1,25},{9,1},{17,9},{25,17},{2,26},{10... | collective-permute-start | bytes 1572872 | tf_op jit(solution)/shard_map/ppermute | solution.py:233
  81.6 11.6 %collective-permute-done.4 = f32[2,1,1,256,256]{3,4,0,2,1:T(8,128)S(1)} collective-permute-done((f32[2,1,1,256,256]{3,4,0,2,1:T(8,128)}, f32[2,1,1,256,256]{3,4,0,2,1:T(8,128)S(1)}, u32[]{:S(2)}, u32[]{:S(2)}) %collective-permute-start.4) | collective-permute-done | bytes 524320 | tf_op jit(solution)/shard_map/ppermute | solution.py:233
  93.2 9.3 %collective-permute-done.5 = f32[2,1,1,256,256]{3,4,0,2,1:T(8,128)S(1)} collective-permute-done((f32[2,1,1,256,256]{3,4,0,2,1:T(8,128)S(1)}, f32[2,1,1,256,256]{3,4,0,2,1:T(8,128)S(1)}, u32[]{:S(2)}, u32[]{:S(2)}) %collective-permute-start.5) | collective-permute-done | bytes 524320 | tf_op jit(solution)/shard_map/ppermute | solution.py:233
  102.6 2.9 %fusion.2 = f32[2,1,512,512]{2,3,0,1:T(8,128)S(1)} fusion(s32[]{:T(128)S(6)} %select_n.421, s32[]{:T(128)S(6)} %select_n.422, f32[2,1,256,256]{2,3,0,1:T(8,128)S(1)} %get-tuple-element.119, s32[]{:T(128)S(6)} %select_n.425, s32[]{:T(128)S(6)} %select_n.426, f32[2,1,256,256]{2,3,0,1:T(8,128)S(1)} %bitcast.291, s32[]{:T(128)S(6)} %select_n.429, ...), kind=kLoop, calls=%fused_computation.14 | loop fusion | flops 1572864 | bytes 4194336 | tf_op jit(solution)/shard_map/add | solution.py:235
  105.6 1.9 %collective-permute-start.7 = (f32[2,1,512,128]{2,3,0,1:T(8,128)S(1)}, f32[2,1,512,128]{2,3,0,1:T(8,128)S(1)}, u32[]{:S(2)}, u32[]{:S(2)}) collective-permute-start(f32[2,1,512,128]{2,3,0,1:T(8,128)S(1)} %get-tuple-element.117), channel_id=1, source_target_pairs={{0,1},{2,3},{4,5},{6,7},{8,9},{10,11},{12,13},{14,15},{16,17},{18,... | collective-permute-start | bytes 1572872 | tf_op jit(solution)/shard_map/ppermute | solution.py:15
  107.5 1.3 %collective-permute-start.8 = (f32[2,1,512,128]{2,3,0,1:T(8,128)S(1)}, f32[2,1,512,128]{2,3,0,1:T(8,128)S(1)}, u32[]{:S(2)}, u32[]{:S(2)}) collective-permute-start(f32[2,1,512,128]{2,3,0,1:T(8,128)S(1)} %get-tuple-element.116), channel_id=1, source_target_pairs={{1,0},{3,2},{5,4},{7,6},{9,8},{11,10},{13,12},{15,14},{17,16},{19,... | collective-permute-start | bytes 1572872 | tf_op jit(solution)/shard_map/ppermute | solution.py:15
  109.1 2.2 %collective-permute-done.8 = f32[2,1,512,128]{2,3,0,1:T(8,128)S(1)} collective-permute-done((f32[2,1,512,128]{2,3,0,1:T(8,128)S(1)}, f32[2,1,512,128]{2,3,0,1:T(8,128)S(1)}, u32[]{:S(2)}, u32[]{:S(2)}) %collective-permute-start.8) | collective-permute-done | bytes 524320 | tf_op jit(solution)/shard_map/ppermute | solution.py:15
  111.5 3.5 %collective-permute-start.9 = (f32[2,1,128,256]{2,3,0,1:T(8,128)S(1)}, f32[2,1,128,256]{2,3,0,1:T(8,128)S(1)}, u32[]{:S(2)}, u32[]{:S(2)}) collective-permute-start(f32[2,1,128,256]{2,3,0,1:T(8,128)S(1)} %get-tuple-element.129), channel_id=1, source_target_pairs={{0,2},{2,4},{4,6},{1,3},{3,5},{5,7},{8,10},{10,12},{12,14},{9,11},... | collective-permute-start | bytes 786440 | tf_op jit(solution)/shard_map/ppermute | solution.py:15
  115.0 1.3 %collective-permute-start.10 = (f32[2,1,128,256]{2,3,0,1:T(8,128)S(1)}, f32[2,1,128,256]{2,3,0,1:T(8,128)S(1)}, u32[]{:S(2)}, u32[]{:S(2)}) collective-permute-start(f32[2,1,128,256]{2,3,0,1:T(8,128)S(1)} %get-tuple-element.128), channel_id=1, source_target_pairs={{2,0},{4,2},{6,4},{3,1},{5,3},{7,5},{10,8},{12,10},{14,12},{11,9},... | collective-permute-start | bytes 786440 | tf_op jit(solution)/shard_map/ppermute | solution.py:15
  116.3 4.5 %collective-permute-done.9 = f32[2,1,128,256]{2,3,0,1:T(8,128)S(1)} collective-permute-done((f32[2,1,128,256]{2,3,0,1:T(8,128)S(1)}, f32[2,1,128,256]{2,3,0,1:T(8,128)S(1)}, u32[]{:S(2)}, u32[]{:S(2)}) %collective-permute-start.9) | collective-permute-done | bytes 262176 | tf_op jit(solution)/shard_map/ppermute | solution.py:15
  120.9 4.1 %collective-permute-done.10 = f32[2,1,128,256]{2,3,0,1:T(8,128)S(1)} collective-permute-done((f32[2,1,128,256]{2,3,0,1:T(8,128)S(1)}, f32[2,1,128,256]{2,3,0,1:T(8,128)S(1)}, u32[]{:S(2)}, u32[]{:S(2)}) %collective-permute-start.10) | collective-permute-done | bytes 262176 | tf_op jit(solution)/shard_map/ppermute | solution.py:15
  (96 shorter events, 27.6 us)
Async XLA Ops:
  0.6 9.5 %copy-start.7 = (s32[1,1,4,2]{2,3,1,0:T(2,128)S(1)}, s32[1,1,4,2]{2,3,1,0:T(2,128)}, u32[]{:S(2)}) copy-start(s32[1,1,4,2]{2,3,1,0:T(2,128)} %param.17) | copy-start | bytes 100
  2.7 13.3 %collective-permute-start = (f32[2,1,128,256]{3,2,1,0:T(8,128)S(1)}, f32[2,1,128,256]{3,2,1,0:T(8,128)S(1)}, u32[]{:S(2)}, u32[]{:S(2)}) collective-permute-start(f32[2,1,128,256]{3,2,1,0:T(8,128)S(1)} %get-tuple-element.163), channel_id=1, source_target_pairs={{0,2},{2,4},{4,6},{1,3},{3,5},{5,7},{8,10},{10,12},{12,14},{9,11},... | collective-permute-start | bytes 786440 | tf_op jit(solution)/shard_map/ppermute | solution.py:28
  7.6 9.7 %collective-permute-start.1 = (f32[2,1,128,256]{3,2,1,0:T(8,128)S(1)}, f32[2,1,128,256]{3,2,1,0:T(8,128)S(1)}, u32[]{:S(2)}, u32[]{:S(2)}) collective-permute-start(f32[2,1,128,256]{3,2,1,0:T(8,128)S(1)} %get-tuple-element.164), channel_id=1, source_target_pairs={{2,0},{4,2},{6,4},{3,1},{5,3},{7,5},{10,8},{12,10},{14,12},{11,9},... | collective-permute-start | bytes 786440 | tf_op jit(solution)/shard_map/ppermute | solution.py:31
  17.4 4.8 %copy-start.6 = (f32[2,256,256]{2,1,0:T(8,128)S(1)}, f32[2,256,256]{2,1,0:T(8,128)}, u32[]{:S(2)}) copy-start(f32[2,256,256]{2,1,0:T(8,128)} %param.15) | copy-start | bytes 1572868
  18.5 4.6 %collective-permute-start.2 = (f32[2,1,512,128]{3,2,1,0:T(8,128)}, f32[2,1,512,128]{3,2,1,0:T(8,128)S(1)}, u32[]{:S(2)}, u32[]{:S(2)}) collective-permute-start(f32[2,1,512,128]{3,2,1,0:T(8,128)} %get-tuple-element.146), channel_id=1, source_target_pairs={{0,1},{2,3},{4,5},{6,7},{8,9},{10,11},{12,13},{14,15},{16,17},{18,... | collective-permute-start | bytes 1572872 | tf_op jit(solution)/shard_map/ppermute | solution.py:28
  20.8 4.0 %collective-permute-start.3 = (f32[2,1,512,128]{3,2,1,0:T(8,128)}, f32[2,1,512,128]{3,2,1,0:T(8,128)S(1)}, u32[]{:S(2)}, u32[]{:S(2)}) collective-permute-start(f32[2,1,512,128]{3,2,1,0:T(8,128)} %get-tuple-element.147), channel_id=1, source_target_pairs={{1,0},{3,2},{5,4},{7,6},{9,8},{11,10},{13,12},{15,14},{17,16},{19,... | collective-permute-start | bytes 1572872 | tf_op jit(solution)/shard_map/ppermute | solution.py:31
  22.2 9.9 %copy-start = (f32[2,256,256]{2,1,0:T(8,128)}, f32[2,256,256]{2,1,0:T(8,128)S(1)}, u32[]{:S(2)}) copy-start(f32[2,256,256]{2,1,0:T(8,128)S(1)} %maximum_multiply_fusion.1) | copy-start | bytes 1572868
  28.2 4.7 %copy-start.3 = (f32[1,256,256]{2,1,0:T(8,128)S(1)}, f32[1,256,256]{2,1,0:T(8,128)}, u32[]{:S(2)}) copy-start(f32[1,256,256]{2,1,0:T(8,128)} %get-tuple-element.158) | copy-start | bytes 786436
  28.2 29.2 %all-to-all-start = ((f32[2,1,4,256,256]{3,4,0,1,2:T(8,128)}), f32[2,1,4,256,256]{3,4,0,1,2:T(8,128)S(1)}, u32[]{:S(2)}, u32[]{:S(2)}) async-start(f32[2,1,4,256,256]{3,4,0,1,2:T(8,128)} %pad_maximum_fusion), calls=%async_computation | async-start | bytes 4194304 | tf_op jit(solution)/shard_map/all_to_all | solution.py:214
  44.6 12.9 %copy-start.4 = (f32[1,256,256]{1,2,0:T(8,128)S(1)}, f32[1,256,256]{1,2,0:T(8,128)}, u32[]{:S(2)}) copy-start(f32[1,256,256]{1,2,0:T(8,128)} %copy.182) | copy-start | bytes 786436
  57.4 1.0 copy-start.5
  64.3 1.2 copy-start.1
  66.6 3.0 %copy-start.2 = (f32[2,256,256]{2,1,0:T(8,128)S(1)}, f32[2,256,256]{2,1,0:T(8,128)}, u32[]{:S(2)}) copy-start(f32[2,256,256]{2,1,0:T(8,128)} %copy.136) | copy-start | bytes 1572868
  77.2 16.0 %collective-permute-start.4 = (f32[2,1,1,256,256]{3,4,0,2,1:T(8,128)}, f32[2,1,1,256,256]{3,4,0,2,1:T(8,128)S(1)}, u32[]{:S(2)}, u32[]{:S(2)}) collective-permute-start(f32[2,1,1,256,256]{3,4,0,2,1:T(8,128)} %get-tuple-element.120), channel_id=1, source_target_pairs={{0,8},{8,16},{16,24},{24,0},{1,9},{9,17},{17,25},{25,1},{2,10},{10... | collective-permute-start | bytes 1572872 | tf_op jit(solution)/shard_map/ppermute | solution.py:233
  78.6 23.9 %collective-permute-start.5 = (f32[2,1,1,256,256]{3,4,0,2,1:T(8,128)S(1)}, f32[2,1,1,256,256]{3,4,0,2,1:T(8,128)S(1)}, u32[]{:S(2)}, u32[]{:S(2)}) collective-permute-start(f32[2,1,1,256,256]{3,4,0,2,1:T(8,128)S(1)} %get-tuple-element.121), channel_id=1, source_target_pairs={{0,16},{8,24},{16,0},{24,8},{1,17},{9,25},{17,1},{25,9},{2,18},{10... | collective-permute-start | bytes 1572872 | tf_op jit(solution)/shard_map/ppermute | solution.py:233
  79.2 23.4 %collective-permute-start.6 = (f32[2,1,1,256,256]{3,4,1,2,0:T(8,128)S(1)}, f32[2,1,1,256,256]{3,4,1,2,0:T(8,128)S(1)}, u32[]{:S(2)}, u32[]{:S(2)}) collective-permute-start(f32[2,1,1,256,256]{3,4,1,2,0:T(8,128)S(1)} %get-tuple-element.118), channel_id=1, source_target_pairs={{0,24},{8,0},{16,8},{24,16},{1,25},{9,1},{17,9},{25,17},{2,26},{10... | collective-permute-start | bytes 1572872 | tf_op jit(solution)/shard_map/ppermute | solution.py:233
  105.6 3.4 %collective-permute-start.7 = (f32[2,1,512,128]{2,3,0,1:T(8,128)S(1)}, f32[2,1,512,128]{2,3,0,1:T(8,128)S(1)}, u32[]{:S(2)}, u32[]{:S(2)}) collective-permute-start(f32[2,1,512,128]{2,3,0,1:T(8,128)S(1)} %get-tuple-element.117), channel_id=1, source_target_pairs={{0,1},{2,3},{4,5},{6,7},{8,9},{10,11},{12,13},{14,15},{16,17},{18,... | collective-permute-start | bytes 1572872 | tf_op jit(solution)/shard_map/ppermute | solution.py:15
  107.5 3.8 %collective-permute-start.8 = (f32[2,1,512,128]{2,3,0,1:T(8,128)S(1)}, f32[2,1,512,128]{2,3,0,1:T(8,128)S(1)}, u32[]{:S(2)}, u32[]{:S(2)}) collective-permute-start(f32[2,1,512,128]{2,3,0,1:T(8,128)S(1)} %get-tuple-element.116), channel_id=1, source_target_pairs={{1,0},{3,2},{5,4},{7,6},{9,8},{11,10},{13,12},{15,14},{17,16},{19,... | collective-permute-start | bytes 1572872 | tf_op jit(solution)/shard_map/ppermute | solution.py:15
  111.5 9.3 %collective-permute-start.9 = (f32[2,1,128,256]{2,3,0,1:T(8,128)S(1)}, f32[2,1,128,256]{2,3,0,1:T(8,128)S(1)}, u32[]{:S(2)}, u32[]{:S(2)}) collective-permute-start(f32[2,1,128,256]{2,3,0,1:T(8,128)S(1)} %get-tuple-element.129), channel_id=1, source_target_pairs={{0,2},{2,4},{4,6},{1,3},{3,5},{5,7},{8,10},{10,12},{12,14},{9,11},... | collective-permute-start | bytes 786440 | tf_op jit(solution)/shard_map/ppermute | solution.py:15
  115.0 10.0 %collective-permute-start.10 = (f32[2,1,128,256]{2,3,0,1:T(8,128)S(1)}, f32[2,1,128,256]{2,3,0,1:T(8,128)S(1)}, u32[]{:S(2)}, u32[]{:S(2)}) collective-permute-start(f32[2,1,128,256]{2,3,0,1:T(8,128)S(1)} %get-tuple-element.128), channel_id=1, source_target_pairs={{2,0},{4,2},{6,4},{3,1},{5,3},{7,5},{10,8},{12,10},{14,12},{11,9},... | collective-permute-start | bytes 786440 | tf_op jit(solution)/shard_map/ppermute | solution.py:15

commit v5 on v4

--- a/solution.py
+++ b/solution.py
@@ -91,6 +91,22 @@
     return jnp.stack((outer_re, outer_im))
 
 
+def propagate_three(matrix, waves, mode):
+    first, second = matrix[0], matrix[1]
+    factors = jnp.stack((first, second, first + second))
+    left = jnp.stack((waves[0], waves[1], waves[0] + waves[1]))
+    prod = jnp.einsum(
+        "nij,nbjk->nbik", factors, left, precision=mode, preferred_element_type=jnp.float32
+    )
+    inner_re = prod[0] - prod[1]
+    inner_im = prod[2] - prod[0] - prod[1]
+    right = jnp.stack((inner_re, inner_im, inner_re + inner_im))
+    prod = jnp.einsum(
+        "nbij,nkj->nbik", right, factors, precision=mode, preferred_element_type=jnp.float32
+    )
+    return jnp.stack((prod[0] - prod[1], prod[2] - prod[0] - prod[1]))
+
+
 def forward_layers(wave, slab, matrices):
     moved_list = []
     for layer in range(slab.shape[1]):
@@ -100,7 +116,7 @@
             (trans_re * wave[0] - trans_im * wave[1], trans_re * wave[1] + trans_im * wave[0])
         )
         moved_list.append(moved)
-        wave = propagate(matrices[layer], moved, exact_mode)
+        wave = propagate_three(matrices[layer], moved, exact_mode)
     return (wave, jnp.stack(moved_list, axis=1))
 
 

time: 127 us -> 128 us (level)
  waiting for transfers between devices: 47.7 us -> 49.7 us
    dot_general x0 -> x8, matrix products: none -> 9.44 us  [the longest x4 5.84 us: propagate_three(): jnp.einsum('nbij,nkj->nbik', right, factors, precision=mode, preferred_el...]
    dot_general x8 -> x4, matrix products: 7.44 us -> 2.41 us  [right_product(): jnp.einsum('bij,kj->bik', waves, matrix, precision=mode, preferred_elemen...]
    dot_general x8 -> x4, matrix products: 7.31 us -> 2.93 us  [left_product(): jnp.einsum('ij,bjk->bik', matrix, waves, precision=mode, preferred_elemen...]
    another operation x4 -> x3, other arithmetic: 2.6 us -> 0.12 us  [adjoint_of(): return jnp.stack((matrix[0].T, -matrix[1].T))]
    all_to_all x1, waiting for transfers between devices: 12.7 us -> 14.7 us  [per_device(): gathered = lax.all_to_all(cut, 'depth', 2, 1, tiled=True)]
    unnamed x20 -> x18, local copies, waits for them, and re-layouts: 4.18 us -> 4.26 us
  transfers between devices with their start and end apart: 12 -> 12, of which waited for: 9 -> 9; matrix products, arithmetic and copies ran while one was open for 13% -> 11% of each run, Pallas kernels for 0% -> 0%
where the time goes in v5:
time: 128 us
  waiting for transfers between devices  49.7 us (39%)
  starting transfers between devices  25 us (20%)
  matrix products  21.3 us (17%)
  other arithmetic  14.5 us (11%)
  local copies, waits for them, and re-layouts  10.3 us (8%)
  between operations  7.2 us (6%)
    ppermute x3, waiting for transfers between devices, per_device(): chunk = lax.ppermute(chunk, 'depth', pairs)  21 us
    all_to_all x1, waiting for transfers between devices, per_device(): gathered = lax.all_to_all(cut, 'depth', 2, 1, tiled=True)  14.7 us
    ppermute x4, waiting for transfers between devices, from_behind(): lax.ppermute(value, axis, [(source, source + steps) for source in range(l...  10.9 us
    ppermute x4, starting transfers between devices, from_behind(): lax.ppermute(value, axis, [(source, source + steps) for source in range(l...  8.01 us
    dot_general x4, matrix products, matmul_exact(): jnp.dot(first, second, precision=exact_mode, preferred_element_type=jnp.f...  6.52 us
    ppermute x2, starting transfers between devices, with_halo(): lax.ppermute(lax.slice_in_dim(block, block.shape[dim] - width, None, axis...  6.25 us
    dot_general x4, matrix products, propagate_three(): jnp.einsum('nbij,nkj->nbik', right, factors, precision=mode, preferred_el...  5.84 us
    ppermute x3, starting transfers between devices, per_device(): chunk = lax.ppermute(chunk, 'depth', pairs)  4.39 us
  transfers between devices with their start and end apart: 12, of which 9 were waited for; matrix products, arithmetic and copies ran while one was open for 11% of the time, Pallas kernels for 0%

profile of v5, /device:TPU:0, one launch (start us, length us, event | category | flops | bytes accessed | tf_op | source)
XLA Modules:
  0.0 127.9 jit_solution(1177688467048057264)
XLA Ops:
  0.6 2.0 %multiply_bitcast_fusion = (f32[1,1,256,256]{3,2,1,0:T(8,128)S(1)}, f32[1,1,256,256]{3,2,1,0:T(8,128)S(1)}) fusion(f32[1,256,256]{2,1,0:T(8,128)} %param.13, f32[1,256,256]{2,1,0:T(8,128)} %param.14), kind=kLoop, calls=%fused_computation.229 | loop fusion | flops 196608 | bytes 1048576 | tf_op jit(solution)/shard_map/stack | solution.py:176
  2.7 4.9 %collective-permute-start = (f32[2,1,128,256]{3,2,1,0:T(8,128)S(1)}, f32[2,1,128,256]{3,2,1,0:T(8,128)S(1)}, u32[]{:S(2)}, u32[]{:S(2)}) collective-permute-start(f32[2,1,128,256]{3,2,1,0:T(8,128)S(1)} %get-tuple-element.173), channel_id=1, source_target_pairs={{0,2},{2,4},{4,6},{1,3},{3,5},{5,7},{8,10},{10,12},{12,14},{9,11},... | collective-permute-start | bytes 786440 | tf_op jit(solution)/shard_map/ppermute | solution.py:28
  7.6 1.3 %collective-permute-start.1 = (f32[2,1,128,256]{3,2,1,0:T(8,128)S(1)}, f32[2,1,128,256]{3,2,1,0:T(8,128)S(1)}, u32[]{:S(2)}, u32[]{:S(2)}) collective-permute-start(f32[2,1,128,256]{3,2,1,0:T(8,128)S(1)} %get-tuple-element.174), channel_id=1, source_target_pairs={{2,0},{4,2},{6,4},{3,1},{5,3},{7,5},{10,8},{12,10},{14,12},{11,9},... | collective-permute-start | bytes 786440 | tf_op jit(solution)/shard_map/ppermute | solution.py:31
  16.0 1.2 collective-permute-done.1
  18.2 1.3 %collective-permute-start.2 = (f32[2,1,512,128]{3,2,1,0:T(8,128)S(1)}, f32[2,1,512,128]{3,2,1,0:T(8,128)S(1)}, u32[]{:S(2)}, u32[]{:S(2)}) collective-permute-start(f32[2,1,512,128]{3,2,1,0:T(8,128)S(1)} %get-tuple-element.154), channel_id=1, source_target_pairs={{0,1},{2,3},{4,5},{6,7},{8,9},{10,11},{12,13},{14,15},{16,17},{18,... | collective-permute-start | bytes 1572872 | tf_op jit(solution)/shard_map/ppermute | solution.py:28
  20.6 1.3 %collective-permute-start.3 = (f32[2,1,512,128]{3,2,1,0:T(8,128)}, f32[2,1,512,128]{3,2,1,0:T(8,128)}, u32[]{:S(2)}, u32[]{:S(2)}) collective-permute-start(f32[2,1,512,128]{3,2,1,0:T(8,128)} %get-tuple-element.155), channel_id=1, source_target_pairs={{1,0},{3,2},{5,4},{7,6},{9,8},{11,10},{13,12},{15,14},{17,16},{19,... | collective-permute-start | bytes 1572872 | tf_op jit(solution)/shard_map/ppermute | solution.py:31
  22.9 1.9 %collective-permute-done.3 = f32[2,1,512,128]{3,2,1,0:T(8,128)} collective-permute-done((f32[2,1,512,128]{3,2,1,0:T(8,128)}, f32[2,1,512,128]{3,2,1,0:T(8,128)}, u32[]{:S(2)}, u32[]{:S(2)}) %collective-permute-start.3) | collective-permute-done | bytes 524320 | tf_op jit(solution)/shard_map/ppermute | solution.py:31
  27.6 1.6 %pad_maximum_fusion = f32[2,1,4,256,256]{3,4,0,1,2:T(8,128)} fusion(f32[2,1,1,256,256]{3,4,0,1,2:T(8,128)S(1)} %bitcast.314, f32[2,1,1,256,256]{3,4,0,1,2:T(8,128)S(1)} %bitcast.313, f32[2,1,1,256,256]{3,4,0,1,2:T(8,128)S(1)} %bitcast.312, f32[2,1,1,256,256]{3,4,0,1,2:T(8,128)S(1)} %bitcast.311), kind=kLoop, calls=%fused_computation.16 | loop fusion | flops 1572864 | bytes 4194304 | tf_op jit(solution)/shard_map/stack | solution.py:221
  29.1 3.8 %all-to-all-start = ((f32[2,1,4,256,256]{3,4,0,1,2:T(8,128)}), f32[2,1,4,256,256]{3,4,0,1,2:T(8,128)S(1)}, u32[]{:S(2)}, u32[]{:S(2)}) async-start(f32[2,1,4,256,256]{3,4,0,1,2:T(8,128)} %pad_maximum_fusion), calls=%async_computation | async-start | bytes 4194304 | tf_op jit(solution)/shard_map/all_to_all | solution.py:230
  32.9 1.1 fusion.172
  36.8 1.6 %fusion.96 = f32[256,256]{0,1:T(8,128)S(1)} fusion(f32[256]{0:T(256)S(1)} %get-tuple-element.195, f32[256]{0:T(256)S(1)} %get-tuple-element.196), kind=kOutput, calls=%fused_computation.221 | convolution fusion | flops 203358208 | bytes 264192 | tf_op jit(solution)/shard_map/dot_general | solution.py:39
  38.4 1.6 %fusion.3 = f32[1,256,256]{1,2,0:T(8,128)S(1)} fusion(f32[256,256]{0,1:T(8,128)S(1)} %fusion.96, f32[256]{0:T(256)S(1)} %get-tuple-element.195, f32[256]{0:T(256)S(1)} %get-tuple-element.196), kind=kOutput, calls=%fused_computation.27 | convolution fusion | flops 203423744 | bytes 526336 | tf_op jit(solution)/shard_map/dot_general | solution.py:39
  40.1 1.6 %fusion.97 = f32[256,256]{0,1:T(8,128)S(1)} fusion(f32[256]{0:T(256)S(1)} %get-tuple-element.195, f32[256]{0:T(256)S(1)} %get-tuple-element.196), kind=kOutput, calls=%fused_computation.223 | convolution fusion | flops 203358208 | bytes 264192 | tf_op jit(solution)/shard_map/dot_general | solution.py:39
  41.7 1.6 %fusion.4 = f32[1,256,256]{1,2,0:T(8,128)S(1)} fusion(f32[256,256]{0,1:T(8,128)S(1)} %fusion.97, f32[256]{0:T(256)S(1)} %get-tuple-element.195, f32[256]{0:T(256)S(1)} %get-tuple-element.196), kind=kOutput, calls=%fused_computation.29 | convolution fusion | flops 203423744 | bytes 526336 | tf_op jit(solution)/shard_map/dot_general | solution.py:39
  43.5 14.7 %all-to-all-done = f32[2,1,4,256,256]{3,4,0,1,2:T(8,128)S(1)} async-done(((f32[2,1,4,256,256]{3,4,0,1,2:T(8,128)}), f32[2,1,4,256,256]{3,4,0,1,2:T(8,128)S(1)}, u32[]{:S(2)}, u32[]{:S(2)}) %all-to-all-start) | async-done | bytes 2097184 | tf_op jit(solution)/shard_map/all_to_all | solution.py:230
  60.2 1.4 %fusion.9 = f32[3,256,256]{1,2,0:T(8,128)S(1)} fusion(f32[1,1,256,256]{2,3,0,1:T(8,128)S(1)} %get-tuple-element.120, f32[1,1,256,256]{2,3,0,1:T(8,128)S(1)} %get-tuple-element.121, f32[1,1,256,256]{2,3,0,1:T(8,128)S(1)} %get-tuple-element.122, f32[1,256,256]{1,2,0:T(8,128)S(1)} %get-tuple-element.163, f32[2,256,256]{1,2,0:T(8,128)S(1)} %maximum_multiply_fusion), kind=kOutput, calls=%fused_computation.40 | convolution fusion | flops 604569600 | bytes 2359296 | tf_op jit(solution)/shard_map/nbij,nkj->nbik/dot_general | solution.py:104
  62.7 1.6 %fusion.18 = f32[3,256,256]{1,2,0:T(8,128)S(1)} fusion(f32[1,1,256,256]{2,3,0,1:T(8,128)S(1)} %get-tuple-element.114, f32[1,1,256,256]{2,3,0,1:T(8,128)S(1)} %get-tuple-element.115, f32[1,1,256,256]{2,3,0,1:T(8,128)S(1)} %get-tuple-element.116, f32[1,256,256]{1,2,0:T(8,128)S(1)} %get-tuple-element.163, f32[2,256,256]{1,2,0:T(8,128)S(1)} %maximum_multiply_fusion), kind=kOutput, calls=%fused_computation.51 | convolution fusion | flops 604569600 | bytes 2359296 | tf_op jit(solution)/shard_map/nbij,nkj->nbik/dot_general | solution.py:104
  65.5 1.4 %fusion.27 = f32[3,256,256]{1,2,0:T(8,128)S(1)} fusion(f32[1,1,256,256]{2,3,0,1:T(8,128)S(1)} %get-tuple-element.108, f32[1,1,256,256]{2,3,0,1:T(8,128)S(1)} %get-tuple-element.109, f32[1,1,256,256]{2,3,0,1:T(8,128)S(1)} %get-tuple-element.110, f32[1,256,256]{1,2,0:T(8,128)S(1)} %get-tuple-element.163, f32[2,256,256]{1,2,0:T(8,128)S(1)} %maximum_multiply_fusion), kind=kOutput, calls=%fused_computation.62 | convolution fusion | flops 604569600 | bytes 2359296 | tf_op jit(solution)/shard_map/nbij,nkj->nbik/dot_general | solution.py:104
  68.0 1.4 %fusion.36 = f32[3,256,256]{2,1,0:T(8,128)S(1)} fusion(f32[1,1,256,256]{2,3,0,1:T(8,128)S(1)} %get-tuple-element.102, f32[1,1,256,256]{2,3,0,1:T(8,128)S(1)} %get-tuple-element.103, f32[1,1,256,256]{2,3,0,1:T(8,128)S(1)} %get-tuple-element.104, f32[1,256,256]{2,1,0:T(8,128)S(1)} %copy-done.3, f32[2,256,256]{2,1,0:T(8,128)S(1)} %copy-done.1), kind=kOutput, calls=%fused_computation.74 | convolution fusion | flops 604569600 | bytes 2359296 | tf_op jit(solution)/shard_map/nbij,nkj->nbik/dot_general | solution.py:104
  77.2 1.2 fusion.41
  78.4 1.4 %collective-permute-start.4 = (f32[2,1,1,256,256]{3,4,0,2,1:T(8,128)}, f32[2,1,1,256,256]{3,4,0,2,1:T(8,128)S(1)}, u32[]{:S(2)}, u32[]{:S(2)}) collective-permute-start(f32[2,1,1,256,256]{3,4,0,2,1:T(8,128)} %get-tuple-element.136), channel_id=1, source_target_pairs={{0,8},{8,16},{16,24},{24,0},{1,9},{9,17},{17,25},{25,1},{2,10},{10... | collective-permute-start | bytes 1572872 | tf_op jit(solution)/shard_map/ppermute | solution.py:249
  80.4 2.4 %collective-permute-start.6 = (f32[2,1,1,256,256]{3,4,1,2,0:T(8,128)S(1)}, f32[2,1,1,256,256]{3,4,1,2,0:T(8,128)S(1)}, u32[]{:S(2)}, u32[]{:S(2)}) collective-permute-start(f32[2,1,1,256,256]{3,4,1,2,0:T(8,128)S(1)} %get-tuple-element.134), channel_id=1, source_target_pairs={{0,24},{8,0},{16,8},{24,16},{1,25},{9,1},{17,9},{25,17},{2,26},{10... | collective-permute-start | bytes 1572872 | tf_op jit(solution)/shard_map/ppermute | solution.py:249
  82.8 11.6 %collective-permute-done.4 = f32[2,1,1,256,256]{3,4,0,2,1:T(8,128)S(1)} collective-permute-done((f32[2,1,1,256,256]{3,4,0,2,1:T(8,128)}, f32[2,1,1,256,256]{3,4,0,2,1:T(8,128)S(1)}, u32[]{:S(2)}, u32[]{:S(2)}) %collective-permute-start.4) | collective-permute-done | bytes 524320 | tf_op jit(solution)/shard_map/ppermute | solution.py:249
  94.4 9.3 %collective-permute-done.5 = f32[2,1,1,256,256]{3,4,0,2,1:T(8,128)S(1)} collective-permute-done((f32[2,1,1,256,256]{3,4,0,2,1:T(8,128)S(1)}, f32[2,1,1,256,256]{3,4,0,2,1:T(8,128)S(1)}, u32[]{:S(2)}, u32[]{:S(2)}) %collective-permute-start.5) | collective-permute-done | bytes 524320 | tf_op jit(solution)/shard_map/ppermute | solution.py:249
  103.7 2.9 %fusion.2 = f32[2,1,512,512]{2,3,0,1:T(8,128)S(1)} fusion(s32[]{:T(128)S(6)} %select_n.421, s32[]{:T(128)S(6)} %select_n.422, f32[2,1,256,256]{2,3,0,1:T(8,128)S(1)} %get-tuple-element.135, s32[]{:T(128)S(6)} %select_n.425, s32[]{:T(128)S(6)} %select_n.426, f32[2,1,256,256]{2,3,0,1:T(8,128)S(1)} %bitcast.315, s32[]{:T(128)S(6)} %select_n.429, ...), kind=kLoop, calls=%fused_computation.14 | loop fusion | flops 1572864 | bytes 4194336 | tf_op jit(solution)/shard_map/add | solution.py:251
  106.8 1.9 %collective-permute-start.7 = (f32[2,1,512,128]{2,3,0,1:T(8,128)S(1)}, f32[2,1,512,128]{2,3,0,1:T(8,128)S(1)}, u32[]{:S(2)}, u32[]{:S(2)}) collective-permute-start(f32[2,1,512,128]{2,3,0,1:T(8,128)S(1)} %get-tuple-element.133), channel_id=1, source_target_pairs={{0,1},{2,3},{4,5},{6,7},{8,9},{10,11},{12,13},{14,15},{16,17},{18,... | collective-permute-start | bytes 1572872 | tf_op jit(solution)/shard_map/ppermute | solution.py:15
  108.7 1.3 %collective-permute-start.8 = (f32[2,1,512,128]{2,3,0,1:T(8,128)S(1)}, f32[2,1,512,128]{2,3,0,1:T(8,128)S(1)}, u32[]{:S(2)}, u32[]{:S(2)}) collective-permute-start(f32[2,1,512,128]{2,3,0,1:T(8,128)S(1)} %get-tuple-element.132), channel_id=1, source_target_pairs={{1,0},{3,2},{5,4},{7,6},{9,8},{11,10},{13,12},{15,14},{17,16},{19,... | collective-permute-start | bytes 1572872 | tf_op jit(solution)/shard_map/ppermute | solution.py:15
  110.3 2.2 %collective-permute-done.8 = f32[2,1,512,128]{2,3,0,1:T(8,128)S(1)} collective-permute-done((f32[2,1,512,128]{2,3,0,1:T(8,128)S(1)}, f32[2,1,512,128]{2,3,0,1:T(8,128)S(1)}, u32[]{:S(2)}, u32[]{:S(2)}) %collective-permute-start.8) | collective-permute-done | bytes 524320 | tf_op jit(solution)/shard_map/ppermute | solution.py:15
  112.7 3.5 %collective-permute-start.9 = (f32[2,1,128,256]{2,3,0,1:T(8,128)S(1)}, f32[2,1,128,256]{2,3,0,1:T(8,128)S(1)}, u32[]{:S(2)}, u32[]{:S(2)}) collective-permute-start(f32[2,1,128,256]{2,3,0,1:T(8,128)S(1)} %get-tuple-element.145), channel_id=1, source_target_pairs={{0,2},{2,4},{4,6},{1,3},{3,5},{5,7},{8,10},{10,12},{12,14},{9,11},... | collective-permute-start | bytes 786440 | tf_op jit(solution)/shard_map/ppermute | solution.py:15
  116.2 1.3 %collective-permute-start.10 = (f32[2,1,128,256]{2,3,0,1:T(8,128)S(1)}, f32[2,1,128,256]{2,3,0,1:T(8,128)S(1)}, u32[]{:S(2)}, u32[]{:S(2)}) collective-permute-start(f32[2,1,128,256]{2,3,0,1:T(8,128)S(1)} %get-tuple-element.144), channel_id=1, source_target_pairs={{2,0},{4,2},{6,4},{3,1},{5,3},{7,5},{10,8},{12,10},{14,12},{11,9},... | collective-permute-start | bytes 786440 | tf_op jit(solution)/shard_map/ppermute | solution.py:15
  117.5 4.5 %collective-permute-done.9 = f32[2,1,128,256]{2,3,0,1:T(8,128)S(1)} collective-permute-done((f32[2,1,128,256]{2,3,0,1:T(8,128)S(1)}, f32[2,1,128,256]{2,3,0,1:T(8,128)S(1)}, u32[]{:S(2)}, u32[]{:S(2)}) %collective-permute-start.9) | collective-permute-done | bytes 262176 | tf_op jit(solution)/shard_map/ppermute | solution.py:15
  122.1 4.1 %collective-permute-done.10 = f32[2,1,128,256]{2,3,0,1:T(8,128)S(1)} collective-permute-done((f32[2,1,128,256]{2,3,0,1:T(8,128)S(1)}, f32[2,1,128,256]{2,3,0,1:T(8,128)S(1)}, u32[]{:S(2)}, u32[]{:S(2)}) %collective-permute-start.10) | collective-permute-done | bytes 262176 | tf_op jit(solution)/shard_map/ppermute | solution.py:15
  (93 shorter events, 25.7 us)
Async XLA Ops:
  0.6 9.5 %copy-start.6 = (s32[1,1,4,2]{2,3,1,0:T(2,128)S(1)}, s32[1,1,4,2]{2,3,1,0:T(2,128)}, u32[]{:S(2)}) copy-start(s32[1,1,4,2]{2,3,1,0:T(2,128)} %param.17) | copy-start | bytes 100
  2.7 13.3 %collective-permute-start = (f32[2,1,128,256]{3,2,1,0:T(8,128)S(1)}, f32[2,1,128,256]{3,2,1,0:T(8,128)S(1)}, u32[]{:S(2)}, u32[]{:S(2)}) collective-permute-start(f32[2,1,128,256]{3,2,1,0:T(8,128)S(1)} %get-tuple-element.173), channel_id=1, source_target_pairs={{0,2},{2,4},{4,6},{1,3},{3,5},{5,7},{8,10},{10,12},{12,14},{9,11},... | collective-permute-start | bytes 786440 | tf_op jit(solution)/shard_map/ppermute | solution.py:28
  7.6 9.7 %collective-permute-start.1 = (f32[2,1,128,256]{3,2,1,0:T(8,128)S(1)}, f32[2,1,128,256]{3,2,1,0:T(8,128)S(1)}, u32[]{:S(2)}, u32[]{:S(2)}) collective-permute-start(f32[2,1,128,256]{3,2,1,0:T(8,128)S(1)} %get-tuple-element.174), channel_id=1, source_target_pairs={{2,0},{4,2},{6,4},{3,1},{5,3},{7,5},{10,8},{12,10},{14,12},{11,9},... | collective-permute-start | bytes 786440 | tf_op jit(solution)/shard_map/ppermute | solution.py:31
  18.2 4.6 %collective-permute-start.2 = (f32[2,1,512,128]{3,2,1,0:T(8,128)S(1)}, f32[2,1,512,128]{3,2,1,0:T(8,128)S(1)}, u32[]{:S(2)}, u32[]{:S(2)}) collective-permute-start(f32[2,1,512,128]{3,2,1,0:T(8,128)S(1)} %get-tuple-element.154), channel_id=1, source_target_pairs={{0,1},{2,3},{4,5},{6,7},{8,9},{10,11},{12,13},{14,15},{16,17},{18,... | collective-permute-start | bytes 1572872 | tf_op jit(solution)/shard_map/ppermute | solution.py:28
  20.6 4.1 %collective-permute-start.3 = (f32[2,1,512,128]{3,2,1,0:T(8,128)}, f32[2,1,512,128]{3,2,1,0:T(8,128)}, u32[]{:S(2)}, u32[]{:S(2)}) collective-permute-start(f32[2,1,512,128]{3,2,1,0:T(8,128)} %get-tuple-element.155), channel_id=1, source_target_pairs={{1,0},{3,2},{5,4},{7,6},{9,8},{11,10},{13,12},{15,14},{17,16},{19,... | collective-permute-start | bytes 1572872 | tf_op jit(solution)/shard_map/ppermute | solution.py:31
  22.0 4.1 %copy-start = (f32[2,256,256]{2,1,0:T(8,128)}, f32[2,256,256]{2,1,0:T(8,128)S(1)}, u32[]{:S(2)}) copy-start(f32[2,256,256]{2,1,0:T(8,128)S(1)} %maximum_multiply_fusion.1) | copy-start | bytes 1572868
  29.1 29.0 %all-to-all-start = ((f32[2,1,4,256,256]{3,4,0,1,2:T(8,128)}), f32[2,1,4,256,256]{3,4,0,1,2:T(8,128)S(1)}, u32[]{:S(2)}, u32[]{:S(2)}) async-start(f32[2,1,4,256,256]{3,4,0,1,2:T(8,128)} %pad_maximum_fusion), calls=%async_computation | async-start | bytes 4194304 | tf_op jit(solution)/shard_map/all_to_all | solution.py:230
  58.2 1.0 copy-start.4
  58.2 1.0 copy-start.5
  65.5 1.5 %copy-start.1 = (f32[2,256,256]{2,1,0:T(8,128)S(1)}, f32[2,256,256]{2,1,0:T(8,128)}, u32[]{:S(2)}) copy-start(f32[2,256,256]{2,1,0:T(8,128)} %copy-done) | copy-start | bytes 1572868
  65.5 1.5 %copy-start.3 = (f32[1,256,256]{2,1,0:T(8,128)S(1)}, f32[1,256,256]{2,1,0:T(8,128)}, u32[]{:S(2)}) copy-start(f32[1,256,256]{2,1,0:T(8,128)} %get-tuple-element.164) | copy-start | bytes 786436
  68.0 2.5 %copy-start.2 = (f32[2,256,256]{2,1,0:T(8,128)S(1)}, f32[2,256,256]{2,1,0:T(8,128)}, u32[]{:S(2)}) copy-start(f32[2,256,256]{2,1,0:T(8,128)} %copy.146) | copy-start | bytes 1572868
  78.4 16.0 %collective-permute-start.4 = (f32[2,1,1,256,256]{3,4,0,2,1:T(8,128)}, f32[2,1,1,256,256]{3,4,0,2,1:T(8,128)S(1)}, u32[]{:S(2)}, u32[]{:S(2)}) collective-permute-start(f32[2,1,1,256,256]{3,4,0,2,1:T(8,128)} %get-tuple-element.136), channel_id=1, source_target_pairs={{0,8},{8,16},{16,24},{24,0},{1,9},{9,17},{17,25},{25,1},{2,10},{10... | collective-permute-start | bytes 1572872 | tf_op jit(solution)/shard_map/ppermute | solution.py:249
  79.8 23.9 %collective-permute-start.5 = (f32[2,1,1,256,256]{3,4,0,2,1:T(8,128)S(1)}, f32[2,1,1,256,256]{3,4,0,2,1:T(8,128)S(1)}, u32[]{:S(2)}, u32[]{:S(2)}) collective-permute-start(f32[2,1,1,256,256]{3,4,0,2,1:T(8,128)S(1)} %get-tuple-element.137), channel_id=1, source_target_pairs={{0,16},{8,24},{16,0},{24,8},{1,17},{9,25},{17,1},{25,9},{2,18},{10... | collective-permute-start | bytes 1572872 | tf_op jit(solution)/shard_map/ppermute | solution.py:249
  80.4 23.4 %collective-permute-start.6 = (f32[2,1,1,256,256]{3,4,1,2,0:T(8,128)S(1)}, f32[2,1,1,256,256]{3,4,1,2,0:T(8,128)S(1)}, u32[]{:S(2)}, u32[]{:S(2)}) collective-permute-start(f32[2,1,1,256,256]{3,4,1,2,0:T(8,128)S(1)} %get-tuple-element.134), channel_id=1, source_target_pairs={{0,24},{8,0},{16,8},{24,16},{1,25},{9,1},{17,9},{25,17},{2,26},{10... | collective-permute-start | bytes 1572872 | tf_op jit(solution)/shard_map/ppermute | solution.py:249
  106.8 3.4 %collective-permute-start.7 = (f32[2,1,512,128]{2,3,0,1:T(8,128)S(1)}, f32[2,1,512,128]{2,3,0,1:T(8,128)S(1)}, u32[]{:S(2)}, u32[]{:S(2)}) collective-permute-start(f32[2,1,512,128]{2,3,0,1:T(8,128)S(1)} %get-tuple-element.133), channel_id=1, source_target_pairs={{0,1},{2,3},{4,5},{6,7},{8,9},{10,11},{12,13},{14,15},{16,17},{18,... | collective-permute-start | bytes 1572872 | tf_op jit(solution)/shard_map/ppermute | solution.py:15
  108.7 3.8 %collective-permute-start.8 = (f32[2,1,512,128]{2,3,0,1:T(8,128)S(1)}, f32[2,1,512,128]{2,3,0,1:T(8,128)S(1)}, u32[]{:S(2)}, u32[]{:S(2)}) collective-permute-start(f32[2,1,512,128]{2,3,0,1:T(8,128)S(1)} %get-tuple-element.132), channel_id=1, source_target_pairs={{1,0},{3,2},{5,4},{7,6},{9,8},{11,10},{13,12},{15,14},{17,16},{19,... | collective-permute-start | bytes 1572872 | tf_op jit(solution)/shard_map/ppermute | solution.py:15
  112.7 9.3 %collective-permute-start.9 = (f32[2,1,128,256]{2,3,0,1:T(8,128)S(1)}, f32[2,1,128,256]{2,3,0,1:T(8,128)S(1)}, u32[]{:S(2)}, u32[]{:S(2)}) collective-permute-start(f32[2,1,128,256]{2,3,0,1:T(8,128)S(1)} %get-tuple-element.145), channel_id=1, source_target_pairs={{0,2},{2,4},{4,6},{1,3},{3,5},{5,7},{8,10},{10,12},{12,14},{9,11},... | collective-permute-start | bytes 786440 | tf_op jit(solution)/shard_map/ppermute | solution.py:15
  116.2 10.0 %collective-permute-start.10 = (f32[2,1,128,256]{2,3,0,1:T(8,128)S(1)}, f32[2,1,128,256]{2,3,0,1:T(8,128)S(1)}, u32[]{:S(2)}, u32[]{:S(2)}) collective-permute-start(f32[2,1,128,256]{2,3,0,1:T(8,128)S(1)} %get-tuple-element.144), channel_id=1, source_target_pairs={{2,0},{4,2},{6,4},{3,1},{5,3},{7,5},{10,8},{12,10},{14,12},{11,9},... | collective-permute-start | bytes 786440 | tf_op jit(solution)/shard_map/ppermute | solution.py:15

commit v6 on v4

--- a/solution.py
+++ b/solution.py
@@ -235,6 +235,7 @@
             grid = grid + place(
                 chunk[:, :, slot], source_rows[shift][slot], source_cols[shift][slot], extended.shape[2:]
             )
+        grid = lax.optimization_barrier(grid)
     owned = fold_both(grid, rim, pass_rows_all, pass_cols_all)
     return (owned[0], owned[1])
 

time: 127 us -> 125 us (0.984)
  waiting for transfers between devices: 47.7 us -> 45.9 us
  other arithmetic: 14.9 us -> 13.4 us
    ppermute x3, waiting for transfers between devices: 21 us -> 19.2 us  [per_device(): chunk = lax.ppermute(chunk, 'depth', pairs)]
    add x1 -> x3, other arithmetic: 2.94 us -> 2.28 us  [per_device(): grid + place(chunk[:, :, slot], source_rows[shift][slot], source_cols[shi...]
  transfers between devices with their start and end apart: 12 -> 12, of which waited for: 9 -> 9; matrix products, arithmetic and copies ran while one was open for 13% -> 15% of each run, Pallas kernels for 0% -> 0%
where the time goes in v6:
time: 125 us
  waiting for transfers between devices  45.9 us (37%)
  starting transfers between devices  25.6 us (20%)
  matrix products  20.6 us (16%)
  other arithmetic  13.4 us (11%)
  local copies, waits for them, and re-layouts  12.1 us (10%)
  between operations  7.13 us (6%)
    ppermute x3, waiting for transfers between devices, per_device(): chunk = lax.ppermute(chunk, 'depth', pairs)  19.2 us
    all_to_all x1, waiting for transfers between devices, per_device(): gathered = lax.all_to_all(cut, 'depth', 2, 1, tiled=True)  12.7 us
    ppermute x4, waiting for transfers between devices, from_behind(): lax.ppermute(value, axis, [(source, source + steps) for source in range(l...  10.9 us
    ppermute x4, starting transfers between devices, from_behind(): lax.ppermute(value, axis, [(source, source + steps) for source in range(l...  8.06 us
    dot_general x8, matrix products, right_product(): jnp.einsum('bij,kj->bik', waves, matrix, precision=mode, preferred_elemen...  7.44 us
    dot_general x8, matrix products, left_product(): jnp.einsum('ij,bjk->bik', matrix, waves, precision=mode, preferred_elemen...  7.31 us
    ppermute x2, starting transfers between devices, with_halo(): lax.ppermute(lax.slice_in_dim(block, block.shape[dim] - width, None, axis...  6.25 us
    dot_general x4, matrix products, matmul_exact(): jnp.dot(first, second, precision=exact_mode, preferred_element_type=jnp.f...  5.8 us
  transfers between devices with their start and end apart: 12, of which 9 were waited for; matrix products, arithmetic and copies ran while one was open for 15% of the time, Pallas kernels for 0%

profile of v6, /device:TPU:0, one launch (start us, length us, event | category | flops | bytes accessed | tf_op | source)
XLA Modules:
  0.0 124.7 jit_solution(16396494602548421813)
XLA Ops:
  0.6 2.0 %multiply_bitcast_fusion = (f32[1,1,256,256]{3,2,1,0:T(8,128)S(1)}, f32[1,1,256,256]{3,2,1,0:T(8,128)S(1)}) fusion(f32[1,256,256]{2,1,0:T(8,128)} %param.13, f32[1,256,256]{2,1,0:T(8,128)} %param.14), kind=kLoop, calls=%fused_computation.211 | loop fusion | flops 196608 | bytes 1048576 | tf_op jit(solution)/shard_map/stack | solution.py:160
  2.7 4.9 %collective-permute-start = (f32[2,1,128,256]{3,2,1,0:T(8,128)S(1)}, f32[2,1,128,256]{3,2,1,0:T(8,128)S(1)}, u32[]{:S(2)}, u32[]{:S(2)}) collective-permute-start(f32[2,1,128,256]{3,2,1,0:T(8,128)S(1)} %get-tuple-element.163), channel_id=1, source_target_pairs={{0,2},{2,4},{4,6},{1,3},{3,5},{5,7},{8,10},{10,12},{12,14},{9,11},... | collective-permute-start | bytes 786440 | tf_op jit(solution)/shard_map/ppermute | solution.py:28
  7.6 1.3 %collective-permute-start.1 = (f32[2,1,128,256]{3,2,1,0:T(8,128)S(1)}, f32[2,1,128,256]{3,2,1,0:T(8,128)S(1)}, u32[]{:S(2)}, u32[]{:S(2)}) collective-permute-start(f32[2,1,128,256]{3,2,1,0:T(8,128)S(1)} %get-tuple-element.164), channel_id=1, source_target_pairs={{2,0},{4,2},{6,4},{3,1},{5,3},{7,5},{10,8},{12,10},{14,12},{11,9},... | collective-permute-start | bytes 786440 | tf_op jit(solution)/shard_map/ppermute | solution.py:31
  15.9 1.3 %collective-permute-done.1 = f32[2,1,128,256]{3,2,1,0:T(8,128)S(1)} collective-permute-done((f32[2,1,128,256]{3,2,1,0:T(8,128)S(1)}, f32[2,1,128,256]{3,2,1,0:T(8,128)S(1)}, u32[]{:S(2)}, u32[]{:S(2)}) %collective-permute-start.1) | collective-permute-done | bytes 262176 | tf_op jit(solution)/shard_map/ppermute | solution.py:31
  17.4 1.1 fusion.144
  18.5 1.3 %collective-permute-start.2 = (f32[2,1,512,128]{3,2,1,0:T(8,128)}, f32[2,1,512,128]{3,2,1,0:T(8,128)S(1)}, u32[]{:S(2)}, u32[]{:S(2)}) collective-permute-start(f32[2,1,512,128]{3,2,1,0:T(8,128)} %get-tuple-element.146), channel_id=1, source_target_pairs={{0,1},{2,3},{4,5},{6,7},{8,9},{10,11},{12,13},{14,15},{16,17},{18,... | collective-permute-start | bytes 1572872 | tf_op jit(solution)/shard_map/ppermute | solution.py:28
  19.8 1.0 sine_negate_fusion
  20.8 1.3 %collective-permute-start.3 = (f32[2,1,512,128]{3,2,1,0:T(8,128)}, f32[2,1,512,128]{3,2,1,0:T(8,128)S(1)}, u32[]{:S(2)}, u32[]{:S(2)}) collective-permute-start(f32[2,1,512,128]{3,2,1,0:T(8,128)} %get-tuple-element.147), channel_id=1, source_target_pairs={{1,0},{3,2},{5,4},{7,6},{9,8},{11,10},{13,12},{15,14},{17,16},{19,... | collective-permute-start | bytes 1572872 | tf_op jit(solution)/shard_map/ppermute | solution.py:31
  23.1 1.8 %collective-permute-done.3 = f32[2,1,512,128]{3,2,1,0:T(8,128)S(1)} collective-permute-done((f32[2,1,512,128]{3,2,1,0:T(8,128)}, f32[2,1,512,128]{3,2,1,0:T(8,128)S(1)}, u32[]{:S(2)}, u32[]{:S(2)}) %collective-permute-start.3) | collective-permute-done | bytes 524320 | tf_op jit(solution)/shard_map/ppermute | solution.py:31
  26.6 1.6 %pad_maximum_fusion = f32[2,1,4,256,256]{3,4,0,1,2:T(8,128)} fusion(f32[2,1,1,256,256]{3,4,0,1,2:T(8,128)S(1)} %bitcast.290, f32[2,1,1,256,256]{3,4,0,1,2:T(8,128)S(1)} %bitcast.289, f32[2,1,1,256,256]{3,4,0,1,2:T(8,128)S(1)} %bitcast.288, f32[2,1,1,256,256]{3,4,0,1,2:T(8,128)S(1)} %bitcast.287), kind=kLoop, calls=%fused_computation.16 | loop fusion | flops 1572864 | bytes 4194304 | tf_op jit(solution)/shard_map/stack | solution.py:205
  28.2 3.9 %all-to-all-start = ((f32[2,1,4,256,256]{3,4,0,1,2:T(8,128)}), f32[2,1,4,256,256]{3,4,0,1,2:T(8,128)S(1)}, u32[]{:S(2)}, u32[]{:S(2)}) async-start(f32[2,1,4,256,256]{3,4,0,1,2:T(8,128)} %pad_maximum_fusion), calls=%async_computation | async-start | bytes 4194304 | tf_op jit(solution)/shard_map/all_to_all | solution.py:214
  36.6 1.4 %fusion.78 = f32[256,256]{1,0:T(8,128)S(1)} fusion(f32[256]{0:T(256)S(1)} %get-tuple-element.185, f32[256]{0:T(256)S(1)} %get-tuple-element.186), kind=kOutput, calls=%fused_computation.204 | convolution fusion | flops 203358208 | bytes 264192 | tf_op jit(solution)/shard_map/dot_general | solution.py:39
  38.1 1.5 %fusion.3 = f32[1,256,256]{2,1,0:T(8,128)S(1)} fusion(f32[256,256]{1,0:T(8,128)S(1)} %fusion.78, f32[256]{0:T(256)S(1)} %get-tuple-element.185, f32[256]{0:T(256)S(1)} %get-tuple-element.186), kind=kOutput, calls=%fused_computation.27 | convolution fusion | flops 203423744 | bytes 526336 | tf_op jit(solution)/shard_map/dot_general | solution.py:39
  39.5 1.4 %fusion.79 = f32[256,256]{1,0:T(8,128)S(1)} fusion(f32[256]{0:T(256)S(1)} %get-tuple-element.185, f32[256]{0:T(256)S(1)} %get-tuple-element.186), kind=kOutput, calls=%fused_computation.206 | convolution fusion | flops 203358208 | bytes 264192 | tf_op jit(solution)/shard_map/dot_general | solution.py:39
  41.0 1.5 %fusion.4 = f32[1,256,256]{2,1,0:T(8,128)S(1)} fusion(f32[256,256]{1,0:T(8,128)S(1)} %fusion.79, f32[256]{0:T(256)S(1)} %get-tuple-element.185, f32[256]{0:T(256)S(1)} %get-tuple-element.186), kind=kOutput, calls=%fused_computation.29 | convolution fusion | flops 203423744 | bytes 526336 | tf_op jit(solution)/shard_map/dot_general | solution.py:39
  43.4 1.2 copy.143
  44.6 12.7 %all-to-all-done = f32[2,1,4,256,256]{3,4,0,1,2:T(8,128)S(1)} async-done(((f32[2,1,4,256,256]{3,4,0,1,2:T(8,128)}), f32[2,1,4,256,256]{3,4,0,1,2:T(8,128)S(1)}, u32[]{:S(2)}, u32[]{:S(2)}) %all-to-all-start) | async-done | bytes 2097184 | tf_op jit(solution)/shard_map/all_to_all | solution.py:214
  61.8 1.0 fusion.22
  63.0 1.3 %convolution_bitcast_fusion.5 = f32[2,512,256]{1,2,0:T(8,128)S(1)} fusion(f32[512,256,1]{1,0,2:T(8,128)S(1)} %bitcast.260, f32[1,1,256,256]{2,3,1,0:T(8,128)S(1)} %bitcast.282, f32[1,1,256,256]{2,3,1,0:T(8,128)S(1)} %bitcast.281), kind=kOutput, calls=%fused_computation.23 | convolution fusion | flops 805437440 | bytes 2097152 | tf_op jit(solution)/shard_map/ij,bjk->bik/dot_general | solution.py:66
  66.6 1.9 %fusion.34 = f32[2,256,512]{2,1,0:T(8,128)S(1)} fusion(f32[512,256,1]{1,0,2:T(8,128)S(1)} %bitcast.276, f32[1,256,256]{1,2,0:T(8,128)S(1)} %get-tuple-element.139, f32[1,256,256]{1,2,0:T(8,128)S(1)} %get-tuple-element.138), kind=kOutput, calls=%fused_computation.72 | convolution fusion | flops 805437440 | bytes 2097152 | tf_op jit(solution)/shard_map/bij,kj->bik/dot_general | solution.py:72
  69.6 1.1 convolution_bitcast_fusion.3
  76.4 1.7 %collective-permute-start.4 = (f32[2,1,1,256,256]{3,4,0,2,1:T(8,128)S(1)}, f32[2,1,1,256,256]{3,4,0,2,1:T(8,128)S(1)}, u32[]{:S(2)}, u32[]{:S(2)}) collective-permute-start(f32[2,1,1,256,256]{3,4,0,2,1:T(8,128)S(1)} %get-tuple-element.120), channel_id=1, source_target_pairs={{0,8},{8,16},{16,24},{24,0},{1,9},{9,17},{17,25},{25,1},{2,10},{10... | collective-permute-start | bytes 1572872 | tf_op jit(solution)/shard_map/ppermute | solution.py:233
  79.4 2.5 %collective-permute-start.6 = (f32[2,1,1,256,256]{3,4,1,2,0:T(8,128)S(1)}, f32[2,1,1,256,256]{3,4,1,2,0:T(8,128)S(1)}, u32[]{:S(2)}, u32[]{:S(2)}) collective-permute-start(f32[2,1,1,256,256]{3,4,1,2,0:T(8,128)S(1)} %get-tuple-element.118), channel_id=1, source_target_pairs={{0,24},{8,0},{16,8},{24,16},{1,25},{9,1},{17,9},{25,17},{2,26},{10... | collective-permute-start | bytes 1572872 | tf_op jit(solution)/shard_map/ppermute | solution.py:233
  81.9 10.6 %collective-permute-done.4 = f32[2,1,1,256,256]{3,4,0,2,1:T(8,128)S(1)} collective-permute-done((f32[2,1,1,256,256]{3,4,0,2,1:T(8,128)S(1)}, f32[2,1,1,256,256]{3,4,0,2,1:T(8,128)S(1)}, u32[]{:S(2)}, u32[]{:S(2)}) %collective-permute-start.4) | collective-permute-done | bytes 524320 | tf_op jit(solution)/shard_map/ppermute | solution.py:233
  93.3 8.6 %collective-permute-done.5 = f32[2,1,1,256,256]{3,4,0,2,1:T(8,128)S(1)} collective-permute-done((f32[2,1,1,256,256]{3,4,0,2,1:T(8,128)S(1)}, f32[2,1,1,256,256]{3,4,0,2,1:T(8,128)S(1)}, u32[]{:S(2)}, u32[]{:S(2)}) %collective-permute-start.5) | collective-permute-done | bytes 524320 | tf_op jit(solution)/shard_map/ppermute | solution.py:233
  103.4 2.0 %collective-permute-start.7 = (f32[2,1,512,128]{2,3,0,1:T(8,128)S(1)}, f32[2,1,512,128]{2,3,0,1:T(8,128)S(1)}, u32[]{:S(2)}, u32[]{:S(2)}) collective-permute-start(f32[2,1,512,128]{2,3,0,1:T(8,128)S(1)} %get-tuple-element.117), channel_id=1, source_target_pairs={{0,1},{2,3},{4,5},{6,7},{8,9},{10,11},{12,13},{14,15},{16,17},{18,... | collective-permute-start | bytes 1572872 | tf_op jit(solution)/shard_map/ppermute | solution.py:15
  105.4 1.3 %collective-permute-start.8 = (f32[2,1,512,128]{2,3,0,1:T(8,128)S(1)}, f32[2,1,512,128]{2,3,0,1:T(8,128)S(1)}, u32[]{:S(2)}, u32[]{:S(2)}) collective-permute-start(f32[2,1,512,128]{2,3,0,1:T(8,128)S(1)} %get-tuple-element.116), channel_id=1, source_target_pairs={{1,0},{3,2},{5,4},{7,6},{9,8},{11,10},{13,12},{15,14},{17,16},{19,... | collective-permute-start | bytes 1572872 | tf_op jit(solution)/shard_map/ppermute | solution.py:15
  107.0 2.2 %collective-permute-done.8 = f32[2,1,512,128]{2,3,0,1:T(8,128)S(1)} collective-permute-done((f32[2,1,512,128]{2,3,0,1:T(8,128)S(1)}, f32[2,1,512,128]{2,3,0,1:T(8,128)S(1)}, u32[]{:S(2)}, u32[]{:S(2)}) %collective-permute-start.8) | collective-permute-done | bytes 524320 | tf_op jit(solution)/shard_map/ppermute | solution.py:15
  109.4 3.5 %collective-permute-start.9 = (f32[2,1,128,256]{2,3,0,1:T(8,128)S(1)}, f32[2,1,128,256]{2,3,0,1:T(8,128)S(1)}, u32[]{:S(2)}, u32[]{:S(2)}) collective-permute-start(f32[2,1,128,256]{2,3,0,1:T(8,128)S(1)} %get-tuple-element.129), channel_id=1, source_target_pairs={{0,2},{2,4},{4,6},{1,3},{3,5},{5,7},{8,10},{10,12},{12,14},{9,11},... | collective-permute-start | bytes 786440 | tf_op jit(solution)/shard_map/ppermute | solution.py:15
  112.9 1.3 %collective-permute-start.10 = (f32[2,1,128,256]{2,3,0,1:T(8,128)S(1)}, f32[2,1,128,256]{2,3,0,1:T(8,128)S(1)}, u32[]{:S(2)}, u32[]{:S(2)}) collective-permute-start(f32[2,1,128,256]{2,3,0,1:T(8,128)S(1)} %get-tuple-element.128), channel_id=1, source_target_pairs={{2,0},{4,2},{6,4},{3,1},{5,3},{7,5},{10,8},{12,10},{14,12},{11,9},... | collective-permute-start | bytes 786440 | tf_op jit(solution)/shard_map/ppermute | solution.py:15
  114.3 4.5 %collective-permute-done.9 = f32[2,1,128,256]{2,3,0,1:T(8,128)S(1)} collective-permute-done((f32[2,1,128,256]{2,3,0,1:T(8,128)S(1)}, f32[2,1,128,256]{2,3,0,1:T(8,128)S(1)}, u32[]{:S(2)}, u32[]{:S(2)}) %collective-permute-start.9) | collective-permute-done | bytes 262176 | tf_op jit(solution)/shard_map/ppermute | solution.py:15
  118.8 4.1 %collective-permute-done.10 = f32[2,1,128,256]{2,3,0,1:T(8,128)S(1)} collective-permute-done((f32[2,1,128,256]{2,3,0,1:T(8,128)S(1)}, f32[2,1,128,256]{2,3,0,1:T(8,128)S(1)}, u32[]{:S(2)}, u32[]{:S(2)}) %collective-permute-start.10) | collective-permute-done | bytes 262176 | tf_op jit(solution)/shard_map/ppermute | solution.py:15
  (99 shorter events, 28.7 us)
Async XLA Ops:
  0.6 9.5 %copy-start.7 = (s32[1,1,4,2]{2,3,1,0:T(2,128)S(1)}, s32[1,1,4,2]{2,3,1,0:T(2,128)}, u32[]{:S(2)}) copy-start(s32[1,1,4,2]{2,3,1,0:T(2,128)} %param.17) | copy-start | bytes 100
  2.7 13.3 %collective-permute-start = (f32[2,1,128,256]{3,2,1,0:T(8,128)S(1)}, f32[2,1,128,256]{3,2,1,0:T(8,128)S(1)}, u32[]{:S(2)}, u32[]{:S(2)}) collective-permute-start(f32[2,1,128,256]{3,2,1,0:T(8,128)S(1)} %get-tuple-element.163), channel_id=1, source_target_pairs={{0,2},{2,4},{4,6},{1,3},{3,5},{5,7},{8,10},{10,12},{12,14},{9,11},... | collective-permute-start | bytes 786440 | tf_op jit(solution)/shard_map/ppermute | solution.py:28
  7.6 9.7 %collective-permute-start.1 = (f32[2,1,128,256]{3,2,1,0:T(8,128)S(1)}, f32[2,1,128,256]{3,2,1,0:T(8,128)S(1)}, u32[]{:S(2)}, u32[]{:S(2)}) collective-permute-start(f32[2,1,128,256]{3,2,1,0:T(8,128)S(1)} %get-tuple-element.164), channel_id=1, source_target_pairs={{2,0},{4,2},{6,4},{3,1},{5,3},{7,5},{10,8},{12,10},{14,12},{11,9},... | collective-permute-start | bytes 786440 | tf_op jit(solution)/shard_map/ppermute | solution.py:31
  17.4 4.8 %copy-start.6 = (f32[2,256,256]{2,1,0:T(8,128)S(1)}, f32[2,256,256]{2,1,0:T(8,128)}, u32[]{:S(2)}) copy-start(f32[2,256,256]{2,1,0:T(8,128)} %param.15) | copy-start | bytes 1572868
  18.5 4.6 %collective-permute-start.2 = (f32[2,1,512,128]{3,2,1,0:T(8,128)}, f32[2,1,512,128]{3,2,1,0:T(8,128)S(1)}, u32[]{:S(2)}, u32[]{:S(2)}) collective-permute-start(f32[2,1,512,128]{3,2,1,0:T(8,128)} %get-tuple-element.146), channel_id=1, source_target_pairs={{0,1},{2,3},{4,5},{6,7},{8,9},{10,11},{12,13},{14,15},{16,17},{18,... | collective-permute-start | bytes 1572872 | tf_op jit(solution)/shard_map/ppermute | solution.py:28
  20.8 4.0 %collective-permute-start.3 = (f32[2,1,512,128]{3,2,1,0:T(8,128)}, f32[2,1,512,128]{3,2,1,0:T(8,128)S(1)}, u32[]{:S(2)}, u32[]{:S(2)}) collective-permute-start(f32[2,1,512,128]{3,2,1,0:T(8,128)} %get-tuple-element.147), channel_id=1, source_target_pairs={{1,0},{3,2},{5,4},{7,6},{9,8},{11,10},{13,12},{15,14},{17,16},{19,... | collective-permute-start | bytes 1572872 | tf_op jit(solution)/shard_map/ppermute | solution.py:31
  22.2 9.9 %copy-start = (f32[2,256,256]{2,1,0:T(8,128)}, f32[2,256,256]{2,1,0:T(8,128)S(1)}, u32[]{:S(2)}) copy-start(f32[2,256,256]{2,1,0:T(8,128)S(1)} %maximum_multiply_fusion.1) | copy-start | bytes 1572868
  28.2 4.7 %copy-start.3 = (f32[1,256,256]{2,1,0:T(8,128)S(1)}, f32[1,256,256]{2,1,0:T(8,128)}, u32[]{:S(2)}) copy-start(f32[1,256,256]{2,1,0:T(8,128)} %get-tuple-element.158) | copy-start | bytes 786436
  28.2 29.2 %all-to-all-start = ((f32[2,1,4,256,256]{3,4,0,1,2:T(8,128)}), f32[2,1,4,256,256]{3,4,0,1,2:T(8,128)S(1)}, u32[]{:S(2)}, u32[]{:S(2)}) async-start(f32[2,1,4,256,256]{3,4,0,1,2:T(8,128)} %pad_maximum_fusion), calls=%async_computation | async-start | bytes 4194304 | tf_op jit(solution)/shard_map/all_to_all | solution.py:214
  44.6 12.9 %copy-start.4 = (f32[1,256,256]{1,2,0:T(8,128)S(1)}, f32[1,256,256]{1,2,0:T(8,128)}, u32[]{:S(2)}) copy-start(f32[1,256,256]{1,2,0:T(8,128)} %copy.182) | copy-start | bytes 786436
  57.4 1.0 copy-start.5
  64.3 1.2 copy-start.1
  66.6 3.0 %copy-start.2 = (f32[2,256,256]{2,1,0:T(8,128)S(1)}, f32[2,256,256]{2,1,0:T(8,128)}, u32[]{:S(2)}) copy-start(f32[2,256,256]{2,1,0:T(8,128)} %copy.136) | copy-start | bytes 1572868
  76.4 16.1 %collective-permute-start.4 = (f32[2,1,1,256,256]{3,4,0,2,1:T(8,128)S(1)}, f32[2,1,1,256,256]{3,4,0,2,1:T(8,128)S(1)}, u32[]{:S(2)}, u32[]{:S(2)}) collective-permute-start(f32[2,1,1,256,256]{3,4,0,2,1:T(8,128)S(1)} %get-tuple-element.120), channel_id=1, source_target_pairs={{0,8},{8,16},{16,24},{24,0},{1,9},{9,17},{17,25},{25,1},{2,10},{10... | collective-permute-start | bytes 1572872 | tf_op jit(solution)/shard_map/ppermute | solution.py:233
  78.1 23.7 %collective-permute-start.5 = (f32[2,1,1,256,256]{3,4,0,2,1:T(8,128)S(1)}, f32[2,1,1,256,256]{3,4,0,2,1:T(8,128)S(1)}, u32[]{:S(2)}, u32[]{:S(2)}) collective-permute-start(f32[2,1,1,256,256]{3,4,0,2,1:T(8,128)S(1)} %get-tuple-element.121), channel_id=1, source_target_pairs={{0,16},{8,24},{16,0},{24,8},{1,17},{9,25},{17,1},{25,9},{2,18},{10... | collective-permute-start | bytes 1572872 | tf_op jit(solution)/shard_map/ppermute | solution.py:233
  79.4 23.2 %collective-permute-start.6 = (f32[2,1,1,256,256]{3,4,1,2,0:T(8,128)S(1)}, f32[2,1,1,256,256]{3,4,1,2,0:T(8,128)S(1)}, u32[]{:S(2)}, u32[]{:S(2)}) collective-permute-start(f32[2,1,1,256,256]{3,4,1,2,0:T(8,128)S(1)} %get-tuple-element.118), channel_id=1, source_target_pairs={{0,24},{8,0},{16,8},{24,16},{1,25},{9,1},{17,9},{25,17},{2,26},{10... | collective-permute-start | bytes 1572872 | tf_op jit(solution)/shard_map/ppermute | solution.py:233
  103.4 3.5 %collective-permute-start.7 = (f32[2,1,512,128]{2,3,0,1:T(8,128)S(1)}, f32[2,1,512,128]{2,3,0,1:T(8,128)S(1)}, u32[]{:S(2)}, u32[]{:S(2)}) collective-permute-start(f32[2,1,512,128]{2,3,0,1:T(8,128)S(1)} %get-tuple-element.117), channel_id=1, source_target_pairs={{0,1},{2,3},{4,5},{6,7},{8,9},{10,11},{12,13},{14,15},{16,17},{18,... | collective-permute-start | bytes 1572872 | tf_op jit(solution)/shard_map/ppermute | solution.py:15
  105.4 3.8 %collective-permute-start.8 = (f32[2,1,512,128]{2,3,0,1:T(8,128)S(1)}, f32[2,1,512,128]{2,3,0,1:T(8,128)S(1)}, u32[]{:S(2)}, u32[]{:S(2)}) collective-permute-start(f32[2,1,512,128]{2,3,0,1:T(8,128)S(1)} %get-tuple-element.116), channel_id=1, source_target_pairs={{1,0},{3,2},{5,4},{7,6},{9,8},{11,10},{13,12},{15,14},{17,16},{19,... | collective-permute-start | bytes 1572872 | tf_op jit(solution)/shard_map/ppermute | solution.py:15
  109.4 9.4 %collective-permute-start.9 = (f32[2,1,128,256]{2,3,0,1:T(8,128)S(1)}, f32[2,1,128,256]{2,3,0,1:T(8,128)S(1)}, u32[]{:S(2)}, u32[]{:S(2)}) collective-permute-start(f32[2,1,128,256]{2,3,0,1:T(8,128)S(1)} %get-tuple-element.129), channel_id=1, source_target_pairs={{0,2},{2,4},{4,6},{1,3},{3,5},{5,7},{8,10},{10,12},{12,14},{9,11},... | collective-permute-start | bytes 786440 | tf_op jit(solution)/shard_map/ppermute | solution.py:15
  112.9 10.0 %collective-permute-start.10 = (f32[2,1,128,256]{2,3,0,1:T(8,128)S(1)}, f32[2,1,128,256]{2,3,0,1:T(8,128)S(1)}, u32[]{:S(2)}, u32[]{:S(2)}) collective-permute-start(f32[2,1,128,256]{2,3,0,1:T(8,128)S(1)} %get-tuple-element.128), channel_id=1, source_target_pairs={{2,0},{4,2},{6,4},{3,1},{5,3},{7,5},{10,8},{12,10},{14,12},{11,9},... | collective-permute-start | bytes 786440 | tf_op jit(solution)/shard_map/ppermute | solution.py:15

commit v7 on v6

--- a/solution.py
+++ b/solution.py
@@ -19,16 +19,19 @@
     return jnp.stack((jnp.where(edge, 1.0, strip[0]), jnp.where(edge, 0.0, strip[1])))
 
 
-def with_halo(block, sides, width):
+def with_halo(block, sides, width, strips=None):
     for axis, dim in sides:
         count = lax.axis_size(axis)
         index = lax.axis_index(axis)
         forward = [(i, i + 1) for i in range(count - 1)]
         backward = [(target, source) for source, target in forward]
-        low = lax.ppermute(
-            lax.slice_in_dim(block, block.shape[dim] - width, None, axis=dim), axis, forward
-        )
-        high = lax.ppermute(lax.slice_in_dim(block, 0, width, axis=dim), axis, backward)
+        if strips is None:
+            last = lax.slice_in_dim(block, block.shape[dim] - width, None, axis=dim)
+            head = lax.slice_in_dim(block, 0, width, axis=dim)
+        else:
+            head, last = strips
+        low = lax.ppermute(last, axis, forward)
+        high = lax.ppermute(head, axis, backward)
         low = outside_filled(low, index == 0)
         high = outside_filled(high, index == count - 1)
         block = jnp.concatenate([low, block, high], axis=dim)
@@ -179,8 +182,12 @@
     depth_index = lax.axis_index("depth")
     row_index = lax.axis_index("row")
     col_index = lax.axis_index("col")
-    stacked = to_transmit(jnp.stack((phase, absorption)))
-    tall_slab = with_halo(stacked, (("row", 2),), rim)
+    raw = jnp.stack((phase, absorption))
+    edges = lax.optimization_barrier(
+        (to_transmit(raw[:, :, :rim]), to_transmit(raw[:, :, tile_rows - rim :]))
+    )
+    stacked = to_transmit(raw)
+    tall_slab = with_halo(stacked, (("row", 2),), rim, strips=edges)
     after = (stacked[0, 0, 0, 0] * 0.0).astype(jnp.int32)
     corners = offsets[0, 0] + after
     row_starts = corners[:, 0] - row_index * tile_rows + rim

time: 125 us -> 126 us (level)
    mul x0 -> x1, other arithmetic: none -> 1.98 us  [to_transmit(): damping * jnp.cos(extended[0])]
    unnamed x20 -> x24, local copies, waits for them, and re-layouts: 4.18 us -> 4.19 us
where the time goes in v7:
time: 126 us
  waiting for transfers between devices  44.8 us (36%)
  starting transfers between devices  26.4 us (21%)
  matrix products  20.6 us (16%)
  other arithmetic  14.4 us (11%)
  local copies, waits for them, and re-layouts  12.2 us (10%)
  between operations  7.22 us (6%)
    ppermute x3, waiting for transfers between devices, per_device(): chunk = lax.ppermute(chunk, 'depth', pairs)  19.2 us
    all_to_all x1, waiting for transfers between devices, per_device(): gathered = lax.all_to_all(cut, 'depth', 2, 1, tiled=True)  12.7 us
    ppermute x4, waiting for transfers between devices, from_behind(): lax.ppermute(value, axis, [(source, source + steps) for source in range(l...  10.9 us
    ppermute x4, starting transfers between devices, from_behind(): lax.ppermute(value, axis, [(source, source + steps) for source in range(l...  8.85 us
    dot_general x8, matrix products, right_product(): jnp.einsum('bij,kj->bik', waves, matrix, precision=mode, preferred_elemen...  7.45 us
    dot_general x8, matrix products, left_product(): jnp.einsum('ij,bjk->bik', matrix, waves, precision=mode, preferred_elemen...  7.3 us
    ppermute x2, starting transfers between devices, with_halo(): low = lax.ppermute(last, axis, forward)  6.25 us
    dot_general x4, matrix products, matmul_exact(): jnp.dot(first, second, precision=exact_mode, preferred_element_type=jnp.f...  5.8 us
  transfers between devices with their start and end apart: 12, of which 9 were waited for; matrix products, arithmetic and copies ran while one was open for 15% of the time, Pallas kernels for 0%

profile of v7, /device:TPU:0, one launch (start us, length us, event | category | flops | bytes accessed | tf_op | source)
XLA Modules:
  0.0 125.5 jit_solution(11746589190695845258)
XLA Ops:
  0.7 2.0 %cosine_multiply_fusion = (f32[1,1,128,256]{3,2,1,0:T(8,128)S(1)}, f32[1,1,128,256]{3,2,1,0:T(8,128)S(1)}, f32[1,1,128,256]{3,2,1,0:T(8,128)S(1)}, f32[1,1,128,256]{3,2,1,0:T(8,128)S(1)}) fusion(f32[1,1,256,256]{3,2,1,0:T(8,128)} %bitcast.293, f32[1,1,256,256]{3,2,1,0:T(8,128)} %bitcast.294), kind=kLoop, calls=%fused_computation.234 | loop fusion | flops 196608 | bytes 1048576 | tf_op jit(solution)/shard_map/mul | solution.py:163
  2.7 4.9 %collective-permute-start = (f32[2,1,128,256]{3,2,1,0:T(8,128)S(1)}, f32[2,1,128,256]{3,2,1,0:T(8,128)S(1)}, u32[]{:S(2)}, u32[]{:S(2)}) collective-permute-start(f32[2,1,128,256]{3,2,1,0:T(8,128)S(1)} %get-tuple-element.69), channel_id=1, source_target_pairs={{0,2},{2,4},{4,6},{1,3},{3,5},{5,7},{8,10},{10,12},{12,14},{9,11},... | collective-permute-start | bytes 786440 | tf_op jit(solution)/shard_map/ppermute | solution.py:33
  7.6 1.3 %collective-permute-start.1 = (f32[2,1,128,256]{3,2,1,0:T(8,128)S(1)}, f32[2,1,128,256]{3,2,1,0:T(8,128)S(1)}, u32[]{:S(2)}, u32[]{:S(2)}) collective-permute-start(f32[2,1,128,256]{3,2,1,0:T(8,128)S(1)} %get-tuple-element.70), channel_id=1, source_target_pairs={{2,0},{4,2},{6,4},{3,1},{5,3},{7,5},{10,8},{12,10},{14,12},{11,9},... | collective-permute-start | bytes 786440 | tf_op jit(solution)/shard_map/ppermute | solution.py:34
  17.4 1.1 fusion.145
  18.5 1.3 %collective-permute-start.2 = (f32[2,1,512,128]{3,2,1,0:T(8,128)}, f32[2,1,512,128]{3,2,1,0:T(8,128)S(1)}, u32[]{:S(2)}, u32[]{:S(2)}) collective-permute-start(f32[2,1,512,128]{3,2,1,0:T(8,128)} %get-tuple-element.150), channel_id=1, source_target_pairs={{0,1},{2,3},{4,5},{6,7},{8,9},{10,11},{12,13},{14,15},{16,17},{18,... | collective-permute-start | bytes 1572872 | tf_op jit(solution)/shard_map/ppermute | solution.py:33
  19.9 1.0 sine_negate_fusion
  20.9 1.3 %collective-permute-start.3 = (f32[2,1,512,128]{3,2,1,0:T(8,128)}, f32[2,1,512,128]{3,2,1,0:T(8,128)S(1)}, u32[]{:S(2)}, u32[]{:S(2)}) collective-permute-start(f32[2,1,512,128]{3,2,1,0:T(8,128)} %get-tuple-element.151), channel_id=1, source_target_pairs={{1,0},{3,2},{5,4},{7,6},{9,8},{11,10},{13,12},{15,14},{17,16},{19,... | collective-permute-start | bytes 1572872 | tf_op jit(solution)/shard_map/ppermute | solution.py:34
  23.2 1.8 %collective-permute-done.3 = f32[2,1,512,128]{3,2,1,0:T(8,128)S(1)} collective-permute-done((f32[2,1,512,128]{3,2,1,0:T(8,128)}, f32[2,1,512,128]{3,2,1,0:T(8,128)S(1)}, u32[]{:S(2)}, u32[]{:S(2)}) %collective-permute-start.3) | collective-permute-done | bytes 524320 | tf_op jit(solution)/shard_map/ppermute | solution.py:34
  26.7 1.6 %pad_maximum_fusion = f32[2,1,4,256,256]{3,4,0,1,2:T(8,128)} fusion(f32[2,1,1,256,256]{3,4,0,1,2:T(8,128)S(1)} %bitcast.292, f32[2,1,1,256,256]{3,4,0,1,2:T(8,128)S(1)} %bitcast.291, f32[2,1,1,256,256]{3,4,0,1,2:T(8,128)S(1)} %bitcast.290, f32[2,1,1,256,256]{3,4,0,1,2:T(8,128)S(1)} %bitcast.289), kind=kLoop, calls=%fused_computation.16 | loop fusion | flops 1572864 | bytes 4194304 | tf_op jit(solution)/shard_map/stack | solution.py:212
  28.3 3.9 %all-to-all-start = ((f32[2,1,4,256,256]{3,4,0,1,2:T(8,128)}), f32[2,1,4,256,256]{3,4,0,1,2:T(8,128)S(1)}, u32[]{:S(2)}, u32[]{:S(2)}) async-start(f32[2,1,4,256,256]{3,4,0,1,2:T(8,128)} %pad_maximum_fusion), calls=%async_computation | async-start | bytes 4194304 | tf_op jit(solution)/shard_map/all_to_all | solution.py:221
  36.7 1.5 %fusion.77 = f32[256,256]{1,0:T(8,128)S(1)} fusion(f32[256]{0:T(256)S(1)} %get-tuple-element.191, f32[256]{0:T(256)S(1)} %get-tuple-element.192), kind=kOutput, calls=%fused_computation.202 | convolution fusion | flops 203358208 | bytes 264192 | tf_op jit(solution)/shard_map/dot_general | solution.py:42
  38.1 1.4 %fusion.3 = f32[1,256,256]{2,1,0:T(8,128)S(1)} fusion(f32[256,256]{1,0:T(8,128)S(1)} %fusion.77, f32[256]{0:T(256)S(1)} %get-tuple-element.191, f32[256]{0:T(256)S(1)} %get-tuple-element.192), kind=kOutput, calls=%fused_computation.27 | convolution fusion | flops 203423744 | bytes 526336 | tf_op jit(solution)/shard_map/dot_general | solution.py:42
  39.6 1.4 %fusion.78 = f32[256,256]{1,0:T(8,128)S(1)} fusion(f32[256]{0:T(256)S(1)} %get-tuple-element.191, f32[256]{0:T(256)S(1)} %get-tuple-element.192), kind=kOutput, calls=%fused_computation.204 | convolution fusion | flops 203358208 | bytes 264192 | tf_op jit(solution)/shard_map/dot_general | solution.py:42
  41.0 1.5 %fusion.4 = f32[1,256,256]{2,1,0:T(8,128)S(1)} fusion(f32[256,256]{1,0:T(8,128)S(1)} %fusion.78, f32[256]{0:T(256)S(1)} %get-tuple-element.191, f32[256]{0:T(256)S(1)} %get-tuple-element.192), kind=kOutput, calls=%fused_computation.29 | convolution fusion | flops 203423744 | bytes 526336 | tf_op jit(solution)/shard_map/dot_general | solution.py:42
  43.4 1.2 copy.143
  44.7 12.7 %all-to-all-done = f32[2,1,4,256,256]{3,4,0,1,2:T(8,128)S(1)} async-done(((f32[2,1,4,256,256]{3,4,0,1,2:T(8,128)}), f32[2,1,4,256,256]{3,4,0,1,2:T(8,128)S(1)}, u32[]{:S(2)}, u32[]{:S(2)}) %all-to-all-start) | async-done | bytes 2097184 | tf_op jit(solution)/shard_map/all_to_all | solution.py:221
  61.8 1.0 fusion.22
  63.0 1.3 %convolution_bitcast_fusion.5 = f32[2,512,256]{1,2,0:T(8,128)S(1)} fusion(f32[512,256,1]{1,0,2:T(8,128)S(1)} %bitcast.262, f32[1,1,256,256]{2,3,1,0:T(8,128)S(1)} %bitcast.284, f32[1,1,256,256]{2,3,1,0:T(8,128)S(1)} %bitcast.283), kind=kOutput, calls=%fused_computation.23 | convolution fusion | flops 805437440 | bytes 2097152 | tf_op jit(solution)/shard_map/ij,bjk->bik/dot_general | solution.py:69
  64.4 1.1 fusion.28
  66.7 1.9 %fusion.34 = f32[2,256,512]{2,1,0:T(8,128)S(1)} fusion(f32[512,256,1]{1,0,2:T(8,128)S(1)} %bitcast.278, f32[1,256,256]{1,2,0:T(8,128)S(1)} %get-tuple-element.143, f32[1,256,256]{1,2,0:T(8,128)S(1)} %get-tuple-element.142), kind=kOutput, calls=%fused_computation.70 | convolution fusion | flops 805437440 | bytes 2097152 | tf_op jit(solution)/shard_map/bij,kj->bik/dot_general | solution.py:75
  69.7 1.1 convolution_bitcast_fusion.3
  76.5 1.7 %collective-permute-start.4 = (f32[2,1,1,256,256]{3,4,0,2,1:T(8,128)S(1)}, f32[2,1,1,256,256]{3,4,0,2,1:T(8,128)S(1)}, u32[]{:S(2)}, u32[]{:S(2)}) collective-permute-start(f32[2,1,1,256,256]{3,4,0,2,1:T(8,128)S(1)} %get-tuple-element.124), channel_id=1, source_target_pairs={{0,8},{8,16},{16,24},{24,0},{1,9},{9,17},{17,25},{25,1},{2,10},{10... | collective-permute-start | bytes 1572872 | tf_op jit(solution)/shard_map/ppermute | solution.py:240
  79.5 2.5 %collective-permute-start.6 = (f32[2,1,1,256,256]{3,4,1,2,0:T(8,128)S(1)}, f32[2,1,1,256,256]{3,4,1,2,0:T(8,128)S(1)}, u32[]{:S(2)}, u32[]{:S(2)}) collective-permute-start(f32[2,1,1,256,256]{3,4,1,2,0:T(8,128)S(1)} %get-tuple-element.122), channel_id=1, source_target_pairs={{0,24},{8,0},{16,8},{24,16},{1,25},{9,1},{17,9},{25,17},{2,26},{10... | collective-permute-start | bytes 1572872 | tf_op jit(solution)/shard_map/ppermute | solution.py:240
  82.0 10.6 %collective-permute-done.4 = f32[2,1,1,256,256]{3,4,0,2,1:T(8,128)S(1)} collective-permute-done((f32[2,1,1,256,256]{3,4,0,2,1:T(8,128)S(1)}, f32[2,1,1,256,256]{3,4,0,2,1:T(8,128)S(1)}, u32[]{:S(2)}, u32[]{:S(2)}) %collective-permute-start.4) | collective-permute-done | bytes 524320 | tf_op jit(solution)/shard_map/ppermute | solution.py:240
  93.3 8.6 %collective-permute-done.5 = f32[2,1,1,256,256]{3,4,0,2,1:T(8,128)S(1)} collective-permute-done((f32[2,1,1,256,256]{3,4,0,2,1:T(8,128)S(1)}, f32[2,1,1,256,256]{3,4,0,2,1:T(8,128)S(1)}, u32[]{:S(2)}, u32[]{:S(2)}) %collective-permute-start.5) | collective-permute-done | bytes 524320 | tf_op jit(solution)/shard_map/ppermute | solution.py:240
  103.5 2.0 %collective-permute-start.7 = (f32[2,1,512,128]{2,3,0,1:T(8,128)S(1)}, f32[2,1,512,128]{2,3,0,1:T(8,128)S(1)}, u32[]{:S(2)}, u32[]{:S(2)}) collective-permute-start(f32[2,1,512,128]{2,3,0,1:T(8,128)S(1)} %get-tuple-element.121), channel_id=1, source_target_pairs={{0,1},{2,3},{4,5},{6,7},{8,9},{10,11},{12,13},{14,15},{16,17},{18,... | collective-permute-start | bytes 1572872 | tf_op jit(solution)/shard_map/ppermute | solution.py:15
  105.5 1.3 %collective-permute-start.8 = (f32[2,1,512,128]{2,3,0,1:T(8,128)S(1)}, f32[2,1,512,128]{2,3,0,1:T(8,128)S(1)}, u32[]{:S(2)}, u32[]{:S(2)}) collective-permute-start(f32[2,1,512,128]{2,3,0,1:T(8,128)S(1)} %get-tuple-element.120), channel_id=1, source_target_pairs={{1,0},{3,2},{5,4},{7,6},{9,8},{11,10},{13,12},{15,14},{17,16},{19,... | collective-permute-start | bytes 1572872 | tf_op jit(solution)/shard_map/ppermute | solution.py:15
  107.1 2.2 %collective-permute-done.8 = f32[2,1,512,128]{2,3,0,1:T(8,128)S(1)} collective-permute-done((f32[2,1,512,128]{2,3,0,1:T(8,128)S(1)}, f32[2,1,512,128]{2,3,0,1:T(8,128)S(1)}, u32[]{:S(2)}, u32[]{:S(2)}) %collective-permute-start.8) | collective-permute-done | bytes 524320 | tf_op jit(solution)/shard_map/ppermute | solution.py:15
  109.5 4.3 %collective-permute-start.9 = (f32[2,1,128,256]{2,3,0,1:T(8,128)S(1)}, f32[2,1,128,256]{2,3,0,1:T(8,128)S(1)}, u32[]{:S(2)}, u32[]{:S(2)}) collective-permute-start(f32[2,1,128,256]{2,3,0,1:T(8,128)S(1)} %get-tuple-element.133), channel_id=1, source_target_pairs={{0,2},{2,4},{4,6},{1,3},{3,5},{5,7},{8,10},{10,12},{12,14},{9,11},... | collective-permute-start | bytes 786440 | tf_op jit(solution)/shard_map/ppermute | solution.py:15
  113.8 1.3 %collective-permute-start.10 = (f32[2,1,128,256]{2,3,0,1:T(8,128)S(1)}, f32[2,1,128,256]{2,3,0,1:T(8,128)S(1)}, u32[]{:S(2)}, u32[]{:S(2)}) collective-permute-start(f32[2,1,128,256]{2,3,0,1:T(8,128)S(1)} %get-tuple-element.132), channel_id=1, source_target_pairs={{2,0},{4,2},{6,4},{3,1},{5,3},{7,5},{10,8},{12,10},{14,12},{11,9},... | collective-permute-start | bytes 786440 | tf_op jit(solution)/shard_map/ppermute | solution.py:15
  115.1 4.5 %collective-permute-done.9 = f32[2,1,128,256]{2,3,0,1:T(8,128)S(1)} collective-permute-done((f32[2,1,128,256]{2,3,0,1:T(8,128)S(1)}, f32[2,1,128,256]{2,3,0,1:T(8,128)S(1)}, u32[]{:S(2)}, u32[]{:S(2)}) %collective-permute-start.9) | collective-permute-done | bytes 262176 | tf_op jit(solution)/shard_map/ppermute | solution.py:15
  119.7 4.1 %collective-permute-done.10 = f32[2,1,128,256]{2,3,0,1:T(8,128)S(1)} collective-permute-done((f32[2,1,128,256]{2,3,0,1:T(8,128)S(1)}, f32[2,1,128,256]{2,3,0,1:T(8,128)S(1)}, u32[]{:S(2)}, u32[]{:S(2)}) %collective-permute-start.10) | collective-permute-done | bytes 262176 | tf_op jit(solution)/shard_map/ppermute | solution.py:15
  (104 shorter events, 29.0 us)
Async XLA Ops:
  0.6 8.3 %copy-start.7 = (f32[1,256,256]{2,1,0:T(8,128)S(1)}, f32[1,256,256]{2,1,0:T(8,128)}, u32[]{:S(2)}) copy-start(f32[1,256,256]{2,1,0:T(8,128)} %param.14) | copy-start | bytes 786436
  0.6 8.3 %copy-start.6 = (f32[1,256,256]{2,1,0:T(8,128)S(1)}, f32[1,256,256]{2,1,0:T(8,128)}, u32[]{:S(2)}) copy-start(f32[1,256,256]{2,1,0:T(8,128)} %param.13) | copy-start | bytes 786436
  0.6 10.5 %copy-start.9 = (s32[1,1,4,2]{2,3,1,0:T(2,128)S(1)}, s32[1,1,4,2]{2,3,1,0:T(2,128)}, u32[]{:S(2)}) copy-start(s32[1,1,4,2]{2,3,1,0:T(2,128)} %param.17) | copy-start | bytes 100
  2.7 14.3 %collective-permute-start = (f32[2,1,128,256]{3,2,1,0:T(8,128)S(1)}, f32[2,1,128,256]{3,2,1,0:T(8,128)S(1)}, u32[]{:S(2)}, u32[]{:S(2)}) collective-permute-start(f32[2,1,128,256]{3,2,1,0:T(8,128)S(1)} %get-tuple-element.69), channel_id=1, source_target_pairs={{0,2},{2,4},{4,6},{1,3},{3,5},{5,7},{8,10},{10,12},{12,14},{9,11},... | collective-permute-start | bytes 786440 | tf_op jit(solution)/shard_map/ppermute | solution.py:33
  7.6 9.7 %collective-permute-start.1 = (f32[2,1,128,256]{3,2,1,0:T(8,128)S(1)}, f32[2,1,128,256]{3,2,1,0:T(8,128)S(1)}, u32[]{:S(2)}, u32[]{:S(2)}) collective-permute-start(f32[2,1,128,256]{3,2,1,0:T(8,128)S(1)} %get-tuple-element.70), channel_id=1, source_target_pairs={{2,0},{4,2},{6,4},{3,1},{5,3},{7,5},{10,8},{12,10},{14,12},{11,9},... | collective-permute-start | bytes 786440 | tf_op jit(solution)/shard_map/ppermute | solution.py:34
  17.4 4.9 %copy-start.8 = (f32[2,256,256]{2,1,0:T(8,128)S(1)}, f32[2,256,256]{2,1,0:T(8,128)}, u32[]{:S(2)}) copy-start(f32[2,256,256]{2,1,0:T(8,128)} %param.15) | copy-start | bytes 1572868
  18.5 4.6 %collective-permute-start.2 = (f32[2,1,512,128]{3,2,1,0:T(8,128)}, f32[2,1,512,128]{3,2,1,0:T(8,128)S(1)}, u32[]{:S(2)}, u32[]{:S(2)}) collective-permute-start(f32[2,1,512,128]{3,2,1,0:T(8,128)} %get-tuple-element.150), channel_id=1, source_target_pairs={{0,1},{2,3},{4,5},{6,7},{8,9},{10,11},{12,13},{14,15},{16,17},{18,... | collective-permute-start | bytes 1572872 | tf_op jit(solution)/shard_map/ppermute | solution.py:33
  20.9 4.0 %collective-permute-start.3 = (f32[2,1,512,128]{3,2,1,0:T(8,128)}, f32[2,1,512,128]{3,2,1,0:T(8,128)S(1)}, u32[]{:S(2)}, u32[]{:S(2)}) collective-permute-start(f32[2,1,512,128]{3,2,1,0:T(8,128)} %get-tuple-element.151), channel_id=1, source_target_pairs={{1,0},{3,2},{5,4},{7,6},{9,8},{11,10},{13,12},{15,14},{17,16},{19,... | collective-permute-start | bytes 1572872 | tf_op jit(solution)/shard_map/ppermute | solution.py:34
  22.2 9.9 %copy-start = (f32[2,256,256]{2,1,0:T(8,128)}, f32[2,256,256]{2,1,0:T(8,128)S(1)}, u32[]{:S(2)}) copy-start(f32[2,256,256]{2,1,0:T(8,128)S(1)} %maximum_multiply_fusion.1) | copy-start | bytes 1572868
  28.3 4.7 %copy-start.3 = (f32[1,256,256]{2,1,0:T(8,128)S(1)}, f32[1,256,256]{2,1,0:T(8,128)}, u32[]{:S(2)}) copy-start(f32[1,256,256]{2,1,0:T(8,128)} %get-tuple-element.162) | copy-start | bytes 786436
  28.3 29.2 %all-to-all-start = ((f32[2,1,4,256,256]{3,4,0,1,2:T(8,128)}), f32[2,1,4,256,256]{3,4,0,1,2:T(8,128)S(1)}, u32[]{:S(2)}, u32[]{:S(2)}) async-start(f32[2,1,4,256,256]{3,4,0,1,2:T(8,128)} %pad_maximum_fusion), calls=%async_computation | async-start | bytes 4194304 | tf_op jit(solution)/shard_map/all_to_all | solution.py:221
  44.7 12.9 %copy-start.4 = (f32[1,256,256]{1,2,0:T(8,128)S(1)}, f32[1,256,256]{1,2,0:T(8,128)}, u32[]{:S(2)}) copy-start(f32[1,256,256]{1,2,0:T(8,128)} %copy.182) | copy-start | bytes 786436
  57.4 1.0 copy-start.5
  64.4 1.2 copy-start.1
  66.7 3.0 %copy-start.2 = (f32[2,256,256]{2,1,0:T(8,128)S(1)}, f32[2,256,256]{2,1,0:T(8,128)}, u32[]{:S(2)}) copy-start(f32[2,256,256]{2,1,0:T(8,128)} %copy.136) | copy-start | bytes 1572868
  76.5 16.1 %collective-permute-start.4 = (f32[2,1,1,256,256]{3,4,0,2,1:T(8,128)S(1)}, f32[2,1,1,256,256]{3,4,0,2,1:T(8,128)S(1)}, u32[]{:S(2)}, u32[]{:S(2)}) collective-permute-start(f32[2,1,1,256,256]{3,4,0,2,1:T(8,128)S(1)} %get-tuple-element.124), channel_id=1, source_target_pairs={{0,8},{8,16},{16,24},{24,0},{1,9},{9,17},{17,25},{25,1},{2,10},{10... | collective-permute-start | bytes 1572872 | tf_op jit(solution)/shard_map/ppermute | solution.py:240
  78.2 23.7 %collective-permute-start.5 = (f32[2,1,1,256,256]{3,4,0,2,1:T(8,128)S(1)}, f32[2,1,1,256,256]{3,4,0,2,1:T(8,128)S(1)}, u32[]{:S(2)}, u32[]{:S(2)}) collective-permute-start(f32[2,1,1,256,256]{3,4,0,2,1:T(8,128)S(1)} %get-tuple-element.125), channel_id=1, source_target_pairs={{0,16},{8,24},{16,0},{24,8},{1,17},{9,25},{17,1},{25,9},{2,18},{10... | collective-permute-start | bytes 1572872 | tf_op jit(solution)/shard_map/ppermute | solution.py:240
  79.5 23.2 %collective-permute-start.6 = (f32[2,1,1,256,256]{3,4,1,2,0:T(8,128)S(1)}, f32[2,1,1,256,256]{3,4,1,2,0:T(8,128)S(1)}, u32[]{:S(2)}, u32[]{:S(2)}) collective-permute-start(f32[2,1,1,256,256]{3,4,1,2,0:T(8,128)S(1)} %get-tuple-element.122), channel_id=1, source_target_pairs={{0,24},{8,0},{16,8},{24,16},{1,25},{9,1},{17,9},{25,17},{2,26},{10... | collective-permute-start | bytes 1572872 | tf_op jit(solution)/shard_map/ppermute | solution.py:240
  103.5 3.4 %collective-permute-start.7 = (f32[2,1,512,128]{2,3,0,1:T(8,128)S(1)}, f32[2,1,512,128]{2,3,0,1:T(8,128)S(1)}, u32[]{:S(2)}, u32[]{:S(2)}) collective-permute-start(f32[2,1,512,128]{2,3,0,1:T(8,128)S(1)} %get-tuple-element.121), channel_id=1, source_target_pairs={{0,1},{2,3},{4,5},{6,7},{8,9},{10,11},{12,13},{14,15},{16,17},{18,... | collective-permute-start | bytes 1572872 | tf_op jit(solution)/shard_map/ppermute | solution.py:15
  105.5 3.8 %collective-permute-start.8 = (f32[2,1,512,128]{2,3,0,1:T(8,128)S(1)}, f32[2,1,512,128]{2,3,0,1:T(8,128)S(1)}, u32[]{:S(2)}, u32[]{:S(2)}) collective-permute-start(f32[2,1,512,128]{2,3,0,1:T(8,128)S(1)} %get-tuple-element.120), channel_id=1, source_target_pairs={{1,0},{3,2},{5,4},{7,6},{9,8},{11,10},{13,12},{15,14},{17,16},{19,... | collective-permute-start | bytes 1572872 | tf_op jit(solution)/shard_map/ppermute | solution.py:15
  109.5 10.2 %collective-permute-start.9 = (f32[2,1,128,256]{2,3,0,1:T(8,128)S(1)}, f32[2,1,128,256]{2,3,0,1:T(8,128)S(1)}, u32[]{:S(2)}, u32[]{:S(2)}) collective-permute-start(f32[2,1,128,256]{2,3,0,1:T(8,128)S(1)} %get-tuple-element.133), channel_id=1, source_target_pairs={{0,2},{2,4},{4,6},{1,3},{3,5},{5,7},{8,10},{10,12},{12,14},{9,11},... | collective-permute-start | bytes 786440 | tf_op jit(solution)/shard_map/ppermute | solution.py:15
  113.8 10.0 %collective-permute-start.10 = (f32[2,1,128,256]{2,3,0,1:T(8,128)S(1)}, f32[2,1,128,256]{2,3,0,1:T(8,128)S(1)}, u32[]{:S(2)}, u32[]{:S(2)}) collective-permute-start(f32[2,1,128,256]{2,3,0,1:T(8,128)S(1)} %get-tuple-element.132), channel_id=1, source_target_pairs={{2,0},{4,2},{6,4},{3,1},{5,3},{7,5},{10,8},{12,10},{14,12},{11,9},... | collective-permute-start | bytes 786440 | tf_op jit(solution)/shard_map/ppermute | solution.py:15

commit v8 on v6

--- a/solution.py
+++ b/solution.py
@@ -168,6 +168,12 @@
     anchor = jnp.zeros((), jnp.int32)
     start = (anchor, anchor, extra_rows - row, extra_cols - col)
     return lax.dynamic_slice(padded, start, patch.shape[:2] + (height, span))
+
+
+def issue_order(count):
+    half = count // 2
+    rest = [shift for shift in range(1, count) if shift != half]
+    return [0, half] + rest if count % 2 == 0 and half > 0 else list(range(count))
 
 
 def per_device(phase, absorption, probe, measured, offsets):
@@ -224,7 +230,7 @@
     unused, phase_grad, absorb_grad = backward_layers(detector, windows, moved, adjoints)
     parts = jnp.stack((phase_grad, absorb_grad))
     grid = jnp.zeros((2, layers) + extended.shape[2:], jnp.float32)
-    for shift in range(depth_count):
+    for shift in issue_order(depth_count):
         chunk = lax.dynamic_slice_in_dim(
             parts, ((depth_index + shift) % depth_count) * layers, layers, axis=1
         )

time: 125 us -> 124 us (level)
  transfers between devices with their start and end apart: 12 -> 12, of which waited for: 9 -> 8; matrix products, arithmetic and copies ran while one was open for 15% -> 15% of each run, Pallas kernels for 0% -> 0%
where the time goes in v8:
time: 124 us
  waiting for transfers between devices  45.7 us (37%)
  starting transfers between devices  24.7 us (20%)
  matrix products  20.6 us (17%)
  other arithmetic  13.4 us (11%)
  local copies, waits for them, and re-layouts  12.1 us (10%)
  between operations  7.13 us (6%)
    ppermute x3, waiting for transfers between devices, per_device(): chunk = lax.ppermute(chunk, 'depth', pairs)  19 us
    all_to_all x1, waiting for transfers between devices, per_device(): gathered = lax.all_to_all(cut, 'depth', 2, 1, tiled=True)  12.7 us
    ppermute x4, waiting for transfers between devices, from_behind(): lax.ppermute(value, axis, [(source, source + steps) for source in range(l...  10.9 us
    dot_general x8, matrix products, right_product(): jnp.einsum('bij,kj->bik', waves, matrix, precision=mode, preferred_elemen...  7.44 us
    ppermute x4, starting transfers between devices, from_behind(): lax.ppermute(value, axis, [(source, source + steps) for source in range(l...  7.42 us
    dot_general x8, matrix products, left_product(): jnp.einsum('ij,bjk->bik', matrix, waves, precision=mode, preferred_elemen...  7.31 us
    ppermute x2, starting transfers between devices, with_halo(): lax.ppermute(lax.slice_in_dim(block, block.shape[dim] - width, None, axis...  6.25 us
    dot_general x4, matrix products, matmul_exact(): jnp.dot(first, second, precision=exact_mode, preferred_element_type=jnp.f...  5.8 us
  transfers between devices with their start and end apart: 12, of which 8 were waited for; matrix products, arithmetic and copies ran while one was open for 15% of the time, Pallas kernels for 0%

profile of v8, /device:TPU:0, one launch (start us, length us, event | category | flops | bytes accessed | tf_op | source)
XLA Modules:
  0.0 123.7 jit_solution(4254038336091822738)
XLA Ops:
  0.6 2.0 %multiply_bitcast_fusion = (f32[1,1,256,256]{3,2,1,0:T(8,128)S(1)}, f32[1,1,256,256]{3,2,1,0:T(8,128)S(1)}) fusion(f32[1,256,256]{2,1,0:T(8,128)} %param.13, f32[1,256,256]{2,1,0:T(8,128)} %param.14), kind=kLoop, calls=%fused_computation.211 | loop fusion | flops 196608 | bytes 1048576 | tf_op jit(solution)/shard_map/stack | solution.py:160
  2.7 4.9 %collective-permute-start = (f32[2,1,128,256]{3,2,1,0:T(8,128)S(1)}, f32[2,1,128,256]{3,2,1,0:T(8,128)S(1)}, u32[]{:S(2)}, u32[]{:S(2)}) collective-permute-start(f32[2,1,128,256]{3,2,1,0:T(8,128)S(1)} %get-tuple-element.163), channel_id=1, source_target_pairs={{0,2},{2,4},{4,6},{1,3},{3,5},{5,7},{8,10},{10,12},{12,14},{9,11},... | collective-permute-start | bytes 786440 | tf_op jit(solution)/shard_map/ppermute | solution.py:28
  7.6 1.3 %collective-permute-start.1 = (f32[2,1,128,256]{3,2,1,0:T(8,128)S(1)}, f32[2,1,128,256]{3,2,1,0:T(8,128)S(1)}, u32[]{:S(2)}, u32[]{:S(2)}) collective-permute-start(f32[2,1,128,256]{3,2,1,0:T(8,128)S(1)} %get-tuple-element.164), channel_id=1, source_target_pairs={{2,0},{4,2},{6,4},{3,1},{5,3},{7,5},{10,8},{12,10},{14,12},{11,9},... | collective-permute-start | bytes 786440 | tf_op jit(solution)/shard_map/ppermute | solution.py:31
  15.9 1.3 %collective-permute-done.1 = f32[2,1,128,256]{3,2,1,0:T(8,128)S(1)} collective-permute-done((f32[2,1,128,256]{3,2,1,0:T(8,128)S(1)}, f32[2,1,128,256]{3,2,1,0:T(8,128)S(1)}, u32[]{:S(2)}, u32[]{:S(2)}) %collective-permute-start.1) | collective-permute-done | bytes 262176 | tf_op jit(solution)/shard_map/ppermute | solution.py:31
  17.4 1.1 fusion.144
  18.5 1.3 %collective-permute-start.2 = (f32[2,1,512,128]{3,2,1,0:T(8,128)}, f32[2,1,512,128]{3,2,1,0:T(8,128)S(1)}, u32[]{:S(2)}, u32[]{:S(2)}) collective-permute-start(f32[2,1,512,128]{3,2,1,0:T(8,128)} %get-tuple-element.146), channel_id=1, source_target_pairs={{0,1},{2,3},{4,5},{6,7},{8,9},{10,11},{12,13},{14,15},{16,17},{18,... | collective-permute-start | bytes 1572872 | tf_op jit(solution)/shard_map/ppermute | solution.py:28
  19.8 1.0 sine_negate_fusion
  20.8 1.3 %collective-permute-start.3 = (f32[2,1,512,128]{3,2,1,0:T(8,128)}, f32[2,1,512,128]{3,2,1,0:T(8,128)S(1)}, u32[]{:S(2)}, u32[]{:S(2)}) collective-permute-start(f32[2,1,512,128]{3,2,1,0:T(8,128)} %get-tuple-element.147), channel_id=1, source_target_pairs={{1,0},{3,2},{5,4},{7,6},{9,8},{11,10},{13,12},{15,14},{17,16},{19,... | collective-permute-start | bytes 1572872 | tf_op jit(solution)/shard_map/ppermute | solution.py:31
  23.1 1.8 %collective-permute-done.3 = f32[2,1,512,128]{3,2,1,0:T(8,128)S(1)} collective-permute-done((f32[2,1,512,128]{3,2,1,0:T(8,128)}, f32[2,1,512,128]{3,2,1,0:T(8,128)S(1)}, u32[]{:S(2)}, u32[]{:S(2)}) %collective-permute-start.3) | collective-permute-done | bytes 524320 | tf_op jit(solution)/shard_map/ppermute | solution.py:31
  26.6 1.6 %pad_maximum_fusion = f32[2,1,4,256,256]{3,4,0,1,2:T(8,128)} fusion(f32[2,1,1,256,256]{3,4,0,1,2:T(8,128)S(1)} %bitcast.290, f32[2,1,1,256,256]{3,4,0,1,2:T(8,128)S(1)} %bitcast.289, f32[2,1,1,256,256]{3,4,0,1,2:T(8,128)S(1)} %bitcast.288, f32[2,1,1,256,256]{3,4,0,1,2:T(8,128)S(1)} %bitcast.287), kind=kLoop, calls=%fused_computation.16 | loop fusion | flops 1572864 | bytes 4194304 | tf_op jit(solution)/shard_map/stack | solution.py:211
  28.2 3.9 %all-to-all-start = ((f32[2,1,4,256,256]{3,4,0,1,2:T(8,128)}), f32[2,1,4,256,256]{3,4,0,1,2:T(8,128)S(1)}, u32[]{:S(2)}, u32[]{:S(2)}) async-start(f32[2,1,4,256,256]{3,4,0,1,2:T(8,128)} %pad_maximum_fusion), calls=%async_computation | async-start | bytes 4194304 | tf_op jit(solution)/shard_map/all_to_all | solution.py:220
  36.6 1.4 %fusion.78 = f32[256,256]{1,0:T(8,128)S(1)} fusion(f32[256]{0:T(256)S(1)} %get-tuple-element.185, f32[256]{0:T(256)S(1)} %get-tuple-element.186), kind=kOutput, calls=%fused_computation.204 | convolution fusion | flops 203358208 | bytes 264192 | tf_op jit(solution)/shard_map/dot_general | solution.py:39
  38.1 1.5 %fusion.3 = f32[1,256,256]{2,1,0:T(8,128)S(1)} fusion(f32[256,256]{1,0:T(8,128)S(1)} %fusion.78, f32[256]{0:T(256)S(1)} %get-tuple-element.185, f32[256]{0:T(256)S(1)} %get-tuple-element.186), kind=kOutput, calls=%fused_computation.27 | convolution fusion | flops 203423744 | bytes 526336 | tf_op jit(solution)/shard_map/dot_general | solution.py:39
  39.5 1.4 %fusion.79 = f32[256,256]{1,0:T(8,128)S(1)} fusion(f32[256]{0:T(256)S(1)} %get-tuple-element.185, f32[256]{0:T(256)S(1)} %get-tuple-element.186), kind=kOutput, calls=%fused_computation.206 | convolution fusion | flops 203358208 | bytes 264192 | tf_op jit(solution)/shard_map/dot_general | solution.py:39
  41.0 1.5 %fusion.4 = f32[1,256,256]{2,1,0:T(8,128)S(1)} fusion(f32[256,256]{1,0:T(8,128)S(1)} %fusion.79, f32[256]{0:T(256)S(1)} %get-tuple-element.185, f32[256]{0:T(256)S(1)} %get-tuple-element.186), kind=kOutput, calls=%fused_computation.29 | convolution fusion | flops 203423744 | bytes 526336 | tf_op jit(solution)/shard_map/dot_general | solution.py:39
  43.4 1.2 copy.143
  44.6 12.7 %all-to-all-done = f32[2,1,4,256,256]{3,4,0,1,2:T(8,128)S(1)} async-done(((f32[2,1,4,256,256]{3,4,0,1,2:T(8,128)}), f32[2,1,4,256,256]{3,4,0,1,2:T(8,128)S(1)}, u32[]{:S(2)}, u32[]{:S(2)}) %all-to-all-start) | async-done | bytes 2097184 | tf_op jit(solution)/shard_map/all_to_all | solution.py:220
  61.8 1.0 fusion.22
  63.0 1.3 %convolution_bitcast_fusion.5 = f32[2,512,256]{1,2,0:T(8,128)S(1)} fusion(f32[512,256,1]{1,0,2:T(8,128)S(1)} %bitcast.260, f32[1,1,256,256]{2,3,1,0:T(8,128)S(1)} %bitcast.282, f32[1,1,256,256]{2,3,1,0:T(8,128)S(1)} %bitcast.281), kind=kOutput, calls=%fused_computation.23 | convolution fusion | flops 805437440 | bytes 2097152 | tf_op jit(solution)/shard_map/ij,bjk->bik/dot_general | solution.py:66
  66.6 1.9 %fusion.34 = f32[2,256,512]{2,1,0:T(8,128)S(1)} fusion(f32[512,256,1]{1,0,2:T(8,128)S(1)} %bitcast.276, f32[1,256,256]{1,2,0:T(8,128)S(1)} %get-tuple-element.139, f32[1,256,256]{1,2,0:T(8,128)S(1)} %get-tuple-element.138), kind=kOutput, calls=%fused_computation.72 | convolution fusion | flops 805437440 | bytes 2097152 | tf_op jit(solution)/shard_map/bij,kj->bik/dot_general | solution.py:72
  68.5 1.0 fusion.74
  69.6 1.1 convolution_bitcast_fusion.3
  76.4 1.5 %collective-permute-start.4 = (f32[2,1,1,256,256]{3,4,0,2,1:T(8,128)S(1)}, f32[2,1,1,256,256]{3,4,0,2,1:T(8,128)S(1)}, u32[]{:S(2)}, u32[]{:S(2)}) collective-permute-start(f32[2,1,1,256,256]{3,4,0,2,1:T(8,128)S(1)} %get-tuple-element.120), channel_id=1, source_target_pairs={{0,16},{8,24},{16,0},{24,8},{1,17},{9,25},{17,1},{25,9},{2,18},{10... | collective-permute-start | bytes 1572872 | tf_op jit(solution)/shard_map/ppermute | solution.py:239
  79.2 2.5 %collective-permute-start.6 = (f32[2,1,1,256,256]{3,4,1,2,0:T(8,128)S(1)}, f32[2,1,1,256,256]{3,4,1,2,0:T(8,128)S(1)}, u32[]{:S(2)}, u32[]{:S(2)}) collective-permute-start(f32[2,1,1,256,256]{3,4,1,2,0:T(8,128)S(1)} %get-tuple-element.118), channel_id=1, source_target_pairs={{0,24},{8,0},{16,8},{24,16},{1,25},{9,1},{17,9},{25,17},{2,26},{10... | collective-permute-start | bytes 1572872 | tf_op jit(solution)/shard_map/ppermute | solution.py:239
  81.6 19.0 %collective-permute-done.4 = f32[2,1,1,256,256]{3,4,0,2,1:T(8,128)S(1)} collective-permute-done((f32[2,1,1,256,256]{3,4,0,2,1:T(8,128)S(1)}, f32[2,1,1,256,256]{3,4,0,2,1:T(8,128)S(1)}, u32[]{:S(2)}, u32[]{:S(2)}) %collective-permute-start.4) | collective-permute-done | bytes 524320 | tf_op jit(solution)/shard_map/ppermute | solution.py:239
  103.1 1.3 %collective-permute-start.7 = (f32[2,1,512,128]{2,3,0,1:T(8,128)S(1)}, f32[2,1,512,128]{2,3,0,1:T(8,128)S(1)}, u32[]{:S(2)}, u32[]{:S(2)}) collective-permute-start(f32[2,1,512,128]{2,3,0,1:T(8,128)S(1)} %get-tuple-element.117), channel_id=1, source_target_pairs={{0,1},{2,3},{4,5},{6,7},{8,9},{10,11},{12,13},{14,15},{16,17},{18,... | collective-permute-start | bytes 1572872 | tf_op jit(solution)/shard_map/ppermute | solution.py:15
  104.4 1.3 %collective-permute-start.8 = (f32[2,1,512,128]{2,3,0,1:T(8,128)S(1)}, f32[2,1,512,128]{2,3,0,1:T(8,128)S(1)}, u32[]{:S(2)}, u32[]{:S(2)}) collective-permute-start(f32[2,1,512,128]{2,3,0,1:T(8,128)S(1)} %get-tuple-element.116), channel_id=1, source_target_pairs={{1,0},{3,2},{5,4},{7,6},{9,8},{11,10},{13,12},{15,14},{17,16},{19,... | collective-permute-start | bytes 1572872 | tf_op jit(solution)/shard_map/ppermute | solution.py:15
  106.0 2.2 %collective-permute-done.8 = f32[2,1,512,128]{2,3,0,1:T(8,128)S(1)} collective-permute-done((f32[2,1,512,128]{2,3,0,1:T(8,128)S(1)}, f32[2,1,512,128]{2,3,0,1:T(8,128)S(1)}, u32[]{:S(2)}, u32[]{:S(2)}) %collective-permute-start.8) | collective-permute-done | bytes 524320 | tf_op jit(solution)/shard_map/ppermute | solution.py:15
  108.4 3.5 %collective-permute-start.9 = (f32[2,1,128,256]{2,3,0,1:T(8,128)S(1)}, f32[2,1,128,256]{2,3,0,1:T(8,128)S(1)}, u32[]{:S(2)}, u32[]{:S(2)}) collective-permute-start(f32[2,1,128,256]{2,3,0,1:T(8,128)S(1)} %get-tuple-element.129), channel_id=1, source_target_pairs={{0,2},{2,4},{4,6},{1,3},{3,5},{5,7},{8,10},{10,12},{12,14},{9,11},... | collective-permute-start | bytes 786440 | tf_op jit(solution)/shard_map/ppermute | solution.py:15
  111.9 1.3 %collective-permute-start.10 = (f32[2,1,128,256]{2,3,0,1:T(8,128)S(1)}, f32[2,1,128,256]{2,3,0,1:T(8,128)S(1)}, u32[]{:S(2)}, u32[]{:S(2)}) collective-permute-start(f32[2,1,128,256]{2,3,0,1:T(8,128)S(1)} %get-tuple-element.128), channel_id=1, source_target_pairs={{2,0},{4,2},{6,4},{3,1},{5,3},{7,5},{10,8},{12,10},{14,12},{11,9},... | collective-permute-start | bytes 786440 | tf_op jit(solution)/shard_map/ppermute | solution.py:15
  113.3 4.5 %collective-permute-done.9 = f32[2,1,128,256]{2,3,0,1:T(8,128)S(1)} collective-permute-done((f32[2,1,128,256]{2,3,0,1:T(8,128)S(1)}, f32[2,1,128,256]{2,3,0,1:T(8,128)S(1)}, u32[]{:S(2)}, u32[]{:S(2)}) %collective-permute-start.9) | collective-permute-done | bytes 262176 | tf_op jit(solution)/shard_map/ppermute | solution.py:15
  117.8 4.1 %collective-permute-done.10 = f32[2,1,128,256]{2,3,0,1:T(8,128)S(1)} collective-permute-done((f32[2,1,128,256]{2,3,0,1:T(8,128)S(1)}, f32[2,1,128,256]{2,3,0,1:T(8,128)S(1)}, u32[]{:S(2)}, u32[]{:S(2)}) %collective-permute-start.10) | collective-permute-done | bytes 262176 | tf_op jit(solution)/shard_map/ppermute | solution.py:15
  (99 shorter events, 27.7 us)
Async XLA Ops:
  0.6 9.5 %copy-start.7 = (s32[1,1,4,2]{2,3,1,0:T(2,128)S(1)}, s32[1,1,4,2]{2,3,1,0:T(2,128)}, u32[]{:S(2)}) copy-start(s32[1,1,4,2]{2,3,1,0:T(2,128)} %param.17) | copy-start | bytes 100
  2.7 13.3 %collective-permute-start = (f32[2,1,128,256]{3,2,1,0:T(8,128)S(1)}, f32[2,1,128,256]{3,2,1,0:T(8,128)S(1)}, u32[]{:S(2)}, u32[]{:S(2)}) collective-permute-start(f32[2,1,128,256]{3,2,1,0:T(8,128)S(1)} %get-tuple-element.163), channel_id=1, source_target_pairs={{0,2},{2,4},{4,6},{1,3},{3,5},{5,7},{8,10},{10,12},{12,14},{9,11},... | collective-permute-start | bytes 786440 | tf_op jit(solution)/shard_map/ppermute | solution.py:28
  7.6 9.7 %collective-permute-start.1 = (f32[2,1,128,256]{3,2,1,0:T(8,128)S(1)}, f32[2,1,128,256]{3,2,1,0:T(8,128)S(1)}, u32[]{:S(2)}, u32[]{:S(2)}) collective-permute-start(f32[2,1,128,256]{3,2,1,0:T(8,128)S(1)} %get-tuple-element.164), channel_id=1, source_target_pairs={{2,0},{4,2},{6,4},{3,1},{5,3},{7,5},{10,8},{12,10},{14,12},{11,9},... | collective-permute-start | bytes 786440 | tf_op jit(solution)/shard_map/ppermute | solution.py:31
  17.4 4.8 %copy-start.6 = (f32[2,256,256]{2,1,0:T(8,128)S(1)}, f32[2,256,256]{2,1,0:T(8,128)}, u32[]{:S(2)}) copy-start(f32[2,256,256]{2,1,0:T(8,128)} %param.15) | copy-start | bytes 1572868
  18.5 4.6 %collective-permute-start.2 = (f32[2,1,512,128]{3,2,1,0:T(8,128)}, f32[2,1,512,128]{3,2,1,0:T(8,128)S(1)}, u32[]{:S(2)}, u32[]{:S(2)}) collective-permute-start(f32[2,1,512,128]{3,2,1,0:T(8,128)} %get-tuple-element.146), channel_id=1, source_target_pairs={{0,1},{2,3},{4,5},{6,7},{8,9},{10,11},{12,13},{14,15},{16,17},{18,... | collective-permute-start | bytes 1572872 | tf_op jit(solution)/shard_map/ppermute | solution.py:28
  20.8 4.0 %collective-permute-start.3 = (f32[2,1,512,128]{3,2,1,0:T(8,128)}, f32[2,1,512,128]{3,2,1,0:T(8,128)S(1)}, u32[]{:S(2)}, u32[]{:S(2)}) collective-permute-start(f32[2,1,512,128]{3,2,1,0:T(8,128)} %get-tuple-element.147), channel_id=1, source_target_pairs={{1,0},{3,2},{5,4},{7,6},{9,8},{11,10},{13,12},{15,14},{17,16},{19,... | collective-permute-start | bytes 1572872 | tf_op jit(solution)/shard_map/ppermute | solution.py:31
  22.2 9.9 %copy-start = (f32[2,256,256]{2,1,0:T(8,128)}, f32[2,256,256]{2,1,0:T(8,128)S(1)}, u32[]{:S(2)}) copy-start(f32[2,256,256]{2,1,0:T(8,128)S(1)} %maximum_multiply_fusion.1) | copy-start | bytes 1572868
  28.2 4.7 %copy-start.3 = (f32[1,256,256]{2,1,0:T(8,128)S(1)}, f32[1,256,256]{2,1,0:T(8,128)}, u32[]{:S(2)}) copy-start(f32[1,256,256]{2,1,0:T(8,128)} %get-tuple-element.158) | copy-start | bytes 786436
  28.2 29.2 %all-to-all-start = ((f32[2,1,4,256,256]{3,4,0,1,2:T(8,128)}), f32[2,1,4,256,256]{3,4,0,1,2:T(8,128)S(1)}, u32[]{:S(2)}, u32[]{:S(2)}) async-start(f32[2,1,4,256,256]{3,4,0,1,2:T(8,128)} %pad_maximum_fusion), calls=%async_computation | async-start | bytes 4194304 | tf_op jit(solution)/shard_map/all_to_all | solution.py:220
  44.6 12.9 %copy-start.4 = (f32[1,256,256]{1,2,0:T(8,128)S(1)}, f32[1,256,256]{1,2,0:T(8,128)}, u32[]{:S(2)}) copy-start(f32[1,256,256]{1,2,0:T(8,128)} %copy.182) | copy-start | bytes 786436
  57.4 1.0 copy-start.5
  64.3 1.2 copy-start.1
  66.6 3.0 %copy-start.2 = (f32[2,256,256]{2,1,0:T(8,128)S(1)}, f32[2,256,256]{2,1,0:T(8,128)}, u32[]{:S(2)}) copy-start(f32[2,256,256]{2,1,0:T(8,128)} %copy.136) | copy-start | bytes 1572868
  76.4 24.3 %collective-permute-start.4 = (f32[2,1,1,256,256]{3,4,0,2,1:T(8,128)S(1)}, f32[2,1,1,256,256]{3,4,0,2,1:T(8,128)S(1)}, u32[]{:S(2)}, u32[]{:S(2)}) collective-permute-start(f32[2,1,1,256,256]{3,4,0,2,1:T(8,128)S(1)} %get-tuple-element.120), channel_id=1, source_target_pairs={{0,16},{8,24},{16,0},{24,8},{1,17},{9,25},{17,1},{25,9},{2,18},{10... | collective-permute-start | bytes 1572872 | tf_op jit(solution)/shard_map/ppermute | solution.py:239
  77.9 23.5 %collective-permute-start.5 = (f32[2,1,1,256,256]{3,4,0,2,1:T(8,128)S(1)}, f32[2,1,1,256,256]{3,4,0,2,1:T(8,128)S(1)}, u32[]{:S(2)}, u32[]{:S(2)}) collective-permute-start(f32[2,1,1,256,256]{3,4,0,2,1:T(8,128)S(1)} %get-tuple-element.121), channel_id=1, source_target_pairs={{0,8},{8,16},{16,24},{24,0},{1,9},{9,17},{17,25},{25,1},{2,10},{10... | collective-permute-start | bytes 1572872 | tf_op jit(solution)/shard_map/ppermute | solution.py:239
  79.2 23.1 %collective-permute-start.6 = (f32[2,1,1,256,256]{3,4,1,2,0:T(8,128)S(1)}, f32[2,1,1,256,256]{3,4,1,2,0:T(8,128)S(1)}, u32[]{:S(2)}, u32[]{:S(2)}) collective-permute-start(f32[2,1,1,256,256]{3,4,1,2,0:T(8,128)S(1)} %get-tuple-element.118), channel_id=1, source_target_pairs={{0,24},{8,0},{16,8},{24,16},{1,25},{9,1},{17,9},{25,17},{2,26},{10... | collective-permute-start | bytes 1572872 | tf_op jit(solution)/shard_map/ppermute | solution.py:239
  103.1 2.8 %collective-permute-start.7 = (f32[2,1,512,128]{2,3,0,1:T(8,128)S(1)}, f32[2,1,512,128]{2,3,0,1:T(8,128)S(1)}, u32[]{:S(2)}, u32[]{:S(2)}) collective-permute-start(f32[2,1,512,128]{2,3,0,1:T(8,128)S(1)} %get-tuple-element.117), channel_id=1, source_target_pairs={{0,1},{2,3},{4,5},{6,7},{8,9},{10,11},{12,13},{14,15},{16,17},{18,... | collective-permute-start | bytes 1572872 | tf_op jit(solution)/shard_map/ppermute | solution.py:15
  104.4 3.8 %collective-permute-start.8 = (f32[2,1,512,128]{2,3,0,1:T(8,128)S(1)}, f32[2,1,512,128]{2,3,0,1:T(8,128)S(1)}, u32[]{:S(2)}, u32[]{:S(2)}) collective-permute-start(f32[2,1,512,128]{2,3,0,1:T(8,128)S(1)} %get-tuple-element.116), channel_id=1, source_target_pairs={{1,0},{3,2},{5,4},{7,6},{9,8},{11,10},{13,12},{15,14},{17,16},{19,... | collective-permute-start | bytes 1572872 | tf_op jit(solution)/shard_map/ppermute | solution.py:15
  108.4 9.4 %collective-permute-start.9 = (f32[2,1,128,256]{2,3,0,1:T(8,128)S(1)}, f32[2,1,128,256]{2,3,0,1:T(8,128)S(1)}, u32[]{:S(2)}, u32[]{:S(2)}) collective-permute-start(f32[2,1,128,256]{2,3,0,1:T(8,128)S(1)} %get-tuple-element.129), channel_id=1, source_target_pairs={{0,2},{2,4},{4,6},{1,3},{3,5},{5,7},{8,10},{10,12},{12,14},{9,11},... | collective-permute-start | bytes 786440 | tf_op jit(solution)/shard_map/ppermute | solution.py:15
  111.9 10.0 %collective-permute-start.10 = (f32[2,1,128,256]{2,3,0,1:T(8,128)S(1)}, f32[2,1,128,256]{2,3,0,1:T(8,128)S(1)}, u32[]{:S(2)}, u32[]{:S(2)}) collective-permute-start(f32[2,1,128,256]{2,3,0,1:T(8,128)S(1)} %get-tuple-element.128), channel_id=1, source_target_pairs={{2,0},{4,2},{6,4},{3,1},{5,3},{7,5},{10,8},{12,10},{14,12},{11,9},... | collective-permute-start | bytes 786440 | tf_op jit(solution)/shard_map/ppermute | solution.py:15

commit v9 on v8

--- a/solution.py
+++ b/solution.py
@@ -93,9 +93,9 @@
 
 def forward_layers(wave, slab, matrices):
     moved_list = []
-    for layer in range(slab.shape[1]):
-        trans_re = slab[0, layer]
-        trans_im = slab[1, layer]
+    for layer in range(len(slab)):
+        trans_re = slab[layer][0]
+        trans_im = slab[layer][1]
         moved = jnp.stack(
             (trans_re * wave[0] - trans_im * wave[1], trans_re * wave[1] + trans_im * wave[0])
         )
@@ -105,7 +105,7 @@
 
 
 def backward_layers(grad, slab, moved, adjoints):
-    layers = slab.shape[1]
+    layers = len(slab)
     phase_parts = [None] * layers
     absorb_parts = [None] * layers
     for layer in reversed(range(layers)):
@@ -114,8 +114,8 @@
         moved_im = moved[1, layer]
         phase_parts[layer] = grad_moved[1] * moved_re - grad_moved[0] * moved_im
         absorb_parts[layer] = -(grad_moved[0] * moved_re + grad_moved[1] * moved_im)
-        trans_re = slab[0, layer]
-        trans_im = slab[1, layer]
+        trans_re = slab[layer][0]
+        trans_im = slab[layer][1]
         grad = jnp.stack(
             (
                 trans_re * grad_moved[0] + trans_im * grad_moved[1],
@@ -217,9 +217,21 @@
         ],
         axis=2,
     )
-    gathered = lax.all_to_all(cut, "depth", 2, 1, tiled=True)
-    windows = gathered
-    total_layers = windows.shape[1]
+    pieces = []
+    for shift in range(depth_count):
+        chunk = lax.dynamic_slice_in_dim(
+            cut, ((depth_index + shift) % depth_count) * share, share, axis=2
+        )
+        if shift > 0:
+            pairs = [(i, (i + shift) % depth_count) for i in range(depth_count)]
+            chunk = lax.ppermute(chunk, "depth", pairs)
+        pieces.append(chunk)
+    windows = []
+    for group in range(depth_count):
+        which = (depth_index - group) % depth_count
+        for layer in range(layers):
+            windows.append(lax.select_n(which, *[piece[:, layer] for piece in pieces]))
+    total_layers = len(windows)
     matrices = [fresnel] * (total_layers - 1) + [far_field]
     adjoints = [adjoint_of(matrix) for matrix in matrices]
     start_wave = probe[:, None]

time: 124 us -> 134 us (1.081)
  local copies, waits for them, and re-layouts: 12.1 us -> 14.8 us
  waiting for transfers between devices: 45.7 us -> 48.4 us
  other arithmetic: 13.4 us -> 15.2 us
  starting transfers between devices: 24.7 us -> 26.2 us
  matrix products: 20.6 us -> 22 us
    ppermute x3 -> x6, waiting for transfers between devices: 19 us -> 35.9 us  [per_device(): chunk = lax.ppermute(chunk, 'depth', pairs)]
    all_to_all x1 -> x0, waiting for transfers between devices: 12.7 us -> none  [per_device(): gathered = lax.all_to_all(cut, 'depth', 2, 1, tiled=True)]
    ppermute x3 -> x6, starting transfers between devices: 4.51 us -> 8.91 us  [per_device(): chunk = lax.ppermute(chunk, 'depth', pairs)]
    all_to_all x1 -> x0, starting transfers between devices: 3.92 us -> none  [per_device(): gathered = lax.all_to_all(cut, 'depth', 2, 1, tiled=True)]
    dynamic_slice x5, local copies, waits for them, and re-layouts: 1.46 us -> 3.89 us  [per_device(): lax.dynamic_slice(extended, (anchor, anchor, row_starts[k], col_starts[k]...]
    select_n x0 -> x1, other arithmetic: none -> 1.58 us  [per_device(): windows.append(lax.select_n(which, *[piece[:, layer] for piece in pieces]))]
    ppermute x2, waiting for transfers between devices: 3.08 us -> 1.66 us  [with_halo(): lax.ppermute(lax.slice_in_dim(block, 0, width, axis=dim), axis, backward)]
    dot_general x4, matrix products: 5.8 us -> 7.21 us  [matmul_exact(): jnp.dot(first, second, precision=exact_mode, preferred_element_type=jnp.f...]
  transfers between devices with their start and end apart: 12 -> 14, of which waited for: 8 -> 9; matrix products, arithmetic and copies ran while one was open for 15% -> 15% of each run, Pallas kernels for 0% -> 0%
where the time goes in v9:
time: 134 us
  waiting for transfers between devices  48.4 us (36%)
  starting transfers between devices  26.2 us (20%)
  matrix products  22 us (16%)
  other arithmetic  15.2 us (11%)
  local copies, waits for them, and re-layouts  14.8 us (11%)
  between operations  7.16 us (5%)
    ppermute x6, waiting for transfers between devices, per_device(): chunk = lax.ppermute(chunk, 'depth', pairs)  35.9 us
    ppermute x4, waiting for transfers between devices, from_behind(): lax.ppermute(value, axis, [(source, source + steps) for source in range(l...  10.9 us
    ppermute x6, starting transfers between devices, per_device(): chunk = lax.ppermute(chunk, 'depth', pairs)  8.91 us
    ppermute x4, starting transfers between devices, from_behind(): lax.ppermute(value, axis, [(source, source + steps) for source in range(l...  8.29 us
    dot_general x8, matrix products, right_product(): jnp.einsum('bij,kj->bik', waves, matrix, precision=mode, preferred_elemen...  7.67 us
    dot_general x4, matrix products, matmul_exact(): jnp.dot(first, second, precision=exact_mode, preferred_element_type=jnp.f...  7.21 us
    dot_general x8, matrix products, left_product(): jnp.einsum('ij,bjk->bik', matrix, waves, precision=mode, preferred_elemen...  7.07 us
    ppermute x2, starting transfers between devices, with_halo(): lax.ppermute(lax.slice_in_dim(block, block.shape[dim] - width, None, axis...  6.42 us
  transfers between devices with their start and end apart: 14, of which 9 were waited for; matrix products, arithmetic and copies ran while one was open for 15% of the time, Pallas kernels for 0%

profile of v9, /device:TPU:0, one launch (start us, length us, event | category | flops | bytes accessed | tf_op | source)
XLA Modules:
  0.0 133.8 jit_solution(12771868936565030348)
XLA Ops:
  0.6 2.0 %multiply_bitcast_fusion = (f32[1,1,256,256]{3,2,1,0:T(8,128)S(1)}, f32[1,1,256,256]{3,2,1,0:T(8,128)S(1)}) fusion(f32[1,256,256]{2,1,0:T(8,128)} %param.13, f32[1,256,256]{2,1,0:T(8,128)} %param.14), kind=kLoop, calls=%fused_computation.214 | loop fusion | flops 196608 | bytes 1048576 | tf_op jit(solution)/shard_map/stack | solution.py:160
  2.6 4.9 %collective-permute-start = (f32[2,1,128,256]{3,2,1,0:T(8,128)S(1)}, f32[2,1,128,256]{3,2,1,0:T(8,128)S(1)}, u32[]{:S(2)}, u32[]{:S(2)}) collective-permute-start(f32[2,1,128,256]{3,2,1,0:T(8,128)S(1)} %get-tuple-element.168), channel_id=1, source_target_pairs={{0,2},{2,4},{4,6},{1,3},{3,5},{5,7},{8,10},{10,12},{12,14},{9,11},... | collective-permute-start | bytes 786440 | tf_op jit(solution)/shard_map/ppermute | solution.py:28
  7.6 1.3 collective-permute-start.1
  9.5 1.4 %fusion.78 = f32[256,256]{1,0:T(8,128)S(1)} fusion(f32[256]{0:T(256)S(1)} %get-tuple-element.190, f32[256]{0:T(256)S(1)} %get-tuple-element.191), kind=kOutput, calls=%fused_computation.207 | convolution fusion | flops 203358208 | bytes 264192 | tf_op jit(solution)/shard_map/dot_general | solution.py:39
  10.9 1.4 %fusion.79 = f32[256,256]{1,0:T(8,128)S(1)} fusion(f32[256]{0:T(256)S(1)} %get-tuple-element.190, f32[256]{0:T(256)S(1)} %get-tuple-element.191), kind=kOutput, calls=%fused_computation.209 | convolution fusion | flops 203358208 | bytes 264192 | tf_op jit(solution)/shard_map/dot_general | solution.py:39
  13.8 2.2 %fusion.3 = f32[1,256,256]{2,1,0:T(8,128)} fusion(f32[256,256]{1,0:T(8,128)S(1)} %fusion.78, f32[256]{0:T(256)S(1)} %get-tuple-element.190, f32[256]{0:T(256)S(1)} %get-tuple-element.191), kind=kOutput, calls=%fused_computation.26 | convolution fusion | flops 203423744 | bytes 526336 | tf_op jit(solution)/shard_map/dot_general | solution.py:39
  22.9 1.5 %collective-permute-start.2 = (f32[2,1,512,128]{3,2,1,0:T(8,128)}, f32[2,1,512,128]{3,2,1,0:T(8,128)S(1)}, u32[]{:S(2)}, u32[]{:S(2)}) collective-permute-start(f32[2,1,512,128]{3,2,1,0:T(8,128)} %get-tuple-element.151), channel_id=1, source_target_pairs={{0,1},{2,3},{4,5},{6,7},{8,9},{10,11},{12,13},{14,15},{16,17},{18,... | collective-permute-start | bytes 1572872 | tf_op jit(solution)/shard_map/ppermute | solution.py:28
  24.4 2.2 %fusion.4 = f32[1,256,256]{2,1,0:T(8,128)} fusion(f32[256,256]{1,0:T(8,128)S(1)} %fusion.79, f32[256]{0:T(256)S(1)} %get-tuple-element.190, f32[256]{0:T(256)S(1)} %get-tuple-element.191), kind=kOutput, calls=%fused_computation.28 | convolution fusion | flops 203423744 | bytes 526336 | tf_op jit(solution)/shard_map/dot_general | solution.py:39
  27.6 1.3 collective-permute-start.3
  30.0 1.7 %collective-permute-done.3 = f32[2,1,512,128]{3,2,1,0:T(8,128)S(1)} collective-permute-done((f32[2,1,512,128]{3,2,1,0:T(8,128)}, f32[2,1,512,128]{3,2,1,0:T(8,128)S(1)}, u32[]{:S(2)}, u32[]{:S(2)}) %collective-permute-start.3) | collective-permute-done | bytes 524320 | tf_op jit(solution)/shard_map/ppermute | solution.py:31
  35.8 1.6 %pad_maximum_fusion = f32[2,1,4,256,256]{3,4,2,1,0:T(8,128)S(1)} fusion(f32[2,1,1,256,256]{3,4,2,1,0:T(8,128)} %bitcast.280, f32[2,1,1,256,256]{3,4,2,1,0:T(8,128)} %bitcast.279, f32[2,1,1,256,256]{3,4,2,1,0:T(8,128)} %bitcast.278, f32[2,1,1,256,256]{3,4,2,1,0:T(8,128)S(1)} %bitcast.277), kind=kLoop, calls=%fused_computation.16 | loop fusion | flops 1572864 | bytes 4194304 | tf_op jit(solution)/shard_map/stack | solution.py:211
  37.4 1.2 constant_dynamic-slice_fusion.2
  38.7 1.5 %collective-permute-start.4 = (f32[2,1,1,256,256]{3,4,2,1,0:T(8,128)}, f32[2,1,1,256,256]{3,4,2,1,0:T(8,128)}, u32[]{:S(2)}, u32[]{:S(2)}) collective-permute-start(f32[2,1,1,256,256]{3,4,2,1,0:T(8,128)} %get-tuple-element.110), channel_id=1, source_target_pairs={{0,8},{8,16},{16,24},{24,0},{1,9},{9,17},{17,25},{25,1},{2,10},{10... | collective-permute-start | bytes 1572872 | tf_op jit(solution)/shard_map/ppermute | solution.py:227
  40.2 1.5 %collective-permute-start.5 = (f32[2,1,1,256,256]{3,4,2,1,0:T(8,128)}, f32[2,1,1,256,256]{3,4,2,1,0:T(8,128)}, u32[]{:S(2)}, u32[]{:S(2)}) collective-permute-start(f32[2,1,1,256,256]{3,4,2,1,0:T(8,128)} %get-tuple-element.112), channel_id=1, source_target_pairs={{0,16},{8,24},{16,0},{24,8},{1,17},{9,25},{17,1},{25,9},{2,18},{10... | collective-permute-start | bytes 1572872 | tf_op jit(solution)/shard_map/ppermute | solution.py:227
  41.7 1.4 %collective-permute-start.6 = (f32[2,1,1,256,256]{3,4,2,1,0:T(8,128)}, f32[2,1,1,256,256]{3,4,2,1,0:T(8,128)}, u32[]{:S(2)}, u32[]{:S(2)}) collective-permute-start(f32[2,1,1,256,256]{3,4,2,1,0:T(8,128)} %get-tuple-element.111), channel_id=1, source_target_pairs={{0,24},{8,0},{16,8},{24,16},{1,25},{9,1},{17,9},{25,17},{2,26},{10... | collective-permute-start | bytes 1572872 | tf_op jit(solution)/shard_map/ppermute | solution.py:227
  45.9 1.1 maximum_multiply_fusion
  47.9 1.2 copy.89
  49.1 5.6 %collective-permute-done.4 = f32[2,1,1,256,256]{3,4,2,1,0:T(8,128)} collective-permute-done((f32[2,1,1,256,256]{3,4,2,1,0:T(8,128)}, f32[2,1,1,256,256]{3,4,2,1,0:T(8,128)}, u32[]{:S(2)}, u32[]{:S(2)}) %collective-permute-start.4) | collective-permute-done | bytes 524320 | tf_op jit(solution)/shard_map/ppermute | solution.py:227
  54.7 10.4 %collective-permute-done.5 = f32[2,1,1,256,256]{3,4,2,1,0:T(8,128)} collective-permute-done((f32[2,1,1,256,256]{3,4,2,1,0:T(8,128)}, f32[2,1,1,256,256]{3,4,2,1,0:T(8,128)}, u32[]{:S(2)}, u32[]{:S(2)}) %collective-permute-start.5) | collective-permute-done | bytes 524320 | tf_op jit(solution)/shard_map/ppermute | solution.py:227
  65.2 1.6 %select_select_fusion = (f32[2,1,1,256,256]{3,4,2,1,0:T(8,128)S(1)}, f32[2,1,1,256,256]{3,4,2,1,0:T(8,128)S(1)}, f32[2,1,1,256,256]{3,4,2,1,0:T(8,128)S(1)}, f32[2,1,1,256,256]{3,4,2,1,0:T(8,128)S(1)}) fusion(f32[2,1,1,256,256]{3,4,2,1,0:T(8,128)} %collective-permute-done.5, f32[2,1,1,256,256]{3,4,2,1,0:T(8,128)} %collective-permute-done.6, ...), kind=kLoop, calls=%fused_computation.105 | loop fusion | flops 1572864 | bytes 4194320 | tf_op jit(solution)/shard_map/select_n | solution.py:233
  70.3 1.1 fusion.22
  74.9 1.9 %fusion.34 = f32[2,256,512]{2,1,0:T(8,128)S(1)} fusion(f32[512,256,1]{1,0,2:T(8,128)S(1)} %bitcast.266, f32[1,256,256]{1,2,0:T(8,128)S(1)} %get-tuple-element.142, f32[1,256,256]{1,2,0:T(8,128)S(1)} %get-tuple-element.141), kind=kOutput, calls=%fused_computation.71 | convolution fusion | flops 805437440 | bytes 2097152 | tf_op jit(solution)/shard_map/bij,kj->bik/dot_general | solution.py:72
  84.9 1.5 %collective-permute-start.7 = (f32[2,1,1,256,256]{3,4,0,2,1:T(8,128)S(1)}, f32[2,1,1,256,256]{3,4,0,2,1:T(8,128)S(1)}, u32[]{:S(2)}, u32[]{:S(2)}) collective-permute-start(f32[2,1,1,256,256]{3,4,0,2,1:T(8,128)S(1)} %get-tuple-element.108), channel_id=1, source_target_pairs={{0,16},{8,24},{16,0},{24,8},{1,17},{9,25},{17,1},{25,9},{2,18},{10... | collective-permute-start | bytes 1572872 | tf_op jit(solution)/shard_map/ppermute | solution.py:251
  87.9 2.2 %collective-permute-start.9 = (f32[2,1,1,256,256]{3,4,1,2,0:T(8,128)S(1)}, f32[2,1,1,256,256]{3,4,1,2,0:T(8,128)S(1)}, u32[]{:S(2)}, u32[]{:S(2)}) collective-permute-start(f32[2,1,1,256,256]{3,4,1,2,0:T(8,128)S(1)} %get-tuple-element.106), channel_id=1, source_target_pairs={{0,24},{8,0},{16,8},{24,16},{1,25},{9,1},{17,9},{25,17},{2,26},{10... | collective-permute-start | bytes 1572872 | tf_op jit(solution)/shard_map/ppermute | solution.py:251
  90.1 19.8 %collective-permute-done.7 = f32[2,1,1,256,256]{3,4,0,2,1:T(8,128)S(1)} collective-permute-done((f32[2,1,1,256,256]{3,4,0,2,1:T(8,128)S(1)}, f32[2,1,1,256,256]{3,4,0,2,1:T(8,128)S(1)}, u32[]{:S(2)}, u32[]{:S(2)}) %collective-permute-start.7) | collective-permute-done | bytes 524320 | tf_op jit(solution)/shard_map/ppermute | solution.py:251
  112.3 1.3 collective-permute-start.10
  113.7 1.3 collective-permute-start.11
  115.2 2.2 %collective-permute-done.11 = f32[2,1,512,128]{2,3,0,1:T(8,128)S(1)} collective-permute-done((f32[2,1,512,128]{2,3,0,1:T(8,128)S(1)}, f32[2,1,512,128]{2,3,0,1:T(8,128)S(1)}, u32[]{:S(2)}, u32[]{:S(2)}) %collective-permute-start.11) | collective-permute-done | bytes 524320 | tf_op jit(solution)/shard_map/ppermute | solution.py:15
  117.7 4.4 %collective-permute-start.12 = (f32[2,1,128,256]{2,3,0,1:T(8,128)S(1)}, f32[2,1,128,256]{2,3,0,1:T(8,128)S(1)}, u32[]{:S(2)}, u32[]{:S(2)}) collective-permute-start(f32[2,1,128,256]{2,3,0,1:T(8,128)S(1)} %get-tuple-element.126), channel_id=1, source_target_pairs={{0,2},{2,4},{4,6},{1,3},{3,5},{5,7},{8,10},{10,12},{12,14},{9,11},... | collective-permute-start | bytes 786440 | tf_op jit(solution)/shard_map/ppermute | solution.py:15
  122.0 1.3 collective-permute-start.13
  123.4 4.5 %collective-permute-done.12 = f32[2,1,128,256]{2,3,0,1:T(8,128)S(1)} collective-permute-done((f32[2,1,128,256]{2,3,0,1:T(8,128)S(1)}, f32[2,1,128,256]{2,3,0,1:T(8,128)S(1)}, u32[]{:S(2)}, u32[]{:S(2)}) %collective-permute-start.12) | collective-permute-done | bytes 262176 | tf_op jit(solution)/shard_map/ppermute | solution.py:15
  127.9 4.1 %collective-permute-done.13 = f32[2,1,128,256]{2,3,0,1:T(8,128)S(1)} collective-permute-done((f32[2,1,128,256]{2,3,0,1:T(8,128)S(1)}, f32[2,1,128,256]{2,3,0,1:T(8,128)S(1)}, u32[]{:S(2)}, u32[]{:S(2)}) %collective-permute-start.13) | collective-permute-done | bytes 262176 | tf_op jit(solution)/shard_map/ppermute | solution.py:15
  (108 shorter events, 34.1 us)
Async XLA Ops:
  2.6 19.1 %collective-permute-start = (f32[2,1,128,256]{3,2,1,0:T(8,128)S(1)}, f32[2,1,128,256]{3,2,1,0:T(8,128)S(1)}, u32[]{:S(2)}, u32[]{:S(2)}) collective-permute-start(f32[2,1,128,256]{3,2,1,0:T(8,128)S(1)} %get-tuple-element.168), channel_id=1, source_target_pairs={{0,2},{2,4},{4,6},{1,3},{3,5},{5,7},{8,10},{10,12},{12,14},{9,11},... | collective-permute-start | bytes 786440 | tf_op jit(solution)/shard_map/ppermute | solution.py:28
  7.6 14.2 %collective-permute-start.1 = (f32[2,1,128,256]{3,2,1,0:T(8,128)S(1)}, f32[2,1,128,256]{3,2,1,0:T(8,128)S(1)}, u32[]{:S(2)}, u32[]{:S(2)}) collective-permute-start(f32[2,1,128,256]{3,2,1,0:T(8,128)S(1)} %get-tuple-element.169), channel_id=1, source_target_pairs={{2,0},{4,2},{6,4},{3,1},{5,3},{7,5},{10,8},{12,10},{14,12},{11,9},... | collective-permute-start | bytes 786440 | tf_op jit(solution)/shard_map/ppermute | solution.py:31
  9.5 3.6 %copy-start.8 = (f32[2,256,256]{2,1,0:T(8,128)S(1)}, f32[2,256,256]{2,1,0:T(8,128)}, u32[]{:S(2)}) copy-start(f32[2,256,256]{2,1,0:T(8,128)} %param.15) | copy-start | bytes 1572868
  10.9 2.9 %copy-start.9 = (s32[1,1,4,2]{2,3,1,0:T(2,128)S(1)}, s32[1,1,4,2]{2,3,1,0:T(2,128)}, u32[]{:S(2)}) copy-start(s32[1,1,4,2]{2,3,1,0:T(2,128)} %param.17) | copy-start | bytes 100
  22.9 7.0 %collective-permute-start.2 = (f32[2,1,512,128]{3,2,1,0:T(8,128)}, f32[2,1,512,128]{3,2,1,0:T(8,128)S(1)}, u32[]{:S(2)}, u32[]{:S(2)}) collective-permute-start(f32[2,1,512,128]{3,2,1,0:T(8,128)} %get-tuple-element.151), channel_id=1, source_target_pairs={{0,1},{2,3},{4,5},{6,7},{8,9},{10,11},{12,13},{14,15},{16,17},{18,... | collective-permute-start | bytes 1572872 | tf_op jit(solution)/shard_map/ppermute | solution.py:28
  27.6 4.0 %collective-permute-start.3 = (f32[2,1,512,128]{3,2,1,0:T(8,128)}, f32[2,1,512,128]{3,2,1,0:T(8,128)S(1)}, u32[]{:S(2)}, u32[]{:S(2)}) collective-permute-start(f32[2,1,512,128]{3,2,1,0:T(8,128)} %get-tuple-element.152), channel_id=1, source_target_pairs={{1,0},{3,2},{5,4},{7,6},{9,8},{11,10},{13,12},{15,14},{17,16},{19,... | collective-permute-start | bytes 1572872 | tf_op jit(solution)/shard_map/ppermute | solution.py:31
  29.0 2.9 %copy-start = (f32[2,256,256]{2,1,0:T(8,128)}, f32[2,256,256]{2,1,0:T(8,128)S(1)}, u32[]{:S(2)}) copy-start(f32[2,256,256]{2,1,0:T(8,128)S(1)} %maximum_multiply_fusion.1) | copy-start | bytes 1572868
  37.4 5.7 %copy-start.6 = (f32[1,256,256]{1,2,0:T(8,128)S(1)}, f32[1,256,256]{1,2,0:T(8,128)}, u32[]{:S(2)}) copy-start(f32[1,256,256]{1,2,0:T(8,128)} %get-tuple-element.160) | copy-start | bytes 786436
  37.4 5.7 %copy-start.7 = (f32[1,256,256]{1,2,0:T(8,128)S(1)}, f32[1,256,256]{1,2,0:T(8,128)}, u32[]{:S(2)}) copy-start(f32[1,256,256]{1,2,0:T(8,128)} %get-tuple-element.161) | copy-start | bytes 786436
  37.4 5.8 %copy-start.3 = (f32[1,256,256]{2,1,0:T(8,128)S(1)}, f32[1,256,256]{2,1,0:T(8,128)}, u32[]{:S(2)}) copy-start(f32[1,256,256]{2,1,0:T(8,128)} %get-tuple-element.163) | copy-start | bytes 786436
  38.7 16.0 %collective-permute-start.4 = (f32[2,1,1,256,256]{3,4,2,1,0:T(8,128)}, f32[2,1,1,256,256]{3,4,2,1,0:T(8,128)}, u32[]{:S(2)}, u32[]{:S(2)}) collective-permute-start(f32[2,1,1,256,256]{3,4,2,1,0:T(8,128)} %get-tuple-element.110), channel_id=1, source_target_pairs={{0,8},{8,16},{16,24},{24,0},{1,9},{9,17},{17,25},{25,1},{2,10},{10... | collective-permute-start | bytes 1572872 | tf_op jit(solution)/shard_map/ppermute | solution.py:227
  40.2 24.9 %collective-permute-start.5 = (f32[2,1,1,256,256]{3,4,2,1,0:T(8,128)}, f32[2,1,1,256,256]{3,4,2,1,0:T(8,128)}, u32[]{:S(2)}, u32[]{:S(2)}) collective-permute-start(f32[2,1,1,256,256]{3,4,2,1,0:T(8,128)} %get-tuple-element.112), channel_id=1, source_target_pairs={{0,16},{8,24},{16,0},{24,8},{1,17},{9,25},{17,1},{25,9},{2,18},{10... | collective-permute-start | bytes 1572872 | tf_op jit(solution)/shard_map/ppermute | solution.py:227
  41.7 23.5 %collective-permute-start.6 = (f32[2,1,1,256,256]{3,4,2,1,0:T(8,128)}, f32[2,1,1,256,256]{3,4,2,1,0:T(8,128)}, u32[]{:S(2)}, u32[]{:S(2)}) collective-permute-start(f32[2,1,1,256,256]{3,4,2,1,0:T(8,128)} %get-tuple-element.111), channel_id=1, source_target_pairs={{0,24},{8,0},{16,8},{24,16},{1,25},{9,1},{17,9},{25,17},{2,26},{10... | collective-permute-start | bytes 1572872 | tf_op jit(solution)/shard_map/ppermute | solution.py:227
  49.1 17.7 %copy-start.4 = (f32[1,256,256]{1,2,0:T(8,128)S(1)}, f32[1,256,256]{1,2,0:T(8,128)}, u32[]{:S(2)}) copy-start(f32[1,256,256]{1,2,0:T(8,128)} %copy.128) | copy-start | bytes 786436
  49.1 17.7 %copy-start.5 = (f32[1,256,256]{1,2,0:T(8,128)S(1)}, f32[1,256,256]{1,2,0:T(8,128)}, u32[]{:S(2)}) copy-start(f32[1,256,256]{1,2,0:T(8,128)} %copy.129) | copy-start | bytes 786436
  72.6 1.2 copy-start.1
  74.9 3.0 %copy-start.2 = (f32[2,256,256]{2,1,0:T(8,128)S(1)}, f32[2,256,256]{2,1,0:T(8,128)}, u32[]{:S(2)}) copy-start(f32[2,256,256]{2,1,0:T(8,128)} %copy.82) | copy-start | bytes 1572868
  84.9 25.0 %collective-permute-start.7 = (f32[2,1,1,256,256]{3,4,0,2,1:T(8,128)S(1)}, f32[2,1,1,256,256]{3,4,0,2,1:T(8,128)S(1)}, u32[]{:S(2)}, u32[]{:S(2)}) collective-permute-start(f32[2,1,1,256,256]{3,4,0,2,1:T(8,128)S(1)} %get-tuple-element.108), channel_id=1, source_target_pairs={{0,16},{8,24},{16,0},{24,8},{1,17},{9,25},{17,1},{25,9},{2,18},{10... | collective-permute-start | bytes 1572872 | tf_op jit(solution)/shard_map/ppermute | solution.py:251
  86.4 24.3 %collective-permute-start.8 = (f32[2,1,1,256,256]{3,4,0,2,1:T(8,128)S(1)}, f32[2,1,1,256,256]{3,4,0,2,1:T(8,128)S(1)}, u32[]{:S(2)}, u32[]{:S(2)}) collective-permute-start(f32[2,1,1,256,256]{3,4,0,2,1:T(8,128)S(1)} %get-tuple-element.109), channel_id=1, source_target_pairs={{0,8},{8,16},{16,24},{24,0},{1,9},{9,17},{17,25},{25,1},{2,10},{10... | collective-permute-start | bytes 1572872 | tf_op jit(solution)/shard_map/ppermute | solution.py:251
  87.9 23.6 %collective-permute-start.9 = (f32[2,1,1,256,256]{3,4,1,2,0:T(8,128)S(1)}, f32[2,1,1,256,256]{3,4,1,2,0:T(8,128)S(1)}, u32[]{:S(2)}, u32[]{:S(2)}) collective-permute-start(f32[2,1,1,256,256]{3,4,1,2,0:T(8,128)S(1)} %get-tuple-element.106), channel_id=1, source_target_pairs={{0,24},{8,0},{16,8},{24,16},{1,25},{9,1},{17,9},{25,17},{2,26},{10... | collective-permute-start | bytes 1572872 | tf_op jit(solution)/shard_map/ppermute | solution.py:251
  112.3 2.8 %collective-permute-start.10 = (f32[2,1,512,128]{2,3,0,1:T(8,128)S(1)}, f32[2,1,512,128]{2,3,0,1:T(8,128)S(1)}, u32[]{:S(2)}, u32[]{:S(2)}) collective-permute-start(f32[2,1,512,128]{2,3,0,1:T(8,128)S(1)} %get-tuple-element.105), channel_id=1, source_target_pairs={{0,1},{2,3},{4,5},{6,7},{8,9},{10,11},{12,13},{14,15},{16,17},{18,... | collective-permute-start | bytes 1572872 | tf_op jit(solution)/shard_map/ppermute | solution.py:15
  113.7 3.8 %collective-permute-start.11 = (f32[2,1,512,128]{2,3,0,1:T(8,128)S(1)}, f32[2,1,512,128]{2,3,0,1:T(8,128)S(1)}, u32[]{:S(2)}, u32[]{:S(2)}) collective-permute-start(f32[2,1,512,128]{2,3,0,1:T(8,128)S(1)} %get-tuple-element.104), channel_id=1, source_target_pairs={{1,0},{3,2},{5,4},{7,6},{9,8},{11,10},{13,12},{15,14},{17,16},{19,... | collective-permute-start | bytes 1572872 | tf_op jit(solution)/shard_map/ppermute | solution.py:15
  117.7 10.2 %collective-permute-start.12 = (f32[2,1,128,256]{2,3,0,1:T(8,128)S(1)}, f32[2,1,128,256]{2,3,0,1:T(8,128)S(1)}, u32[]{:S(2)}, u32[]{:S(2)}) collective-permute-start(f32[2,1,128,256]{2,3,0,1:T(8,128)S(1)} %get-tuple-element.126), channel_id=1, source_target_pairs={{0,2},{2,4},{4,6},{1,3},{3,5},{5,7},{8,10},{10,12},{12,14},{9,11},... | collective-permute-start | bytes 786440 | tf_op jit(solution)/shard_map/ppermute | solution.py:15
  122.0 10.0 %collective-permute-start.13 = (f32[2,1,128,256]{2,3,0,1:T(8,128)S(1)}, f32[2,1,128,256]{2,3,0,1:T(8,128)S(1)}, u32[]{:S(2)}, u32[]{:S(2)}) collective-permute-start(f32[2,1,128,256]{2,3,0,1:T(8,128)S(1)} %get-tuple-element.125), channel_id=1, source_target_pairs={{2,0},{4,2},{6,4},{3,1},{5,3},{7,5},{10,8},{12,10},{14,12},{11,9},... | collective-permute-start | bytes 786440 | tf_op jit(solution)/shard_map/ppermute | solution.py:15

commit v10 on v8

--- a/solution.py
+++ b/solution.py
@@ -100,7 +100,7 @@
             (trans_re * wave[0] - trans_im * wave[1], trans_re * wave[1] + trans_im * wave[0])
         )
         moved_list.append(moved)
-        wave = propagate(matrices[layer], moved, exact_mode)
+        wave = propagate(matrices[layer], moved, exact_mode if layer == slab.shape[1] - 1 else wave_mode)
     return (wave, jnp.stack(moved_list, axis=1))
 
 

time: 124 us -> 122 us (0.984)
  matrix products: 20.6 us -> 18 us
    dot_general x8, matrix products: 7.44 us -> 6.12 us  [right_product(): jnp.einsum('bij,kj->bik', waves, matrix, precision=mode, preferred_elemen...]
    dot_general x8, matrix products: 7.31 us -> 6.07 us  [left_product(): jnp.einsum('ij,bjk->bik', matrix, waves, precision=mode, preferred_elemen...]
where the time goes in v10:
time: 122 us; the launch traced here: 121 us
  waiting for transfers between devices  45.8 us (38%)
  starting transfers between devices  24.7 us (20%)
  matrix products  18 us (15%)
  other arithmetic  13.4 us (11%)
  local copies, waits for them, and re-layouts  12.4 us (10%)
  between operations  7.12 us (6%)
    ppermute x3, waiting for transfers between devices, per_device(): chunk = lax.ppermute(chunk, 'depth', pairs)  19 us
    all_to_all x1, waiting for transfers between devices, per_device(): gathered = lax.all_to_all(cut, 'depth', 2, 1, tiled=True)  12.7 us
    ppermute x4, waiting for transfers between devices, from_behind(): lax.ppermute(value, axis, [(source, source + steps) for source in range(l...  10.9 us
    ppermute x4, starting transfers between devices, from_behind(): lax.ppermute(value, axis, [(source, source + steps) for source in range(l...  7.38 us
    ppermute x2, starting transfers between devices, with_halo(): lax.ppermute(lax.slice_in_dim(block, block.shape[dim] - width, None, axis...  6.25 us
    dot_general x8, matrix products, right_product(): jnp.einsum('bij,kj->bik', waves, matrix, precision=mode, preferred_elemen...  6.12 us
    dot_general x8, matrix products, left_product(): jnp.einsum('ij,bjk->bik', matrix, waves, precision=mode, preferred_elemen...  6.07 us
    dot_general x4, matrix products, matmul_exact(): jnp.dot(first, second, precision=exact_mode, preferred_element_type=jnp.f...  5.8 us
  transfers between devices with their start and end apart: 12, of which 8 were waited for; matrix products, arithmetic and copies ran while one was open for 15% of the time, Pallas kernels for 0%

profile of v10, /device:TPU:0, one launch (start us, length us, event | category | flops | bytes accessed | tf_op | source)
XLA Modules:
  0.0 121.4 jit_solution(11266057421490252960)
XLA Ops:
  0.6 2.0 %multiply_bitcast_fusion = (f32[1,1,256,256]{3,2,1,0:T(8,128)S(1)}, f32[1,1,256,256]{3,2,1,0:T(8,128)S(1)}) fusion(f32[1,256,256]{2,1,0:T(8,128)} %param.13, f32[1,256,256]{2,1,0:T(8,128)} %param.14), kind=kLoop, calls=%fused_computation.211 | loop fusion | flops 196608 | bytes 1048576 | tf_op jit(solution)/shard_map/stack | solution.py:160
  2.7 4.9 %collective-permute-start = (f32[2,1,128,256]{3,2,1,0:T(8,128)S(1)}, f32[2,1,128,256]{3,2,1,0:T(8,128)S(1)}, u32[]{:S(2)}, u32[]{:S(2)}) collective-permute-start(f32[2,1,128,256]{3,2,1,0:T(8,128)S(1)} %get-tuple-element.163), channel_id=1, source_target_pairs={{0,2},{2,4},{4,6},{1,3},{3,5},{5,7},{8,10},{10,12},{12,14},{9,11},... | collective-permute-start | bytes 786440 | tf_op jit(solution)/shard_map/ppermute | solution.py:28
  7.6 1.3 %collective-permute-start.1 = (f32[2,1,128,256]{3,2,1,0:T(8,128)S(1)}, f32[2,1,128,256]{3,2,1,0:T(8,128)S(1)}, u32[]{:S(2)}, u32[]{:S(2)}) collective-permute-start(f32[2,1,128,256]{3,2,1,0:T(8,128)S(1)} %get-tuple-element.164), channel_id=1, source_target_pairs={{2,0},{4,2},{6,4},{3,1},{5,3},{7,5},{10,8},{12,10},{14,12},{11,9},... | collective-permute-start | bytes 786440 | tf_op jit(solution)/shard_map/ppermute | solution.py:31
  15.9 1.3 %collective-permute-done.1 = f32[2,1,128,256]{3,2,1,0:T(8,128)S(1)} collective-permute-done((f32[2,1,128,256]{3,2,1,0:T(8,128)S(1)}, f32[2,1,128,256]{3,2,1,0:T(8,128)S(1)}, u32[]{:S(2)}, u32[]{:S(2)}) %collective-permute-start.1) | collective-permute-done | bytes 262176 | tf_op jit(solution)/shard_map/ppermute | solution.py:31
  17.4 1.1 fusion.144
  18.5 1.3 %collective-permute-start.2 = (f32[2,1,512,128]{3,2,1,0:T(8,128)}, f32[2,1,512,128]{3,2,1,0:T(8,128)S(1)}, u32[]{:S(2)}, u32[]{:S(2)}) collective-permute-start(f32[2,1,512,128]{3,2,1,0:T(8,128)} %get-tuple-element.146), channel_id=1, source_target_pairs={{0,1},{2,3},{4,5},{6,7},{8,9},{10,11},{12,13},{14,15},{16,17},{18,... | collective-permute-start | bytes 1572872 | tf_op jit(solution)/shard_map/ppermute | solution.py:28
  19.8 1.0 sine_negate_fusion
  20.8 1.3 %collective-permute-start.3 = (f32[2,1,512,128]{3,2,1,0:T(8,128)}, f32[2,1,512,128]{3,2,1,0:T(8,128)S(1)}, u32[]{:S(2)}, u32[]{:S(2)}) collective-permute-start(f32[2,1,512,128]{3,2,1,0:T(8,128)} %get-tuple-element.147), channel_id=1, source_target_pairs={{1,0},{3,2},{5,4},{7,6},{9,8},{11,10},{13,12},{15,14},{17,16},{19,... | collective-permute-start | bytes 1572872 | tf_op jit(solution)/shard_map/ppermute | solution.py:31
  23.1 1.8 %collective-permute-done.3 = f32[2,1,512,128]{3,2,1,0:T(8,128)S(1)} collective-permute-done((f32[2,1,512,128]{3,2,1,0:T(8,128)}, f32[2,1,512,128]{3,2,1,0:T(8,128)S(1)}, u32[]{:S(2)}, u32[]{:S(2)}) %collective-permute-start.3) | collective-permute-done | bytes 524320 | tf_op jit(solution)/shard_map/ppermute | solution.py:31
  26.6 1.6 %pad_maximum_fusion = f32[2,1,4,256,256]{3,4,0,1,2:T(8,128)} fusion(f32[2,1,1,256,256]{3,4,0,1,2:T(8,128)S(1)} %bitcast.290, f32[2,1,1,256,256]{3,4,0,1,2:T(8,128)S(1)} %bitcast.289, f32[2,1,1,256,256]{3,4,0,1,2:T(8,128)S(1)} %bitcast.288, f32[2,1,1,256,256]{3,4,0,1,2:T(8,128)S(1)} %bitcast.287), kind=kLoop, calls=%fused_computation.16 | loop fusion | flops 1572864 | bytes 4194304 | tf_op jit(solution)/shard_map/stack | solution.py:211
  28.2 3.9 %all-to-all-start = ((f32[2,1,4,256,256]{3,4,0,1,2:T(8,128)}), f32[2,1,4,256,256]{3,4,0,1,2:T(8,128)S(1)}, u32[]{:S(2)}, u32[]{:S(2)}) async-start(f32[2,1,4,256,256]{3,4,0,1,2:T(8,128)} %pad_maximum_fusion), calls=%async_computation | async-start | bytes 4194304 | tf_op jit(solution)/shard_map/all_to_all | solution.py:220
  35.6 1.0 copy.136
  36.6 1.4 %fusion.78 = f32[256,256]{1,0:T(8,128)S(1)} fusion(f32[256]{0:T(256)S(1)} %get-tuple-element.185, f32[256]{0:T(256)S(1)} %get-tuple-element.186), kind=kOutput, calls=%fused_computation.204 | convolution fusion | flops 203358208 | bytes 264192 | tf_op jit(solution)/shard_map/dot_general | solution.py:39
  38.1 1.5 %fusion.3 = f32[1,256,256]{2,1,0:T(8,128)S(1)} fusion(f32[256,256]{1,0:T(8,128)S(1)} %fusion.78, f32[256]{0:T(256)S(1)} %get-tuple-element.185, f32[256]{0:T(256)S(1)} %get-tuple-element.186), kind=kOutput, calls=%fused_computation.27 | convolution fusion | flops 203423744 | bytes 526336 | tf_op jit(solution)/shard_map/dot_general | solution.py:39
  39.5 1.4 %fusion.79 = f32[256,256]{1,0:T(8,128)S(1)} fusion(f32[256]{0:T(256)S(1)} %get-tuple-element.185, f32[256]{0:T(256)S(1)} %get-tuple-element.186), kind=kOutput, calls=%fused_computation.206 | convolution fusion | flops 203358208 | bytes 264192 | tf_op jit(solution)/shard_map/dot_general | solution.py:39
  41.0 1.5 %fusion.4 = f32[1,256,256]{2,1,0:T(8,128)S(1)} fusion(f32[256,256]{1,0:T(8,128)S(1)} %fusion.79, f32[256]{0:T(256)S(1)} %get-tuple-element.185, f32[256]{0:T(256)S(1)} %get-tuple-element.186), kind=kOutput, calls=%fused_computation.29 | convolution fusion | flops 203423744 | bytes 526336 | tf_op jit(solution)/shard_map/dot_general | solution.py:39
  43.4 1.2 %copy.143 = f32[2,256,256]{2,1,0:T(8,128)S(1)} copy(f32[2,256,256]{1,2,0:T(8,128)} %pad_maximum_fusion.2) | data formatting | bytes 1048576 | tf_op jit(solution)/shard_map/stack | solution.py:62
  44.6 12.7 %all-to-all-done = f32[2,1,4,256,256]{3,4,0,1,2:T(8,128)S(1)} async-done(((f32[2,1,4,256,256]{3,4,0,1,2:T(8,128)}), f32[2,1,4,256,256]{3,4,0,1,2:T(8,128)S(1)}, u32[]{:S(2)}, u32[]{:S(2)}) %all-to-all-start) | async-done | bytes 2097184 | tf_op jit(solution)/shard_map/all_to_all | solution.py:220
  63.0 1.3 %convolution_bitcast_fusion.4 = f32[2,512,256]{1,2,0:T(8,128)S(1)} fusion(f32[512,256,1]{1,0,2:T(8,128)S(1)} %bitcast.275, f32[1,1,256,256]{2,3,1,0:T(8,128)S(1)} %bitcast.284, f32[1,1,256,256]{2,3,1,0:T(8,128)S(1)} %bitcast.283), kind=kOutput, calls=%fused_computation.22 | convolution fusion | flops 805437440 | bytes 2097152 | tf_op jit(solution)/shard_map/ij,bjk->bik/dot_general | solution.py:66
  64.4 1.9 %fusion.34 = f32[2,256,512]{2,1,0:T(8,128)S(1)} fusion(f32[512,256,1]{1,0,2:T(8,128)S(1)} %bitcast.276, f32[1,256,256]{1,2,0:T(8,128)S(1)} %get-tuple-element.139, f32[1,256,256]{1,2,0:T(8,128)S(1)} %get-tuple-element.138), kind=kOutput, calls=%fused_computation.72 | convolution fusion | flops 805437440 | bytes 2097152 | tf_op jit(solution)/shard_map/bij,kj->bik/dot_general | solution.py:72
  66.3 1.0 fusion.74
  67.3 1.1 convolution_bitcast_fusion.3
  74.1 1.5 %collective-permute-start.4 = (f32[2,1,1,256,256]{3,4,0,2,1:T(8,128)S(1)}, f32[2,1,1,256,256]{3,4,0,2,1:T(8,128)S(1)}, u32[]{:S(2)}, u32[]{:S(2)}) collective-permute-start(f32[2,1,1,256,256]{3,4,0,2,1:T(8,128)S(1)} %get-tuple-element.120), channel_id=1, source_target_pairs={{0,16},{8,24},{16,0},{24,8},{1,17},{9,25},{17,1},{25,9},{2,18},{10... | collective-permute-start | bytes 1572872 | tf_op jit(solution)/shard_map/ppermute | solution.py:239
  76.9 2.5 %collective-permute-start.6 = (f32[2,1,1,256,256]{3,4,1,2,0:T(8,128)S(1)}, f32[2,1,1,256,256]{3,4,1,2,0:T(8,128)S(1)}, u32[]{:S(2)}, u32[]{:S(2)}) collective-permute-start(f32[2,1,1,256,256]{3,4,1,2,0:T(8,128)S(1)} %get-tuple-element.118), channel_id=1, source_target_pairs={{0,24},{8,0},{16,8},{24,16},{1,25},{9,1},{17,9},{25,17},{2,26},{10... | collective-permute-start | bytes 1572872 | tf_op jit(solution)/shard_map/ppermute | solution.py:239
  79.4 19.0 %collective-permute-done.4 = f32[2,1,1,256,256]{3,4,0,2,1:T(8,128)S(1)} collective-permute-done((f32[2,1,1,256,256]{3,4,0,2,1:T(8,128)S(1)}, f32[2,1,1,256,256]{3,4,0,2,1:T(8,128)S(1)}, u32[]{:S(2)}, u32[]{:S(2)}) %collective-permute-start.4) | collective-permute-done | bytes 524320 | tf_op jit(solution)/shard_map/ppermute | solution.py:239
  100.8 1.3 %collective-permute-start.7 = (f32[2,1,512,128]{2,3,0,1:T(8,128)S(1)}, f32[2,1,512,128]{2,3,0,1:T(8,128)S(1)}, u32[]{:S(2)}, u32[]{:S(2)}) collective-permute-start(f32[2,1,512,128]{2,3,0,1:T(8,128)S(1)} %get-tuple-element.117), channel_id=1, source_target_pairs={{0,1},{2,3},{4,5},{6,7},{8,9},{10,11},{12,13},{14,15},{16,17},{18,... | collective-permute-start | bytes 1572872 | tf_op jit(solution)/shard_map/ppermute | solution.py:15
  102.1 1.3 %collective-permute-start.8 = (f32[2,1,512,128]{2,3,0,1:T(8,128)S(1)}, f32[2,1,512,128]{2,3,0,1:T(8,128)S(1)}, u32[]{:S(2)}, u32[]{:S(2)}) collective-permute-start(f32[2,1,512,128]{2,3,0,1:T(8,128)S(1)} %get-tuple-element.116), channel_id=1, source_target_pairs={{1,0},{3,2},{5,4},{7,6},{9,8},{11,10},{13,12},{15,14},{17,16},{19,... | collective-permute-start | bytes 1572872 | tf_op jit(solution)/shard_map/ppermute | solution.py:15
  103.7 2.2 %collective-permute-done.8 = f32[2,1,512,128]{2,3,0,1:T(8,128)S(1)} collective-permute-done((f32[2,1,512,128]{2,3,0,1:T(8,128)S(1)}, f32[2,1,512,128]{2,3,0,1:T(8,128)S(1)}, u32[]{:S(2)}, u32[]{:S(2)}) %collective-permute-start.8) | collective-permute-done | bytes 524320 | tf_op jit(solution)/shard_map/ppermute | solution.py:15
  106.1 3.5 %collective-permute-start.9 = (f32[2,1,128,256]{2,3,0,1:T(8,128)S(1)}, f32[2,1,128,256]{2,3,0,1:T(8,128)S(1)}, u32[]{:S(2)}, u32[]{:S(2)}) collective-permute-start(f32[2,1,128,256]{2,3,0,1:T(8,128)S(1)} %get-tuple-element.129), channel_id=1, source_target_pairs={{0,2},{2,4},{4,6},{1,3},{3,5},{5,7},{8,10},{10,12},{12,14},{9,11},... | collective-permute-start | bytes 786440 | tf_op jit(solution)/shard_map/ppermute | solution.py:15
  109.6 1.3 %collective-permute-start.10 = (f32[2,1,128,256]{2,3,0,1:T(8,128)S(1)}, f32[2,1,128,256]{2,3,0,1:T(8,128)S(1)}, u32[]{:S(2)}, u32[]{:S(2)}) collective-permute-start(f32[2,1,128,256]{2,3,0,1:T(8,128)S(1)} %get-tuple-element.128), channel_id=1, source_target_pairs={{2,0},{4,2},{6,4},{3,1},{5,3},{7,5},{10,8},{12,10},{14,12},{11,9},... | collective-permute-start | bytes 786440 | tf_op jit(solution)/shard_map/ppermute | solution.py:15
  111.0 4.5 %collective-permute-done.9 = f32[2,1,128,256]{2,3,0,1:T(8,128)S(1)} collective-permute-done((f32[2,1,128,256]{2,3,0,1:T(8,128)S(1)}, f32[2,1,128,256]{2,3,0,1:T(8,128)S(1)}, u32[]{:S(2)}, u32[]{:S(2)}) %collective-permute-start.9) | collective-permute-done | bytes 262176 | tf_op jit(solution)/shard_map/ppermute | solution.py:15
  115.5 4.1 %collective-permute-done.10 = f32[2,1,128,256]{2,3,0,1:T(8,128)S(1)} collective-permute-done((f32[2,1,128,256]{2,3,0,1:T(8,128)S(1)}, f32[2,1,128,256]{2,3,0,1:T(8,128)S(1)}, u32[]{:S(2)}, u32[]{:S(2)}) %collective-permute-start.10) | collective-permute-done | bytes 262176 | tf_op jit(solution)/shard_map/ppermute | solution.py:15
  (99 shorter events, 25.5 us)
Async XLA Ops:
  0.6 9.5 %copy-start.7 = (s32[1,1,4,2]{2,3,1,0:T(2,128)S(1)}, s32[1,1,4,2]{2,3,1,0:T(2,128)}, u32[]{:S(2)}) copy-start(s32[1,1,4,2]{2,3,1,0:T(2,128)} %param.17) | copy-start | bytes 100
  2.7 13.3 %collective-permute-start = (f32[2,1,128,256]{3,2,1,0:T(8,128)S(1)}, f32[2,1,128,256]{3,2,1,0:T(8,128)S(1)}, u32[]{:S(2)}, u32[]{:S(2)}) collective-permute-start(f32[2,1,128,256]{3,2,1,0:T(8,128)S(1)} %get-tuple-element.163), channel_id=1, source_target_pairs={{0,2},{2,4},{4,6},{1,3},{3,5},{5,7},{8,10},{10,12},{12,14},{9,11},... | collective-permute-start | bytes 786440 | tf_op jit(solution)/shard_map/ppermute | solution.py:28
  7.6 9.7 %collective-permute-start.1 = (f32[2,1,128,256]{3,2,1,0:T(8,128)S(1)}, f32[2,1,128,256]{3,2,1,0:T(8,128)S(1)}, u32[]{:S(2)}, u32[]{:S(2)}) collective-permute-start(f32[2,1,128,256]{3,2,1,0:T(8,128)S(1)} %get-tuple-element.164), channel_id=1, source_target_pairs={{2,0},{4,2},{6,4},{3,1},{5,3},{7,5},{10,8},{12,10},{14,12},{11,9},... | collective-permute-start | bytes 786440 | tf_op jit(solution)/shard_map/ppermute | solution.py:31
  17.4 4.8 %copy-start.6 = (f32[2,256,256]{2,1,0:T(8,128)S(1)}, f32[2,256,256]{2,1,0:T(8,128)}, u32[]{:S(2)}) copy-start(f32[2,256,256]{2,1,0:T(8,128)} %param.15) | copy-start | bytes 1572868
  18.5 4.5 %collective-permute-start.2 = (f32[2,1,512,128]{3,2,1,0:T(8,128)}, f32[2,1,512,128]{3,2,1,0:T(8,128)S(1)}, u32[]{:S(2)}, u32[]{:S(2)}) collective-permute-start(f32[2,1,512,128]{3,2,1,0:T(8,128)} %get-tuple-element.146), channel_id=1, source_target_pairs={{0,1},{2,3},{4,5},{6,7},{8,9},{10,11},{12,13},{14,15},{16,17},{18,... | collective-permute-start | bytes 1572872 | tf_op jit(solution)/shard_map/ppermute | solution.py:28
  20.8 4.0 %collective-permute-start.3 = (f32[2,1,512,128]{3,2,1,0:T(8,128)}, f32[2,1,512,128]{3,2,1,0:T(8,128)S(1)}, u32[]{:S(2)}, u32[]{:S(2)}) collective-permute-start(f32[2,1,512,128]{3,2,1,0:T(8,128)} %get-tuple-element.147), channel_id=1, source_target_pairs={{1,0},{3,2},{5,4},{7,6},{9,8},{11,10},{13,12},{15,14},{17,16},{19,... | collective-permute-start | bytes 1572872 | tf_op jit(solution)/shard_map/ppermute | solution.py:31
  22.2 9.9 %copy-start = (f32[2,256,256]{2,1,0:T(8,128)}, f32[2,256,256]{2,1,0:T(8,128)S(1)}, u32[]{:S(2)}) copy-start(f32[2,256,256]{2,1,0:T(8,128)S(1)} %maximum_multiply_fusion.1) | copy-start | bytes 1572868
  28.2 4.7 %copy-start.3 = (f32[1,256,256]{2,1,0:T(8,128)S(1)}, f32[1,256,256]{2,1,0:T(8,128)}, u32[]{:S(2)}) copy-start(f32[1,256,256]{2,1,0:T(8,128)} %get-tuple-element.158) | copy-start | bytes 786436
  28.2 29.2 %all-to-all-start = ((f32[2,1,4,256,256]{3,4,0,1,2:T(8,128)}), f32[2,1,4,256,256]{3,4,0,1,2:T(8,128)S(1)}, u32[]{:S(2)}, u32[]{:S(2)}) async-start(f32[2,1,4,256,256]{3,4,0,1,2:T(8,128)} %pad_maximum_fusion), calls=%async_computation | async-start | bytes 4194304 | tf_op jit(solution)/shard_map/all_to_all | solution.py:220
  44.6 12.9 %copy-start.4 = (f32[1,256,256]{1,2,0:T(8,128)S(1)}, f32[1,256,256]{1,2,0:T(8,128)}, u32[]{:S(2)}) copy-start(f32[1,256,256]{1,2,0:T(8,128)} %copy.182) | copy-start | bytes 786436
  57.4 1.0 copy-start.5
  62.0 1.0 copy-start.1
  64.3 3.0 %copy-start.2 = (f32[2,256,256]{2,1,0:T(8,128)S(1)}, f32[2,256,256]{2,1,0:T(8,128)}, u32[]{:S(2)}) copy-start(f32[2,256,256]{2,1,0:T(8,128)} %copy.136) | copy-start | bytes 1572868
  74.1 24.3 %collective-permute-start.4 = (f32[2,1,1,256,256]{3,4,0,2,1:T(8,128)S(1)}, f32[2,1,1,256,256]{3,4,0,2,1:T(8,128)S(1)}, u32[]{:S(2)}, u32[]{:S(2)}) collective-permute-start(f32[2,1,1,256,256]{3,4,0,2,1:T(8,128)S(1)} %get-tuple-element.120), channel_id=1, source_target_pairs={{0,16},{8,24},{16,0},{24,8},{1,17},{9,25},{17,1},{25,9},{2,18},{10... | collective-permute-start | bytes 1572872 | tf_op jit(solution)/shard_map/ppermute | solution.py:239
  75.7 23.5 %collective-permute-start.5 = (f32[2,1,1,256,256]{3,4,0,2,1:T(8,128)S(1)}, f32[2,1,1,256,256]{3,4,0,2,1:T(8,128)S(1)}, u32[]{:S(2)}, u32[]{:S(2)}) collective-permute-start(f32[2,1,1,256,256]{3,4,0,2,1:T(8,128)S(1)} %get-tuple-element.121), channel_id=1, source_target_pairs={{0,8},{8,16},{16,24},{24,0},{1,9},{9,17},{17,25},{25,1},{2,10},{10... | collective-permute-start | bytes 1572872 | tf_op jit(solution)/shard_map/ppermute | solution.py:239
  76.9 23.0 %collective-permute-start.6 = (f32[2,1,1,256,256]{3,4,1,2,0:T(8,128)S(1)}, f32[2,1,1,256,256]{3,4,1,2,0:T(8,128)S(1)}, u32[]{:S(2)}, u32[]{:S(2)}) collective-permute-start(f32[2,1,1,256,256]{3,4,1,2,0:T(8,128)S(1)} %get-tuple-element.118), channel_id=1, source_target_pairs={{0,24},{8,0},{16,8},{24,16},{1,25},{9,1},{17,9},{25,17},{2,26},{10... | collective-permute-start | bytes 1572872 | tf_op jit(solution)/shard_map/ppermute | solution.py:239
  100.8 2.8 %collective-permute-start.7 = (f32[2,1,512,128]{2,3,0,1:T(8,128)S(1)}, f32[2,1,512,128]{2,3,0,1:T(8,128)S(1)}, u32[]{:S(2)}, u32[]{:S(2)}) collective-permute-start(f32[2,1,512,128]{2,3,0,1:T(8,128)S(1)} %get-tuple-element.117), channel_id=1, source_target_pairs={{0,1},{2,3},{4,5},{6,7},{8,9},{10,11},{12,13},{14,15},{16,17},{18,... | collective-permute-start | bytes 1572872 | tf_op jit(solution)/shard_map/ppermute | solution.py:15
  102.1 3.8 %collective-permute-start.8 = (f32[2,1,512,128]{2,3,0,1:T(8,128)S(1)}, f32[2,1,512,128]{2,3,0,1:T(8,128)S(1)}, u32[]{:S(2)}, u32[]{:S(2)}) collective-permute-start(f32[2,1,512,128]{2,3,0,1:T(8,128)S(1)} %get-tuple-element.116), channel_id=1, source_target_pairs={{1,0},{3,2},{5,4},{7,6},{9,8},{11,10},{13,12},{15,14},{17,16},{19,... | collective-permute-start | bytes 1572872 | tf_op jit(solution)/shard_map/ppermute | solution.py:15
  106.1 9.3 %collective-permute-start.9 = (f32[2,1,128,256]{2,3,0,1:T(8,128)S(1)}, f32[2,1,128,256]{2,3,0,1:T(8,128)S(1)}, u32[]{:S(2)}, u32[]{:S(2)}) collective-permute-start(f32[2,1,128,256]{2,3,0,1:T(8,128)S(1)} %get-tuple-element.129), channel_id=1, source_target_pairs={{0,2},{2,4},{4,6},{1,3},{3,5},{5,7},{8,10},{10,12},{12,14},{9,11},... | collective-permute-start | bytes 786440 | tf_op jit(solution)/shard_map/ppermute | solution.py:15
  109.6 10.0 %collective-permute-start.10 = (f32[2,1,128,256]{2,3,0,1:T(8,128)S(1)}, f32[2,1,128,256]{2,3,0,1:T(8,128)S(1)}, u32[]{:S(2)}, u32[]{:S(2)}) collective-permute-start(f32[2,1,128,256]{2,3,0,1:T(8,128)S(1)} %get-tuple-element.128), channel_id=1, source_target_pairs={{2,0},{4,2},{6,4},{3,1},{5,3},{7,5},{10,8},{12,10},{14,12},{11,9},... | collective-permute-start | bytes 786440 | tf_op jit(solution)/shard_map/ppermute | solution.py:15

commit v11 on v8

--- a/solution.py
+++ b/solution.py
@@ -187,6 +187,15 @@
     col_index = lax.axis_index("col")
     stacked = to_transmit(jnp.stack((phase, absorption)))
     tall_slab = with_halo(stacked, (("row", 2),), rim)
+    col_count = lax.axis_size("col")
+    col_forward = [(i, i + 1) for i in range(col_count - 1)]
+    col_backward = [(target, source) for source, target in col_forward]
+    from_left = outside_filled(
+        lax.ppermute(stacked[:, :, :, tile_cols - rim :], "col", col_forward), col_index == 0
+    )
+    from_right = outside_filled(
+        lax.ppermute(stacked[:, :, :, :rim], "col", col_backward), col_index == col_count - 1
+    )
     after = (stacked[0, 0, 0, 0] * 0.0).astype(jnp.int32)
     corners = offsets[0, 0] + after
     row_starts = corners[:, 0] - row_index * tile_rows + rim
@@ -203,7 +212,25 @@
     row_starts, col_starts, source_rows, source_cols, tall_slab = lax.optimization_barrier(
         (row_starts, col_starts, source_rows, source_cols, tall_slab)
     )
-    extended = with_halo(tall_slab, (("col", 3),), rim)
+    above = tall_slab[:, :, :rim]
+    below = tall_slab[:, :, rim + tile_rows :]
+    corner_left = outside_filled(
+        lax.ppermute(
+            jnp.concatenate((above[:, :, :, tile_cols - rim :], below[:, :, :, tile_cols - rim :]), axis=2),
+            "col",
+            col_forward,
+        ),
+        col_index == 0,
+    )
+    corner_right = outside_filled(
+        lax.ppermute(
+            jnp.concatenate((above[:, :, :, :rim], below[:, :, :, :rim]), axis=2), "col", col_backward
+        ),
+        col_index == col_count - 1,
+    )
+    left_side = jnp.concatenate((corner_left[:, :, :rim], from_left, corner_left[:, :, rim:]), axis=2)
+    right_side = jnp.concatenate((corner_right[:, :, :rim], from_right, corner_right[:, :, rim:]), axis=2)
+    extended = jnp.concatenate((left_side, tall_slab, right_side), axis=3)
     anchor = jnp.zeros((), jnp.int32)
     fresnel, far_field = build_tables(width)
     share = probes // depth_count

time: 124 us -> 132 us (1.065)
  starting transfers between devices: 24.7 us -> 30.1 us
  other arithmetic: 13.4 us -> 17.3 us
    ppermute x0 -> x4, starting transfers between devices: none -> 7.08 us  [the longest x1 3.04 us: per_device(): lax.ppermute(jnp.concatenate((above[:, :, :, tile_cols - rim:], below[:,...]
    ppermute x2 -> x1, waiting for transfers between devices: 3.08 us -> 0.01 us  [with_halo(): lax.ppermute(lax.slice_in_dim(block, 0, width, axis=dim), axis, backward)]
    ppermute x0 -> x4, waiting for transfers between devices: none -> 2.34 us  [the longest x1 2.33 us: per_device(): lax.ppermute(jnp.concatenate((above[:, :, :, :rim], below[:, :, :, :rim])...]
    concatenate x0 -> x3, other arithmetic: none -> 2.19 us  [the longest x1 0.75 us: per_device(): extended = jnp.concatenate((left_side, tall_slab, right_side), axis=3)]
    ppermute x2 -> x1, starting transfers between devices: 6.25 us -> 4.94 us  [with_halo(): lax.ppermute(lax.slice_in_dim(block, block.shape[dim] - width, None, axis...]
    another operation x2 -> x3, other arithmetic: 2 us -> 2.89 us  [to_transmit(): jnp.stack((damping * jnp.cos(extended[0]), damping * jnp.sin(extended[0])))]
  transfers between devices with their start and end apart: 12 -> 14, of which waited for: 8 -> 7; matrix products, arithmetic and copies ran while one was open for 15% -> 16% of each run, Pallas kernels for 0% -> 0%
where the time goes in v11:
time: 132 us; the launch traced here: 131 us
  waiting for transfers between devices  45 us (34%)
  starting transfers between devices  30.1 us (23%)
  matrix products  20.6 us (16%)
  other arithmetic  17.3 us (13%)
  local copies, waits for them, and re-layouts  11.1 us (8%)
  between operations  7.24 us (5%)
    ppermute x3, waiting for transfers between devices, per_device(): chunk = lax.ppermute(chunk, 'depth', pairs)  19 us
    all_to_all x1, waiting for transfers between devices, per_device(): gathered = lax.all_to_all(cut, 'depth', 2, 1, tiled=True)  12.7 us
    ppermute x4, waiting for transfers between devices, from_behind(): lax.ppermute(value, axis, [(source, source + steps) for source in range(l...  10.9 us
    ppermute x4, starting transfers between devices, from_behind(): lax.ppermute(value, axis, [(source, source + steps) for source in range(l...  8.31 us
    dot_general x8, matrix products, right_product(): jnp.einsum('bij,kj->bik', waves, matrix, precision=mode, preferred_elemen...  7.45 us
    dot_general x8, matrix products, left_product(): jnp.einsum('ij,bjk->bik', matrix, waves, precision=mode, preferred_elemen...  7.31 us
    dot_general x4, matrix products, matmul_exact(): jnp.dot(first, second, precision=exact_mode, preferred_element_type=jnp.f...  5.81 us
    ppermute x1, starting transfers between devices, with_halo(): lax.ppermute(lax.slice_in_dim(block, block.shape[dim] - width, None, axis...  4.94 us
  transfers between devices with their start and end apart: 14, of which 7 were waited for; matrix products, arithmetic and copies ran while one was open for 16% of the time, Pallas kernels for 0%

profile of v11, /device:TPU:0, one launch (start us, length us, event | category | flops | bytes accessed | tf_op | source)
XLA Modules:
  0.0 131.2 jit_solution(4580100261703644150)
XLA Ops:
  0.7 2.0 %multiply_bitcast_fusion = (f32[1,1,256,256]{3,2,1,0:T(8,128)S(1)}, f32[1,1,256,256]{3,2,1,0:T(8,128)S(1)}) fusion(f32[1,256,256]{2,1,0:T(8,128)} %param.13, f32[1,256,256]{2,1,0:T(8,128)} %param.14), kind=kLoop, calls=%fused_computation.227 | loop fusion | flops 196608 | bytes 1048576 | tf_op jit(solution)/shard_map/stack | solution.py:160
  2.7 4.9 %collective-permute-start = (f32[2,1,128,256]{3,2,1,0:T(8,128)S(1)}, f32[2,1,128,256]{3,2,1,0:T(8,128)S(1)}, u32[]{:S(2)}, u32[]{:S(2)}) collective-permute-start(f32[2,1,128,256]{3,2,1,0:T(8,128)S(1)} %get-tuple-element.163), channel_id=1, source_target_pairs={{0,2},{2,4},{4,6},{1,3},{3,5},{5,7},{8,10},{10,12},{12,14},{9,11},... | collective-permute-start | bytes 786440 | tf_op jit(solution)/shard_map/ppermute | solution.py:28
  7.7 1.3 collective-permute-start.1
  9.8 1.5 %collective-permute-start.3 = (f32[2,1,256,128]{3,2,1,0:T(8,128)}, f32[2,1,256,128]{3,2,1,0:T(8,128)S(1)}, u32[]{:S(2)}, u32[]{:S(2)}) collective-permute-start(f32[2,1,256,128]{3,2,1,0:T(8,128)} %get-tuple-element.161), channel_id=1, source_target_pairs={{0,1},{2,3},{4,5},{6,7},{8,9},{10,11},{12,13},{14,15},{16,17},{18,... | collective-permute-start | bytes 786440 | tf_op jit(solution)/shard_map/ppermute | solution.py:194
  11.3 1.3 collective-permute-start.5
  14.5 1.0 sine_negate_fusion
  22.5 3.0 %collective-permute-start.2 = (f32[2,1,256,128]{3,2,1,0:T(8,128)}, f32[2,1,256,128]{3,2,1,0:T(8,128)S(1)}, u32[]{:S(2)}, u32[]{:S(2)}) collective-permute-start(f32[2,1,256,128]{3,2,1,0:T(8,128)} %pad_maximum_fusion.4), channel_id=1, source_target_pairs={{0,1},{2,3},{4,5},{6,7},{8,9},{10,11},{12,13},{14,15},{16,17},{18,... | collective-permute-start | bytes 786440 | tf_op jit(solution)/shard_map/ppermute | solution.py:218
  26.2 1.3 collective-permute-start.4
  27.7 2.3 %collective-permute-done.4 = f32[2,1,256,128]{3,2,1,0:T(8,128)} collective-permute-done((f32[2,1,256,128]{3,2,1,0:T(8,128)}, f32[2,1,256,128]{3,2,1,0:T(8,128)}, u32[]{:S(2)}, u32[]{:S(2)}) %collective-permute-start.4) | collective-permute-done | bytes 262176 | tf_op jit(solution)/shard_map/ppermute | solution.py:226
  33.3 1.6 %pad_maximum_fusion = f32[2,1,4,256,256]{3,4,0,1,2:T(8,128)} fusion(f32[2,1,1,256,256]{3,4,0,1,2:T(8,128)S(1)} %bitcast.290, f32[2,1,1,256,256]{3,4,0,1,2:T(8,128)S(1)} %bitcast.289, f32[2,1,1,256,256]{3,4,0,1,2:T(8,128)S(1)} %bitcast.288, f32[2,1,1,256,256]{3,4,0,1,2:T(8,128)S(1)} %bitcast.287), kind=kLoop, calls=%fused_computation.24 | loop fusion | flops 1572864 | bytes 4194304 | tf_op jit(solution)/shard_map/stack | solution.py:238
  34.8 3.9 %all-to-all-start = ((f32[2,1,4,256,256]{3,4,0,1,2:T(8,128)}), f32[2,1,4,256,256]{3,4,0,1,2:T(8,128)S(1)}, u32[]{:S(2)}, u32[]{:S(2)}) async-start(f32[2,1,4,256,256]{3,4,0,1,2:T(8,128)} %pad_maximum_fusion), calls=%async_computation | async-start | bytes 4194304 | tf_op jit(solution)/shard_map/all_to_all | solution.py:247
  43.2 1.5 %fusion.84 = f32[256,256]{1,0:T(8,128)S(1)} fusion(f32[256]{0:T(256)S(1)} %get-tuple-element.193, f32[256]{0:T(256)S(1)} %get-tuple-element.194), kind=kOutput, calls=%fused_computation.220 | convolution fusion | flops 203358208 | bytes 264192 | tf_op jit(solution)/shard_map/dot_general | solution.py:39
  44.7 1.4 %fusion.7 = f32[1,256,256]{2,1,0:T(8,128)S(1)} fusion(f32[256,256]{1,0:T(8,128)S(1)} %fusion.84, f32[256]{0:T(256)S(1)} %get-tuple-element.193, f32[256]{0:T(256)S(1)} %get-tuple-element.194), kind=kOutput, calls=%fused_computation.35 | convolution fusion | flops 203423744 | bytes 526336 | tf_op jit(solution)/shard_map/dot_general | solution.py:39
  46.2 1.5 %fusion.85 = f32[256,256]{1,0:T(8,128)S(1)} fusion(f32[256]{0:T(256)S(1)} %get-tuple-element.193, f32[256]{0:T(256)S(1)} %get-tuple-element.194), kind=kOutput, calls=%fused_computation.222 | convolution fusion | flops 203358208 | bytes 264192 | tf_op jit(solution)/shard_map/dot_general | solution.py:39
  47.6 1.5 %fusion.8 = f32[1,256,256]{2,1,0:T(8,128)S(1)} fusion(f32[256,256]{1,0:T(8,128)S(1)} %fusion.85, f32[256]{0:T(256)S(1)} %get-tuple-element.193, f32[256]{0:T(256)S(1)} %get-tuple-element.194), kind=kOutput, calls=%fused_computation.37 | convolution fusion | flops 203423744 | bytes 526336 | tf_op jit(solution)/shard_map/dot_general | solution.py:39
  50.0 1.2 copy.143
  51.3 12.7 %all-to-all-done = f32[2,1,4,256,256]{3,4,0,1,2:T(8,128)S(1)} async-done(((f32[2,1,4,256,256]{3,4,0,1,2:T(8,128)}), f32[2,1,4,256,256]{3,4,0,1,2:T(8,128)S(1)}, u32[]{:S(2)}, u32[]{:S(2)}) %all-to-all-start) | async-done | bytes 2097184 | tf_op jit(solution)/shard_map/all_to_all | solution.py:247
  66.1 1.0 fusion.20
  68.4 1.0 fusion.26
  69.6 1.3 convolution_bitcast_fusion.5
  73.3 1.9 %fusion.38 = f32[2,256,512]{2,1,0:T(8,128)S(1)} fusion(f32[512,256,1]{1,0,2:T(8,128)S(1)} %bitcast.276, f32[1,256,256]{1,2,0:T(8,128)S(1)} %get-tuple-element.139, f32[1,256,256]{1,2,0:T(8,128)S(1)} %get-tuple-element.138), kind=kOutput, calls=%fused_computation.84 | convolution fusion | flops 805437440 | bytes 2097152 | tf_op jit(solution)/shard_map/bij,kj->bik/dot_general | solution.py:72
  76.2 1.1 convolution_bitcast_fusion.3
  83.0 1.6 %collective-permute-start.6 = (f32[2,1,1,256,256]{3,4,0,2,1:T(8,128)S(1)}, f32[2,1,1,256,256]{3,4,0,2,1:T(8,128)S(1)}, u32[]{:S(2)}, u32[]{:S(2)}) collective-permute-start(f32[2,1,1,256,256]{3,4,0,2,1:T(8,128)S(1)} %get-tuple-element.120), channel_id=1, source_target_pairs={{0,16},{8,24},{16,0},{24,8},{1,17},{9,25},{17,1},{25,9},{2,18},{10... | collective-permute-start | bytes 1572872 | tf_op jit(solution)/shard_map/ppermute | solution.py:266
  85.8 2.5 %collective-permute-start.8 = (f32[2,1,1,256,256]{3,4,1,2,0:T(8,128)S(1)}, f32[2,1,1,256,256]{3,4,1,2,0:T(8,128)S(1)}, u32[]{:S(2)}, u32[]{:S(2)}) collective-permute-start(f32[2,1,1,256,256]{3,4,1,2,0:T(8,128)S(1)} %get-tuple-element.118), channel_id=1, source_target_pairs={{0,24},{8,0},{16,8},{24,16},{1,25},{9,1},{17,9},{25,17},{2,26},{10... | collective-permute-start | bytes 1572872 | tf_op jit(solution)/shard_map/ppermute | solution.py:266
  88.3 19.0 %collective-permute-done.6 = f32[2,1,1,256,256]{3,4,0,2,1:T(8,128)S(1)} collective-permute-done((f32[2,1,1,256,256]{3,4,0,2,1:T(8,128)S(1)}, f32[2,1,1,256,256]{3,4,0,2,1:T(8,128)S(1)}, u32[]{:S(2)}, u32[]{:S(2)}) %collective-permute-start.6) | collective-permute-done | bytes 524320 | tf_op jit(solution)/shard_map/ppermute | solution.py:266
  109.7 1.3 %collective-permute-start.9 = (f32[2,1,512,128]{2,3,0,1:T(8,128)S(1)}, f32[2,1,512,128]{2,3,0,1:T(8,128)S(1)}, u32[]{:S(2)}, u32[]{:S(2)}) collective-permute-start(f32[2,1,512,128]{2,3,0,1:T(8,128)S(1)} %get-tuple-element.117), channel_id=1, source_target_pairs={{0,1},{2,3},{4,5},{6,7},{8,9},{10,11},{12,13},{14,15},{16,17},{18,... | collective-permute-start | bytes 1572872 | tf_op jit(solution)/shard_map/ppermute | solution.py:15
  111.0 1.3 collective-permute-start.10
  112.6 2.2 %collective-permute-done.10 = f32[2,1,512,128]{2,3,0,1:T(8,128)S(1)} collective-permute-done((f32[2,1,512,128]{2,3,0,1:T(8,128)S(1)}, f32[2,1,512,128]{2,3,0,1:T(8,128)S(1)}, u32[]{:S(2)}, u32[]{:S(2)}) %collective-permute-start.10) | collective-permute-done | bytes 524320 | tf_op jit(solution)/shard_map/ppermute | solution.py:15
  115.0 4.4 %collective-permute-start.11 = (f32[2,1,128,256]{2,3,0,1:T(8,128)S(1)}, f32[2,1,128,256]{2,3,0,1:T(8,128)S(1)}, u32[]{:S(2)}, u32[]{:S(2)}) collective-permute-start(f32[2,1,128,256]{2,3,0,1:T(8,128)S(1)} %get-tuple-element.129), channel_id=1, source_target_pairs={{0,2},{2,4},{4,6},{1,3},{3,5},{5,7},{8,10},{10,12},{12,14},{9,11},... | collective-permute-start | bytes 786440 | tf_op jit(solution)/shard_map/ppermute | solution.py:15
  119.4 1.3 collective-permute-start.12
  120.8 4.5 %collective-permute-done.11 = f32[2,1,128,256]{2,3,0,1:T(8,128)S(1)} collective-permute-done((f32[2,1,128,256]{2,3,0,1:T(8,128)S(1)}, f32[2,1,128,256]{2,3,0,1:T(8,128)S(1)}, u32[]{:S(2)}, u32[]{:S(2)}) %collective-permute-start.11) | collective-permute-done | bytes 262176 | tf_op jit(solution)/shard_map/ppermute | solution.py:15
  125.3 4.1 %collective-permute-done.12 = f32[2,1,128,256]{2,3,0,1:T(8,128)S(1)} collective-permute-done((f32[2,1,128,256]{2,3,0,1:T(8,128)S(1)}, f32[2,1,128,256]{2,3,0,1:T(8,128)S(1)}, u32[]{:S(2)}, u32[]{:S(2)}) %collective-permute-start.12) | collective-permute-done | bytes 262176 | tf_op jit(solution)/shard_map/ppermute | solution.py:15
  (110 shorter events, 31.5 us)
Async XLA Ops:
  0.6 13.1 %copy-start.6 = (f32[2,256,256]{2,1,0:T(8,128)S(1)}, f32[2,256,256]{2,1,0:T(8,128)}, u32[]{:S(2)}) copy-start(f32[2,256,256]{2,1,0:T(8,128)} %param.15) | copy-start | bytes 1572868
  0.6 13.9 %copy-start.7 = (s32[1,1,4,2]{2,3,1,0:T(2,128)S(1)}, s32[1,1,4,2]{2,3,1,0:T(2,128)}, u32[]{:S(2)}) copy-start(s32[1,1,4,2]{2,3,1,0:T(2,128)} %param.17) | copy-start | bytes 100
  2.7 18.8 %collective-permute-start = (f32[2,1,128,256]{3,2,1,0:T(8,128)S(1)}, f32[2,1,128,256]{3,2,1,0:T(8,128)S(1)}, u32[]{:S(2)}, u32[]{:S(2)}) collective-permute-start(f32[2,1,128,256]{3,2,1,0:T(8,128)S(1)} %get-tuple-element.163), channel_id=1, source_target_pairs={{0,2},{2,4},{4,6},{1,3},{3,5},{5,7},{8,10},{10,12},{12,14},{9,11},... | collective-permute-start | bytes 786440 | tf_op jit(solution)/shard_map/ppermute | solution.py:28
  7.7 13.9 %collective-permute-start.1 = (f32[2,1,128,256]{3,2,1,0:T(8,128)S(1)}, f32[2,1,128,256]{3,2,1,0:T(8,128)S(1)}, u32[]{:S(2)}, u32[]{:S(2)}) collective-permute-start(f32[2,1,128,256]{3,2,1,0:T(8,128)S(1)} %get-tuple-element.164), channel_id=1, source_target_pairs={{2,0},{4,2},{6,4},{3,1},{5,3},{7,5},{10,8},{12,10},{14,12},{11,9},... | collective-permute-start | bytes 786440 | tf_op jit(solution)/shard_map/ppermute | solution.py:31
  9.8 17.7 %collective-permute-start.3 = (f32[2,1,256,128]{3,2,1,0:T(8,128)}, f32[2,1,256,128]{3,2,1,0:T(8,128)S(1)}, u32[]{:S(2)}, u32[]{:S(2)}) collective-permute-start(f32[2,1,256,128]{3,2,1,0:T(8,128)} %get-tuple-element.161), channel_id=1, source_target_pairs={{0,1},{2,3},{4,5},{6,7},{8,9},{10,11},{12,13},{14,15},{16,17},{18,... | collective-permute-start | bytes 786440 | tf_op jit(solution)/shard_map/ppermute | solution.py:194
  11.3 16.3 %collective-permute-start.5 = (f32[2,1,256,128]{3,2,1,0:T(8,128)}, f32[2,1,256,128]{3,2,1,0:T(8,128)S(1)}, u32[]{:S(2)}, u32[]{:S(2)}) collective-permute-start(f32[2,1,256,128]{3,2,1,0:T(8,128)} %get-tuple-element.162), channel_id=1, source_target_pairs={{1,0},{3,2},{5,4},{7,6},{9,8},{11,10},{13,12},{15,14},{17,16},{19,... | collective-permute-start | bytes 786440 | tf_op jit(solution)/shard_map/ppermute | solution.py:197
  15.6 23.2 %copy-start = (f32[2,256,256]{2,1,0:T(8,128)}, f32[2,256,256]{2,1,0:T(8,128)S(1)}, u32[]{:S(2)}) copy-start(f32[2,256,256]{2,1,0:T(8,128)S(1)} %maximum_multiply_fusion.1) | copy-start | bytes 1572868
  22.5 5.1 %collective-permute-start.2 = (f32[2,1,256,128]{3,2,1,0:T(8,128)}, f32[2,1,256,128]{3,2,1,0:T(8,128)S(1)}, u32[]{:S(2)}, u32[]{:S(2)}) collective-permute-start(f32[2,1,256,128]{3,2,1,0:T(8,128)} %pad_maximum_fusion.4), channel_id=1, source_target_pairs={{0,1},{2,3},{4,5},{6,7},{8,9},{10,11},{12,13},{14,15},{16,17},{18,... | collective-permute-start | bytes 786440 | tf_op jit(solution)/shard_map/ppermute | solution.py:218
  26.2 3.8 %collective-permute-start.4 = (f32[2,1,256,128]{3,2,1,0:T(8,128)}, f32[2,1,256,128]{3,2,1,0:T(8,128)}, u32[]{:S(2)}, u32[]{:S(2)}) collective-permute-start(f32[2,1,256,128]{3,2,1,0:T(8,128)} %pad_maximum_fusion.5), channel_id=1, source_target_pairs={{1,0},{3,2},{5,4},{7,6},{9,8},{11,10},{13,12},{15,14},{17,16},{19,... | collective-permute-start | bytes 786440 | tf_op jit(solution)/shard_map/ppermute | solution.py:226
  34.8 4.7 %copy-start.3 = (f32[1,256,256]{2,1,0:T(8,128)S(1)}, f32[1,256,256]{2,1,0:T(8,128)}, u32[]{:S(2)}) copy-start(f32[1,256,256]{2,1,0:T(8,128)} %get-tuple-element.160) | copy-start | bytes 786436
  34.8 29.2 %all-to-all-start = ((f32[2,1,4,256,256]{3,4,0,1,2:T(8,128)}), f32[2,1,4,256,256]{3,4,0,1,2:T(8,128)S(1)}, u32[]{:S(2)}, u32[]{:S(2)}) async-start(f32[2,1,4,256,256]{3,4,0,1,2:T(8,128)} %pad_maximum_fusion), calls=%async_computation | async-start | bytes 4194304 | tf_op jit(solution)/shard_map/all_to_all | solution.py:247
  51.3 12.9 %copy-start.4 = (f32[1,256,256]{1,2,0:T(8,128)S(1)}, f32[1,256,256]{1,2,0:T(8,128)}, u32[]{:S(2)}) copy-start(f32[1,256,256]{1,2,0:T(8,128)} %copy.182) | copy-start | bytes 786436
  64.0 1.0 copy-start.5
  71.0 1.2 copy-start.1
  73.3 3.0 %copy-start.2 = (f32[2,256,256]{2,1,0:T(8,128)S(1)}, f32[2,256,256]{2,1,0:T(8,128)}, u32[]{:S(2)}) copy-start(f32[2,256,256]{2,1,0:T(8,128)} %copy.136) | copy-start | bytes 1572868
  83.0 24.3 %collective-permute-start.6 = (f32[2,1,1,256,256]{3,4,0,2,1:T(8,128)S(1)}, f32[2,1,1,256,256]{3,4,0,2,1:T(8,128)S(1)}, u32[]{:S(2)}, u32[]{:S(2)}) collective-permute-start(f32[2,1,1,256,256]{3,4,0,2,1:T(8,128)S(1)} %get-tuple-element.120), channel_id=1, source_target_pairs={{0,16},{8,24},{16,0},{24,8},{1,17},{9,25},{17,1},{25,9},{2,18},{10... | collective-permute-start | bytes 1572872 | tf_op jit(solution)/shard_map/ppermute | solution.py:266
  84.6 23.5 %collective-permute-start.7 = (f32[2,1,1,256,256]{3,4,0,2,1:T(8,128)S(1)}, f32[2,1,1,256,256]{3,4,0,2,1:T(8,128)S(1)}, u32[]{:S(2)}, u32[]{:S(2)}) collective-permute-start(f32[2,1,1,256,256]{3,4,0,2,1:T(8,128)S(1)} %get-tuple-element.121), channel_id=1, source_target_pairs={{0,8},{8,16},{16,24},{24,0},{1,9},{9,17},{17,25},{25,1},{2,10},{10... | collective-permute-start | bytes 1572872 | tf_op jit(solution)/shard_map/ppermute | solution.py:266
  85.8 23.0 %collective-permute-start.8 = (f32[2,1,1,256,256]{3,4,1,2,0:T(8,128)S(1)}, f32[2,1,1,256,256]{3,4,1,2,0:T(8,128)S(1)}, u32[]{:S(2)}, u32[]{:S(2)}) collective-permute-start(f32[2,1,1,256,256]{3,4,1,2,0:T(8,128)S(1)} %get-tuple-element.118), channel_id=1, source_target_pairs={{0,24},{8,0},{16,8},{24,16},{1,25},{9,1},{17,9},{25,17},{2,26},{10... | collective-permute-start | bytes 1572872 | tf_op jit(solution)/shard_map/ppermute | solution.py:266
  109.7 2.8 %collective-permute-start.9 = (f32[2,1,512,128]{2,3,0,1:T(8,128)S(1)}, f32[2,1,512,128]{2,3,0,1:T(8,128)S(1)}, u32[]{:S(2)}, u32[]{:S(2)}) collective-permute-start(f32[2,1,512,128]{2,3,0,1:T(8,128)S(1)} %get-tuple-element.117), channel_id=1, source_target_pairs={{0,1},{2,3},{4,5},{6,7},{8,9},{10,11},{12,13},{14,15},{16,17},{18,... | collective-permute-start | bytes 1572872 | tf_op jit(solution)/shard_map/ppermute | solution.py:15
  111.0 3.8 %collective-permute-start.10 = (f32[2,1,512,128]{2,3,0,1:T(8,128)S(1)}, f32[2,1,512,128]{2,3,0,1:T(8,128)S(1)}, u32[]{:S(2)}, u32[]{:S(2)}) collective-permute-start(f32[2,1,512,128]{2,3,0,1:T(8,128)S(1)} %get-tuple-element.116), channel_id=1, source_target_pairs={{1,0},{3,2},{5,4},{7,6},{9,8},{11,10},{13,12},{15,14},{17,16},{19,... | collective-permute-start | bytes 1572872 | tf_op jit(solution)/shard_map/ppermute | solution.py:15
  115.0 10.2 %collective-permute-start.11 = (f32[2,1,128,256]{2,3,0,1:T(8,128)S(1)}, f32[2,1,128,256]{2,3,0,1:T(8,128)S(1)}, u32[]{:S(2)}, u32[]{:S(2)}) collective-permute-start(f32[2,1,128,256]{2,3,0,1:T(8,128)S(1)} %get-tuple-element.129), channel_id=1, source_target_pairs={{0,2},{2,4},{4,6},{1,3},{3,5},{5,7},{8,10},{10,12},{12,14},{9,11},... | collective-permute-start | bytes 786440 | tf_op jit(solution)/shard_map/ppermute | solution.py:15
  119.4 10.0 %collective-permute-start.12 = (f32[2,1,128,256]{2,3,0,1:T(8,128)S(1)}, f32[2,1,128,256]{2,3,0,1:T(8,128)S(1)}, u32[]{:S(2)}, u32[]{:S(2)}) collective-permute-start(f32[2,1,128,256]{2,3,0,1:T(8,128)S(1)} %get-tuple-element.128), channel_id=1, source_target_pairs={{2,0},{4,2},{6,4},{3,1},{5,3},{7,5},{10,8},{12,10},{14,12},{11,9},... | collective-permute-start | bytes 786440 | tf_op jit(solution)/shard_map/ppermute | solution.py:15

commit v12 on v8

--- a/solution.py
+++ b/solution.py
@@ -218,17 +218,17 @@
         axis=2,
     )
     gathered = lax.all_to_all(cut, "depth", 2, 1, tiled=True)
-    windows = gathered
+    windows = jnp.swapaxes(gathered, -1, -2)
     total_layers = windows.shape[1]
     matrices = [fresnel] * (total_layers - 1) + [far_field]
     adjoints = [adjoint_of(matrix) for matrix in matrices]
-    start_wave = probe[:, None]
+    start_wave = jnp.swapaxes(probe, -1, -2)[:, None]
     far_wave, moved = forward_layers(start_wave, windows, matrices)
-    target = lax.dynamic_slice_in_dim(measured[0, 0], first, share)
+    target = jnp.swapaxes(lax.dynamic_slice_in_dim(measured[0, 0], first, share), -1, -2)
     power = far_wave[0] ** 2 + far_wave[1] ** 2
     detector = far_wave * (0.25 * (power - target))[None]
     unused, phase_grad, absorb_grad = backward_layers(detector, windows, moved, adjoints)
-    parts = jnp.stack((phase_grad, absorb_grad))
+    parts = jnp.swapaxes(jnp.stack((phase_grad, absorb_grad)), -1, -2)
     grid = jnp.zeros((2, layers) + extended.shape[2:], jnp.float32)
     for shift in issue_order(depth_count):
         chunk = lax.dynamic_slice_in_dim(

time: 124 us -> 123 us (level)
  local copies, waits for them, and re-layouts: 12.1 us -> 8.95 us
    unnamed x20 -> x16, local copies, waits for them, and re-layouts: 4.18 us -> 0.94 us
    all_to_all x1, waiting for transfers between devices: 12.7 us -> 14.5 us  [per_device(): gathered = lax.all_to_all(cut, 'depth', 2, 1, tiled=True)]
  transfers between devices with their start and end apart: 12 -> 12, of which waited for: 8 -> 8; matrix products, arithmetic and copies ran while one was open for 15% -> 14% of each run, Pallas kernels for 0% -> 0%
where the time goes in v12:
time: 123 us
  waiting for transfers between devices  46.8 us (38%)
  starting transfers between devices  25.4 us (21%)
  matrix products  20.6 us (17%)
  other arithmetic  13.8 us (11%)
  local copies, waits for them, and re-layouts  8.95 us (7%)
  between operations  7.22 us (6%)
    ppermute x3, waiting for transfers between devices, per_device(): chunk = lax.ppermute(chunk, 'depth', pairs)  19.4 us
    all_to_all x1, waiting for transfers between devices, per_device(): gathered = lax.all_to_all(cut, 'depth', 2, 1, tiled=True)  14.5 us
    ppermute x4, waiting for transfers between devices, from_behind(): lax.ppermute(value, axis, [(source, source + steps) for source in range(l...  10.9 us
    ppermute x4, starting transfers between devices, from_behind(): lax.ppermute(value, axis, [(source, source + steps) for source in range(l...  7.48 us
    dot_general x8, matrix products, right_product(): jnp.einsum('bij,kj->bik', waves, matrix, precision=mode, preferred_elemen...  7.45 us
    dot_general x8, matrix products, left_product(): jnp.einsum('ij,bjk->bik', matrix, waves, precision=mode, preferred_elemen...  7.32 us
    ppermute x2, starting transfers between devices, with_halo(): lax.ppermute(lax.slice_in_dim(block, block.shape[dim] - width, None, axis...  7.02 us
    dot_general x4, matrix products, matmul_exact(): jnp.dot(first, second, precision=exact_mode, preferred_element_type=jnp.f...  5.8 us
  transfers between devices with their start and end apart: 12, of which 8 were waited for; matrix products, arithmetic and copies ran while one was open for 14% of the time, Pallas kernels for 0%

profile of v12, /device:TPU:0, one launch (start us, length us, event | category | flops | bytes accessed | tf_op | source)
XLA Modules:
  0.0 122.7 jit_solution(5925963635587539741)
XLA Ops:
  0.7 2.0 %multiply_bitcast_fusion = (f32[1,1,256,256]{3,2,1,0:T(8,128)S(1)}, f32[1,1,256,256]{3,2,1,0:T(8,128)S(1)}) fusion(f32[1,256,256]{2,1,0:T(8,128)} %param.13, f32[1,256,256]{2,1,0:T(8,128)} %param.14), kind=kLoop, calls=%fused_computation.216 | loop fusion | flops 196608 | bytes 1048576 | tf_op jit(solution)/shard_map/stack | solution.py:160
  2.8 4.9 %collective-permute-start = (f32[2,1,128,256]{3,2,1,0:T(8,128)S(1)}, f32[2,1,128,256]{3,2,1,0:T(8,128)S(1)}, u32[]{:S(2)}, u32[]{:S(2)}) collective-permute-start(f32[2,1,128,256]{3,2,1,0:T(8,128)S(1)} %get-tuple-element.155), channel_id=1, source_target_pairs={{0,2},{2,4},{4,6},{1,3},{3,5},{5,7},{8,10},{10,12},{12,14},{9,11},... | collective-permute-start | bytes 786440 | tf_op jit(solution)/shard_map/ppermute | solution.py:28
  7.7 1.3 %collective-permute-start.1 = (f32[2,1,128,256]{3,2,1,0:T(8,128)S(1)}, f32[2,1,128,256]{3,2,1,0:T(8,128)S(1)}, u32[]{:S(2)}, u32[]{:S(2)}) collective-permute-start(f32[2,1,128,256]{3,2,1,0:T(8,128)S(1)} %get-tuple-element.156), channel_id=1, source_target_pairs={{2,0},{4,2},{6,4},{3,1},{5,3},{7,5},{10,8},{12,10},{14,12},{11,9},... | collective-permute-start | bytes 786440 | tf_op jit(solution)/shard_map/ppermute | solution.py:31
  16.1 1.2 %collective-permute-done.1 = f32[2,1,128,256]{3,2,1,0:T(8,128)S(1)} collective-permute-done((f32[2,1,128,256]{3,2,1,0:T(8,128)S(1)}, f32[2,1,128,256]{3,2,1,0:T(8,128)S(1)}, u32[]{:S(2)}, u32[]{:S(2)}) %collective-permute-start.1) | collective-permute-done | bytes 262176 | tf_op jit(solution)/shard_map/ppermute | solution.py:31
  17.5 1.1 fusion.145
  18.5 2.1 %collective-permute-start.2 = (f32[2,1,512,128]{3,2,1,0:T(8,128)}, f32[2,1,512,128]{3,2,1,0:T(8,128)}, u32[]{:S(2)}, u32[]{:S(2)}) collective-permute-start(f32[2,1,512,128]{3,2,1,0:T(8,128)} %get-tuple-element.140), channel_id=1, source_target_pairs={{0,1},{2,3},{4,5},{6,7},{8,9},{10,11},{12,13},{14,15},{16,17},{18,... | collective-permute-start | bytes 1572872 | tf_op jit(solution)/shard_map/ppermute | solution.py:28
  21.7 1.3 %collective-permute-start.3 = (f32[2,1,512,128]{3,2,1,0:T(8,128)}, f32[2,1,512,128]{3,2,1,0:T(8,128)S(1)}, u32[]{:S(2)}, u32[]{:S(2)}) collective-permute-start(f32[2,1,512,128]{3,2,1,0:T(8,128)} %get-tuple-element.141), channel_id=1, source_target_pairs={{1,0},{3,2},{5,4},{7,6},{9,8},{11,10},{13,12},{15,14},{17,16},{19,... | collective-permute-start | bytes 1572872 | tf_op jit(solution)/shard_map/ppermute | solution.py:31
  24.0 1.1 slice_select_fusion.3
  26.6 1.6 %pad_maximum_fusion = f32[2,1,4,256,256]{4,3,0,1,2:T(8,128)} fusion(f32[2,1,1,256,256]{4,3,0,1,2:T(8,128)S(1)} %get-tuple-element.117, f32[2,1,1,256,256]{4,3,0,1,2:T(8,128)S(1)} %get-tuple-element.118, f32[2,1,1,256,256]{4,3,0,1,2:T(8,128)S(1)} %get-tuple-element.119, f32[2,1,1,256,256]{4,3,0,1,2:T(8,128)S(1)} %get-tuple-element.116), kind=kLoop, calls=%fused_computation.16 | loop fusion | flops 1572864 | bytes 4194304 | tf_op jit(solution)/shard_map/stack | solution.py:211
  28.2 3.8 %all-to-all-start = ((f32[2,1,4,256,256]{4,3,0,1,2:T(8,128)}), f32[2,1,4,256,256]{4,3,0,1,2:T(8,128)S(1)}, u32[]{:S(2)}, u32[]{:S(2)}) async-start(f32[2,1,4,256,256]{4,3,0,1,2:T(8,128)} %pad_maximum_fusion), calls=%async_computation | async-start | bytes 4194304 | tf_op jit(solution)/shard_map/all_to_all | solution.py:220
  32.9 1.1 pad_maximum_fusion.1
  35.0 1.4 %fusion.79 = f32[256,256]{1,0:T(8,128)S(1)} fusion(f32[256]{0:T(256)S(1)} %get-tuple-element.177, f32[256]{0:T(256)S(1)} %get-tuple-element.178), kind=kOutput, calls=%fused_computation.209 | convolution fusion | flops 203358208 | bytes 264192 | tf_op jit(solution)/shard_map/dot_general | solution.py:39
  36.5 1.5 %fusion.3 = f32[1,256,256]{2,1,0:T(8,128)S(1)} fusion(f32[256,256]{1,0:T(8,128)S(1)} %fusion.79, f32[256]{0:T(256)S(1)} %get-tuple-element.177, f32[256]{0:T(256)S(1)} %get-tuple-element.178), kind=kOutput, calls=%fused_computation.27 | convolution fusion | flops 203423744 | bytes 526336 | tf_op jit(solution)/shard_map/dot_general | solution.py:39
  38.0 1.4 %fusion.80 = f32[256,256]{1,0:T(8,128)S(1)} fusion(f32[256]{0:T(256)S(1)} %get-tuple-element.177, f32[256]{0:T(256)S(1)} %get-tuple-element.178), kind=kOutput, calls=%fused_computation.211 | convolution fusion | flops 203358208 | bytes 264192 | tf_op jit(solution)/shard_map/dot_general | solution.py:39
  39.4 1.5 %fusion.4 = f32[1,256,256]{2,1,0:T(8,128)S(1)} fusion(f32[256,256]{1,0:T(8,128)S(1)} %fusion.80, f32[256]{0:T(256)S(1)} %get-tuple-element.177, f32[256]{0:T(256)S(1)} %get-tuple-element.178), kind=kOutput, calls=%fused_computation.29 | convolution fusion | flops 203423744 | bytes 526336 | tf_op jit(solution)/shard_map/dot_general | solution.py:39
  41.8 1.2 %copy.126 = f32[2,256,256]{2,1,0:T(8,128)S(1)} copy(f32[2,256,256]{1,2,0:T(8,128)} %pad_maximum_fusion.2) | data formatting | bytes 1048576 | tf_op jit(solution)/shard_map/stack | solution.py:62
  43.0 14.5 %all-to-all-done = f32[2,1,4,256,256]{4,3,0,1,2:T(8,128)S(1)} async-done(((f32[2,1,4,256,256]{4,3,0,1,2:T(8,128)}), f32[2,1,4,256,256]{4,3,0,1,2:T(8,128)S(1)}, u32[]{:S(2)}, u32[]{:S(2)}) %all-to-all-start) | async-done | bytes 2097184 | tf_op jit(solution)/shard_map/all_to_all | solution.py:220
  59.8 1.1 fusion.17
  62.1 1.1 fusion.23
  63.3 1.3 %convolution_bitcast_fusion.5 = f32[2,512,256]{1,2,0:T(8,128)S(1)} fusion(f32[512,256,1]{1,0,2:T(8,128)S(1)} %bitcast.279, f32[1,1,256,256]{2,3,1,0:T(8,128)S(1)} %bitcast.301, f32[1,1,256,256]{2,3,1,0:T(8,128)S(1)} %bitcast.300), kind=kOutput, calls=%fused_computation.23 | convolution fusion | flops 805437440 | bytes 2097152 | tf_op jit(solution)/shard_map/ij,bjk->bik/dot_general | solution.py:66
  67.0 1.9 %fusion.35 = f32[2,256,512]{2,1,0:T(8,128)S(1)} fusion(f32[512,256,1]{1,0,2:T(8,128)S(1)} %bitcast.295, f32[1,256,256]{1,2,0:T(8,128)S(1)} %get-tuple-element.133, f32[1,256,256]{1,2,0:T(8,128)S(1)} %get-tuple-element.132), kind=kOutput, calls=%fused_computation.73 | convolution fusion | flops 805437440 | bytes 2097152 | tf_op jit(solution)/shard_map/bij,kj->bik/dot_general | solution.py:72
  69.0 1.1 convolution_bitcast_fusion.3
  75.8 1.5 %collective-permute-start.4 = (f32[2,1,1,256,256]{4,3,0,2,1:T(8,128)S(1)}, f32[2,1,1,256,256]{4,3,0,2,1:T(8,128)S(1)}, u32[]{:S(2)}, u32[]{:S(2)}) collective-permute-start(f32[2,1,1,256,256]{4,3,0,2,1:T(8,128)S(1)} %get-tuple-element.114), channel_id=1, source_target_pairs={{0,16},{8,24},{16,0},{24,8},{1,17},{9,25},{17,1},{25,9},{2,18},{10... | collective-permute-start | bytes 1572872 | tf_op jit(solution)/shard_map/ppermute | solution.py:239
  78.6 2.5 %collective-permute-start.6 = (f32[2,1,1,256,256]{4,3,1,2,0:T(8,128)S(1)}, f32[2,1,1,256,256]{4,3,1,2,0:T(8,128)S(1)}, u32[]{:S(2)}, u32[]{:S(2)}) collective-permute-start(f32[2,1,1,256,256]{4,3,1,2,0:T(8,128)S(1)} %get-tuple-element.112), channel_id=1, source_target_pairs={{0,24},{8,0},{16,8},{24,16},{1,25},{9,1},{17,9},{25,17},{2,26},{10... | collective-permute-start | bytes 1572872 | tf_op jit(solution)/shard_map/ppermute | solution.py:239
  81.1 19.4 %collective-permute-done.4 = f32[2,1,1,256,256]{4,3,0,2,1:T(8,128)S(1)} collective-permute-done((f32[2,1,1,256,256]{4,3,0,2,1:T(8,128)S(1)}, f32[2,1,1,256,256]{4,3,0,2,1:T(8,128)S(1)}, u32[]{:S(2)}, u32[]{:S(2)}) %collective-permute-start.4) | collective-permute-done | bytes 524320 | tf_op jit(solution)/shard_map/ppermute | solution.py:239
  102.9 1.3 %collective-permute-start.7 = (f32[2,1,512,128]{3,2,0,1:T(8,128)S(1)}, f32[2,1,512,128]{3,2,0,1:T(8,128)S(1)}, u32[]{:S(2)}, u32[]{:S(2)}) collective-permute-start(f32[2,1,512,128]{3,2,0,1:T(8,128)S(1)} %get-tuple-element.111), channel_id=1, source_target_pairs={{0,1},{2,3},{4,5},{6,7},{8,9},{10,11},{12,13},{14,15},{16,17},{18,... | collective-permute-start | bytes 1572872 | tf_op jit(solution)/shard_map/ppermute | solution.py:15
  104.3 1.3 %collective-permute-start.8 = (f32[2,1,512,128]{3,2,0,1:T(8,128)S(1)}, f32[2,1,512,128]{3,2,0,1:T(8,128)S(1)}, u32[]{:S(2)}, u32[]{:S(2)}) collective-permute-start(f32[2,1,512,128]{3,2,0,1:T(8,128)S(1)} %get-tuple-element.110), channel_id=1, source_target_pairs={{1,0},{3,2},{5,4},{7,6},{9,8},{11,10},{13,12},{15,14},{17,16},{19,... | collective-permute-start | bytes 1572872 | tf_op jit(solution)/shard_map/ppermute | solution.py:15
  105.8 2.2 %collective-permute-done.8 = f32[2,1,512,128]{3,2,0,1:T(8,128)S(1)} collective-permute-done((f32[2,1,512,128]{3,2,0,1:T(8,128)S(1)}, f32[2,1,512,128]{3,2,0,1:T(8,128)S(1)}, u32[]{:S(2)}, u32[]{:S(2)}) %collective-permute-start.8) | collective-permute-done | bytes 524320 | tf_op jit(solution)/shard_map/ppermute | solution.py:15
  108.2 3.6 %collective-permute-start.9 = (f32[2,1,128,256]{3,2,0,1:T(8,128)S(1)}, f32[2,1,128,256]{3,2,0,1:T(8,128)S(1)}, u32[]{:S(2)}, u32[]{:S(2)}) collective-permute-start(f32[2,1,128,256]{3,2,0,1:T(8,128)S(1)} %get-tuple-element.123), channel_id=1, source_target_pairs={{0,2},{2,4},{4,6},{1,3},{3,5},{5,7},{8,10},{10,12},{12,14},{9,11},... | collective-permute-start | bytes 786440 | tf_op jit(solution)/shard_map/ppermute | solution.py:15
  111.8 1.3 %collective-permute-start.10 = (f32[2,1,128,256]{3,2,0,1:T(8,128)S(1)}, f32[2,1,128,256]{3,2,0,1:T(8,128)S(1)}, u32[]{:S(2)}, u32[]{:S(2)}) collective-permute-start(f32[2,1,128,256]{3,2,0,1:T(8,128)S(1)} %get-tuple-element.122), channel_id=1, source_target_pairs={{2,0},{4,2},{6,4},{3,1},{5,3},{7,5},{10,8},{12,10},{14,12},{11,9},... | collective-permute-start | bytes 786440 | tf_op jit(solution)/shard_map/ppermute | solution.py:15
  113.1 4.5 %collective-permute-done.9 = f32[2,1,128,256]{3,2,0,1:T(8,128)S(1)} collective-permute-done((f32[2,1,128,256]{3,2,0,1:T(8,128)S(1)}, f32[2,1,128,256]{3,2,0,1:T(8,128)S(1)}, u32[]{:S(2)}, u32[]{:S(2)}) %collective-permute-start.9) | collective-permute-done | bytes 262176 | tf_op jit(solution)/shard_map/ppermute | solution.py:15
  117.7 4.1 %collective-permute-done.10 = f32[2,1,128,256]{3,2,0,1:T(8,128)S(1)} collective-permute-done((f32[2,1,128,256]{3,2,0,1:T(8,128)S(1)}, f32[2,1,128,256]{3,2,0,1:T(8,128)S(1)}, u32[]{:S(2)}, u32[]{:S(2)}) %collective-permute-start.10) | collective-permute-done | bytes 262176 | tf_op jit(solution)/shard_map/ppermute | solution.py:15
  (92 shorter events, 24.4 us)
Async XLA Ops:
  0.6 31.4 %copy-start = (f32[1,1,4,256,256]{4,3,2,1,0:T(8,128)S(1)}, f32[1,1,4,256,256]{4,3,2,1,0:T(8,128)}, u32[]{:S(2)}) copy-start(f32[1,1,4,256,256]{4,3,2,1,0:T(8,128)} %param.16) | copy-start | bytes 3145732
  0.6 9.5 %copy-start.7 = (s32[1,1,4,2]{2,3,1,0:T(2,128)S(1)}, s32[1,1,4,2]{2,3,1,0:T(2,128)}, u32[]{:S(2)}) copy-start(s32[1,1,4,2]{2,3,1,0:T(2,128)} %param.17) | copy-start | bytes 100
  2.8 13.3 %collective-permute-start = (f32[2,1,128,256]{3,2,1,0:T(8,128)S(1)}, f32[2,1,128,256]{3,2,1,0:T(8,128)S(1)}, u32[]{:S(2)}, u32[]{:S(2)}) collective-permute-start(f32[2,1,128,256]{3,2,1,0:T(8,128)S(1)} %get-tuple-element.155), channel_id=1, source_target_pairs={{0,2},{2,4},{4,6},{1,3},{3,5},{5,7},{8,10},{10,12},{12,14},{9,11},... | collective-permute-start | bytes 786440 | tf_op jit(solution)/shard_map/ppermute | solution.py:28
  7.7 9.7 %collective-permute-start.1 = (f32[2,1,128,256]{3,2,1,0:T(8,128)S(1)}, f32[2,1,128,256]{3,2,1,0:T(8,128)S(1)}, u32[]{:S(2)}, u32[]{:S(2)}) collective-permute-start(f32[2,1,128,256]{3,2,1,0:T(8,128)S(1)} %get-tuple-element.156), channel_id=1, source_target_pairs={{2,0},{4,2},{6,4},{3,1},{5,3},{7,5},{10,8},{12,10},{14,12},{11,9},... | collective-permute-start | bytes 786440 | tf_op jit(solution)/shard_map/ppermute | solution.py:31
  18.5 5.4 %collective-permute-start.2 = (f32[2,1,512,128]{3,2,1,0:T(8,128)}, f32[2,1,512,128]{3,2,1,0:T(8,128)}, u32[]{:S(2)}, u32[]{:S(2)}) collective-permute-start(f32[2,1,512,128]{3,2,1,0:T(8,128)} %get-tuple-element.140), channel_id=1, source_target_pairs={{0,1},{2,3},{4,5},{6,7},{8,9},{10,11},{12,13},{14,15},{16,17},{18,... | collective-permute-start | bytes 1572872 | tf_op jit(solution)/shard_map/ppermute | solution.py:28
  21.7 4.0 %collective-permute-start.3 = (f32[2,1,512,128]{3,2,1,0:T(8,128)}, f32[2,1,512,128]{3,2,1,0:T(8,128)S(1)}, u32[]{:S(2)}, u32[]{:S(2)}) collective-permute-start(f32[2,1,512,128]{3,2,1,0:T(8,128)} %get-tuple-element.141), channel_id=1, source_target_pairs={{1,0},{3,2},{5,4},{7,6},{9,8},{11,10},{13,12},{15,14},{17,16},{19,... | collective-permute-start | bytes 1572872 | tf_op jit(solution)/shard_map/ppermute | solution.py:31
  23.0 2.9 %copy-start.2 = (f32[2,256,256]{2,1,0:T(8,128)}, f32[2,256,256]{2,1,0:T(8,128)S(1)}, u32[]{:S(2)}) copy-start(f32[2,256,256]{2,1,0:T(8,128)S(1)} %maximum_multiply_fusion.1) | copy-start | bytes 1572868
  28.2 29.4 %all-to-all-start = ((f32[2,1,4,256,256]{4,3,0,1,2:T(8,128)}), f32[2,1,4,256,256]{4,3,0,1,2:T(8,128)S(1)}, u32[]{:S(2)}, u32[]{:S(2)}) async-start(f32[2,1,4,256,256]{4,3,0,1,2:T(8,128)} %pad_maximum_fusion), calls=%async_computation | async-start | bytes 4194304 | tf_op jit(solution)/shard_map/all_to_all | solution.py:220
  57.6 1.0 copy-start.6
  64.6 1.2 copy-start.3
  66.9 2.0 %copy-start.5 = (f32[1,1,1,256,256]{3,4,2,1,0:T(8,128)S(1)}, f32[1,1,1,256,256]{3,4,2,1,0:T(8,128)}, u32[]{:S(2)}) copy-start(f32[1,1,1,256,256]{3,4,2,1,0:T(8,128)} %copy.118) | copy-start | bytes 786436
  67.0 2.0 %copy-start.4 = (f32[2,256,256]{2,1,0:T(8,128)S(1)}, f32[2,256,256]{2,1,0:T(8,128)}, u32[]{:S(2)}) copy-start(f32[2,256,256]{2,1,0:T(8,128)} %copy.119) | copy-start | bytes 1572868
  75.8 24.7 %collective-permute-start.4 = (f32[2,1,1,256,256]{4,3,0,2,1:T(8,128)S(1)}, f32[2,1,1,256,256]{4,3,0,2,1:T(8,128)S(1)}, u32[]{:S(2)}, u32[]{:S(2)}) collective-permute-start(f32[2,1,1,256,256]{4,3,0,2,1:T(8,128)S(1)} %get-tuple-element.114), channel_id=1, source_target_pairs={{0,16},{8,24},{16,0},{24,8},{1,17},{9,25},{17,1},{25,9},{2,18},{10... | collective-permute-start | bytes 1572872 | tf_op jit(solution)/shard_map/ppermute | solution.py:239
  77.4 23.9 %collective-permute-start.5 = (f32[2,1,1,256,256]{4,3,0,2,1:T(8,128)S(1)}, f32[2,1,1,256,256]{4,3,0,2,1:T(8,128)S(1)}, u32[]{:S(2)}, u32[]{:S(2)}) collective-permute-start(f32[2,1,1,256,256]{4,3,0,2,1:T(8,128)S(1)} %get-tuple-element.115), channel_id=1, source_target_pairs={{0,8},{8,16},{16,24},{24,0},{1,9},{9,17},{17,25},{25,1},{2,10},{10... | collective-permute-start | bytes 1572872 | tf_op jit(solution)/shard_map/ppermute | solution.py:239
  78.6 23.4 %collective-permute-start.6 = (f32[2,1,1,256,256]{4,3,1,2,0:T(8,128)S(1)}, f32[2,1,1,256,256]{4,3,1,2,0:T(8,128)S(1)}, u32[]{:S(2)}, u32[]{:S(2)}) collective-permute-start(f32[2,1,1,256,256]{4,3,1,2,0:T(8,128)S(1)} %get-tuple-element.112), channel_id=1, source_target_pairs={{0,24},{8,0},{16,8},{24,16},{1,25},{9,1},{17,9},{25,17},{2,26},{10... | collective-permute-start | bytes 1572872 | tf_op jit(solution)/shard_map/ppermute | solution.py:239
  102.9 2.8 %collective-permute-start.7 = (f32[2,1,512,128]{3,2,0,1:T(8,128)S(1)}, f32[2,1,512,128]{3,2,0,1:T(8,128)S(1)}, u32[]{:S(2)}, u32[]{:S(2)}) collective-permute-start(f32[2,1,512,128]{3,2,0,1:T(8,128)S(1)} %get-tuple-element.111), channel_id=1, source_target_pairs={{0,1},{2,3},{4,5},{6,7},{8,9},{10,11},{12,13},{14,15},{16,17},{18,... | collective-permute-start | bytes 1572872 | tf_op jit(solution)/shard_map/ppermute | solution.py:15
  104.3 3.8 %collective-permute-start.8 = (f32[2,1,512,128]{3,2,0,1:T(8,128)S(1)}, f32[2,1,512,128]{3,2,0,1:T(8,128)S(1)}, u32[]{:S(2)}, u32[]{:S(2)}) collective-permute-start(f32[2,1,512,128]{3,2,0,1:T(8,128)S(1)} %get-tuple-element.110), channel_id=1, source_target_pairs={{1,0},{3,2},{5,4},{7,6},{9,8},{11,10},{13,12},{15,14},{17,16},{19,... | collective-permute-start | bytes 1572872 | tf_op jit(solution)/shard_map/ppermute | solution.py:15
  108.2 14.5 %copy-start.1 = (f32[1,1,4,256,256]{4,3,2,1,0:T(8,128)S(1)}, f32[1,1,4,256,256]{4,3,2,1,0:T(8,128)}, u32[]{:S(2)}) copy-start(f32[1,1,4,256,256]{4,3,2,1,0:T(8,128)} %param.16) | copy-start | bytes 3145732
  108.2 9.4 %collective-permute-start.9 = (f32[2,1,128,256]{3,2,0,1:T(8,128)S(1)}, f32[2,1,128,256]{3,2,0,1:T(8,128)S(1)}, u32[]{:S(2)}, u32[]{:S(2)}) collective-permute-start(f32[2,1,128,256]{3,2,0,1:T(8,128)S(1)} %get-tuple-element.123), channel_id=1, source_target_pairs={{0,2},{2,4},{4,6},{1,3},{3,5},{5,7},{8,10},{10,12},{12,14},{9,11},... | collective-permute-start | bytes 786440 | tf_op jit(solution)/shard_map/ppermute | solution.py:15
  111.8 10.0 %collective-permute-start.10 = (f32[2,1,128,256]{3,2,0,1:T(8,128)S(1)}, f32[2,1,128,256]{3,2,0,1:T(8,128)S(1)}, u32[]{:S(2)}, u32[]{:S(2)}) collective-permute-start(f32[2,1,128,256]{3,2,0,1:T(8,128)S(1)} %get-tuple-element.122), channel_id=1, source_target_pairs={{2,0},{4,2},{6,4},{3,1},{5,3},{7,5},{10,8},{12,10},{14,12},{11,9},... | collective-permute-start | bytes 786440 | tf_op jit(solution)/shard_map/ppermute | solution.py:15

commit v13 on v12

--- a/solution.py
+++ b/solution.py
@@ -96,9 +96,12 @@
     for layer in range(slab.shape[1]):
         trans_re = slab[0, layer]
         trans_im = slab[1, layer]
-        moved = jnp.stack(
-            (trans_re * wave[0] - trans_im * wave[1], trans_re * wave[1] + trans_im * wave[0])
-        )
+        if layer == 0:
+            moved = jnp.stack((trans_re, trans_im))
+        else:
+            moved = jnp.stack(
+                (trans_re * wave[0] - trans_im * wave[1], trans_re * wave[1] + trans_im * wave[0])
+            )
         moved_list.append(moved)
         wave = propagate(matrices[layer], moved, exact_mode)
     return (wave, jnp.stack(moved_list, axis=1))
@@ -217,12 +220,21 @@
         ],
         axis=2,
     )
+    lead = cut[:, 0]
+    lit = jnp.stack(
+        (
+            lead[0] * probe[0] - lead[1] * probe[1],
+            lead[0] * probe[1] + lead[1] * probe[0],
+        )
+    )
+    lead = jnp.where(depth_index == 0, lit, lead)
+    cut = jnp.concatenate((lead[:, None], cut[:, 1:]), axis=1)
     gathered = lax.all_to_all(cut, "depth", 2, 1, tiled=True)
     windows = jnp.swapaxes(gathered, -1, -2)
     total_layers = windows.shape[1]
     matrices = [fresnel] * (total_layers - 1) + [far_field]
     adjoints = [adjoint_of(matrix) for matrix in matrices]
-    start_wave = jnp.swapaxes(probe, -1, -2)[:, None]
+    start_wave = None
     far_wave, moved = forward_layers(start_wave, windows, matrices)
     target = jnp.swapaxes(lax.dynamic_slice_in_dim(measured[0, 0], first, share), -1, -2)
     power = far_wave[0] ** 2 + far_wave[1] ** 2

time: 123 us -> 125 us (1.016)
  other arithmetic: 13.8 us -> 15.4 us
  waiting for transfers between devices: 46.8 us -> 48.1 us
    select_n x0 -> x1, other arithmetic: none -> 1.72 us  [per_device(): lead = jnp.where(depth_index == 0, lit, lead)]
    another operation x1, other arithmetic: 1.55 us -> 0.19 us  [per_device(): jnp.stack([lax.dynamic_slice(extended, (anchor, anchor, row_starts[k], co...]
where the time goes in v13:
time: 125 us
  waiting for transfers between devices  48.1 us (38%)
  starting transfers between devices  25.4 us (20%)
  matrix products  20.6 us (16%)
  other arithmetic  15.4 us (12%)
  local copies, waits for them, and re-layouts  8.11 us (6%)
  between operations  7.14 us (6%)
    ppermute x3, waiting for transfers between devices, per_device(): chunk = lax.ppermute(chunk, 'depth', pairs)  20 us
    all_to_all x1, waiting for transfers between devices, per_device(): gathered = lax.all_to_all(cut, 'depth', 2, 1, tiled=True)  15.1 us
    ppermute x4, waiting for transfers between devices, from_behind(): lax.ppermute(value, axis, [(source, source + steps) for source in range(l...  10.9 us
    ppermute x4, starting transfers between devices, from_behind(): lax.ppermute(value, axis, [(source, source + steps) for source in range(l...  7.52 us
    dot_general x8, matrix products, right_product(): jnp.einsum('bij,kj->bik', waves, matrix, precision=mode, preferred_elemen...  7.44 us
    dot_general x8, matrix products, left_product(): jnp.einsum('ij,bjk->bik', matrix, waves, precision=mode, preferred_elemen...  7.32 us
    ppermute x2, starting transfers between devices, with_halo(): lax.ppermute(lax.slice_in_dim(block, block.shape[dim] - width, None, axis...  7.04 us
    dot_general x4, matrix products, matmul_exact(): jnp.dot(first, second, precision=exact_mode, preferred_element_type=jnp.f...  5.8 us
  transfers between devices with their start and end apart: 12, of which 8 were waited for; matrix products, arithmetic and copies ran while one was open for 14% of the time, Pallas kernels for 0%

profile of v13, /device:TPU:0, one launch (start us, length us, event | category | flops | bytes accessed | tf_op | source)
XLA Modules:
  0.0 124.7 jit_solution(12733810262457026383)
XLA Ops:
  0.7 2.0 %multiply_bitcast_fusion = (f32[1,1,256,256]{3,2,1,0:T(8,128)S(1)}, f32[1,1,256,256]{3,2,1,0:T(8,128)S(1)}) fusion(f32[1,256,256]{2,1,0:T(8,128)} %param.13, f32[1,256,256]{2,1,0:T(8,128)} %param.14), kind=kLoop, calls=%fused_computation.224 | loop fusion | flops 196608 | bytes 1048576 | tf_op jit(solution)/shard_map/stack | solution.py:163
  2.8 4.9 %collective-permute-start = (f32[2,1,128,256]{3,2,1,0:T(8,128)S(1)}, f32[2,1,128,256]{3,2,1,0:T(8,128)S(1)}, u32[]{:S(2)}, u32[]{:S(2)}) collective-permute-start(f32[2,1,128,256]{3,2,1,0:T(8,128)S(1)} %get-tuple-element.159), channel_id=1, source_target_pairs={{0,2},{2,4},{4,6},{1,3},{3,5},{5,7},{8,10},{10,12},{12,14},{9,11},... | collective-permute-start | bytes 786440 | tf_op jit(solution)/shard_map/ppermute | solution.py:28
  7.7 1.3 %collective-permute-start.1 = (f32[2,1,128,256]{3,2,1,0:T(8,128)S(1)}, f32[2,1,128,256]{3,2,1,0:T(8,128)S(1)}, u32[]{:S(2)}, u32[]{:S(2)}) collective-permute-start(f32[2,1,128,256]{3,2,1,0:T(8,128)S(1)} %get-tuple-element.160), channel_id=1, source_target_pairs={{2,0},{4,2},{6,4},{3,1},{5,3},{7,5},{10,8},{12,10},{14,12},{11,9},... | collective-permute-start | bytes 786440 | tf_op jit(solution)/shard_map/ppermute | solution.py:31
  16.0 1.4 %collective-permute-done.1 = f32[2,1,128,256]{3,2,1,0:T(8,128)S(1)} collective-permute-done((f32[2,1,128,256]{3,2,1,0:T(8,128)S(1)}, f32[2,1,128,256]{3,2,1,0:T(8,128)S(1)}, u32[]{:S(2)}, u32[]{:S(2)}) %collective-permute-start.1) | collective-permute-done | bytes 262176 | tf_op jit(solution)/shard_map/ppermute | solution.py:31
  17.5 1.1 fusion.150
  18.6 2.1 %collective-permute-start.2 = (f32[2,1,512,128]{3,2,1,0:T(8,128)}, f32[2,1,512,128]{3,2,1,0:T(8,128)}, u32[]{:S(2)}, u32[]{:S(2)}) collective-permute-start(f32[2,1,512,128]{3,2,1,0:T(8,128)} %get-tuple-element.142), channel_id=1, source_target_pairs={{0,1},{2,3},{4,5},{6,7},{8,9},{10,11},{12,13},{14,15},{16,17},{18,... | collective-permute-start | bytes 1572872 | tf_op jit(solution)/shard_map/ppermute | solution.py:28
  21.7 1.3 %collective-permute-start.3 = (f32[2,1,512,128]{3,2,1,0:T(8,128)}, f32[2,1,512,128]{3,2,1,0:T(8,128)}, u32[]{:S(2)}, u32[]{:S(2)}) collective-permute-start(f32[2,1,512,128]{3,2,1,0:T(8,128)} %get-tuple-element.143), channel_id=1, source_target_pairs={{1,0},{3,2},{5,4},{7,6},{9,8},{11,10},{13,12},{15,14},{17,16},{19,... | collective-permute-start | bytes 1572872 | tf_op jit(solution)/shard_map/ppermute | solution.py:31
  24.0 1.1 slice_select_fusion.3
  25.9 1.1 slice_select_fusion.1
  28.4 1.7 %maximum_select_fusion = f32[2,1,4,256,256]{4,3,0,1,2:T(8,128)} fusion(f32[1,1,4,256,256]{4,3,0,1,2:T(8,128)S(1)} %get-tuple-element.111, f32[1,1,4,256,256]{4,3,0,1,2:T(8,128)S(1)} %get-tuple-element.110, pred[]{:T(512)S(6)} %eq.28, f32[2,1,1,256,256]{4,3,0,1,2:T(8,128)S(1)} %get-tuple-element.121, f32[2,1,1,256,256]{4,3,0,1,2:T(8,128)S(1)} %get-tuple-element.122, ...), kind=kLoop, calls=%fused_computation.17 | loop fusion | flops 2621440 | bytes 6291457 | tf_op jit(solution)/shard_map/jit(_where)/select_n | solution.py:230
  30.1 3.8 %all-to-all-start = ((f32[2,1,4,256,256]{4,3,0,1,2:T(8,128)}), f32[2,1,4,256,256]{4,3,0,1,2:T(8,128)S(1)}, u32[]{:S(2)}, u32[]{:S(2)}) async-start(f32[2,1,4,256,256]{4,3,0,1,2:T(8,128)} %maximum_select_fusion), calls=%async_computation | async-start | bytes 4194304 | tf_op jit(solution)/shard_map/all_to_all | solution.py:232
  34.8 1.1 pad_maximum_fusion.1
  36.9 1.4 %fusion.84 = f32[256,256]{1,0:T(8,128)S(1)} fusion(f32[256]{0:T(256)S(1)} %get-tuple-element.181, f32[256]{0:T(256)S(1)} %get-tuple-element.182), kind=kOutput, calls=%fused_computation.217 | convolution fusion | flops 203358208 | bytes 264192 | tf_op jit(solution)/shard_map/dot_general | solution.py:39
  38.4 1.4 %fusion.3 = f32[1,256,256]{2,1,0:T(8,128)S(1)} fusion(f32[256,256]{1,0:T(8,128)S(1)} %fusion.84, f32[256]{0:T(256)S(1)} %get-tuple-element.181, f32[256]{0:T(256)S(1)} %get-tuple-element.182), kind=kOutput, calls=%fused_computation.28 | convolution fusion | flops 203423744 | bytes 526336 | tf_op jit(solution)/shard_map/dot_general | solution.py:39
  39.9 1.4 %fusion.85 = f32[256,256]{1,0:T(8,128)S(1)} fusion(f32[256]{0:T(256)S(1)} %get-tuple-element.181, f32[256]{0:T(256)S(1)} %get-tuple-element.182), kind=kOutput, calls=%fused_computation.219 | convolution fusion | flops 203358208 | bytes 264192 | tf_op jit(solution)/shard_map/dot_general | solution.py:39
  41.3 1.5 %fusion.4 = f32[1,256,256]{2,1,0:T(8,128)S(1)} fusion(f32[256,256]{1,0:T(8,128)S(1)} %fusion.85, f32[256]{0:T(256)S(1)} %get-tuple-element.181, f32[256]{0:T(256)S(1)} %get-tuple-element.182), kind=kOutput, calls=%fused_computation.30 | convolution fusion | flops 203423744 | bytes 526336 | tf_op jit(solution)/shard_map/dot_general | solution.py:39
  43.7 1.2 copy.126
  44.9 15.1 %all-to-all-done = f32[2,1,4,256,256]{4,3,0,1,2:T(8,128)S(1)} async-done(((f32[2,1,4,256,256]{4,3,0,1,2:T(8,128)}), f32[2,1,4,256,256]{4,3,0,1,2:T(8,128)S(1)}, u32[]{:S(2)}, u32[]{:S(2)}) %all-to-all-start) | async-done | bytes 2097184 | tf_op jit(solution)/shard_map/all_to_all | solution.py:232
  61.4 1.1 fusion.17
  63.6 1.1 fusion.23
  64.8 1.3 %convolution_bitcast_fusion.5 = f32[2,512,256]{1,2,0:T(8,128)S(1)} fusion(f32[512,256,1]{1,0,2:T(8,128)S(1)} %bitcast.292, f32[1,1,256,256]{2,3,1,0:T(8,128)S(1)} %bitcast.315, f32[1,1,256,256]{2,3,1,0:T(8,128)S(1)} %bitcast.314), kind=kOutput, calls=%fused_computation.24 | convolution fusion | flops 805437440 | bytes 2097152 | tf_op jit(solution)/shard_map/ij,bjk->bik/dot_general | solution.py:66
  68.5 1.9 %fusion.35 = f32[2,256,512]{2,1,0:T(8,128)S(1)} fusion(f32[512,256,1]{1,0,2:T(8,128)S(1)} %bitcast.309, f32[1,256,256]{1,2,0:T(8,128)S(1)} %get-tuple-element.135, f32[1,256,256]{1,2,0:T(8,128)S(1)} %get-tuple-element.134), kind=kOutput, calls=%fused_computation.76 | convolution fusion | flops 805437440 | bytes 2097152 | tf_op jit(solution)/shard_map/bij,kj->bik/dot_general | solution.py:72
  77.3 1.5 %collective-permute-start.4 = (f32[2,1,1,256,256]{4,3,0,2,1:T(8,128)S(1)}, f32[2,1,1,256,256]{4,3,0,2,1:T(8,128)S(1)}, u32[]{:S(2)}, u32[]{:S(2)}) collective-permute-start(f32[2,1,1,256,256]{4,3,0,2,1:T(8,128)S(1)} %get-tuple-element.116), channel_id=1, source_target_pairs={{0,16},{8,24},{16,0},{24,8},{1,17},{9,25},{17,1},{25,9},{2,18},{10... | collective-permute-start | bytes 1572872 | tf_op jit(solution)/shard_map/ppermute | solution.py:251
  80.1 2.4 %collective-permute-start.6 = (f32[2,1,1,256,256]{4,3,1,2,0:T(8,128)S(1)}, f32[2,1,1,256,256]{4,3,1,2,0:T(8,128)S(1)}, u32[]{:S(2)}, u32[]{:S(2)}) collective-permute-start(f32[2,1,1,256,256]{4,3,1,2,0:T(8,128)S(1)} %get-tuple-element.114), channel_id=1, source_target_pairs={{0,24},{8,0},{16,8},{24,16},{1,25},{9,1},{17,9},{25,17},{2,26},{10... | collective-permute-start | bytes 1572872 | tf_op jit(solution)/shard_map/ppermute | solution.py:251
  82.5 20.0 %collective-permute-done.4 = f32[2,1,1,256,256]{4,3,0,2,1:T(8,128)S(1)} collective-permute-done((f32[2,1,1,256,256]{4,3,0,2,1:T(8,128)S(1)}, f32[2,1,1,256,256]{4,3,0,2,1:T(8,128)S(1)}, u32[]{:S(2)}, u32[]{:S(2)}) %collective-permute-start.4) | collective-permute-done | bytes 524320 | tf_op jit(solution)/shard_map/ppermute | solution.py:251
  104.9 1.3 %collective-permute-start.7 = (f32[2,1,512,128]{3,2,0,1:T(8,128)S(1)}, f32[2,1,512,128]{3,2,0,1:T(8,128)S(1)}, u32[]{:S(2)}, u32[]{:S(2)}) collective-permute-start(f32[2,1,512,128]{3,2,0,1:T(8,128)S(1)} %get-tuple-element.113), channel_id=1, source_target_pairs={{0,1},{2,3},{4,5},{6,7},{8,9},{10,11},{12,13},{14,15},{16,17},{18,... | collective-permute-start | bytes 1572872 | tf_op jit(solution)/shard_map/ppermute | solution.py:15
  106.3 1.3 %collective-permute-start.8 = (f32[2,1,512,128]{3,2,0,1:T(8,128)S(1)}, f32[2,1,512,128]{3,2,0,1:T(8,128)S(1)}, u32[]{:S(2)}, u32[]{:S(2)}) collective-permute-start(f32[2,1,512,128]{3,2,0,1:T(8,128)S(1)} %get-tuple-element.112), channel_id=1, source_target_pairs={{1,0},{3,2},{5,4},{7,6},{9,8},{11,10},{13,12},{15,14},{17,16},{19,... | collective-permute-start | bytes 1572872 | tf_op jit(solution)/shard_map/ppermute | solution.py:15
  107.9 2.2 %collective-permute-done.8 = f32[2,1,512,128]{3,2,0,1:T(8,128)S(1)} collective-permute-done((f32[2,1,512,128]{3,2,0,1:T(8,128)S(1)}, f32[2,1,512,128]{3,2,0,1:T(8,128)S(1)}, u32[]{:S(2)}, u32[]{:S(2)}) %collective-permute-start.8) | collective-permute-done | bytes 524320 | tf_op jit(solution)/shard_map/ppermute | solution.py:15
  110.2 3.6 %collective-permute-start.9 = (f32[2,1,128,256]{3,2,0,1:T(8,128)S(1)}, f32[2,1,128,256]{3,2,0,1:T(8,128)S(1)}, u32[]{:S(2)}, u32[]{:S(2)}) collective-permute-start(f32[2,1,128,256]{3,2,0,1:T(8,128)S(1)} %get-tuple-element.125), channel_id=1, source_target_pairs={{0,2},{2,4},{4,6},{1,3},{3,5},{5,7},{8,10},{10,12},{12,14},{9,11},... | collective-permute-start | bytes 786440 | tf_op jit(solution)/shard_map/ppermute | solution.py:15
  113.9 1.3 %collective-permute-start.10 = (f32[2,1,128,256]{3,2,0,1:T(8,128)S(1)}, f32[2,1,128,256]{3,2,0,1:T(8,128)S(1)}, u32[]{:S(2)}, u32[]{:S(2)}) collective-permute-start(f32[2,1,128,256]{3,2,0,1:T(8,128)S(1)} %get-tuple-element.124), channel_id=1, source_target_pairs={{2,0},{4,2},{6,4},{3,1},{5,3},{7,5},{10,8},{12,10},{14,12},{11,9},... | collective-permute-start | bytes 786440 | tf_op jit(solution)/shard_map/ppermute | solution.py:15
  115.2 4.5 %collective-permute-done.9 = f32[2,1,128,256]{3,2,0,1:T(8,128)S(1)} collective-permute-done((f32[2,1,128,256]{3,2,0,1:T(8,128)S(1)}, f32[2,1,128,256]{3,2,0,1:T(8,128)S(1)}, u32[]{:S(2)}, u32[]{:S(2)}) %collective-permute-start.9) | collective-permute-done | bytes 262176 | tf_op jit(solution)/shard_map/ppermute | solution.py:15
  119.7 4.1 %collective-permute-done.10 = f32[2,1,128,256]{3,2,0,1:T(8,128)S(1)} collective-permute-done((f32[2,1,128,256]{3,2,0,1:T(8,128)S(1)}, f32[2,1,128,256]{3,2,0,1:T(8,128)S(1)}, u32[]{:S(2)}, u32[]{:S(2)}) %collective-permute-start.10) | collective-permute-done | bytes 262176 | tf_op jit(solution)/shard_map/ppermute | solution.py:15
  (95 shorter events, 25.1 us)
Async XLA Ops:
  0.6 33.2 %copy-start = (f32[1,1,4,256,256]{4,3,2,1,0:T(8,128)S(1)}, f32[1,1,4,256,256]{4,3,2,1,0:T(8,128)}, u32[]{:S(2)}) copy-start(f32[1,1,4,256,256]{4,3,2,1,0:T(8,128)} %param.16) | copy-start | bytes 3145732
  0.6 9.5 %copy-start.7 = (s32[1,1,4,2]{2,3,1,0:T(2,128)S(1)}, s32[1,1,4,2]{2,3,1,0:T(2,128)}, u32[]{:S(2)}) copy-start(s32[1,1,4,2]{2,3,1,0:T(2,128)} %param.17) | copy-start | bytes 100
  2.8 13.2 %collective-permute-start = (f32[2,1,128,256]{3,2,1,0:T(8,128)S(1)}, f32[2,1,128,256]{3,2,1,0:T(8,128)S(1)}, u32[]{:S(2)}, u32[]{:S(2)}) collective-permute-start(f32[2,1,128,256]{3,2,1,0:T(8,128)S(1)} %get-tuple-element.159), channel_id=1, source_target_pairs={{0,2},{2,4},{4,6},{1,3},{3,5},{5,7},{8,10},{10,12},{12,14},{9,11},... | collective-permute-start | bytes 786440 | tf_op jit(solution)/shard_map/ppermute | solution.py:28
  7.7 9.7 %collective-permute-start.1 = (f32[2,1,128,256]{3,2,1,0:T(8,128)S(1)}, f32[2,1,128,256]{3,2,1,0:T(8,128)S(1)}, u32[]{:S(2)}, u32[]{:S(2)}) collective-permute-start(f32[2,1,128,256]{3,2,1,0:T(8,128)S(1)} %get-tuple-element.160), channel_id=1, source_target_pairs={{2,0},{4,2},{6,4},{3,1},{5,3},{7,5},{10,8},{12,10},{14,12},{11,9},... | collective-permute-start | bytes 786440 | tf_op jit(solution)/shard_map/ppermute | solution.py:31
  17.4 3.3 %copy-start.6 = (f32[2,256,256]{2,1,0:T(8,128)S(1)}, f32[2,256,256]{2,1,0:T(8,128)}, u32[]{:S(2)}) copy-start(f32[2,256,256]{2,1,0:T(8,128)} %param.15) | copy-start | bytes 1572868
  18.6 5.5 %collective-permute-start.2 = (f32[2,1,512,128]{3,2,1,0:T(8,128)}, f32[2,1,512,128]{3,2,1,0:T(8,128)}, u32[]{:S(2)}, u32[]{:S(2)}) collective-permute-start(f32[2,1,512,128]{3,2,1,0:T(8,128)} %get-tuple-element.142), channel_id=1, source_target_pairs={{0,1},{2,3},{4,5},{6,7},{8,9},{10,11},{12,13},{14,15},{16,17},{18,... | collective-permute-start | bytes 1572872 | tf_op jit(solution)/shard_map/ppermute | solution.py:28
  21.7 4.1 %collective-permute-start.3 = (f32[2,1,512,128]{3,2,1,0:T(8,128)}, f32[2,1,512,128]{3,2,1,0:T(8,128)}, u32[]{:S(2)}, u32[]{:S(2)}) collective-permute-start(f32[2,1,512,128]{3,2,1,0:T(8,128)} %get-tuple-element.143), channel_id=1, source_target_pairs={{1,0},{3,2},{5,4},{7,6},{9,8},{11,10},{13,12},{15,14},{17,16},{19,... | collective-permute-start | bytes 1572872 | tf_op jit(solution)/shard_map/ppermute | solution.py:31
  23.1 4.1 %copy-start.2 = (f32[2,256,256]{2,1,0:T(8,128)}, f32[2,256,256]{2,1,0:T(8,128)S(1)}, u32[]{:S(2)}) copy-start(f32[2,256,256]{2,1,0:T(8,128)S(1)} %maximum_multiply_fusion.1) | copy-start | bytes 1572868
  30.1 30.0 %all-to-all-start = ((f32[2,1,4,256,256]{4,3,0,1,2:T(8,128)}), f32[2,1,4,256,256]{4,3,0,1,2:T(8,128)S(1)}, u32[]{:S(2)}, u32[]{:S(2)}) async-start(f32[2,1,4,256,256]{4,3,0,1,2:T(8,128)} %maximum_select_fusion), calls=%async_computation | async-start | bytes 4194304 | tf_op jit(solution)/shard_map/all_to_all | solution.py:232
  66.2 1.2 copy-start.3
  68.4 2.0 %copy-start.5 = (f32[1,1,1,256,256]{3,4,2,1,0:T(8,128)S(1)}, f32[1,1,1,256,256]{3,4,2,1,0:T(8,128)}, u32[]{:S(2)}) copy-start(f32[1,1,1,256,256]{3,4,2,1,0:T(8,128)} %copy.118) | copy-start | bytes 786436
  68.5 2.0 %copy-start.4 = (f32[2,256,256]{2,1,0:T(8,128)S(1)}, f32[2,256,256]{2,1,0:T(8,128)}, u32[]{:S(2)}) copy-start(f32[2,256,256]{2,1,0:T(8,128)} %copy.119) | copy-start | bytes 1572868
  77.3 25.2 %collective-permute-start.4 = (f32[2,1,1,256,256]{4,3,0,2,1:T(8,128)S(1)}, f32[2,1,1,256,256]{4,3,0,2,1:T(8,128)S(1)}, u32[]{:S(2)}, u32[]{:S(2)}) collective-permute-start(f32[2,1,1,256,256]{4,3,0,2,1:T(8,128)S(1)} %get-tuple-element.116), channel_id=1, source_target_pairs={{0,16},{8,24},{16,0},{24,8},{1,17},{9,25},{17,1},{25,9},{2,18},{10... | collective-permute-start | bytes 1572872 | tf_op jit(solution)/shard_map/ppermute | solution.py:251
  78.8 24.5 %collective-permute-start.5 = (f32[2,1,1,256,256]{4,3,0,2,1:T(8,128)S(1)}, f32[2,1,1,256,256]{4,3,0,2,1:T(8,128)S(1)}, u32[]{:S(2)}, u32[]{:S(2)}) collective-permute-start(f32[2,1,1,256,256]{4,3,0,2,1:T(8,128)S(1)} %get-tuple-element.117), channel_id=1, source_target_pairs={{0,8},{8,16},{16,24},{24,0},{1,9},{9,17},{17,25},{25,1},{2,10},{10... | collective-permute-start | bytes 1572872 | tf_op jit(solution)/shard_map/ppermute | solution.py:251
  80.1 24.0 %collective-permute-start.6 = (f32[2,1,1,256,256]{4,3,1,2,0:T(8,128)S(1)}, f32[2,1,1,256,256]{4,3,1,2,0:T(8,128)S(1)}, u32[]{:S(2)}, u32[]{:S(2)}) collective-permute-start(f32[2,1,1,256,256]{4,3,1,2,0:T(8,128)S(1)} %get-tuple-element.114), channel_id=1, source_target_pairs={{0,24},{8,0},{16,8},{24,16},{1,25},{9,1},{17,9},{25,17},{2,26},{10... | collective-permute-start | bytes 1572872 | tf_op jit(solution)/shard_map/ppermute | solution.py:251
  104.9 2.8 %collective-permute-start.7 = (f32[2,1,512,128]{3,2,0,1:T(8,128)S(1)}, f32[2,1,512,128]{3,2,0,1:T(8,128)S(1)}, u32[]{:S(2)}, u32[]{:S(2)}) collective-permute-start(f32[2,1,512,128]{3,2,0,1:T(8,128)S(1)} %get-tuple-element.113), channel_id=1, source_target_pairs={{0,1},{2,3},{4,5},{6,7},{8,9},{10,11},{12,13},{14,15},{16,17},{18,... | collective-permute-start | bytes 1572872 | tf_op jit(solution)/shard_map/ppermute | solution.py:15
  106.3 3.8 %collective-permute-start.8 = (f32[2,1,512,128]{3,2,0,1:T(8,128)S(1)}, f32[2,1,512,128]{3,2,0,1:T(8,128)S(1)}, u32[]{:S(2)}, u32[]{:S(2)}) collective-permute-start(f32[2,1,512,128]{3,2,0,1:T(8,128)S(1)} %get-tuple-element.112), channel_id=1, source_target_pairs={{1,0},{3,2},{5,4},{7,6},{9,8},{11,10},{13,12},{15,14},{17,16},{19,... | collective-permute-start | bytes 1572872 | tf_op jit(solution)/shard_map/ppermute | solution.py:15
  110.2 14.5 %copy-start.1 = (f32[1,1,4,256,256]{4,3,2,1,0:T(8,128)S(1)}, f32[1,1,4,256,256]{4,3,2,1,0:T(8,128)}, u32[]{:S(2)}) copy-start(f32[1,1,4,256,256]{4,3,2,1,0:T(8,128)} %param.16) | copy-start | bytes 3145732
  110.2 9.5 %collective-permute-start.9 = (f32[2,1,128,256]{3,2,0,1:T(8,128)S(1)}, f32[2,1,128,256]{3,2,0,1:T(8,128)S(1)}, u32[]{:S(2)}, u32[]{:S(2)}) collective-permute-start(f32[2,1,128,256]{3,2,0,1:T(8,128)S(1)} %get-tuple-element.125), channel_id=1, source_target_pairs={{0,2},{2,4},{4,6},{1,3},{3,5},{5,7},{8,10},{10,12},{12,14},{9,11},... | collective-permute-start | bytes 786440 | tf_op jit(solution)/shard_map/ppermute | solution.py:15
  113.9 10.0 %collective-permute-start.10 = (f32[2,1,128,256]{3,2,0,1:T(8,128)S(1)}, f32[2,1,128,256]{3,2,0,1:T(8,128)S(1)}, u32[]{:S(2)}, u32[]{:S(2)}) collective-permute-start(f32[2,1,128,256]{3,2,0,1:T(8,128)S(1)} %get-tuple-element.124), channel_id=1, source_target_pairs={{2,0},{4,2},{6,4},{3,1},{5,3},{7,5},{10,8},{12,10},{14,12},{11,9},... | collective-permute-start | bytes 786440 | tf_op jit(solution)/shard_map/ppermute | solution.py:15

commit v14 on v12

--- a/solution.py
+++ b/solution.py
@@ -174,6 +174,15 @@
     half = count // 2
     rest = [shift for shift in range(1, count) if shift != half]
     return [0, half] + rest if count % 2 == 0 and half > 0 else list(range(count))
+
+
+def place_region(patch, row, col, rows, cols):
+    height = rows[0] + rows[1]
+    span = cols[0] + cols[1] + 2 * patch.shape[-1]
+    padded = jnp.pad(patch, ((0, 0), (0, 0), (height, height), (span, span)))
+    anchor = jnp.zeros((), jnp.int32)
+    start = (anchor, anchor, height - row + rows[0], span - col + cols[0])
+    return lax.dynamic_slice(padded, start, patch.shape[:2] + (rows[1], cols[1]))
 
 
 def per_device(phase, absorption, probe, measured, offsets):
@@ -229,7 +238,9 @@
     detector = far_wave * (0.25 * (power - target))[None]
     unused, phase_grad, absorb_grad = backward_layers(detector, windows, moved, adjoints)
     parts = jnp.swapaxes(jnp.stack((phase_grad, absorb_grad)), -1, -2)
-    grid = jnp.zeros((2, layers) + extended.shape[2:], jnp.float32)
+    frame_rows, frame_cols = extended.shape[2:]
+    regions = [(0, rim), (rim, frame_cols - 2 * rim), (frame_cols - rim, rim)]
+    pieces = [jnp.zeros((2, layers, frame_rows, wide), jnp.float32) for start, wide in regions]
     for shift in issue_order(depth_count):
         chunk = lax.dynamic_slice_in_dim(
             parts, ((depth_index + shift) % depth_count) * layers, layers, axis=1
@@ -238,11 +249,25 @@
             pairs = [(i, (i + shift) % depth_count) for i in range(depth_count)]
             chunk = lax.ppermute(chunk, "depth", pairs)
         for slot in range(share):
-            grid = grid + place(
-                chunk[:, :, slot], source_rows[shift][slot], source_cols[shift][slot], extended.shape[2:]
-            )
-        grid = lax.optimization_barrier(grid)
-    owned = fold_both(grid, rim, pass_rows_all, pass_cols_all)
+            pieces = [
+                piece
+                + place_region(
+                    chunk[:, :, slot],
+                    source_rows[shift][slot],
+                    source_cols[shift][slot],
+                    (0, frame_rows),
+                    region,
+                )
+                for piece, region in zip(pieces, regions)
+            ]
+        if shift == 0:
+            pieces = list(lax.optimization_barrier(tuple(pieces)))
+    left_strip, core, right_strip = pieces
+    from_left = pass_cols_all(right_strip, 1)
+    from_right = pass_cols_all(left_strip, -1)
+    core = core.at[:, :, :, :rim].add(from_left)
+    core = core.at[:, :, :, frame_cols - 3 * rim :].add(from_right)
+    owned = fold_rows(core, rim, pass_rows_all)
     return (owned[0], owned[1])
 
 

time: 123 us -> 128 us (1.041)
  other arithmetic: 13.8 us -> 18.5 us
    add x3 -> x2, other arithmetic: 2.3 us -> 6 us  [per_device(): piece + place_region(chunk[:, :, slot], source_rows[shift][slot], source_...]
    ppermute x3, waiting for transfers between devices: 19.4 us -> 20.8 us  [per_device(): chunk = lax.ppermute(chunk, 'depth', pairs)]
  transfers between devices with their start and end apart: 12 -> 12, of which waited for: 8 -> 7; matrix products, arithmetic and copies ran while one was open for 14% -> 15% of each run, Pallas kernels for 0% -> 0%
where the time goes in v14:
time: 128 us; the launch traced here: 127 us
  waiting for transfers between devices  46.9 us (37%)
  starting transfers between devices  25.3 us (20%)
  matrix products  20.6 us (16%)
  other arithmetic  18.5 us (14%)
  local copies, waits for them, and re-layouts  8.99 us (7%)
  between operations  7.14 us (6%)
    ppermute x3, waiting for transfers between devices, per_device(): chunk = lax.ppermute(chunk, 'depth', pairs)  20.8 us
    all_to_all x1, waiting for transfers between devices, per_device(): gathered = lax.all_to_all(cut, 'depth', 2, 1, tiled=True)  14.5 us
    ppermute x4, waiting for transfers between devices, from_behind(): lax.ppermute(value, axis, [(source, source + steps) for source in range(l...  9.6 us
    ppermute x4, starting transfers between devices, from_behind(): lax.ppermute(value, axis, [(source, source + steps) for source in range(l...  7.49 us
    dot_general x8, matrix products, right_product(): jnp.einsum('bij,kj->bik', waves, matrix, precision=mode, preferred_elemen...  7.44 us
    dot_general x8, matrix products, left_product(): jnp.einsum('ij,bjk->bik', matrix, waves, precision=mode, preferred_elemen...  7.32 us
    ppermute x2, starting transfers between devices, with_halo(): lax.ppermute(lax.slice_in_dim(block, block.shape[dim] - width, None, axis...  7.02 us
    add x2, other arithmetic, per_device(): piece + place_region(chunk[:, :, slot], source_rows[shift][slot], source_...  6 us
  transfers between devices with their start and end apart: 12, of which 7 were waited for; matrix products, arithmetic and copies ran while one was open for 15% of the time, Pallas kernels for 0%

profile of v14, /device:TPU:0, one launch (start us, length us, event | category | flops | bytes accessed | tf_op | source)
XLA Modules:
  0.0 127.4 jit_solution(5359785961813182756)
XLA Ops:
  0.7 2.0 %multiply_bitcast_fusion = (f32[1,1,256,256]{3,2,1,0:T(8,128)S(1)}, f32[1,1,256,256]{3,2,1,0:T(8,128)S(1)}) fusion(f32[1,256,256]{2,1,0:T(8,128)} %param.13, f32[1,256,256]{2,1,0:T(8,128)} %param.14), kind=kLoop, calls=%fused_computation.230 | loop fusion | flops 196608 | bytes 1048576 | tf_op jit(solution)/shard_map/stack | solution.py:160
  2.8 4.9 %collective-permute-start = (f32[2,1,128,256]{3,2,1,0:T(8,128)S(1)}, f32[2,1,128,256]{3,2,1,0:T(8,128)S(1)}, u32[]{:S(2)}, u32[]{:S(2)}) collective-permute-start(f32[2,1,128,256]{3,2,1,0:T(8,128)S(1)} %get-tuple-element.163), channel_id=1, source_target_pairs={{0,2},{2,4},{4,6},{1,3},{3,5},{5,7},{8,10},{10,12},{12,14},{9,11},... | collective-permute-start | bytes 786440 | tf_op jit(solution)/shard_map/ppermute | solution.py:28
  7.7 1.3 %collective-permute-start.1 = (f32[2,1,128,256]{3,2,1,0:T(8,128)S(1)}, f32[2,1,128,256]{3,2,1,0:T(8,128)S(1)}, u32[]{:S(2)}, u32[]{:S(2)}) collective-permute-start(f32[2,1,128,256]{3,2,1,0:T(8,128)S(1)} %get-tuple-element.164), channel_id=1, source_target_pairs={{2,0},{4,2},{6,4},{3,1},{5,3},{7,5},{10,8},{12,10},{14,12},{11,9},... | collective-permute-start | bytes 786440 | tf_op jit(solution)/shard_map/ppermute | solution.py:31
  16.0 1.3 %collective-permute-done.1 = f32[2,1,128,256]{3,2,1,0:T(8,128)S(1)} collective-permute-done((f32[2,1,128,256]{3,2,1,0:T(8,128)S(1)}, f32[2,1,128,256]{3,2,1,0:T(8,128)S(1)}, u32[]{:S(2)}, u32[]{:S(2)}) %collective-permute-start.1) | collective-permute-done | bytes 262176 | tf_op jit(solution)/shard_map/ppermute | solution.py:31
  17.5 1.1 fusion.150
  18.5 2.1 %collective-permute-start.2 = (f32[2,1,512,128]{3,2,1,0:T(8,128)}, f32[2,1,512,128]{3,2,1,0:T(8,128)}, u32[]{:S(2)}, u32[]{:S(2)}) collective-permute-start(f32[2,1,512,128]{3,2,1,0:T(8,128)} %get-tuple-element.146), channel_id=1, source_target_pairs={{0,1},{2,3},{4,5},{6,7},{8,9},{10,11},{12,13},{14,15},{16,17},{18,... | collective-permute-start | bytes 1572872 | tf_op jit(solution)/shard_map/ppermute | solution.py:28
  21.7 1.3 %collective-permute-start.3 = (f32[2,1,512,128]{3,2,1,0:T(8,128)}, f32[2,1,512,128]{3,2,1,0:T(8,128)S(1)}, u32[]{:S(2)}, u32[]{:S(2)}) collective-permute-start(f32[2,1,512,128]{3,2,1,0:T(8,128)} %get-tuple-element.147), channel_id=1, source_target_pairs={{1,0},{3,2},{5,4},{7,6},{9,8},{11,10},{13,12},{15,14},{17,16},{19,... | collective-permute-start | bytes 1572872 | tf_op jit(solution)/shard_map/ppermute | solution.py:31
  23.9 1.1 slice_select_fusion.3
  26.6 1.6 %pad_maximum_fusion = f32[2,1,4,256,256]{4,3,0,1,2:T(8,128)} fusion(f32[2,1,1,256,256]{4,3,0,1,2:T(8,128)S(1)} %get-tuple-element.121, f32[2,1,1,256,256]{4,3,0,1,2:T(8,128)S(1)} %get-tuple-element.122, f32[2,1,1,256,256]{4,3,0,1,2:T(8,128)S(1)} %get-tuple-element.123, f32[2,1,1,256,256]{4,3,0,1,2:T(8,128)S(1)} %get-tuple-element.120), kind=kLoop, calls=%fused_computation.21 | loop fusion | flops 1572864 | bytes 4194304 | tf_op jit(solution)/shard_map/stack | solution.py:220
  28.2 3.8 %all-to-all-start = ((f32[2,1,4,256,256]{4,3,0,1,2:T(8,128)}), f32[2,1,4,256,256]{4,3,0,1,2:T(8,128)S(1)}, u32[]{:S(2)}, u32[]{:S(2)}) async-start(f32[2,1,4,256,256]{4,3,0,1,2:T(8,128)} %pad_maximum_fusion), calls=%async_computation | async-start | bytes 4194304 | tf_op jit(solution)/shard_map/all_to_all | solution.py:229
  32.9 1.1 pad_maximum_fusion.1
  35.0 1.5 %fusion.85 = f32[256,256]{1,0:T(8,128)S(1)} fusion(f32[256]{0:T(256)S(1)} %get-tuple-element.185, f32[256]{0:T(256)S(1)} %get-tuple-element.186), kind=kOutput, calls=%fused_computation.223 | convolution fusion | flops 203358208 | bytes 264192 | tf_op jit(solution)/shard_map/dot_general | solution.py:39
  36.5 1.4 %fusion = f32[1,256,256]{2,1,0:T(8,128)S(1)} fusion(f32[256,256]{1,0:T(8,128)S(1)} %fusion.85, f32[256]{0:T(256)S(1)} %get-tuple-element.185, f32[256]{0:T(256)S(1)} %get-tuple-element.186), kind=kOutput, calls=%fused_computation.32 | convolution fusion | flops 203423744 | bytes 526336 | tf_op jit(solution)/shard_map/dot_general | solution.py:39
  37.9 1.4 %fusion.86 = f32[256,256]{1,0:T(8,128)S(1)} fusion(f32[256]{0:T(256)S(1)} %get-tuple-element.185, f32[256]{0:T(256)S(1)} %get-tuple-element.186), kind=kOutput, calls=%fused_computation.225 | convolution fusion | flops 203358208 | bytes 264192 | tf_op jit(solution)/shard_map/dot_general | solution.py:39
  39.4 1.5 %fusion.1 = f32[1,256,256]{2,1,0:T(8,128)S(1)} fusion(f32[256,256]{1,0:T(8,128)S(1)} %fusion.86, f32[256]{0:T(256)S(1)} %get-tuple-element.185, f32[256]{0:T(256)S(1)} %get-tuple-element.186), kind=kOutput, calls=%fused_computation.34 | convolution fusion | flops 203423744 | bytes 526336 | tf_op jit(solution)/shard_map/dot_general | solution.py:39
  41.8 1.2 copy.126
  43.0 14.5 %all-to-all-done = f32[2,1,4,256,256]{4,3,0,1,2:T(8,128)S(1)} async-done(((f32[2,1,4,256,256]{4,3,0,1,2:T(8,128)}), f32[2,1,4,256,256]{4,3,0,1,2:T(8,128)S(1)}, u32[]{:S(2)}, u32[]{:S(2)}) %all-to-all-start) | async-done | bytes 2097184 | tf_op jit(solution)/shard_map/all_to_all | solution.py:229
  63.3 1.3 %convolution_bitcast_fusion.5 = f32[2,512,256]{1,2,0:T(8,128)S(1)} fusion(f32[512,256,1]{1,0,2:T(8,128)S(1)} %bitcast.279, f32[1,1,256,256]{2,3,1,0:T(8,128)S(1)} %bitcast.301, f32[1,1,256,256]{2,3,1,0:T(8,128)S(1)} %bitcast.300), kind=kOutput, calls=%fused_computation.28 | convolution fusion | flops 805437440 | bytes 2097152 | tf_op jit(solution)/shard_map/ij,bjk->bik/dot_general | solution.py:66
  67.0 1.9 %fusion.41 = f32[2,256,512]{2,1,0:T(8,128)S(1)} fusion(f32[512,256,1]{1,0,2:T(8,128)S(1)} %bitcast.295, f32[1,256,256]{1,2,0:T(8,128)S(1)} %get-tuple-element.139, f32[1,256,256]{1,2,0:T(8,128)S(1)} %get-tuple-element.138), kind=kOutput, calls=%fused_computation.87 | convolution fusion | flops 805437440 | bytes 2097152 | tf_op jit(solution)/shard_map/bij,kj->bik/dot_general | solution.py:72
  75.6 1.2 fusion.16
  76.8 1.5 %collective-permute-start.4 = (f32[2,1,1,256,256]{4,3,0,2,1:T(8,128)}, f32[2,1,1,256,256]{4,3,0,2,1:T(8,128)S(1)}, u32[]{:S(2)}, u32[]{:S(2)}) collective-permute-start(f32[2,1,1,256,256]{4,3,0,2,1:T(8,128)} %get-tuple-element.116), channel_id=1, source_target_pairs={{0,16},{8,24},{16,0},{24,8},{1,17},{9,25},{17,1},{25,9},{2,18},{10... | collective-permute-start | bytes 1572872 | tf_op jit(solution)/shard_map/ppermute | solution.py:250
  78.8 2.4 %collective-permute-start.6 = (f32[2,1,1,256,256]{4,3,1,2,0:T(8,128)}, f32[2,1,1,256,256]{4,3,1,2,0:T(8,128)}, u32[]{:S(2)}, u32[]{:S(2)}) collective-permute-start(f32[2,1,1,256,256]{4,3,1,2,0:T(8,128)} %get-tuple-element.119), channel_id=1, source_target_pairs={{0,24},{8,0},{16,8},{24,16},{1,25},{9,1},{17,9},{25,17},{2,26},{10... | collective-permute-start | bytes 1572872 | tf_op jit(solution)/shard_map/ppermute | solution.py:250
  82.2 19.5 %collective-permute-done.4 = f32[2,1,1,256,256]{4,3,0,2,1:T(8,128)S(1)} collective-permute-done((f32[2,1,1,256,256]{4,3,0,2,1:T(8,128)}, f32[2,1,1,256,256]{4,3,0,2,1:T(8,128)S(1)}, u32[]{:S(2)}, u32[]{:S(2)}) %collective-permute-start.4) | collective-permute-done | bytes 524320 | tf_op jit(solution)/shard_map/ppermute | solution.py:250
  101.7 1.3 %collective-permute-done.6 = f32[2,1,1,256,256]{4,3,1,2,0:T(8,128)} collective-permute-done((f32[2,1,1,256,256]{4,3,1,2,0:T(8,128)}, f32[2,1,1,256,256]{4,3,1,2,0:T(8,128)}, u32[]{:S(2)}, u32[]{:S(2)}) %collective-permute-start.6) | collective-permute-done | bytes 524320 | tf_op jit(solution)/shard_map/ppermute | solution.py:250
  103.0 3.6 %fusion.7 = (f32[2,1,512,128]{3,2,0,1:T(8,128)S(1)}, f32[2,1,512,128]{3,2,0,1:T(8,128)}) fusion(s32[]{:T(128)S(6)} %select_n.467, s32[]{:T(128)S(6)} %select_n.474, f32[2,1,256,256]{3,2,0,1:T(8,128)} %bitcast.104, s32[]{:T(128)S(6)} %select_n.463, s32[]{:T(128)S(6)} %select_n.473, f32[2,1,256,256]{3,2,0,1:T(8,128)S(1)} %bitcast.308, ...), kind=kLoop, calls=%fused_computation.43 | loop fusion | flops 786432 | bytes 3670052 | tf_op jit(solution)/shard_map/add | solution.py:253
  106.6 1.3 %collective-permute-start.7 = (f32[2,1,512,128]{3,2,0,1:T(8,128)}, f32[2,1,512,128]{3,2,0,1:T(8,128)S(1)}, u32[]{:S(2)}, u32[]{:S(2)}) collective-permute-start(f32[2,1,512,128]{3,2,0,1:T(8,128)} %get-tuple-element.125), channel_id=1, source_target_pairs={{0,1},{2,3},{4,5},{6,7},{8,9},{10,11},{12,13},{14,15},{16,17},{18,... | collective-permute-start | bytes 1572872 | tf_op jit(solution)/shard_map/ppermute | solution.py:15
  107.9 1.3 %collective-permute-start.8 = (f32[2,1,512,128]{3,2,0,1:T(8,128)S(1)}, f32[2,1,512,128]{3,2,0,1:T(8,128)S(1)}, u32[]{:S(2)}, u32[]{:S(2)}) collective-permute-start(f32[2,1,512,128]{3,2,0,1:T(8,128)S(1)} %get-tuple-element.124), channel_id=1, source_target_pairs={{1,0},{3,2},{5,4},{7,6},{9,8},{11,10},{13,12},{15,14},{17,16},{19,... | collective-permute-start | bytes 1572872 | tf_op jit(solution)/shard_map/ppermute | solution.py:15
  109.2 2.4 %fusion.4 = f32[2,1,512,256]{3,2,0,1:T(8,128)S(1)} fusion(s32[]{:T(128)S(6)} %select_n.467, s32[]{:T(128)S(6)} %select_n.468, f32[2,1,256,256]{3,2,0,1:T(8,128)} %bitcast.104, s32[]{:T(128)S(6)} %select_n.463, s32[]{:T(128)S(6)} %select_n.464, f32[2,1,256,256]{3,2,0,1:T(8,128)S(1)} %bitcast.309, f32[2,1,512,256]{3,2,0,1:T(8,128)S(1)} %pad_dynamic-slice_fusion.7, ...), kind=kLoop, calls=%fused_computation.37 | loop fusion | flops 786432 | bytes 3670040 | tf_op jit(solution)/shard_map/add | solution.py:253
  111.9 3.6 %collective-permute-start.9 = (f32[2,1,128,256]{3,2,0,1:T(8,128)S(1)}, f32[2,1,128,256]{3,2,0,1:T(8,128)S(1)}, u32[]{:S(2)}, u32[]{:S(2)}) collective-permute-start(f32[2,1,128,256]{3,2,0,1:T(8,128)S(1)} %get-tuple-element.129), channel_id=1, source_target_pairs={{0,2},{2,4},{4,6},{1,3},{3,5},{5,7},{8,10},{10,12},{12,14},{9,11},... | collective-permute-start | bytes 786440 | tf_op jit(solution)/shard_map/ppermute | solution.py:15
  115.6 1.3 %collective-permute-start.10 = (f32[2,1,128,256]{3,2,0,1:T(8,128)S(1)}, f32[2,1,128,256]{3,2,0,1:T(8,128)S(1)}, u32[]{:S(2)}, u32[]{:S(2)}) collective-permute-start(f32[2,1,128,256]{3,2,0,1:T(8,128)S(1)} %get-tuple-element.128), channel_id=1, source_target_pairs={{2,0},{4,2},{6,4},{3,1},{5,3},{7,5},{10,8},{12,10},{14,12},{11,9},... | collective-permute-start | bytes 786440 | tf_op jit(solution)/shard_map/ppermute | solution.py:15
  116.9 5.1 %collective-permute-done.9 = f32[2,1,128,256]{3,2,0,1:T(8,128)S(1)} collective-permute-done((f32[2,1,128,256]{3,2,0,1:T(8,128)S(1)}, f32[2,1,128,256]{3,2,0,1:T(8,128)S(1)}, u32[]{:S(2)}, u32[]{:S(2)}) %collective-permute-start.9) | collective-permute-done | bytes 262176 | tf_op jit(solution)/shard_map/ppermute | solution.py:15
  122.1 4.5 %collective-permute-done.10 = f32[2,1,128,256]{3,2,0,1:T(8,128)S(1)} collective-permute-done((f32[2,1,128,256]{3,2,0,1:T(8,128)S(1)}, f32[2,1,128,256]{3,2,0,1:T(8,128)S(1)}, u32[]{:S(2)}, u32[]{:S(2)}) %collective-permute-start.10) | collective-permute-done | bytes 262176 | tf_op jit(solution)/shard_map/ppermute | solution.py:15
  (90 shorter events, 25.0 us)
Async XLA Ops:
  0.6 31.3 %copy-start = (f32[1,1,4,256,256]{4,3,2,1,0:T(8,128)S(1)}, f32[1,1,4,256,256]{4,3,2,1,0:T(8,128)}, u32[]{:S(2)}) copy-start(f32[1,1,4,256,256]{4,3,2,1,0:T(8,128)} %param.16) | copy-start | bytes 3145732
  0.6 9.5 %copy-start.7 = (s32[1,1,4,2]{2,3,1,0:T(2,128)S(1)}, s32[1,1,4,2]{2,3,1,0:T(2,128)}, u32[]{:S(2)}) copy-start(s32[1,1,4,2]{2,3,1,0:T(2,128)} %param.17) | copy-start | bytes 100
  2.8 13.3 %collective-permute-start = (f32[2,1,128,256]{3,2,1,0:T(8,128)S(1)}, f32[2,1,128,256]{3,2,1,0:T(8,128)S(1)}, u32[]{:S(2)}, u32[]{:S(2)}) collective-permute-start(f32[2,1,128,256]{3,2,1,0:T(8,128)S(1)} %get-tuple-element.163), channel_id=1, source_target_pairs={{0,2},{2,4},{4,6},{1,3},{3,5},{5,7},{8,10},{10,12},{12,14},{9,11},... | collective-permute-start | bytes 786440 | tf_op jit(solution)/shard_map/ppermute | solution.py:28
  7.7 9.7 %collective-permute-start.1 = (f32[2,1,128,256]{3,2,1,0:T(8,128)S(1)}, f32[2,1,128,256]{3,2,1,0:T(8,128)S(1)}, u32[]{:S(2)}, u32[]{:S(2)}) collective-permute-start(f32[2,1,128,256]{3,2,1,0:T(8,128)S(1)} %get-tuple-element.164), channel_id=1, source_target_pairs={{2,0},{4,2},{6,4},{3,1},{5,3},{7,5},{10,8},{12,10},{14,12},{11,9},... | collective-permute-start | bytes 786440 | tf_op jit(solution)/shard_map/ppermute | solution.py:31
  18.5 5.4 %collective-permute-start.2 = (f32[2,1,512,128]{3,2,1,0:T(8,128)}, f32[2,1,512,128]{3,2,1,0:T(8,128)}, u32[]{:S(2)}, u32[]{:S(2)}) collective-permute-start(f32[2,1,512,128]{3,2,1,0:T(8,128)} %get-tuple-element.146), channel_id=1, source_target_pairs={{0,1},{2,3},{4,5},{6,7},{8,9},{10,11},{12,13},{14,15},{16,17},{18,... | collective-permute-start | bytes 1572872 | tf_op jit(solution)/shard_map/ppermute | solution.py:28
  21.7 4.0 %collective-permute-start.3 = (f32[2,1,512,128]{3,2,1,0:T(8,128)}, f32[2,1,512,128]{3,2,1,0:T(8,128)S(1)}, u32[]{:S(2)}, u32[]{:S(2)}) collective-permute-start(f32[2,1,512,128]{3,2,1,0:T(8,128)} %get-tuple-element.147), channel_id=1, source_target_pairs={{1,0},{3,2},{5,4},{7,6},{9,8},{11,10},{13,12},{15,14},{17,16},{19,... | collective-permute-start | bytes 1572872 | tf_op jit(solution)/shard_map/ppermute | solution.py:31
  23.0 2.9 %copy-start.2 = (f32[2,256,256]{2,1,0:T(8,128)}, f32[2,256,256]{2,1,0:T(8,128)S(1)}, u32[]{:S(2)}) copy-start(f32[2,256,256]{2,1,0:T(8,128)S(1)} %maximum_multiply_fusion.1) | copy-start | bytes 1572868
  28.2 29.4 %all-to-all-start = ((f32[2,1,4,256,256]{4,3,0,1,2:T(8,128)}), f32[2,1,4,256,256]{4,3,0,1,2:T(8,128)S(1)}, u32[]{:S(2)}, u32[]{:S(2)}) async-start(f32[2,1,4,256,256]{4,3,0,1,2:T(8,128)} %pad_maximum_fusion), calls=%async_computation | async-start | bytes 4194304 | tf_op jit(solution)/shard_map/all_to_all | solution.py:229
  57.6 1.0 copy-start.6
  64.6 1.2 copy-start.3
  66.9 2.0 %copy-start.5 = (f32[1,1,1,256,256]{3,4,2,1,0:T(8,128)S(1)}, f32[1,1,1,256,256]{3,4,2,1,0:T(8,128)}, u32[]{:S(2)}) copy-start(f32[1,1,1,256,256]{3,4,2,1,0:T(8,128)} %copy.118) | copy-start | bytes 786436
  66.9 2.0 %copy-start.4 = (f32[2,256,256]{2,1,0:T(8,128)S(1)}, f32[2,256,256]{2,1,0:T(8,128)}, u32[]{:S(2)}) copy-start(f32[2,256,256]{2,1,0:T(8,128)} %copy.119) | copy-start | bytes 1572868
  76.8 24.8 %collective-permute-start.4 = (f32[2,1,1,256,256]{4,3,0,2,1:T(8,128)}, f32[2,1,1,256,256]{4,3,0,2,1:T(8,128)S(1)}, u32[]{:S(2)}, u32[]{:S(2)}) collective-permute-start(f32[2,1,1,256,256]{4,3,0,2,1:T(8,128)} %get-tuple-element.116), channel_id=1, source_target_pairs={{0,16},{8,24},{16,0},{24,8},{1,17},{9,25},{17,1},{25,9},{2,18},{10... | collective-permute-start | bytes 1572872 | tf_op jit(solution)/shard_map/ppermute | solution.py:250
  78.3 23.4 %collective-permute-start.5 = (f32[2,1,1,256,256]{4,3,0,2,1:T(8,128)}, f32[2,1,1,256,256]{4,3,0,2,1:T(8,128)S(1)}, u32[]{:S(2)}, u32[]{:S(2)}) collective-permute-start(f32[2,1,1,256,256]{4,3,0,2,1:T(8,128)} %get-tuple-element.118), channel_id=1, source_target_pairs={{0,8},{8,16},{16,24},{24,0},{1,9},{9,17},{17,25},{25,1},{2,10},{10... | collective-permute-start | bytes 1572872 | tf_op jit(solution)/shard_map/ppermute | solution.py:250
  78.8 24.2 %collective-permute-start.6 = (f32[2,1,1,256,256]{4,3,1,2,0:T(8,128)}, f32[2,1,1,256,256]{4,3,1,2,0:T(8,128)}, u32[]{:S(2)}, u32[]{:S(2)}) collective-permute-start(f32[2,1,1,256,256]{4,3,1,2,0:T(8,128)} %get-tuple-element.119), channel_id=1, source_target_pairs={{0,24},{8,0},{16,8},{24,16},{1,25},{9,1},{17,9},{25,17},{2,26},{10... | collective-permute-start | bytes 1572872 | tf_op jit(solution)/shard_map/ppermute | solution.py:250
  106.6 5.1 %collective-permute-start.7 = (f32[2,1,512,128]{3,2,0,1:T(8,128)}, f32[2,1,512,128]{3,2,0,1:T(8,128)S(1)}, u32[]{:S(2)}, u32[]{:S(2)}) collective-permute-start(f32[2,1,512,128]{3,2,0,1:T(8,128)} %get-tuple-element.125), channel_id=1, source_target_pairs={{0,1},{2,3},{4,5},{6,7},{8,9},{10,11},{12,13},{14,15},{16,17},{18,... | collective-permute-start | bytes 1572872 | tf_op jit(solution)/shard_map/ppermute | solution.py:15
  107.9 3.9 %collective-permute-start.8 = (f32[2,1,512,128]{3,2,0,1:T(8,128)S(1)}, f32[2,1,512,128]{3,2,0,1:T(8,128)S(1)}, u32[]{:S(2)}, u32[]{:S(2)}) collective-permute-start(f32[2,1,512,128]{3,2,0,1:T(8,128)S(1)} %get-tuple-element.124), channel_id=1, source_target_pairs={{1,0},{3,2},{5,4},{7,6},{9,8},{11,10},{13,12},{15,14},{17,16},{19,... | collective-permute-start | bytes 1572872 | tf_op jit(solution)/shard_map/ppermute | solution.py:15
  111.9 15.5 %copy-start.1 = (f32[1,1,4,256,256]{4,3,2,1,0:T(8,128)S(1)}, f32[1,1,4,256,256]{4,3,2,1,0:T(8,128)}, u32[]{:S(2)}) copy-start(f32[1,1,4,256,256]{4,3,2,1,0:T(8,128)} %param.16) | copy-start | bytes 3145732
  111.9 10.1 %collective-permute-start.9 = (f32[2,1,128,256]{3,2,0,1:T(8,128)S(1)}, f32[2,1,128,256]{3,2,0,1:T(8,128)S(1)}, u32[]{:S(2)}, u32[]{:S(2)}) collective-permute-start(f32[2,1,128,256]{3,2,0,1:T(8,128)S(1)} %get-tuple-element.129), channel_id=1, source_target_pairs={{0,2},{2,4},{4,6},{1,3},{3,5},{5,7},{8,10},{10,12},{12,14},{9,11},... | collective-permute-start | bytes 786440 | tf_op jit(solution)/shard_map/ppermute | solution.py:15
  115.6 11.0 %collective-permute-start.10 = (f32[2,1,128,256]{3,2,0,1:T(8,128)S(1)}, f32[2,1,128,256]{3,2,0,1:T(8,128)S(1)}, u32[]{:S(2)}, u32[]{:S(2)}) collective-permute-start(f32[2,1,128,256]{3,2,0,1:T(8,128)S(1)} %get-tuple-element.128), channel_id=1, source_target_pairs={{2,0},{4,2},{6,4},{3,1},{5,3},{7,5},{10,8},{12,10},{14,12},{11,9},... | collective-permute-start | bytes 786440 | tf_op jit(solution)/shard_map/ppermute | solution.py:15

commit v15 on v12

--- a/solution.py
+++ b/solution.py
@@ -230,7 +230,7 @@
     unused, phase_grad, absorb_grad = backward_layers(detector, windows, moved, adjoints)
     parts = jnp.swapaxes(jnp.stack((phase_grad, absorb_grad)), -1, -2)
     grid = jnp.zeros((2, layers) + extended.shape[2:], jnp.float32)
-    for shift in issue_order(depth_count):
+    for shift in range(depth_count):
         chunk = lax.dynamic_slice_in_dim(
             parts, ((depth_index + shift) % depth_count) * layers, layers, axis=1
         )

time: 123 us -> 124 us (level)
  transfers between devices with their start and end apart: 12 -> 12, of which waited for: 8 -> 9; matrix products, arithmetic and copies ran while one was open for 14% -> 14% of each run, Pallas kernels for 0% -> 0%
where the time goes in v15:
time: 124 us
  waiting for transfers between devices  46.9 us (38%)
  starting transfers between devices  26.2 us (21%)
  matrix products  20.6 us (17%)
  other arithmetic  13.8 us (11%)
  local copies, waits for them, and re-layouts  8.95 us (7%)
  between operations  7.22 us (6%)
    ppermute x3, waiting for transfers between devices, per_device(): chunk = lax.ppermute(chunk, 'depth', pairs)  19.6 us
    all_to_all x1, waiting for transfers between devices, per_device(): gathered = lax.all_to_all(cut, 'depth', 2, 1, tiled=True)  14.5 us
    ppermute x4, waiting for transfers between devices, from_behind(): lax.ppermute(value, axis, [(source, source + steps) for source in range(l...  10.9 us
    ppermute x4, starting transfers between devices, from_behind(): lax.ppermute(value, axis, [(source, source + steps) for source in range(l...  8.11 us
    dot_general x8, matrix products, right_product(): jnp.einsum('bij,kj->bik', waves, matrix, precision=mode, preferred_elemen...  7.45 us
    dot_general x8, matrix products, left_product(): jnp.einsum('ij,bjk->bik', matrix, waves, precision=mode, preferred_elemen...  7.32 us
    ppermute x2, starting transfers between devices, with_halo(): lax.ppermute(lax.slice_in_dim(block, block.shape[dim] - width, None, axis...  7.02 us
    dot_general x4, matrix products, matmul_exact(): jnp.dot(first, second, precision=exact_mode, preferred_element_type=jnp.f...  5.8 us
  transfers between devices with their start and end apart: 12, of which 9 were waited for; matrix products, arithmetic and copies ran while one was open for 14% of the time, Pallas kernels for 0%

profile of v15, /device:TPU:0, one launch (start us, length us, event | category | flops | bytes accessed | tf_op | source)
XLA Modules:
  0.0 123.7 jit_solution(10668065577652131614)
XLA Ops:
  0.7 2.0 %multiply_bitcast_fusion = (f32[1,1,256,256]{3,2,1,0:T(8,128)S(1)}, f32[1,1,256,256]{3,2,1,0:T(8,128)S(1)}) fusion(f32[1,256,256]{2,1,0:T(8,128)} %param.13, f32[1,256,256]{2,1,0:T(8,128)} %param.14), kind=kLoop, calls=%fused_computation.216 | loop fusion | flops 196608 | bytes 1048576 | tf_op jit(solution)/shard_map/stack | solution.py:160
  2.8 4.9 %collective-permute-start = (f32[2,1,128,256]{3,2,1,0:T(8,128)S(1)}, f32[2,1,128,256]{3,2,1,0:T(8,128)S(1)}, u32[]{:S(2)}, u32[]{:S(2)}) collective-permute-start(f32[2,1,128,256]{3,2,1,0:T(8,128)S(1)} %get-tuple-element.155), channel_id=1, source_target_pairs={{0,2},{2,4},{4,6},{1,3},{3,5},{5,7},{8,10},{10,12},{12,14},{9,11},... | collective-permute-start | bytes 786440 | tf_op jit(solution)/shard_map/ppermute | solution.py:28
  7.7 1.3 %collective-permute-start.1 = (f32[2,1,128,256]{3,2,1,0:T(8,128)S(1)}, f32[2,1,128,256]{3,2,1,0:T(8,128)S(1)}, u32[]{:S(2)}, u32[]{:S(2)}) collective-permute-start(f32[2,1,128,256]{3,2,1,0:T(8,128)S(1)} %get-tuple-element.156), channel_id=1, source_target_pairs={{2,0},{4,2},{6,4},{3,1},{5,3},{7,5},{10,8},{12,10},{14,12},{11,9},... | collective-permute-start | bytes 786440 | tf_op jit(solution)/shard_map/ppermute | solution.py:31
  16.1 1.2 %collective-permute-done.1 = f32[2,1,128,256]{3,2,1,0:T(8,128)S(1)} collective-permute-done((f32[2,1,128,256]{3,2,1,0:T(8,128)S(1)}, f32[2,1,128,256]{3,2,1,0:T(8,128)S(1)}, u32[]{:S(2)}, u32[]{:S(2)}) %collective-permute-start.1) | collective-permute-done | bytes 262176 | tf_op jit(solution)/shard_map/ppermute | solution.py:31
  17.5 1.1 fusion.145
  18.5 2.1 %collective-permute-start.2 = (f32[2,1,512,128]{3,2,1,0:T(8,128)}, f32[2,1,512,128]{3,2,1,0:T(8,128)}, u32[]{:S(2)}, u32[]{:S(2)}) collective-permute-start(f32[2,1,512,128]{3,2,1,0:T(8,128)} %get-tuple-element.140), channel_id=1, source_target_pairs={{0,1},{2,3},{4,5},{6,7},{8,9},{10,11},{12,13},{14,15},{16,17},{18,... | collective-permute-start | bytes 1572872 | tf_op jit(solution)/shard_map/ppermute | solution.py:28
  21.7 1.3 %collective-permute-start.3 = (f32[2,1,512,128]{3,2,1,0:T(8,128)}, f32[2,1,512,128]{3,2,1,0:T(8,128)S(1)}, u32[]{:S(2)}, u32[]{:S(2)}) collective-permute-start(f32[2,1,512,128]{3,2,1,0:T(8,128)} %get-tuple-element.141), channel_id=1, source_target_pairs={{1,0},{3,2},{5,4},{7,6},{9,8},{11,10},{13,12},{15,14},{17,16},{19,... | collective-permute-start | bytes 1572872 | tf_op jit(solution)/shard_map/ppermute | solution.py:31
  24.0 1.1 slice_select_fusion.3
  26.6 1.6 %pad_maximum_fusion = f32[2,1,4,256,256]{4,3,0,1,2:T(8,128)} fusion(f32[2,1,1,256,256]{4,3,0,1,2:T(8,128)S(1)} %get-tuple-element.117, f32[2,1,1,256,256]{4,3,0,1,2:T(8,128)S(1)} %get-tuple-element.118, f32[2,1,1,256,256]{4,3,0,1,2:T(8,128)S(1)} %get-tuple-element.119, f32[2,1,1,256,256]{4,3,0,1,2:T(8,128)S(1)} %get-tuple-element.116), kind=kLoop, calls=%fused_computation.16 | loop fusion | flops 1572864 | bytes 4194304 | tf_op jit(solution)/shard_map/stack | solution.py:211
  28.2 3.8 %all-to-all-start = ((f32[2,1,4,256,256]{4,3,0,1,2:T(8,128)}), f32[2,1,4,256,256]{4,3,0,1,2:T(8,128)S(1)}, u32[]{:S(2)}, u32[]{:S(2)}) async-start(f32[2,1,4,256,256]{4,3,0,1,2:T(8,128)} %pad_maximum_fusion), calls=%async_computation | async-start | bytes 4194304 | tf_op jit(solution)/shard_map/all_to_all | solution.py:220
  32.9 1.1 pad_maximum_fusion.1
  35.0 1.4 %fusion.79 = f32[256,256]{1,0:T(8,128)S(1)} fusion(f32[256]{0:T(256)S(1)} %get-tuple-element.177, f32[256]{0:T(256)S(1)} %get-tuple-element.178), kind=kOutput, calls=%fused_computation.209 | convolution fusion | flops 203358208 | bytes 264192 | tf_op jit(solution)/shard_map/dot_general | solution.py:39
  36.5 1.5 %fusion.3 = f32[1,256,256]{2,1,0:T(8,128)S(1)} fusion(f32[256,256]{1,0:T(8,128)S(1)} %fusion.79, f32[256]{0:T(256)S(1)} %get-tuple-element.177, f32[256]{0:T(256)S(1)} %get-tuple-element.178), kind=kOutput, calls=%fused_computation.27 | convolution fusion | flops 203423744 | bytes 526336 | tf_op jit(solution)/shard_map/dot_general | solution.py:39
  38.0 1.4 %fusion.80 = f32[256,256]{1,0:T(8,128)S(1)} fusion(f32[256]{0:T(256)S(1)} %get-tuple-element.177, f32[256]{0:T(256)S(1)} %get-tuple-element.178), kind=kOutput, calls=%fused_computation.211 | convolution fusion | flops 203358208 | bytes 264192 | tf_op jit(solution)/shard_map/dot_general | solution.py:39
  39.4 1.5 %fusion.4 = f32[1,256,256]{2,1,0:T(8,128)S(1)} fusion(f32[256,256]{1,0:T(8,128)S(1)} %fusion.80, f32[256]{0:T(256)S(1)} %get-tuple-element.177, f32[256]{0:T(256)S(1)} %get-tuple-element.178), kind=kOutput, calls=%fused_computation.29 | convolution fusion | flops 203423744 | bytes 526336 | tf_op jit(solution)/shard_map/dot_general | solution.py:39
  41.8 1.2 copy.126
  43.0 14.5 %all-to-all-done = f32[2,1,4,256,256]{4,3,0,1,2:T(8,128)S(1)} async-done(((f32[2,1,4,256,256]{4,3,0,1,2:T(8,128)}), f32[2,1,4,256,256]{4,3,0,1,2:T(8,128)S(1)}, u32[]{:S(2)}, u32[]{:S(2)}) %all-to-all-start) | async-done | bytes 2097184 | tf_op jit(solution)/shard_map/all_to_all | solution.py:220
  59.8 1.1 fusion.17
  62.1 1.1 fusion.23
  63.3 1.3 %convolution_bitcast_fusion.5 = f32[2,512,256]{1,2,0:T(8,128)S(1)} fusion(f32[512,256,1]{1,0,2:T(8,128)S(1)} %bitcast.279, f32[1,1,256,256]{2,3,1,0:T(8,128)S(1)} %bitcast.301, f32[1,1,256,256]{2,3,1,0:T(8,128)S(1)} %bitcast.300), kind=kOutput, calls=%fused_computation.23 | convolution fusion | flops 805437440 | bytes 2097152 | tf_op jit(solution)/shard_map/ij,bjk->bik/dot_general | solution.py:66
  67.0 1.9 %fusion.35 = f32[2,256,512]{2,1,0:T(8,128)S(1)} fusion(f32[512,256,1]{1,0,2:T(8,128)S(1)} %bitcast.295, f32[1,256,256]{1,2,0:T(8,128)S(1)} %get-tuple-element.133, f32[1,256,256]{1,2,0:T(8,128)S(1)} %get-tuple-element.132), kind=kOutput, calls=%fused_computation.73 | convolution fusion | flops 805437440 | bytes 2097152 | tf_op jit(solution)/shard_map/bij,kj->bik/dot_general | solution.py:72
  75.8 1.7 %collective-permute-start.4 = (f32[2,1,1,256,256]{4,3,0,2,1:T(8,128)S(1)}, f32[2,1,1,256,256]{4,3,0,2,1:T(8,128)S(1)}, u32[]{:S(2)}, u32[]{:S(2)}) collective-permute-start(f32[2,1,1,256,256]{4,3,0,2,1:T(8,128)S(1)} %get-tuple-element.114), channel_id=1, source_target_pairs={{0,8},{8,16},{16,24},{24,0},{1,9},{9,17},{17,25},{25,1},{2,10},{10... | collective-permute-start | bytes 1572872 | tf_op jit(solution)/shard_map/ppermute | solution.py:239
  78.9 2.4 %collective-permute-start.6 = (f32[2,1,1,256,256]{4,3,1,2,0:T(8,128)S(1)}, f32[2,1,1,256,256]{4,3,1,2,0:T(8,128)S(1)}, u32[]{:S(2)}, u32[]{:S(2)}) collective-permute-start(f32[2,1,1,256,256]{4,3,1,2,0:T(8,128)S(1)} %get-tuple-element.112), channel_id=1, source_target_pairs={{0,24},{8,0},{16,8},{24,16},{1,25},{9,1},{17,9},{25,17},{2,26},{10... | collective-permute-start | bytes 1572872 | tf_op jit(solution)/shard_map/ppermute | solution.py:239
  81.3 10.6 %collective-permute-done.4 = f32[2,1,1,256,256]{4,3,0,2,1:T(8,128)S(1)} collective-permute-done((f32[2,1,1,256,256]{4,3,0,2,1:T(8,128)S(1)}, f32[2,1,1,256,256]{4,3,0,2,1:T(8,128)S(1)}, u32[]{:S(2)}, u32[]{:S(2)}) %collective-permute-start.4) | collective-permute-done | bytes 524320 | tf_op jit(solution)/shard_map/ppermute | solution.py:239
  92.7 9.0 %collective-permute-done.5 = f32[2,1,1,256,256]{4,3,0,2,1:T(8,128)S(1)} collective-permute-done((f32[2,1,1,256,256]{4,3,0,2,1:T(8,128)S(1)}, f32[2,1,1,256,256]{4,3,0,2,1:T(8,128)S(1)}, u32[]{:S(2)}, u32[]{:S(2)}) %collective-permute-start.5) | collective-permute-done | bytes 524320 | tf_op jit(solution)/shard_map/ppermute | solution.py:239
  103.3 2.0 %collective-permute-start.7 = (f32[2,1,512,128]{3,2,0,1:T(8,128)S(1)}, f32[2,1,512,128]{3,2,0,1:T(8,128)S(1)}, u32[]{:S(2)}, u32[]{:S(2)}) collective-permute-start(f32[2,1,512,128]{3,2,0,1:T(8,128)S(1)} %get-tuple-element.111), channel_id=1, source_target_pairs={{0,1},{2,3},{4,5},{6,7},{8,9},{10,11},{12,13},{14,15},{16,17},{18,... | collective-permute-start | bytes 1572872 | tf_op jit(solution)/shard_map/ppermute | solution.py:15
  105.3 1.3 %collective-permute-start.8 = (f32[2,1,512,128]{3,2,0,1:T(8,128)S(1)}, f32[2,1,512,128]{3,2,0,1:T(8,128)S(1)}, u32[]{:S(2)}, u32[]{:S(2)}) collective-permute-start(f32[2,1,512,128]{3,2,0,1:T(8,128)S(1)} %get-tuple-element.110), channel_id=1, source_target_pairs={{1,0},{3,2},{5,4},{7,6},{9,8},{11,10},{13,12},{15,14},{17,16},{19,... | collective-permute-start | bytes 1572872 | tf_op jit(solution)/shard_map/ppermute | solution.py:15
  106.8 2.2 %collective-permute-done.8 = f32[2,1,512,128]{3,2,0,1:T(8,128)S(1)} collective-permute-done((f32[2,1,512,128]{3,2,0,1:T(8,128)S(1)}, f32[2,1,512,128]{3,2,0,1:T(8,128)S(1)}, u32[]{:S(2)}, u32[]{:S(2)}) %collective-permute-start.8) | collective-permute-done | bytes 524320 | tf_op jit(solution)/shard_map/ppermute | solution.py:15
  109.2 3.6 %collective-permute-start.9 = (f32[2,1,128,256]{3,2,0,1:T(8,128)S(1)}, f32[2,1,128,256]{3,2,0,1:T(8,128)S(1)}, u32[]{:S(2)}, u32[]{:S(2)}) collective-permute-start(f32[2,1,128,256]{3,2,0,1:T(8,128)S(1)} %get-tuple-element.123), channel_id=1, source_target_pairs={{0,2},{2,4},{4,6},{1,3},{3,5},{5,7},{8,10},{10,12},{12,14},{9,11},... | collective-permute-start | bytes 786440 | tf_op jit(solution)/shard_map/ppermute | solution.py:15
  112.8 1.3 %collective-permute-start.10 = (f32[2,1,128,256]{3,2,0,1:T(8,128)S(1)}, f32[2,1,128,256]{3,2,0,1:T(8,128)S(1)}, u32[]{:S(2)}, u32[]{:S(2)}) collective-permute-start(f32[2,1,128,256]{3,2,0,1:T(8,128)S(1)} %get-tuple-element.122), channel_id=1, source_target_pairs={{2,0},{4,2},{6,4},{3,1},{5,3},{7,5},{10,8},{12,10},{14,12},{11,9},... | collective-permute-start | bytes 786440 | tf_op jit(solution)/shard_map/ppermute | solution.py:15
  114.1 4.5 %collective-permute-done.9 = f32[2,1,128,256]{3,2,0,1:T(8,128)S(1)} collective-permute-done((f32[2,1,128,256]{3,2,0,1:T(8,128)S(1)}, f32[2,1,128,256]{3,2,0,1:T(8,128)S(1)}, u32[]{:S(2)}, u32[]{:S(2)}) %collective-permute-start.9) | collective-permute-done | bytes 262176 | tf_op jit(solution)/shard_map/ppermute | solution.py:15
  118.7 4.1 %collective-permute-done.10 = f32[2,1,128,256]{3,2,0,1:T(8,128)S(1)} collective-permute-done((f32[2,1,128,256]{3,2,0,1:T(8,128)S(1)}, f32[2,1,128,256]{3,2,0,1:T(8,128)S(1)}, u32[]{:S(2)}, u32[]{:S(2)}) %collective-permute-start.10) | collective-permute-done | bytes 262176 | tf_op jit(solution)/shard_map/ppermute | solution.py:15
  (92 shorter events, 25.5 us)
Async XLA Ops:
  0.6 31.4 %copy-start = (f32[1,1,4,256,256]{4,3,2,1,0:T(8,128)S(1)}, f32[1,1,4,256,256]{4,3,2,1,0:T(8,128)}, u32[]{:S(2)}) copy-start(f32[1,1,4,256,256]{4,3,2,1,0:T(8,128)} %param.16) | copy-start | bytes 3145732
  0.6 9.5 %copy-start.7 = (s32[1,1,4,2]{2,3,1,0:T(2,128)S(1)}, s32[1,1,4,2]{2,3,1,0:T(2,128)}, u32[]{:S(2)}) copy-start(s32[1,1,4,2]{2,3,1,0:T(2,128)} %param.17) | copy-start | bytes 100
  2.8 13.3 %collective-permute-start = (f32[2,1,128,256]{3,2,1,0:T(8,128)S(1)}, f32[2,1,128,256]{3,2,1,0:T(8,128)S(1)}, u32[]{:S(2)}, u32[]{:S(2)}) collective-permute-start(f32[2,1,128,256]{3,2,1,0:T(8,128)S(1)} %get-tuple-element.155), channel_id=1, source_target_pairs={{0,2},{2,4},{4,6},{1,3},{3,5},{5,7},{8,10},{10,12},{12,14},{9,11},... | collective-permute-start | bytes 786440 | tf_op jit(solution)/shard_map/ppermute | solution.py:28
  7.7 9.7 %collective-permute-start.1 = (f32[2,1,128,256]{3,2,1,0:T(8,128)S(1)}, f32[2,1,128,256]{3,2,1,0:T(8,128)S(1)}, u32[]{:S(2)}, u32[]{:S(2)}) collective-permute-start(f32[2,1,128,256]{3,2,1,0:T(8,128)S(1)} %get-tuple-element.156), channel_id=1, source_target_pairs={{2,0},{4,2},{6,4},{3,1},{5,3},{7,5},{10,8},{12,10},{14,12},{11,9},... | collective-permute-start | bytes 786440 | tf_op jit(solution)/shard_map/ppermute | solution.py:31
  18.5 5.4 %collective-permute-start.2 = (f32[2,1,512,128]{3,2,1,0:T(8,128)}, f32[2,1,512,128]{3,2,1,0:T(8,128)}, u32[]{:S(2)}, u32[]{:S(2)}) collective-permute-start(f32[2,1,512,128]{3,2,1,0:T(8,128)} %get-tuple-element.140), channel_id=1, source_target_pairs={{0,1},{2,3},{4,5},{6,7},{8,9},{10,11},{12,13},{14,15},{16,17},{18,... | collective-permute-start | bytes 1572872 | tf_op jit(solution)/shard_map/ppermute | solution.py:28
  21.7 4.0 %collective-permute-start.3 = (f32[2,1,512,128]{3,2,1,0:T(8,128)}, f32[2,1,512,128]{3,2,1,0:T(8,128)S(1)}, u32[]{:S(2)}, u32[]{:S(2)}) collective-permute-start(f32[2,1,512,128]{3,2,1,0:T(8,128)} %get-tuple-element.141), channel_id=1, source_target_pairs={{1,0},{3,2},{5,4},{7,6},{9,8},{11,10},{13,12},{15,14},{17,16},{19,... | collective-permute-start | bytes 1572872 | tf_op jit(solution)/shard_map/ppermute | solution.py:31
  23.0 2.9 %copy-start.2 = (f32[2,256,256]{2,1,0:T(8,128)}, f32[2,256,256]{2,1,0:T(8,128)S(1)}, u32[]{:S(2)}) copy-start(f32[2,256,256]{2,1,0:T(8,128)S(1)} %maximum_multiply_fusion.1) | copy-start | bytes 1572868
  28.2 29.4 %all-to-all-start = ((f32[2,1,4,256,256]{4,3,0,1,2:T(8,128)}), f32[2,1,4,256,256]{4,3,0,1,2:T(8,128)S(1)}, u32[]{:S(2)}, u32[]{:S(2)}) async-start(f32[2,1,4,256,256]{4,3,0,1,2:T(8,128)} %pad_maximum_fusion), calls=%async_computation | async-start | bytes 4194304 | tf_op jit(solution)/shard_map/all_to_all | solution.py:220
  57.6 1.0 copy-start.6
  64.6 1.2 copy-start.3
  66.9 2.0 %copy-start.5 = (f32[1,1,1,256,256]{3,4,2,1,0:T(8,128)S(1)}, f32[1,1,1,256,256]{3,4,2,1,0:T(8,128)}, u32[]{:S(2)}) copy-start(f32[1,1,1,256,256]{3,4,2,1,0:T(8,128)} %copy.118) | copy-start | bytes 786436
  67.0 2.0 %copy-start.4 = (f32[2,256,256]{2,1,0:T(8,128)S(1)}, f32[2,256,256]{2,1,0:T(8,128)}, u32[]{:S(2)}) copy-start(f32[2,256,256]{2,1,0:T(8,128)} %copy.119) | copy-start | bytes 1572868
  75.8 16.1 %collective-permute-start.4 = (f32[2,1,1,256,256]{4,3,0,2,1:T(8,128)S(1)}, f32[2,1,1,256,256]{4,3,0,2,1:T(8,128)S(1)}, u32[]{:S(2)}, u32[]{:S(2)}) collective-permute-start(f32[2,1,1,256,256]{4,3,0,2,1:T(8,128)S(1)} %get-tuple-element.114), channel_id=1, source_target_pairs={{0,8},{8,16},{16,24},{24,0},{1,9},{9,17},{17,25},{25,1},{2,10},{10... | collective-permute-start | bytes 1572872 | tf_op jit(solution)/shard_map/ppermute | solution.py:239
  77.6 24.1 %collective-permute-start.5 = (f32[2,1,1,256,256]{4,3,0,2,1:T(8,128)S(1)}, f32[2,1,1,256,256]{4,3,0,2,1:T(8,128)S(1)}, u32[]{:S(2)}, u32[]{:S(2)}) collective-permute-start(f32[2,1,1,256,256]{4,3,0,2,1:T(8,128)S(1)} %get-tuple-element.115), channel_id=1, source_target_pairs={{0,16},{8,24},{16,0},{24,8},{1,17},{9,25},{17,1},{25,9},{2,18},{10... | collective-permute-start | bytes 1572872 | tf_op jit(solution)/shard_map/ppermute | solution.py:239
  78.9 23.6 %collective-permute-start.6 = (f32[2,1,1,256,256]{4,3,1,2,0:T(8,128)S(1)}, f32[2,1,1,256,256]{4,3,1,2,0:T(8,128)S(1)}, u32[]{:S(2)}, u32[]{:S(2)}) collective-permute-start(f32[2,1,1,256,256]{4,3,1,2,0:T(8,128)S(1)} %get-tuple-element.112), channel_id=1, source_target_pairs={{0,24},{8,0},{16,8},{24,16},{1,25},{9,1},{17,9},{25,17},{2,26},{10... | collective-permute-start | bytes 1572872 | tf_op jit(solution)/shard_map/ppermute | solution.py:239
  103.3 3.5 %collective-permute-start.7 = (f32[2,1,512,128]{3,2,0,1:T(8,128)S(1)}, f32[2,1,512,128]{3,2,0,1:T(8,128)S(1)}, u32[]{:S(2)}, u32[]{:S(2)}) collective-permute-start(f32[2,1,512,128]{3,2,0,1:T(8,128)S(1)} %get-tuple-element.111), channel_id=1, source_target_pairs={{0,1},{2,3},{4,5},{6,7},{8,9},{10,11},{12,13},{14,15},{16,17},{18,... | collective-permute-start | bytes 1572872 | tf_op jit(solution)/shard_map/ppermute | solution.py:15
  105.3 3.8 %collective-permute-start.8 = (f32[2,1,512,128]{3,2,0,1:T(8,128)S(1)}, f32[2,1,512,128]{3,2,0,1:T(8,128)S(1)}, u32[]{:S(2)}, u32[]{:S(2)}) collective-permute-start(f32[2,1,512,128]{3,2,0,1:T(8,128)S(1)} %get-tuple-element.110), channel_id=1, source_target_pairs={{1,0},{3,2},{5,4},{7,6},{9,8},{11,10},{13,12},{15,14},{17,16},{19,... | collective-permute-start | bytes 1572872 | tf_op jit(solution)/shard_map/ppermute | solution.py:15
  109.2 14.5 %copy-start.1 = (f32[1,1,4,256,256]{4,3,2,1,0:T(8,128)S(1)}, f32[1,1,4,256,256]{4,3,2,1,0:T(8,128)}, u32[]{:S(2)}) copy-start(f32[1,1,4,256,256]{4,3,2,1,0:T(8,128)} %param.16) | copy-start | bytes 3145732
  109.2 9.4 %collective-permute-start.9 = (f32[2,1,128,256]{3,2,0,1:T(8,128)S(1)}, f32[2,1,128,256]{3,2,0,1:T(8,128)S(1)}, u32[]{:S(2)}, u32[]{:S(2)}) collective-permute-start(f32[2,1,128,256]{3,2,0,1:T(8,128)S(1)} %get-tuple-element.123), channel_id=1, source_target_pairs={{0,2},{2,4},{4,6},{1,3},{3,5},{5,7},{8,10},{10,12},{12,14},{9,11},... | collective-permute-start | bytes 786440 | tf_op jit(solution)/shard_map/ppermute | solution.py:15
  112.8 10.0 %collective-permute-start.10 = (f32[2,1,128,256]{3,2,0,1:T(8,128)S(1)}, f32[2,1,128,256]{3,2,0,1:T(8,128)S(1)}, u32[]{:S(2)}, u32[]{:S(2)}) collective-permute-start(f32[2,1,128,256]{3,2,0,1:T(8,128)S(1)} %get-tuple-element.122), channel_id=1, source_target_pairs={{2,0},{4,2},{6,4},{3,1},{5,3},{7,5},{10,8},{12,10},{14,12},{11,9},... | collective-permute-start | bytes 786440 | tf_op jit(solution)/shard_map/ppermute | solution.py:15

commit v16 on v12

--- a/solution.py
+++ b/solution.py
@@ -241,7 +241,8 @@
             grid = grid + place(
                 chunk[:, :, slot], source_rows[shift][slot], source_cols[shift][slot], extended.shape[2:]
             )
-        grid = lax.optimization_barrier(grid)
+        if shift == 0:
+            grid = lax.optimization_barrier(grid)
     owned = fold_both(grid, rim, pass_rows_all, pass_cols_all)
     return (owned[0], owned[1])
 

time: 123 us -> 126 us (1.024)
  transfers between devices with their start and end apart: 12 -> 12, of which waited for: 8 -> 9; matrix products, arithmetic and copies ran while one was open for 14% -> 13% of each run, Pallas kernels for 0% -> 0%
where the time goes in v16:
time: 126 us; the launch traced here: 125 us
  waiting for transfers between devices  48 us (38%)
  starting transfers between devices  25.9 us (21%)
  matrix products  20.6 us (16%)
  other arithmetic  14.4 us (11%)
  local copies, waits for them, and re-layouts  8.95 us (7%)
  between operations  7.19 us (6%)
    ppermute x3, waiting for transfers between devices, per_device(): chunk = lax.ppermute(chunk, 'depth', pairs)  20.6 us
    all_to_all x1, waiting for transfers between devices, per_device(): gathered = lax.all_to_all(cut, 'depth', 2, 1, tiled=True)  14.5 us
    ppermute x4, waiting for transfers between devices, from_behind(): lax.ppermute(value, axis, [(source, source + steps) for source in range(l...  10.9 us
    ppermute x4, starting transfers between devices, from_behind(): lax.ppermute(value, axis, [(source, source + steps) for source in range(l...  8.11 us
    dot_general x8, matrix products, right_product(): jnp.einsum('bij,kj->bik', waves, matrix, precision=mode, preferred_elemen...  7.45 us
    dot_general x8, matrix products, left_product(): jnp.einsum('ij,bjk->bik', matrix, waves, precision=mode, preferred_elemen...  7.32 us
    ppermute x2, starting transfers between devices, with_halo(): lax.ppermute(lax.slice_in_dim(block, block.shape[dim] - width, None, axis...  7.02 us
    dot_general x4, matrix products, matmul_exact(): jnp.dot(first, second, precision=exact_mode, preferred_element_type=jnp.f...  5.8 us
  transfers between devices with their start and end apart: 12, of which 9 were waited for; matrix products, arithmetic and copies ran while one was open for 13% of the time, Pallas kernels for 0%

profile of v16, /device:TPU:0, one launch (start us, length us, event | category | flops | bytes accessed | tf_op | source)
XLA Modules:
  0.0 125.0 jit_solution(5874019623273518719)
XLA Ops:
  0.7 2.0 %multiply_bitcast_fusion = (f32[1,1,256,256]{3,2,1,0:T(8,128)S(1)}, f32[1,1,256,256]{3,2,1,0:T(8,128)S(1)}) fusion(f32[1,256,256]{2,1,0:T(8,128)} %param.13, f32[1,256,256]{2,1,0:T(8,128)} %param.14), kind=kLoop, calls=%fused_computation.216 | loop fusion | flops 196608 | bytes 1048576 | tf_op jit(solution)/shard_map/stack | solution.py:160
  2.8 4.9 %collective-permute-start = (f32[2,1,128,256]{3,2,1,0:T(8,128)S(1)}, f32[2,1,128,256]{3,2,1,0:T(8,128)S(1)}, u32[]{:S(2)}, u32[]{:S(2)}) collective-permute-start(f32[2,1,128,256]{3,2,1,0:T(8,128)S(1)} %get-tuple-element.155), channel_id=1, source_target_pairs={{0,2},{2,4},{4,6},{1,3},{3,5},{5,7},{8,10},{10,12},{12,14},{9,11},... | collective-permute-start | bytes 786440 | tf_op jit(solution)/shard_map/ppermute | solution.py:28
  7.7 1.3 %collective-permute-start.1 = (f32[2,1,128,256]{3,2,1,0:T(8,128)S(1)}, f32[2,1,128,256]{3,2,1,0:T(8,128)S(1)}, u32[]{:S(2)}, u32[]{:S(2)}) collective-permute-start(f32[2,1,128,256]{3,2,1,0:T(8,128)S(1)} %get-tuple-element.156), channel_id=1, source_target_pairs={{2,0},{4,2},{6,4},{3,1},{5,3},{7,5},{10,8},{12,10},{14,12},{11,9},... | collective-permute-start | bytes 786440 | tf_op jit(solution)/shard_map/ppermute | solution.py:31
  16.1 1.2 collective-permute-done.1
  17.5 1.1 fusion.145
  18.5 2.1 %collective-permute-start.2 = (f32[2,1,512,128]{3,2,1,0:T(8,128)}, f32[2,1,512,128]{3,2,1,0:T(8,128)}, u32[]{:S(2)}, u32[]{:S(2)}) collective-permute-start(f32[2,1,512,128]{3,2,1,0:T(8,128)} %get-tuple-element.140), channel_id=1, source_target_pairs={{0,1},{2,3},{4,5},{6,7},{8,9},{10,11},{12,13},{14,15},{16,17},{18,... | collective-permute-start | bytes 1572872 | tf_op jit(solution)/shard_map/ppermute | solution.py:28
  21.7 1.3 %collective-permute-start.3 = (f32[2,1,512,128]{3,2,1,0:T(8,128)}, f32[2,1,512,128]{3,2,1,0:T(8,128)S(1)}, u32[]{:S(2)}, u32[]{:S(2)}) collective-permute-start(f32[2,1,512,128]{3,2,1,0:T(8,128)} %get-tuple-element.141), channel_id=1, source_target_pairs={{1,0},{3,2},{5,4},{7,6},{9,8},{11,10},{13,12},{15,14},{17,16},{19,... | collective-permute-start | bytes 1572872 | tf_op jit(solution)/shard_map/ppermute | solution.py:31
  24.0 1.1 slice_select_fusion.3
  26.6 1.6 %pad_maximum_fusion = f32[2,1,4,256,256]{4,3,0,1,2:T(8,128)} fusion(f32[2,1,1,256,256]{4,3,0,1,2:T(8,128)S(1)} %get-tuple-element.117, f32[2,1,1,256,256]{4,3,0,1,2:T(8,128)S(1)} %get-tuple-element.118, f32[2,1,1,256,256]{4,3,0,1,2:T(8,128)S(1)} %get-tuple-element.119, f32[2,1,1,256,256]{4,3,0,1,2:T(8,128)S(1)} %get-tuple-element.116), kind=kLoop, calls=%fused_computation.16 | loop fusion | flops 1572864 | bytes 4194304 | tf_op jit(solution)/shard_map/stack | solution.py:211
  28.2 3.8 %all-to-all-start = ((f32[2,1,4,256,256]{4,3,0,1,2:T(8,128)}), f32[2,1,4,256,256]{4,3,0,1,2:T(8,128)S(1)}, u32[]{:S(2)}, u32[]{:S(2)}) async-start(f32[2,1,4,256,256]{4,3,0,1,2:T(8,128)} %pad_maximum_fusion), calls=%async_computation | async-start | bytes 4194304 | tf_op jit(solution)/shard_map/all_to_all | solution.py:220
  32.9 1.1 pad_maximum_fusion.1
  35.0 1.4 %fusion.79 = f32[256,256]{1,0:T(8,128)S(1)} fusion(f32[256]{0:T(256)S(1)} %get-tuple-element.177, f32[256]{0:T(256)S(1)} %get-tuple-element.178), kind=kOutput, calls=%fused_computation.209 | convolution fusion | flops 203358208 | bytes 264192 | tf_op jit(solution)/shard_map/dot_general | solution.py:39
  36.5 1.5 %fusion.3 = f32[1,256,256]{2,1,0:T(8,128)S(1)} fusion(f32[256,256]{1,0:T(8,128)S(1)} %fusion.79, f32[256]{0:T(256)S(1)} %get-tuple-element.177, f32[256]{0:T(256)S(1)} %get-tuple-element.178), kind=kOutput, calls=%fused_computation.27 | convolution fusion | flops 203423744 | bytes 526336 | tf_op jit(solution)/shard_map/dot_general | solution.py:39
  38.0 1.4 %fusion.80 = f32[256,256]{1,0:T(8,128)S(1)} fusion(f32[256]{0:T(256)S(1)} %get-tuple-element.177, f32[256]{0:T(256)S(1)} %get-tuple-element.178), kind=kOutput, calls=%fused_computation.211 | convolution fusion | flops 203358208 | bytes 264192 | tf_op jit(solution)/shard_map/dot_general | solution.py:39
  39.4 1.5 %fusion.4 = f32[1,256,256]{2,1,0:T(8,128)S(1)} fusion(f32[256,256]{1,0:T(8,128)S(1)} %fusion.80, f32[256]{0:T(256)S(1)} %get-tuple-element.177, f32[256]{0:T(256)S(1)} %get-tuple-element.178), kind=kOutput, calls=%fused_computation.29 | convolution fusion | flops 203423744 | bytes 526336 | tf_op jit(solution)/shard_map/dot_general | solution.py:39
  41.8 1.2 copy.126
  43.0 14.5 %all-to-all-done = f32[2,1,4,256,256]{4,3,0,1,2:T(8,128)S(1)} async-done(((f32[2,1,4,256,256]{4,3,0,1,2:T(8,128)}), f32[2,1,4,256,256]{4,3,0,1,2:T(8,128)S(1)}, u32[]{:S(2)}, u32[]{:S(2)}) %all-to-all-start) | async-done | bytes 2097184 | tf_op jit(solution)/shard_map/all_to_all | solution.py:220
  63.3 1.3 %convolution_bitcast_fusion.5 = f32[2,512,256]{1,2,0:T(8,128)S(1)} fusion(f32[512,256,1]{1,0,2:T(8,128)S(1)} %bitcast.279, f32[1,1,256,256]{2,3,1,0:T(8,128)S(1)} %bitcast.301, f32[1,1,256,256]{2,3,1,0:T(8,128)S(1)} %bitcast.300), kind=kOutput, calls=%fused_computation.23 | convolution fusion | flops 805437440 | bytes 2097152 | tf_op jit(solution)/shard_map/ij,bjk->bik/dot_general | solution.py:66
  67.0 1.9 %fusion.35 = f32[2,256,512]{2,1,0:T(8,128)S(1)} fusion(f32[512,256,1]{1,0,2:T(8,128)S(1)} %bitcast.295, f32[1,256,256]{1,2,0:T(8,128)S(1)} %get-tuple-element.133, f32[1,256,256]{1,2,0:T(8,128)S(1)} %get-tuple-element.132), kind=kOutput, calls=%fused_computation.73 | convolution fusion | flops 805437440 | bytes 2097152 | tf_op jit(solution)/shard_map/bij,kj->bik/dot_general | solution.py:72
  76.7 1.4 %collective-permute-start.5 = (f32[2,1,1,256,256]{4,3,0,2,1:T(8,128)}, f32[2,1,1,256,256]{4,3,0,2,1:T(8,128)S(1)}, u32[]{:S(2)}, u32[]{:S(2)}) collective-permute-start(f32[2,1,1,256,256]{4,3,0,2,1:T(8,128)} %get-tuple-element.115), channel_id=1, source_target_pairs={{0,8},{8,16},{16,24},{24,0},{1,9},{9,17},{17,25},{25,1},{2,10},{10... | collective-permute-start | bytes 1572872 | tf_op jit(solution)/shard_map/ppermute | solution.py:239
  78.1 1.5 %collective-permute-start.6 = (f32[2,1,1,256,256]{4,3,1,2,0:T(8,128)S(1)}, f32[2,1,1,256,256]{4,3,1,2,0:T(8,128)S(1)}, u32[]{:S(2)}, u32[]{:S(2)}) collective-permute-start(f32[2,1,1,256,256]{4,3,1,2,0:T(8,128)S(1)} %get-tuple-element.112), channel_id=1, source_target_pairs={{0,24},{8,0},{16,8},{24,16},{1,25},{9,1},{17,9},{25,17},{2,26},{10... | collective-permute-start | bytes 1572872 | tf_op jit(solution)/shard_map/ppermute | solution.py:239
  79.6 1.5 %collective-permute-start.4 = (f32[2,1,1,256,256]{4,3,0,2,1:T(8,128)S(1)}, f32[2,1,1,256,256]{4,3,0,2,1:T(8,128)S(1)}, u32[]{:S(2)}, u32[]{:S(2)}) collective-permute-start(f32[2,1,1,256,256]{4,3,0,2,1:T(8,128)S(1)} %get-tuple-element.114), channel_id=1, source_target_pairs={{0,16},{8,24},{16,0},{24,8},{1,17},{9,25},{17,1},{25,9},{2,18},{10... | collective-permute-start | bytes 1572872 | tf_op jit(solution)/shard_map/ppermute | solution.py:239
  81.8 10.9 %collective-permute-done.5 = f32[2,1,1,256,256]{4,3,0,2,1:T(8,128)S(1)} collective-permute-done((f32[2,1,1,256,256]{4,3,0,2,1:T(8,128)}, f32[2,1,1,256,256]{4,3,0,2,1:T(8,128)S(1)}, u32[]{:S(2)}, u32[]{:S(2)}) %collective-permute-start.5) | collective-permute-done | bytes 524320 | tf_op jit(solution)/shard_map/ppermute | solution.py:239
  92.7 9.8 %collective-permute-done.6 = f32[2,1,1,256,256]{4,3,1,2,0:T(8,128)S(1)} collective-permute-done((f32[2,1,1,256,256]{4,3,1,2,0:T(8,128)S(1)}, f32[2,1,1,256,256]{4,3,1,2,0:T(8,128)S(1)}, u32[]{:S(2)}, u32[]{:S(2)}) %collective-permute-start.6) | collective-permute-done | bytes 524320 | tf_op jit(solution)/shard_map/ppermute | solution.py:239
  102.4 2.1 %fusion.2 = f32[2,1,512,512]{3,2,0,1:T(8,128)S(1)} fusion(f32[2,1,512,512]{3,2,0,1:T(8,128)S(1)} %pad_dynamic-slice_fusion.3, s32[]{:T(128)S(6)} %select_n.425, s32[]{:T(128)S(6)} %select_n.426, f32[2,1,256,256]{3,2,0,1:T(8,128)S(1)} %bitcast.309, s32[]{:T(128)S(6)} %select_n.429, s32[]{:T(128)S(6)} %select_n.430, f32[2,1,256,256]{3,2,0,1:T(8,128)S(1)} %bitcast.307, ...), kind=kLoop, calls=%fused_computation.14 | loop fusion | flops 1572864 | bytes 5767192 | tf_op jit(solution)/shard_map/add | solution.py:241
  104.6 1.9 %collective-permute-start.7 = (f32[2,1,512,128]{3,2,0,1:T(8,128)S(1)}, f32[2,1,512,128]{3,2,0,1:T(8,128)S(1)}, u32[]{:S(2)}, u32[]{:S(2)}) collective-permute-start(f32[2,1,512,128]{3,2,0,1:T(8,128)S(1)} %get-tuple-element.111), channel_id=1, source_target_pairs={{0,1},{2,3},{4,5},{6,7},{8,9},{10,11},{12,13},{14,15},{16,17},{18,... | collective-permute-start | bytes 1572872 | tf_op jit(solution)/shard_map/ppermute | solution.py:15
  106.6 1.3 %collective-permute-start.8 = (f32[2,1,512,128]{3,2,0,1:T(8,128)S(1)}, f32[2,1,512,128]{3,2,0,1:T(8,128)S(1)}, u32[]{:S(2)}, u32[]{:S(2)}) collective-permute-start(f32[2,1,512,128]{3,2,0,1:T(8,128)S(1)} %get-tuple-element.110), channel_id=1, source_target_pairs={{1,0},{3,2},{5,4},{7,6},{9,8},{11,10},{13,12},{15,14},{17,16},{19,... | collective-permute-start | bytes 1572872 | tf_op jit(solution)/shard_map/ppermute | solution.py:15
  108.2 2.2 %collective-permute-done.8 = f32[2,1,512,128]{3,2,0,1:T(8,128)S(1)} collective-permute-done((f32[2,1,512,128]{3,2,0,1:T(8,128)S(1)}, f32[2,1,512,128]{3,2,0,1:T(8,128)S(1)}, u32[]{:S(2)}, u32[]{:S(2)}) %collective-permute-start.8) | collective-permute-done | bytes 524320 | tf_op jit(solution)/shard_map/ppermute | solution.py:15
  110.5 3.6 %collective-permute-start.9 = (f32[2,1,128,256]{3,2,0,1:T(8,128)S(1)}, f32[2,1,128,256]{3,2,0,1:T(8,128)S(1)}, u32[]{:S(2)}, u32[]{:S(2)}) collective-permute-start(f32[2,1,128,256]{3,2,0,1:T(8,128)S(1)} %get-tuple-element.123), channel_id=1, source_target_pairs={{0,2},{2,4},{4,6},{1,3},{3,5},{5,7},{8,10},{10,12},{12,14},{9,11},... | collective-permute-start | bytes 786440 | tf_op jit(solution)/shard_map/ppermute | solution.py:15
  114.1 1.3 %collective-permute-start.10 = (f32[2,1,128,256]{3,2,0,1:T(8,128)S(1)}, f32[2,1,128,256]{3,2,0,1:T(8,128)S(1)}, u32[]{:S(2)}, u32[]{:S(2)}) collective-permute-start(f32[2,1,128,256]{3,2,0,1:T(8,128)S(1)} %get-tuple-element.122), channel_id=1, source_target_pairs={{2,0},{4,2},{6,4},{3,1},{5,3},{7,5},{10,8},{12,10},{14,12},{11,9},... | collective-permute-start | bytes 786440 | tf_op jit(solution)/shard_map/ppermute | solution.py:15
  115.5 4.5 %collective-permute-done.9 = f32[2,1,128,256]{3,2,0,1:T(8,128)S(1)} collective-permute-done((f32[2,1,128,256]{3,2,0,1:T(8,128)S(1)}, f32[2,1,128,256]{3,2,0,1:T(8,128)S(1)}, u32[]{:S(2)}, u32[]{:S(2)}) %collective-permute-start.9) | collective-permute-done | bytes 262176 | tf_op jit(solution)/shard_map/ppermute | solution.py:15
  120.0 4.1 %collective-permute-done.10 = f32[2,1,128,256]{3,2,0,1:T(8,128)S(1)} collective-permute-done((f32[2,1,128,256]{3,2,0,1:T(8,128)S(1)}, f32[2,1,128,256]{3,2,0,1:T(8,128)S(1)}, u32[]{:S(2)}, u32[]{:S(2)}) %collective-permute-start.10) | collective-permute-done | bytes 262176 | tf_op jit(solution)/shard_map/ppermute | solution.py:15
  (90 shorter events, 25.6 us)
Async XLA Ops:
  0.6 31.4 %copy-start = (f32[1,1,4,256,256]{4,3,2,1,0:T(8,128)S(1)}, f32[1,1,4,256,256]{4,3,2,1,0:T(8,128)}, u32[]{:S(2)}) copy-start(f32[1,1,4,256,256]{4,3,2,1,0:T(8,128)} %param.16) | copy-start | bytes 3145732
  0.6 9.5 %copy-start.7 = (s32[1,1,4,2]{2,3,1,0:T(2,128)S(1)}, s32[1,1,4,2]{2,3,1,0:T(2,128)}, u32[]{:S(2)}) copy-start(s32[1,1,4,2]{2,3,1,0:T(2,128)} %param.17) | copy-start | bytes 100
  2.8 13.3 %collective-permute-start = (f32[2,1,128,256]{3,2,1,0:T(8,128)S(1)}, f32[2,1,128,256]{3,2,1,0:T(8,128)S(1)}, u32[]{:S(2)}, u32[]{:S(2)}) collective-permute-start(f32[2,1,128,256]{3,2,1,0:T(8,128)S(1)} %get-tuple-element.155), channel_id=1, source_target_pairs={{0,2},{2,4},{4,6},{1,3},{3,5},{5,7},{8,10},{10,12},{12,14},{9,11},... | collective-permute-start | bytes 786440 | tf_op jit(solution)/shard_map/ppermute | solution.py:28
  7.7 9.7 %collective-permute-start.1 = (f32[2,1,128,256]{3,2,1,0:T(8,128)S(1)}, f32[2,1,128,256]{3,2,1,0:T(8,128)S(1)}, u32[]{:S(2)}, u32[]{:S(2)}) collective-permute-start(f32[2,1,128,256]{3,2,1,0:T(8,128)S(1)} %get-tuple-element.156), channel_id=1, source_target_pairs={{2,0},{4,2},{6,4},{3,1},{5,3},{7,5},{10,8},{12,10},{14,12},{11,9},... | collective-permute-start | bytes 786440 | tf_op jit(solution)/shard_map/ppermute | solution.py:31
  18.5 5.4 %collective-permute-start.2 = (f32[2,1,512,128]{3,2,1,0:T(8,128)}, f32[2,1,512,128]{3,2,1,0:T(8,128)}, u32[]{:S(2)}, u32[]{:S(2)}) collective-permute-start(f32[2,1,512,128]{3,2,1,0:T(8,128)} %get-tuple-element.140), channel_id=1, source_target_pairs={{0,1},{2,3},{4,5},{6,7},{8,9},{10,11},{12,13},{14,15},{16,17},{18,... | collective-permute-start | bytes 1572872 | tf_op jit(solution)/shard_map/ppermute | solution.py:28
  21.7 4.0 %collective-permute-start.3 = (f32[2,1,512,128]{3,2,1,0:T(8,128)}, f32[2,1,512,128]{3,2,1,0:T(8,128)S(1)}, u32[]{:S(2)}, u32[]{:S(2)}) collective-permute-start(f32[2,1,512,128]{3,2,1,0:T(8,128)} %get-tuple-element.141), channel_id=1, source_target_pairs={{1,0},{3,2},{5,4},{7,6},{9,8},{11,10},{13,12},{15,14},{17,16},{19,... | collective-permute-start | bytes 1572872 | tf_op jit(solution)/shard_map/ppermute | solution.py:31
  23.0 2.9 %copy-start.2 = (f32[2,256,256]{2,1,0:T(8,128)}, f32[2,256,256]{2,1,0:T(8,128)S(1)}, u32[]{:S(2)}) copy-start(f32[2,256,256]{2,1,0:T(8,128)S(1)} %maximum_multiply_fusion.1) | copy-start | bytes 1572868
  28.2 29.4 %all-to-all-start = ((f32[2,1,4,256,256]{4,3,0,1,2:T(8,128)}), f32[2,1,4,256,256]{4,3,0,1,2:T(8,128)S(1)}, u32[]{:S(2)}, u32[]{:S(2)}) async-start(f32[2,1,4,256,256]{4,3,0,1,2:T(8,128)} %pad_maximum_fusion), calls=%async_computation | async-start | bytes 4194304 | tf_op jit(solution)/shard_map/all_to_all | solution.py:220
  57.6 1.0 copy-start.6
  64.6 1.2 copy-start.3
  66.9 2.0 %copy-start.5 = (f32[1,1,1,256,256]{3,4,2,1,0:T(8,128)S(1)}, f32[1,1,1,256,256]{3,4,2,1,0:T(8,128)}, u32[]{:S(2)}) copy-start(f32[1,1,1,256,256]{3,4,2,1,0:T(8,128)} %copy.118) | copy-start | bytes 786436
  67.0 2.0 %copy-start.4 = (f32[2,256,256]{2,1,0:T(8,128)S(1)}, f32[2,256,256]{2,1,0:T(8,128)}, u32[]{:S(2)}) copy-start(f32[2,256,256]{2,1,0:T(8,128)} %copy.119) | copy-start | bytes 1572868
  76.7 16.0 %collective-permute-start.5 = (f32[2,1,1,256,256]{4,3,0,2,1:T(8,128)}, f32[2,1,1,256,256]{4,3,0,2,1:T(8,128)S(1)}, u32[]{:S(2)}, u32[]{:S(2)}) collective-permute-start(f32[2,1,1,256,256]{4,3,0,2,1:T(8,128)} %get-tuple-element.115), channel_id=1, source_target_pairs={{0,8},{8,16},{16,24},{24,0},{1,9},{9,17},{17,25},{25,1},{2,10},{10... | collective-permute-start | bytes 1572872 | tf_op jit(solution)/shard_map/ppermute | solution.py:239
  78.1 24.3 %collective-permute-start.6 = (f32[2,1,1,256,256]{4,3,1,2,0:T(8,128)S(1)}, f32[2,1,1,256,256]{4,3,1,2,0:T(8,128)S(1)}, u32[]{:S(2)}, u32[]{:S(2)}) collective-permute-start(f32[2,1,1,256,256]{4,3,1,2,0:T(8,128)S(1)} %get-tuple-element.112), channel_id=1, source_target_pairs={{0,24},{8,0},{16,8},{24,16},{1,25},{9,1},{17,9},{25,17},{2,26},{10... | collective-permute-start | bytes 1572872 | tf_op jit(solution)/shard_map/ppermute | solution.py:239
  79.6 22.8 %collective-permute-start.4 = (f32[2,1,1,256,256]{4,3,0,2,1:T(8,128)S(1)}, f32[2,1,1,256,256]{4,3,0,2,1:T(8,128)S(1)}, u32[]{:S(2)}, u32[]{:S(2)}) collective-permute-start(f32[2,1,1,256,256]{4,3,0,2,1:T(8,128)S(1)} %get-tuple-element.114), channel_id=1, source_target_pairs={{0,16},{8,24},{16,0},{24,8},{1,17},{9,25},{17,1},{25,9},{2,18},{10... | collective-permute-start | bytes 1572872 | tf_op jit(solution)/shard_map/ppermute | solution.py:239
  104.6 3.4 %collective-permute-start.7 = (f32[2,1,512,128]{3,2,0,1:T(8,128)S(1)}, f32[2,1,512,128]{3,2,0,1:T(8,128)S(1)}, u32[]{:S(2)}, u32[]{:S(2)}) collective-permute-start(f32[2,1,512,128]{3,2,0,1:T(8,128)S(1)} %get-tuple-element.111), channel_id=1, source_target_pairs={{0,1},{2,3},{4,5},{6,7},{8,9},{10,11},{12,13},{14,15},{16,17},{18,... | collective-permute-start | bytes 1572872 | tf_op jit(solution)/shard_map/ppermute | solution.py:15
  106.6 3.8 %collective-permute-start.8 = (f32[2,1,512,128]{3,2,0,1:T(8,128)S(1)}, f32[2,1,512,128]{3,2,0,1:T(8,128)S(1)}, u32[]{:S(2)}, u32[]{:S(2)}) collective-permute-start(f32[2,1,512,128]{3,2,0,1:T(8,128)S(1)} %get-tuple-element.110), channel_id=1, source_target_pairs={{1,0},{3,2},{5,4},{7,6},{9,8},{11,10},{13,12},{15,14},{17,16},{19,... | collective-permute-start | bytes 1572872 | tf_op jit(solution)/shard_map/ppermute | solution.py:15
  110.5 14.5 %copy-start.1 = (f32[1,1,4,256,256]{4,3,2,1,0:T(8,128)S(1)}, f32[1,1,4,256,256]{4,3,2,1,0:T(8,128)}, u32[]{:S(2)}) copy-start(f32[1,1,4,256,256]{4,3,2,1,0:T(8,128)} %param.16) | copy-start | bytes 3145732
  110.5 9.4 %collective-permute-start.9 = (f32[2,1,128,256]{3,2,0,1:T(8,128)S(1)}, f32[2,1,128,256]{3,2,0,1:T(8,128)S(1)}, u32[]{:S(2)}, u32[]{:S(2)}) collective-permute-start(f32[2,1,128,256]{3,2,0,1:T(8,128)S(1)} %get-tuple-element.123), channel_id=1, source_target_pairs={{0,2},{2,4},{4,6},{1,3},{3,5},{5,7},{8,10},{10,12},{12,14},{9,11},... | collective-permute-start | bytes 786440 | tf_op jit(solution)/shard_map/ppermute | solution.py:15
  114.1 10.0 %collective-permute-start.10 = (f32[2,1,128,256]{3,2,0,1:T(8,128)S(1)}, f32[2,1,128,256]{3,2,0,1:T(8,128)S(1)}, u32[]{:S(2)}, u32[]{:S(2)}) collective-permute-start(f32[2,1,128,256]{3,2,0,1:T(8,128)S(1)} %get-tuple-element.122), channel_id=1, source_target_pairs={{2,0},{4,2},{6,4},{3,1},{5,3},{7,5},{10,8},{12,10},{14,12},{11,9},... | collective-permute-start | bytes 786440 | tf_op jit(solution)/shard_map/ppermute | solution.py:15
